TPU v7x, 32 devices: a whole 2x2x4 slice. The times are simulated.
32 devices in a mesh: fh: 2 (over y), wa: 4 (over x, core), ha: 4 (over z).
Axes of the slice: x: 2, y: 2, z: 4, core: 2. Of those that a mesh axis runs over, the one named last changes fastest.
Arguments:
- queries: bfloat16 [2, 4, 384, 1536], P('fh', 'wa', None, 'ha'), may hold values from -6 to 6
- key_states: bfloat16 [2, 4, 384, 1536], P('fh', 'wa', None, 'ha'), may hold values from -6 to 6
- value_states: bfloat16 [2, 4, 384, 1536], P('fh', 'wa', None, 'ha'), may hold values from -6 to 6
- valid_mask: int32 [2, 4, 384], P('fh', 'wa'), may hold values from 0 to 1, as said below
- out_weight: bfloat16 [1536, 3072], P('ha'), may hold values from -0.15625 to 0.15625
- out_cotangent: bfloat16 [2, 4, 384, 3072], P('fh', 'wa', 'ha'), may hold values from -6 to 6
Outputs:
- layer_out: bfloat16 [2, 4, 384, 3072], P('fh', 'wa', 'ha')
- grad_queries: bfloat16 [2, 4, 384, 1536], P('fh', 'wa', None, 'ha')
- grad_keys: bfloat16 [2, 4, 384, 1536], P('fh', 'wa', None, 'ha')
- grad_values: bfloat16 [2, 4, 384, 1536], P('fh', 'wa', None, 'ha')
- grad_weight: float32 [3072, 1536], P(('fh', 'wa'), 'ha')
Inputs may be any that keep to these rules, and one draw needn't show every extreme that they name: `valid_mask`: within each tile of 384 tokens the valid tokens come first, and at least half of the tile is valid.
All inputs are finite; a program needn't handle non-finite values.
Results may differ from a plain program's by a relative error of at most 0.015.
Values may be sent and summed in bfloat16 or wider, within the bound.
No kernel may reach another device: no remote copies, remote signals or barrier semaphores. Data moves between devices by JAX's collectives and lax.ppermute only.
A program may use at most 128 MiB of HBM per device.

v0:
```python
import jax
import jax.numpy as jnp
from jax import lax
from jax.sharding import PartitionSpec as P

HD = 128


masked_score = -1e30


def extended_2(block, sides, width):
    for axis, dim in sides:
        count = lax.axis_size(axis)
        forward = [(i, i + 1) for i in range(count - 1)]
        backward = [(target, source) for source, target in forward]
        low = lax.ppermute(
            lax.slice_in_dim(block, block.shape[dim] - width, None, axis=dim), axis, forward
        )
        high = lax.ppermute(lax.slice_in_dim(block, 0, width, axis=dim), axis, backward)
        block = jnp.concatenate([low, block, high], axis=dim)
    return block


def shifted(value, axis, steps):
    count = lax.axis_size(axis)
    first, last = (max(0, -steps), min(count, count - steps))
    return lax.ppermute(value, axis, [(source, source + steps) for source in range(first, last)])


def window(extended):
    return extended.reshape((9 * extended.shape[2],) + extended.shape[3:])


def head_cut(matrix, head):
    return lax.dynamic_slice_in_dim(matrix, head * HD, HD, 1)


def contract_last(left, right):
    return lax.dot_general(
        left, right, (((1,), (1,)), ((), ())), preferred_element_type=jnp.float32
    )


def contract_first(left, right):
    return lax.dot_general(
        left, right, (((0,), (0,)), ((), ())), preferred_element_type=jnp.float32
    )


def body(queries, key_states, value_states, valid_mask, out_weight, out_cotangent):
    tile_rows, tile_columns, tile_tokens, features = queries.shape
    head_count = features // HD
    head_ids = jnp.arange(head_count, dtype=jnp.int32)
    score_scale = HD ** (-0.5)
    tile_count = tile_rows * tile_columns
    model_width = out_weight.shape[1]
    tile_ids = jnp.arange(tile_count, dtype=jnp.int32)
    key_flags = valid_mask.astype(jnp.bfloat16)
    key_wide, value_wide, flag_wide = (
        extended_2(key_states, (("fh", 0), ("wa", 1)), 1),
        extended_2(value_states, (("fh", 0), ("wa", 1)), 1),
        extended_2(key_flags, (("fh", 0), ("wa", 1)), 1),
    )

    def head_scores(query_tile, key_block, allowed, head):
        scores = contract_last(head_cut(query_tile, head), head_cut(key_block, head)) * score_scale
        return jnp.where(allowed[None, :], scores, masked_score)

    def forward_tile(tile_index):
        row_index = tile_index // tile_columns
        column_index = tile_index % tile_columns
        key_block = window(key_wide)
        value_block = window(value_wide)
        allowed = window(flag_wide) > 0
        query_tile = queries[row_index, column_index]

        def forward_one_head(head):
            scores = head_scores(query_tile, key_block, allowed, head)
            row_max = jnp.max(scores, axis=1)
            exp_terms = jnp.exp(scores - row_max[:, None])
            row_total = jnp.sum(exp_terms, axis=1)
            soft_probs = (exp_terms / row_total[:, None]).astype(jnp.bfloat16)
            attended_head = jnp.dot(
                soft_probs, head_cut(value_block, head), preferred_element_type=jnp.float32
            )
            return (attended_head.astype(jnp.bfloat16), row_max, row_total)

        attended_heads, row_max, row_total = lax.map(forward_one_head, head_ids)
        return (
            jnp.swapaxes(attended_heads, 0, 1).reshape(tile_tokens, features),
            row_max,
            row_total,
        )

    attended, row_maxes, row_totals = lax.map(forward_tile, tile_ids)
    by_token = jnp.swapaxes(attended, 0, 1)
    share_rows = tile_tokens // lax.axis_size("ha")
    picked = by_token
    mixed_rows = lax.psum_scatter(
        jnp.einsum("rtf,fd->rtd", picked, out_weight, preferred_element_type=jnp.float32),
        "ha",
        scatter_dimension=0,
        tiled=True,
    )
    layer_out = (
        jnp.swapaxes(mixed_rows, 0, 1)
        .astype(jnp.bfloat16)
        .reshape(tile_rows, tile_columns, share_rows, model_width)
    )
    cotangent_all = lax.all_gather(out_cotangent, "ha", axis=2, tiled=True)
    cotangent_flat = cotangent_all.reshape(tile_count * tile_tokens, model_width)
    grad_attended = contract_last(cotangent_flat, out_weight).astype(jnp.bfloat16)
    attended_flat = attended.reshape(tile_count * tile_tokens, features)
    picked = cotangent_flat
    grad_weight = lax.psum_scatter(
        contract_first(picked, attended_flat), ("fh", "wa"), scatter_dimension=0, tiled=True
    )
    row_dot = jnp.sum(
        (grad_attended.astype(jnp.float32) * attended_flat.astype(jnp.float32)).reshape(
            tile_count, tile_tokens, head_count, HD
        ),
        axis=3,
    )
    row_dot_heads = jnp.transpose(row_dot, (0, 2, 1))
    grad_tiles = grad_attended.reshape(tile_count, tile_tokens, features)

    def query_side(tile_index):
        row_index = tile_index // tile_columns
        column_index = tile_index % tile_columns
        key_block = window(key_wide)
        value_block = window(value_wide)
        allowed = window(flag_wide) > 0
        query_tile = queries[row_index, column_index]
        grad_tile = grad_tiles[tile_index]

        def query_one_head(head):
            scores = head_scores(query_tile, key_block, allowed, head)
            weights = (
                jnp.exp(scores - row_maxes[tile_index, head][:, None])
                / row_totals[tile_index, head][:, None]
            )
            soft_probs = weights.astype(jnp.bfloat16)
            grad_head = head_cut(grad_tile, head)
            grad_probs = contract_last(grad_head, head_cut(value_block, head))
            grad_scores = (
                weights * (grad_probs - row_dot_heads[tile_index, head][:, None])
            ).astype(jnp.bfloat16)
            grad_query = (
                jnp.dot(grad_scores, head_cut(key_block, head), preferred_element_type=jnp.float32)
                * score_scale
            ).astype(jnp.bfloat16)
            key_part = contract_first(grad_scores, head_cut(query_tile, head)) * score_scale
            value_part = contract_first(soft_probs, grad_head)
            return (grad_query, jnp.stack((key_part, value_part)))

        grad_heads, parts = lax.map(query_one_head, head_ids)
        both_parts = jnp.transpose(parts, (1, 2, 0, 3)).reshape(2, 3, 3, tile_tokens, features)
        return (
            jnp.swapaxes(grad_heads, 0, 1).reshape(tile_tokens, features),
            both_parts,
            row_index,
            column_index,
        )

    zero_buffer = jnp.zeros(
        (2, tile_rows + 2, tile_columns + 2, tile_tokens, features), jnp.float32
    )

    def backward_tile(partials, tile_index):
        grad_query, both_parts, row_index, column_index = query_side(tile_index)
        partials = partials + both_parts
        return (partials, grad_query)

    partials, grad_rows = lax.scan(backward_tile, zero_buffer, tile_ids)
    from_right = shifted(partials[:, :, 0], "wa", -1)
    from_left = shifted(partials[:, :, tile_columns + 1], "wa", 1)
    middle = partials[:, :, 1 : tile_columns + 1]
    middle = middle.at[:, :, tile_columns - 1].add(from_right)
    middle = middle.at[:, :, 0].add(from_left)
    from_below = shifted(middle[:, 0], "fh", -1)
    from_above = shifted(middle[:, tile_rows + 1], "fh", 1)
    middle = middle[:, 1 : tile_rows + 1]
    middle = middle.at[:, tile_rows - 1].add(from_below)
    middle = middle.at[:, 0].add(from_above)
    grad_keys = middle[0].astype(jnp.bfloat16)
    grad_values = middle[1].astype(jnp.bfloat16)
    grad_queries = grad_rows.reshape(tile_rows, tile_columns, tile_tokens, features)
    return (layer_out, grad_queries, grad_keys, grad_values, grad_weight)


def solution(mesh):
    return jax.shard_map(
        body,
        mesh=mesh,
        in_specs=(
            P("fh", "wa", None, "ha"),
            P("fh", "wa", None, "ha"),
            P("fh", "wa", None, "ha"),
            P("fh", "wa", None),
            P("ha", None),
            P("fh", "wa", "ha", None),
        ),
        out_specs=(
            P("fh", "wa", "ha", None),
            P("fh", "wa", None, "ha"),
            P("fh", "wa", None, "ha"),
            P("fh", "wa", None, "ha"),
            P(("fh", "wa"), "ha"),
        ),
        check_vma=False,
    )
```

profile of v0, /device:TPU:1, one launch (start us, length us, event | category | flops | bytes accessed | tf_op | source)
XLA Modules:
  0.0 300.9 jit_solution(6301146157295228838)
XLA Ops:
  7.2 4.1 %collective-permute-start.4 = (bf16[1,1,384,384]{3,2,1,0:T(8,128)(2,1)}, bf16[1,1,384,384]{3,2,1,0:T(8,128)(2,1)S(1)}, u32[]{:S(2)}, u32[]{:S(2)}) collective-permute-start(bf16[1,1,384,384]{3,2,1,0:T(8,128)(2,1)} %param.19), channel_id=1, source_target_pairs={{0,16},{1,17},{2,18},{3,19},{4,20},{5,21},{6,22},{7,23},{8,24},{9,... | collective-permute-start | bytes 884744 | tf_op jit(solution)/shard_map/ppermute | solution.py:17
  12.7 4.0 %collective-permute-start.8 = (bf16[1,1,384,384]{3,2,1,0:T(8,128)(2,1)}, bf16[1,1,384,384]{3,2,1,0:T(8,128)(2,1)S(1)}, u32[]{:S(2)}, u32[]{:S(2)}) collective-permute-start(bf16[1,1,384,384]{3,2,1,0:T(8,128)(2,1)} %param.20), channel_id=1, source_target_pairs={{0,16},{1,17},{2,18},{3,19},{4,20},{5,21},{6,22},{7,23},{8,24},{9,... | collective-permute-start | bytes 884744 | tf_op jit(solution)/shard_map/ppermute | solution.py:17
  19.1 2.0 collective-permute-done.5
  21.1 4.7 %collective-permute-start.7 = (bf16[3,1,384,384]{3,2,1,0:T(8,128)(2,1)S(1)}, bf16[3,1,384,384]{3,2,1,0:T(8,128)(2,1)}, u32[]{:S(2)}, u32[]{:S(2)}) collective-permute-start(bf16[3,1,384,384]{3,2,1,0:T(8,128)(2,1)S(1)} %constant_dynamic-update-slice_fusion.1), channel_id=1, source_target_pairs={{4,0},{8,4},{12,8},{5,1},{9,5},{13,9},{6,2},{10,6},{14,10},{7,3},{... | collective-permute-start | bytes 2654216 | tf_op jit(solution)/shard_map/ppermute | solution.py:20
  25.8 3.0 %collective-permute-start.6 = (bf16[3,1,384,384]{3,2,1,0:T(8,128)(2,1)S(1)}, bf16[3,1,384,384]{3,2,1,0:T(8,128)(2,1)}, u32[]{:S(2)}, u32[]{:S(2)}) collective-permute-start(bf16[3,1,384,384]{3,2,1,0:T(8,128)(2,1)S(1)} %constant_dynamic-update-slice_fusion.1), channel_id=1, source_target_pairs={{0,4},{4,8},{8,12},{1,5},{5,9},{9,13},{2,6},{6,10},{10,14},{3,7},{... | collective-permute-start | bytes 2654216 | tf_op jit(solution)/shard_map/ppermute | solution.py:17
  29.6 1.7 constant_dynamic-update-slice_fusion.5
  32.0 2.2 collective-permute-start.11
  34.2 3.4 %collective-permute-start.10 = (bf16[3,1,384,384]{3,2,1,0:T(8,128)(2,1)}, bf16[3,1,384,384]{3,2,1,0:T(8,128)(2,1)}, u32[]{:S(2)}, u32[]{:S(2)}) collective-permute-start(bf16[3,1,384,384]{3,2,1,0:T(8,128)(2,1)} %constant_dynamic-update-slice_fusion.4), channel_id=1, source_target_pairs={{0,4},{4,8},{8,12},{1,5},{5,9},{9,13},{2,6},{6,10},{10,14},{3,7},{... | collective-permute-start | bytes 2654216 | tf_op jit(solution)/shard_map/ppermute | solution.py:17
  38.9 3.0 %collective-permute-done.1 = bf16[1,1,384]{2,1,0:T(2,128)(2,1)S(1)} collective-permute-done((bf16[1,1,384]{2,1,0:T(2,128)(2,1)S(1)}, bf16[1,1,384]{2,1,0:T(2,128)(2,1)S(1)}, u32[]{:S(2)}, u32[]{:S(2)}) %collective-permute-start.1) | collective-permute-done | bytes 800 | tf_op jit(solution)/shard_map/ppermute | solution.py:20
  41.9 1.7 collective-permute-start
  44.9 3.6 %collective-permute-start.3 = (bf16[3,1,384]{2,1,0:T(2,128)(2,1)}, bf16[3,1,384]{2,1,0:T(2,128)(2,1)S(1)}, u32[]{:S(2)}, u32[]{:S(2)}) collective-permute-start(bf16[3,1,384]{2,1,0:T(2,128)(2,1)} %pad_maximum_fusion.2), channel_id=1, source_target_pairs={{4,0},{8,4},{12,8},{5,1},{9,5},{13,9},{6,2},{10,6},{14,10},{7,3},{... | collective-permute-start | bytes 6920 | tf_op jit(solution)/shard_map/ppermute | solution.py:20
  48.6 2.6 collective-permute-done.3
  51.2 1.9 collective-permute-start.2
  55.4 3.3 %pad_maximum_fusion = bf16[3,3,384,384]{3,2,1,0:T(8,128)(2,1)} fusion(bf16[3,1,384,384]{3,2,1,0:T(8,128)(2,1)} %collective-permute-done.7, bf16[3,1,384,384]{3,2,1,0:T(8,128)(2,1)S(1)} %constant_dynamic-update-slice_fusion.1, bf16[3,1,384,384]{3,2,1,0:T(8,128)(2,1)} %collective-permute-done.6), kind=kLoop, calls=%fused_computation.57 | loop fusion | flops 2654208 | bytes 5308416 | tf_op jit(solution)/shard_map/concatenate | solution.py:21
  58.7 3.6 %pad_maximum_fusion.1 = bf16[3,3,384,384]{3,2,1,0:T(8,128)(2,1)} fusion(bf16[3,1,384,384]{3,2,1,0:T(8,128)(2,1)} %collective-permute-done.11, bf16[3,1,384,384]{3,2,1,0:T(8,128)(2,1)} %constant_dynamic-update-slice_fusion.4, bf16[3,1,384,384]{3,2,1,0:T(8,128)(2,1)} %collective-permute-done.10), kind=kLoop, calls=%fused_computation.58 | loop fusion | flops 2654208 | bytes 5308416 | tf_op jit(solution)/shard_map/concatenate | solution.py:21
  62.3 27.6 %while.51 = (s32[]{:T(128)}, bf16[3,384,128]{2,1,0:T(8,128)(2,1)S(1)}, f32[3,384]{1,0:T(4,128)}, f32[3,384]{1,0:T(4,128)}, pred[3456]{0:T(1024)(128)(4,1)S(1)}, ...) while((s32[]{:T(128)}, ...), condition=%wide.region_3.4_spmd, body=%wide.region_0.3_spmd.sunk | while | flops 690142464 | bytes 17917008 | solution.py:89
  63.5 2.4 fusion.77
  66.7 2.2 fusion.79
  72.8 2.3 fusion.77
  75.9 2.2 fusion.79
  82.0 2.3 fusion.77
  85.1 2.2 fusion.79
  90.1 15.1 %all-gather.2.cloned.1.call-done = bf16[1,1,384,3072]{3,2,1,0:T(8,128)(2,1)} async-done(((bf16[1,1,96,3072]{3,2,1,0:T(8,128)(2,1)}), bf16[1,1,384,3072]{3,2,1,0:T(8,128)(2,1)}) %all-gather.2.cloned.1.call-update) | async-done | bytes 2359312 | tf_op jit(solution)/shard_map/all_gather | solution.py:111
  105.2 5.2 %convolution_bitcast_fusion.1 = f32[3072,384]{0,1:T(8,128)} fusion(bf16[384,384]{0,1:T(8,128)(2,1)S(1)} %bitcast.112, bf16[1,1,384,3072]{3,2,1,0:T(8,128)(2,1)} %all-gather.2.cloned.1.call-done), kind=kOutput, calls=%fused_computation.50 | convolution fusion | flops 905969664 | bytes 7372800 | tf_op jit(solution)/shard_map/dot_general | solution.py:46
  110.7 3.5 %convolution_bitcast_fusion.2 = f32[384,1,3072]{2,0,1:T(8,128)} fusion(bf16[384,384]{0,1:T(8,128)(2,1)S(1)} %bitcast.113, bf16[384,3072]{1,0:T(8,128)(2,1)S(1)} %copy-done), kind=kOutput, calls=%fused_computation.51 | convolution fusion | flops 905969664 | bytes 7372800 | tf_op jit(solution)/shard_map/rtf,fd->rtd/dot_general | solution.py:101
  114.3 4.2 %convert_multiply_fusion = (f32[384,384]{0,1:T(8,128)S(1)}, bf16[384,384]{0,1:T(8,128)(2,1)}) fusion(bf16[384,3,128]{0,2,1:T(8,128)(2,1)S(1)} %copy.17, bf16[384,3072]{1,0:T(8,128)(2,1)S(1)} %copy-done, bf16[1,1,384,3072]{3,2,1,0:T(8,128)(2,1)} %all-gather.2.cloned.1.call-done), kind=kOutput, calls=%fused_computation.69 | convolution fusion | flops 906559488 | bytes 5898240 | tf_op jit(solution)/shard_map/dot_general | solution.py:40
  118.5 61.3 %while.52 = (s32[]{:T(128)}, bf16[3,384,128]{1,2,0:T(8,128)(2,1)}, f32[3,2,3456,128]{3,2,1,0:T(8,128)}, pred[3456]{0:T(1024)(128)(4,1)S(1)}, s32[3]{0:T(128)S(1)...) while((s32[]{:T(128)}, bf16[3,384,128]{1,2,0:T(8,128)(2,1)}, ...), condition=%wide.region_7.8_spmd, body=%wide.region_6.7_spmd.sunk | while | flops 1710735360 | bytes 38063260 | solution.py:157
  122.5 2.8 fusion.91
  125.2 1.8 convolution_bitcast_fusion.4
  127.0 2.3 fusion.93
  129.3 2.7 fusion.94
  132.0 1.8 fusion.95
  133.8 1.6 copy.35
  135.5 1.5 constant_dynamic-update-slice_fusion.8
  137.0 2.0 fusion.96
  142.9 2.7 fusion.91
  145.6 1.8 convolution_bitcast_fusion.4
  147.4 2.3 fusion.93
  149.7 2.7 fusion.94
  152.4 1.8 fusion.95
  154.2 1.6 copy.35
  157.4 2.0 fusion.96
  163.3 2.7 fusion.91
  166.0 1.8 convolution_bitcast_fusion.4
  167.8 2.3 fusion.93
  170.1 2.7 fusion.94
  172.7 1.8 fusion.95
  174.6 1.6 copy.35
  177.8 2.0 fusion.96
  179.7 19.3 %copy.20 = f32[2,3456,3,128]{3,2,1,0:T(4,128)} copy(f32[2,3456,3,128]{3,1,0,2:T(8,128)} %bitcast.111) | data formatting | bytes 21233664 | tf_op jit(solution)/shard_map/while/body/eval_jaxpr/transpose | solution.py:158
  199.1 17.5 %reshape.277 = f32[2,3,3,384,384]{4,3,2,1,0:T(8,128)} reshape(f32[2,3456,3,128]{3,2,1,0:T(4,128)} %copy.20) | data formatting | bytes 21233664 | tf_op jit(solution)/shard_map/while/body/eval_jaxpr/reshape | solution.py:158
  216.5 3.6 %slice_bitcast_fusion.1 = (f32[2,3,384,384]{3,2,1,0:T(8,128)S(1)}, f32[2,3,384,384]{3,2,1,0:T(8,128)S(1)}) fusion(f32[2,3,3,384,384]{4,3,2,1,0:T(8,128)} %reshape.277), kind=kLoop, calls=%fused_computation.53 | loop fusion | bytes 14155776 | tf_op jit(solution)/shard_map/squeeze | solution.py:176
  220.1 2.3 collective-permute-start.12
  222.4 3.3 %collective-permute-start.13 = (f32[2,3,384,384]{3,2,1,0:T(8,128)S(1)}, f32[2,3,384,384]{3,2,1,0:T(8,128)S(1)}, u32[]{:S(2)}, u32[]{:S(2)}) collective-permute-start(f32[2,3,384,384]{3,2,1,0:T(8,128)S(1)} %get-tuple-element.342), channel_id=1, source_target_pairs={{0,4},{4,8},{8,12},{1,5},{5,9},{9,13},{2,6},{6,10},{10,14},{3,7},{... | collective-permute-start | bytes 10616840 | tf_op jit(solution)/shard_map/ppermute | solution.py:28
  225.7 37.2 %collective-permute-done.12 = f32[2,3,384,384]{3,2,1,0:T(8,128)S(1)} collective-permute-done((f32[2,3,384,384]{3,2,1,0:T(8,128)S(1)}, f32[2,3,384,384]{3,2,1,0:T(8,128)S(1)}, u32[]{:S(2)}, u32[]{:S(2)}) %collective-permute-start.12) | collective-permute-done | bytes 3538976 | tf_op jit(solution)/shard_map/ppermute | solution.py:28
  264.1 2.7 fusion.38
  266.8 1.7 copy-done.2
  270.0 5.1 %collective-permute-start.15 = (f32[2,1,384,384]{3,2,0,1:T(8,128)S(1)}, f32[2,1,384,384]{3,2,0,1:T(8,128)}, u32[]{:S(2)}, u32[]{:S(2)}) collective-permute-start(f32[2,1,384,384]{3,2,0,1:T(8,128)S(1)} %get-tuple-element.344), channel_id=1, source_target_pairs={{0,16},{1,17},{2,18},{3,19},{4,20},{5,21},{6,22},{7,23},{8,24},{9,... | collective-permute-start | bytes 3538952 | tf_op jit(solution)/shard_map/ppermute | solution.py:28
  275.1 1.8 copy.25
  277.0 8.7 %collective-permute-done.14 = f32[2,1,384,384]{3,2,0,1:T(8,128)S(1)} collective-permute-done((f32[2,1,384,384]{3,2,0,1:T(8,128)S(1)}, f32[2,1,384,384]{3,2,0,1:T(8,128)S(1)}, u32[]{:S(2)}, u32[]{:S(2)}) %collective-permute-start.14) | collective-permute-done | bytes 1179680 | tf_op jit(solution)/shard_map/ppermute | solution.py:28
  285.7 1.5 collective-permute-done.15
  287.2 1.9 fusion.47
  290.1 2.1 copy.26
  292.2 2.2 convert_bitcast_fusion
  (82 shorter events, 33.3 us)
Async XLA Ops:
  7.2 103.5 %copy-start = (bf16[384,3072]{1,0:T(8,128)(2,1)S(1)}, bf16[384,3072]{1,0:T(8,128)(2,1)}, u32[]{:S(2)}) copy-start(bf16[384,3072]{1,0:T(8,128)(2,1)} %param.22) | copy-start | bytes 7077892
  7.2 30.4 %copy-start.5 = (s32[1,1,384]{2,1,0:T(1,128)S(1)}, s32[1,1,384]{2,1,0:T(1,128)}, u32[]{:S(2)}) copy-start(s32[1,1,384]{2,1,0:T(1,128)} %param.21) | copy-start | bytes 4612
  7.2 98.0 %all-gather.2.cloned.1.call-start = ((), (), s32[]{:S(2)}) async-start(), calls=%async_computation.3 | async-start | bytes 2949120 | tf_op jit(solution)/shard_map/all_gather | solution.py:111
  7.2 10.8 %collective-permute-start.4 = (bf16[1,1,384,384]{3,2,1,0:T(8,128)(2,1)}, bf16[1,1,384,384]{3,2,1,0:T(8,128)(2,1)S(1)}, u32[]{:S(2)}, u32[]{:S(2)}) collective-permute-start(bf16[1,1,384,384]{3,2,1,0:T(8,128)(2,1)} %param.19), channel_id=1, source_target_pairs={{0,16},{1,17},{2,18},{3,19},{4,20},{5,21},{6,22},{7,23},{8,24},{9,... | collective-permute-start | bytes 884744 | tf_op jit(solution)/shard_map/ppermute | solution.py:17
  11.4 9.7 %collective-permute-start.5 = (bf16[1,1,384,384]{3,2,1,0:T(8,128)(2,1)}, bf16[1,1,384,384]{3,2,1,0:T(8,128)(2,1)S(1)}, u32[]{:S(2)}, u32[]{:S(2)}) collective-permute-start(bf16[1,1,384,384]{3,2,1,0:T(8,128)(2,1)} %param.19), channel_id=1, source_target_pairs={{16,0},{17,1},{18,2},{19,3},{20,4},{21,5},{22,6},{23,7},{24,8},{25... | collective-permute-start | bytes 884744 | tf_op jit(solution)/shard_map/ppermute | solution.py:20
  12.7 16.1 %collective-permute-start.8 = (bf16[1,1,384,384]{3,2,1,0:T(8,128)(2,1)}, bf16[1,1,384,384]{3,2,1,0:T(8,128)(2,1)S(1)}, u32[]{:S(2)}, u32[]{:S(2)}) collective-permute-start(bf16[1,1,384,384]{3,2,1,0:T(8,128)(2,1)} %param.20), channel_id=1, source_target_pairs={{0,16},{1,17},{2,18},{3,19},{4,20},{5,21},{6,22},{7,23},{8,24},{9,... | collective-permute-start | bytes 884744 | tf_op jit(solution)/shard_map/ppermute | solution.py:17
  16.7 14.6 %collective-permute-start.9 = (bf16[1,1,384,384]{3,2,1,0:T(8,128)(2,1)}, bf16[1,1,384,384]{3,2,1,0:T(8,128)(2,1)S(1)}, u32[]{:S(2)}, u32[]{:S(2)}) collective-permute-start(bf16[1,1,384,384]{3,2,1,0:T(8,128)(2,1)} %param.20), channel_id=1, source_target_pairs={{16,0},{17,1},{18,2},{19,3},{20,4},{21,5},{22,6},{23,7},{24,8},{25... | collective-permute-start | bytes 884744 | tf_op jit(solution)/shard_map/ppermute | solution.py:20
  21.1 34.3 %collective-permute-start.7 = (bf16[3,1,384,384]{3,2,1,0:T(8,128)(2,1)S(1)}, bf16[3,1,384,384]{3,2,1,0:T(8,128)(2,1)}, u32[]{:S(2)}, u32[]{:S(2)}) collective-permute-start(bf16[3,1,384,384]{3,2,1,0:T(8,128)(2,1)S(1)} %constant_dynamic-update-slice_fusion.1), channel_id=1, source_target_pairs={{4,0},{8,4},{12,8},{5,1},{9,5},{13,9},{6,2},{10,6},{14,10},{7,3},{... | collective-permute-start | bytes 2654216 | tf_op jit(solution)/shard_map/ppermute | solution.py:20
  25.8 29.6 %collective-permute-start.6 = (bf16[3,1,384,384]{3,2,1,0:T(8,128)(2,1)S(1)}, bf16[3,1,384,384]{3,2,1,0:T(8,128)(2,1)}, u32[]{:S(2)}, u32[]{:S(2)}) collective-permute-start(bf16[3,1,384,384]{3,2,1,0:T(8,128)(2,1)S(1)} %constant_dynamic-update-slice_fusion.1), channel_id=1, source_target_pairs={{0,4},{4,8},{8,12},{1,5},{5,9},{9,13},{2,6},{6,10},{10,14},{3,7},{... | collective-permute-start | bytes 2654216 | tf_op jit(solution)/shard_map/ppermute | solution.py:17
  32.0 26.7 %collective-permute-start.11 = (bf16[3,1,384,384]{3,2,1,0:T(8,128)(2,1)}, bf16[3,1,384,384]{3,2,1,0:T(8,128)(2,1)}, u32[]{:S(2)}, u32[]{:S(2)}) collective-permute-start(bf16[3,1,384,384]{3,2,1,0:T(8,128)(2,1)} %constant_dynamic-update-slice_fusion.4), channel_id=1, source_target_pairs={{4,0},{8,4},{12,8},{5,1},{9,5},{13,9},{6,2},{10,6},{14,10},{7,3},{... | collective-permute-start | bytes 2654216 | tf_op jit(solution)/shard_map/ppermute | solution.py:20
  34.2 24.5 %collective-permute-start.10 = (bf16[3,1,384,384]{3,2,1,0:T(8,128)(2,1)}, bf16[3,1,384,384]{3,2,1,0:T(8,128)(2,1)}, u32[]{:S(2)}, u32[]{:S(2)}) collective-permute-start(bf16[3,1,384,384]{3,2,1,0:T(8,128)(2,1)} %constant_dynamic-update-slice_fusion.4), channel_id=1, source_target_pairs={{0,4},{4,8},{8,12},{1,5},{5,9},{9,13},{2,6},{6,10},{10,14},{3,7},{... | collective-permute-start | bytes 2654216 | tf_op jit(solution)/shard_map/ppermute | solution.py:17
  37.6 4.3 %collective-permute-start.1 = (bf16[1,1,384]{2,1,0:T(2,128)(2,1)S(1)}, bf16[1,1,384]{2,1,0:T(2,128)(2,1)S(1)}, u32[]{:S(2)}, u32[]{:S(2)}) collective-permute-start(bf16[1,1,384]{2,1,0:T(2,128)(2,1)S(1)} %convert_element_type.69), channel_id=1, source_target_pairs={{16,0},{17,1},{18,2},{19,3},{20,4},{21,5},{22,6},{23,7},{24,8},{25... | collective-permute-start | bytes 2312 | tf_op jit(solution)/shard_map/ppermute | solution.py:20
  41.9 2.4 collective-permute-start
  44.3 8.9 %copy-start.3 = (bf16[1,1,384]{2,1,0:T(2,128)(2,1)}, bf16[1,1,384]{2,1,0:T(2,128)(2,1)S(1)}, u32[]{:S(2)}) copy-start(bf16[1,1,384]{2,1,0:T(2,128)(2,1)S(1)} %collective-permute-done) | copy-start | bytes 2308
  44.9 6.3 %collective-permute-start.3 = (bf16[3,1,384]{2,1,0:T(2,128)(2,1)}, bf16[3,1,384]{2,1,0:T(2,128)(2,1)S(1)}, u32[]{:S(2)}, u32[]{:S(2)}) collective-permute-start(bf16[3,1,384]{2,1,0:T(2,128)(2,1)} %pad_maximum_fusion.2), channel_id=1, source_target_pairs={{4,0},{8,4},{12,8},{5,1},{9,5},{13,9},{6,2},{10,6},{14,10},{7,3},{... | collective-permute-start | bytes 6920 | tf_op jit(solution)/shard_map/ppermute | solution.py:20
  51.2 2.0 copy-start.4
  51.2 3.4 %collective-permute-start.2 = (bf16[3,1,384]{2,1,0:T(2,128)(2,1)}, bf16[3,1,384]{2,1,0:T(2,128)(2,1)}, u32[]{:S(2)}, u32[]{:S(2)}) collective-permute-start(bf16[3,1,384]{2,1,0:T(2,128)(2,1)} %pad_maximum_fusion.2), channel_id=1, source_target_pairs={{0,4},{4,8},{8,12},{1,5},{5,9},{9,13},{2,6},{6,10},{10,14},{3,7},{... | collective-permute-start | bytes 6920 | tf_op jit(solution)/shard_map/ppermute | solution.py:17
  53.2 236.9 %reduce-scatter.5.cloned.1.call-start = ((), (), s32[]{:S(2)}) async-start(), calls=%async_computation.4 | async-start | bytes 5308416 | tf_op jit(solution)/shard_map/reduce_scatter | solution.py:116
  110.4 181.7 %reduce-scatter.3.cloned.1.call-start = ((), (), s32[]{:S(2)}) async-start(), calls=%async_computation.2 | async-start | bytes 5898240 | tf_op jit(solution)/shard_map/reduce_scatter | solution.py:100
  220.1 42.8 %collective-permute-start.12 = (f32[2,3,384,384]{3,2,1,0:T(8,128)S(1)}, f32[2,3,384,384]{3,2,1,0:T(8,128)S(1)}, u32[]{:S(2)}, u32[]{:S(2)}) collective-permute-start(f32[2,3,384,384]{3,2,1,0:T(8,128)S(1)} %get-tuple-element.341), channel_id=1, source_target_pairs={{4,0},{8,4},{12,8},{5,1},{9,5},{13,9},{6,2},{10,6},{14,10},{7,3},{... | collective-permute-start | bytes 10616840 | tf_op jit(solution)/shard_map/ppermute | solution.py:28
  222.4 41.7 %collective-permute-start.13 = (f32[2,3,384,384]{3,2,1,0:T(8,128)S(1)}, f32[2,3,384,384]{3,2,1,0:T(8,128)S(1)}, u32[]{:S(2)}, u32[]{:S(2)}) collective-permute-start(f32[2,3,384,384]{3,2,1,0:T(8,128)S(1)} %get-tuple-element.342), channel_id=1, source_target_pairs={{0,4},{4,8},{8,12},{1,5},{5,9},{9,13},{2,6},{6,10},{10,14},{3,7},{... | collective-permute-start | bytes 10616840 | tf_op jit(solution)/shard_map/ppermute | solution.py:28
  266.8 1.7 copy-start.2
  268.7 16.9 %collective-permute-start.14 = (f32[2,1,384,384]{3,2,0,1:T(8,128)S(1)}, f32[2,1,384,384]{3,2,0,1:T(8,128)S(1)}, u32[]{:S(2)}, u32[]{:S(2)}) collective-permute-start(f32[2,1,384,384]{3,2,0,1:T(8,128)S(1)} %get-tuple-element.343), channel_id=1, source_target_pairs={{16,0},{17,1},{18,2},{19,3},{20,4},{21,5},{22,6},{23,7},{24,8},{25... | collective-permute-start | bytes 3538952 | tf_op jit(solution)/shard_map/ppermute | solution.py:28
  270.0 17.2 %collective-permute-start.15 = (f32[2,1,384,384]{3,2,0,1:T(8,128)S(1)}, f32[2,1,384,384]{3,2,0,1:T(8,128)}, u32[]{:S(2)}, u32[]{:S(2)}) collective-permute-start(f32[2,1,384,384]{3,2,0,1:T(8,128)S(1)} %get-tuple-element.344), channel_id=1, source_target_pairs={{0,16},{1,17},{2,18},{3,19},{4,20},{5,21},{6,22},{7,23},{8,24},{9,... | collective-permute-start | bytes 3538952 | tf_op jit(solution)/shard_map/ppermute | solution.py:28
  287.2 7.1 %copy-start.1 = (bf16[384,3072]{1,0:T(8,128)(2,1)S(1)}, bf16[384,3072]{1,0:T(8,128)(2,1)}, u32[]{:S(2)}) copy-start(bf16[384,3072]{1,0:T(8,128)(2,1)} %param.22) | copy-start | bytes 7077892
Sparse Core Ops, SparseCore 0:
  53.3 51.8 all-gather.1
  110.6 52.7 reduce-scatter.4
  165.8 85.2 reduce-scatter.2
where the time goes:
time: 306 us; the launch traced here: 301 us
  local copies, waits for them, and re-layouts  74.9 us (24%)
  waiting for transfers between devices  73.5 us (24%)
  matrix products  60.1 us (20%)
  starting transfers between devices  44.8 us (15%)
  other arithmetic  23.6 us (8%)
  between operations  14.1 us (5%)
  loops' own time  9.95 us (3%)
    ppermute x4, waiting for transfers between devices, shifted(): lax.ppermute(value, axis, [(source, source + steps) for source in range(f...  48.7 us
    dot_general x10, matrix products, contract_last(): lax.dot_general(left, right, (((1,), (1,)), ((), ())), preferred_element_...  26.1 us
    transpose x1, local copies, waits for them, and re-layouts, query_side(): jnp.transpose(parts, (1, 2, 0, 3)).reshape(2, 3, 3, tile_tokens, features)  19.3 us
    ppermute x6, starting transfers between devices, extended_2(): lax.ppermute(lax.slice_in_dim(block, block.shape[dim] - width, None, axis...  18.1 us
    reshape x1, local copies, waits for them, and re-layouts, query_side(): jnp.transpose(parts, (1, 2, 0, 3)).reshape(2, 3, 3, tile_tokens, features)  17.5 us
    dynamic_update_slice x12, local copies, waits for them, and re-layouts, forward_tile(): attended_heads, row_max, row_total = lax.map(forward_one_head, head_ids)  17.4 us
    dot_general x7, matrix products, contract_first(): lax.dot_general(left, right, (((0,), (0,)), ((), ())), preferred_element_...  16 us
    all_gather x1, waiting for transfers between devices, body(): cotangent_all = lax.all_gather(out_cotangent, 'ha', axis=2, tiled=True)  15.1 us
  transfers between devices with their start and end apart: 19, of which 10 were waited for; matrix products, arithmetic and copies ran while one was open for 50% of the time, Pallas kernels for 0%

commit v1 on v0

v1 whole, which is shorter than its diff:
```python
import functools

import jax
import jax.numpy as jnp
from jax import lax
from jax.experimental import pallas as pl
from jax.experimental.pallas import tpu as pltpu
from jax.sharding import PartitionSpec as P

HD = 128
MASKED = -1e30
QCHUNK = 128
FLAG_ROWS = 16


def shift_pairs(count, steps):
    return [(source, source + steps) for source in range(count) if 0 <= source + steps < count]


def shifted(value, axis, steps):
    return lax.ppermute(value, axis, shift_pairs(lax.axis_size(axis), steps))


def cyclic(value, axis, steps):
    count = lax.axis_size(axis)
    return lax.ppermute(value, axis, [(i, (i + steps) % count) for i in range(count)])


def scores_of(mask_ref, q_ref, k_ref, scale):
    q = q_ref[...]
    k = k_ref[...].reshape(-1, HD)
    s = lax.dot_general(q, k, (((1,), (1,)), ((), ())), preferred_element_type=jnp.float32)
    s = s * scale
    return jnp.where(mask_ref[...] > 0, s, MASKED)


def forward_kernel(scale, mask_ref, q_ref, k_ref, v_ref, o_ref):
    s = scores_of(mask_ref, q_ref, k_ref, scale)
    m = jnp.max(s, axis=1, keepdims=True)
    e = jnp.exp(s - m)
    total = jnp.sum(e, axis=1, keepdims=True)
    p = (e / total).astype(jnp.bfloat16)
    v = v_ref[...].reshape(-1, HD)
    o_ref[...] = jnp.dot(p, v, preferred_element_type=jnp.float32).astype(o_ref.dtype)


def backward_kernel(scale, mask_ref, q_ref, k_ref, v_ref, o_ref, do_ref, dq_ref, dkv_ref):
    chunk = pl.program_id(1)
    s = scores_of(mask_ref, q_ref, k_ref, scale)
    m = jnp.max(s, axis=1, keepdims=True)
    e = jnp.exp(s - m)
    total = jnp.sum(e, axis=1, keepdims=True)
    w = e / total
    p = w.astype(jnp.bfloat16)
    do = do_ref[...]
    row_dot = jnp.sum(
        do.astype(jnp.float32) * o_ref[...].astype(jnp.float32), axis=1, keepdims=True
    )
    k = k_ref[...].reshape(-1, HD)
    v = v_ref[...].reshape(-1, HD)
    dp = lax.dot_general(do, v, (((1,), (1,)), ((), ())), preferred_element_type=jnp.float32)
    ds = (w * (dp - row_dot)).astype(jnp.bfloat16)
    dq = jnp.dot(ds, k, preferred_element_type=jnp.float32) * scale
    dq_ref[...] = dq.astype(dq_ref.dtype)
    contract0 = (((0,), (0,)), ((), ()))
    dk = lax.dot_general(ds, q_ref[...], contract0, preferred_element_type=jnp.float32) * scale
    dv = lax.dot_general(p, do, contract0, preferred_element_type=jnp.float32)
    tiles, tokens = k_ref.shape[0], k_ref.shape[1]
    dk = dk.reshape(tiles, tokens, HD)
    dv = dv.reshape(tiles, tokens, HD)

    @pl.when(chunk == 0)
    def _():
        dkv_ref[:, :tokens, :] = dk
        dkv_ref[:, tokens:, :] = dv

    @pl.when(chunk > 0)
    def _():
        dkv_ref[:, :tokens, :] += dk
        dkv_ref[:, tokens:, :] += dv


def attention_forward(mask, queries, window):
    tokens, features = queries.shape
    tiles = window.shape[0]
    heads = features // HD
    chunks = tokens // QCHUNK
    scale = HD ** (-0.5)
    return pl.pallas_call(
        functools.partial(forward_kernel, scale),
        grid=(heads, chunks),
        in_specs=[
            pl.BlockSpec((1, tiles * tokens), lambda h, c: (0, 0)),
            pl.BlockSpec((QCHUNK, HD), lambda h, c: (c, h)),
            pl.BlockSpec((tiles, tokens, HD), lambda h, c: (0, 0, h)),
            pl.BlockSpec((tiles, tokens, HD), lambda h, c: (0, 1, h)),
        ],
        out_specs=pl.BlockSpec((QCHUNK, HD), lambda h, c: (c, h)),
        out_shape=jax.ShapeDtypeStruct((tokens, features), jnp.bfloat16),
        name="tile_attention_forward",
    )(mask, queries, window, window)


def attention_backward(mask, queries, window, attended, grad_attended):
    tokens, features = queries.shape
    tiles = window.shape[0]
    heads = features // HD
    chunks = tokens // QCHUNK
    scale = HD ** (-0.5)
    return pl.pallas_call(
        functools.partial(backward_kernel, scale),
        grid=(heads, chunks),
        in_specs=[
            pl.BlockSpec((1, tiles * tokens), lambda h, c: (0, 0)),
            pl.BlockSpec((QCHUNK, HD), lambda h, c: (c, h)),
            pl.BlockSpec((tiles, tokens, HD), lambda h, c: (0, 0, h)),
            pl.BlockSpec((tiles, tokens, HD), lambda h, c: (0, 1, h)),
            pl.BlockSpec((QCHUNK, HD), lambda h, c: (c, h)),
            pl.BlockSpec((QCHUNK, HD), lambda h, c: (c, h)),
        ],
        out_specs=[
            pl.BlockSpec((QCHUNK, HD), lambda h, c: (c, h)),
            pl.BlockSpec((tiles, 2 * tokens, HD), lambda h, c: (0, 0, h)),
        ],
        out_shape=[
            jax.ShapeDtypeStruct((tokens, features), jnp.bfloat16),
            jax.ShapeDtypeStruct((tiles, 2 * tokens, features), jnp.float32),
        ],
        name="tile_attention_backward",
    )(mask, queries, window, window, attended, grad_attended)


def gather_over(piece, axis):
    count = lax.axis_size(axis)
    me = lax.axis_index(axis)
    received = [piece] + [cyclic(piece, axis, steps) for steps in range(1, count)]
    ordered = jnp.stack([received[(-k) % count] for k in range(count)])
    return jnp.roll(ordered, me, axis=0)


def scatter_sum(full, axis, dim):
    count = lax.axis_size(axis)
    me = lax.axis_index(axis)
    size = full.shape[dim] // count

    def part(index):
        return lax.dynamic_slice_in_dim(full, index * size, size, axis=dim)

    total = part(me).astype(jnp.float32)
    for steps in range(1, count):
        sent = part((me + steps) % count).astype(jnp.bfloat16)
        total = total + cyclic(sent, axis, steps).astype(jnp.float32)
    return total


def body(queries, key_states, value_states, valid_mask, out_weight, out_cotangent):
    tile_rows, tile_columns, tokens, features = queries.shape
    assert tile_rows == 1 and tile_columns == 1
    model_width = out_weight.shape[1]
    q = queries[0, 0]
    flag_rows = jnp.zeros((FLAG_ROWS, features), jnp.bfloat16)
    flag_rows = flag_rows.at[0, :tokens].set(valid_mask[0, 0].astype(jnp.bfloat16))
    packed = jnp.concatenate([key_states[0, 0], value_states[0, 0], flag_rows], axis=0)

    with jax.named_scope("halo_exchange"):
        column = jnp.stack([shifted(packed, "fh", 1), packed, shifted(packed, "fh", -1)])
        window = jnp.concatenate(
            [shifted(column, "wa", 1), column, shifted(column, "wa", -1)], axis=0
        )
    tiles = window.shape[0]
    mask = window[:, 2 * tokens, :tokens].reshape(1, tiles * tokens).astype(jnp.float32)

    with jax.named_scope("cotangent_gather"):
        cot_pieces = gather_over(out_cotangent[0, 0], "ha")
        cot_all = cot_pieces.reshape(-1, model_width)

    with jax.named_scope("attention_forward"):
        attended = attention_forward(mask, q, window)

    with jax.named_scope("output_projection"):
        projected = jnp.dot(attended, out_weight, preferred_element_type=jnp.float32)
        layer_out = scatter_sum(projected, "ha", 0).astype(jnp.bfloat16)

    with jax.named_scope("grad_attended"):
        grad_attended = lax.dot_general(
            cot_all, out_weight, (((1,), (1,)), ((), ())), preferred_element_type=jnp.float32
        ).astype(jnp.bfloat16)

    with jax.named_scope("attention_backward"):
        grad_q, partials = attention_backward(mask, q, window, attended, grad_attended)

    with jax.named_scope("grad_weight"):
        weight_part = lax.dot_general(
            cot_all, attended, (((0,), (0,)), ((), ())), preferred_element_type=jnp.float32
        )
        grad_weight = scatter_sum(scatter_sum(weight_part, "fh", 0), "wa", 0)

    with jax.named_scope("halo_reduction"):
        sides = partials.astype(jnp.bfloat16)
        middle = (
            partials[3:6]
            + shifted(sides[0:3], "wa", -1).astype(jnp.float32)
            + shifted(sides[6:9], "wa", 1).astype(jnp.float32)
        )
        middle_sides = middle.astype(jnp.bfloat16)
        own = (
            middle[1]
            + shifted(middle_sides[0], "fh", -1).astype(jnp.float32)
            + shifted(middle_sides[2], "fh", 1).astype(jnp.float32)
        )
    grad_keys = own[:tokens].astype(jnp.bfloat16)
    grad_values = own[tokens:].astype(jnp.bfloat16)
    expand = lambda x: x[None, None]
    return (
        expand(layer_out),
        expand(grad_q),
        expand(grad_keys),
        expand(grad_values),
        grad_weight,
    )


def solution(mesh):
    return jax.shard_map(
        body,
        mesh=mesh,
        in_specs=(
            P("fh", "wa", None, "ha"),
            P("fh", "wa", None, "ha"),
            P("fh", "wa", None, "ha"),
            P("fh", "wa", None),
            P("ha", None),
            P("fh", "wa", "ha", None),
        ),
        out_specs=(
            P("fh", "wa", "ha", None),
            P("fh", "wa", None, "ha"),
            P("fh", "wa", None, "ha"),
            P("fh", "wa", None, "ha"),
            P(("fh", "wa"), "ha"),
        ),
        check_vma=False,
    )
```

time: 306 us -> 224 us (0.73)
  the two profiles are of different devices: /device:TPU:1 before, /device:TPU:28 now
where the time goes in v1:
time: 224 us; the launch traced here: 223 us
  waiting for transfers between devices  80.5 us (36%)
  starting transfers between devices  62.5 us (28%)
  Pallas kernels  37.1 us (17%)
  local copies, waits for them, and re-layouts  17.9 us (8%)
  other arithmetic  16.9 us (8%)
  matrix products  6.85 us (3%)
    ppermute x10, waiting for transfers between devices, cyclic(): lax.ppermute(value, axis, [(i, (i + steps) % count) for i in range(count)])  66.2 us
    ppermute x8, starting transfers between devices, shifted(): return lax.ppermute(value, axis, shift_pairs(lax.axis_size(axis), steps))  38.8 us
    ppermute x10, starting transfers between devices, cyclic(): lax.ppermute(value, axis, [(i, (i + steps) % count) for i in range(count)])  23.7 us
    pallas_call x1, Pallas kernels, attention_backward(): pl.pallas_call(functools.partial(backward_kernel, scale), grid=(heads, ch...  23.1 us
    ppermute x8, waiting for transfers between devices, shifted(): return lax.ppermute(value, axis, shift_pairs(lax.axis_size(axis), steps))  14.3 us
    pallas_call x1, Pallas kernels, attention_forward(): pl.pallas_call(functools.partial(forward_kernel, scale), grid=(heads, chu...  14 us
    unnamed x30, local copies, waits for them, and re-layouts  12.6 us
    convert_element_type x1, other arithmetic, body(): sides = partials.astype(jnp.bfloat16)  4.67 us
  transfers between devices with their start and end apart: 18, of which 7 were waited for; matrix products, arithmetic and copies ran while one was open for 13% of the time, Pallas kernels for 10%

profile of v1, /device:TPU:28, one launch (start us, length us, event | category | flops | bytes accessed | tf_op | source)
XLA Modules:
  0.0 222.8 jit_solution(16134905522929364796)
XLA Ops:
  0.6 0.0 copy-start
  0.6 0.5 collective-permute-start.7
  1.1 0.3 collective-permute-start.8
  1.5 3.0 %collective-permute-start.9 = (bf16[96,3072]{1,0:T(8,128)(2,1)}, bf16[96,3072]{1,0:T(8,128)(2,1)S(1)}, u32[]{:S(2)}, u32[]{:S(2)}) collective-permute-start(bf16[96,3072]{1,0:T(8,128)(2,1)} %bitcast.59), channel_id=1, source_target_pairs={{0,1},{1,2},{2,3},{3,0},{4,5},{5,6},{6,7},{7,4},{8,9},{9,10},{10,1... | collective-permute-start | bytes 1769480 | tf_op jit(solution)/shard_map/cotangent_gather/ppermute | solution.py:26
  4.5 0.7 convert_bitcast_fusion
  5.2 2.0 fusion.6
  7.2 1.3 collective-permute-start
  8.5 6.2 %collective-permute-start.1 = (bf16[784,384]{1,0:T(8,128)(2,1)}, bf16[784,384]{1,0:T(8,128)(2,1)}, u32[]{:S(2)}, u32[]{:S(2)}) collective-permute-start(bf16[784,384]{1,0:T(8,128)(2,1)} %get-tuple-element.34), channel_id=1, source_target_pairs={{16,0},{17,1},{18,2},{19,3},{20,4},{21,5},{22,6},{23,7},{24,8},{25... | collective-permute-start | bytes 1806344 | tf_op jit(solution)/shard_map/halo_exchange/ppermute | solution.py:21
  14.7 1.2 bitcast_dynamic-update-slice_fusion.6
  15.8 3.3 %collective-permute-done.7 = bf16[96,3072]{1,0:T(8,128)(2,1)} collective-permute-done((bf16[96,3072]{1,0:T(8,128)(2,1)}, bf16[96,3072]{1,0:T(8,128)(2,1)}, u32[]{:S(2)}, u32[]{:S(2)}) %collective-permute-start.7) | collective-permute-done | bytes 589856 | tf_op jit(solution)/shard_map/cotangent_gather/ppermute | solution.py:26
  19.1 1.1 bitcast_dynamic-update-slice_fusion.4
  20.2 23.1 %collective-permute-done.8 = bf16[96,3072]{1,0:T(8,128)(2,1)} collective-permute-done((bf16[96,3072]{1,0:T(8,128)(2,1)}, bf16[96,3072]{1,0:T(8,128)(2,1)}, u32[]{:S(2)}, u32[]{:S(2)}) %collective-permute-start.8) | collective-permute-done | bytes 589856 | tf_op jit(solution)/shard_map/cotangent_gather/ppermute | solution.py:26
  43.4 1.1 bitcast_dynamic-update-slice_fusion.2
  44.5 0.0 collective-permute-done.9
  44.6 1.1 bitcast_dynamic-update-slice_fusion.5
  45.7 0.0 collective-permute-done.1
  45.7 1.5 pad_maximum_fusion
  47.2 1.4 collective-permute-start.2
  48.6 1.1 bitcast_dynamic-update-slice_fusion.3
  49.7 1.3 collective-permute-start.3
  51.1 0.2 constant_dynamic-slice_fusion
  51.3 2.1 convolution_convert_fusion.do_ref
  53.4 0.2 constant_dynamic-update-slice_fusion.4
  53.6 1.2 constant_dynamic-update-slice_fusion.3
  54.8 0.1 constant_dynamic-update-slice_fusion.2
  54.9 1.2 constant_dynamic-update-slice_fusion.1
  56.1 0.9 collective-permute-done.3
  57.0 0.4 constant_dynamic-update-slice_fusion.k_ref.v_ref
  57.3 2.3 %copy-done.1 = bf16[9,784,384]{2,1,0:T(8,128)(2,1)} copy-done((bf16[9,784,384]{2,1,0:T(8,128)(2,1)}, bf16[9,784,384]{2,1,0:T(8,128)(2,1)S(1)}, u32[]{:S(2)}) %copy-start.1) | copy-done | bytes 5419032
  59.7 0.6 convert.6.mask_ref
  60.3 14.0 %tile_attention_forward.1.o_ref = bf16[384,384]{1,0:T(8,128)(2,1)} custom-call(f32[1,3456]{1,0:T(1,128)} %convert.6.mask_ref, bf16[384,384]{1,0:T(8,128)(2,1)} %bitcast.60, bf16[9,784,384]{2,1,0:T(8,128)(2,1)} %copy-done.1, bf16[9,784,384]{2,1,0:T(8,128)(2,1)} %copy-done.1), custom_call_target="tpu_custom_call" | custom-call | tf_op jit(solution)/shard_map/attention_forward/tile_attention_forward/pallas_call | solution.py:89
  74.3 3.3 %fusion.10 = f32[3072,384]{1,0:T(8,128)S(1)} fusion(bf16[384,3072]{1,0:T(8,128)(2,1)} %bitcast.56, bf16[384,384]{1,0:T(8,128)(2,1)} %tile_attention_forward.1.o_ref), kind=kOutput, calls=%fused_computation.44 | convolution fusion | flops 905969664 | bytes 7372800 | tf_op jit(solution)/shard_map/grad_weight/dot_general | solution.py:193
  77.7 2.1 copy-done.2
  79.7 1.2 dynamic-slice_convert_fusion
  81.0 0.5 collective-permute-start.14
  81.5 23.1 %tile_attention_backward.1 = (bf16[384,384]{1,0:T(8,128)(2,1)}, f32[9,768,384]{2,1,0:T(8,128)}) custom-call(f32[1,3456]{1,0:T(1,128)} %convert.6.mask_ref, bf16[384,384]{1,0:T(8,128)(2,1)} %bitcast.61, bf16[9,784,384]{2,1,0:T(8,128)(2,1)} %copy-done.1, bf16[9,784,384]{2,1,0:T(8,128)(2,1)} %copy-done.1, bf16[384,384]{1,0:T(8,128)(2,1)} %tile_attention_forward.1.o_ref, ...), custom_call_target="tpu_custom_call" | custom-call | tf_op jit(solution)/shard_map/attention_backward/tile_attention_backward/pallas_call | solution.py:110
  104.6 4.7 %convert_element_type.96 = bf16[9,768,384]{2,1,0:T(8,128)(2,1)S(1)} convert(f32[9,768,384]{2,1,0:T(8,128)} %get-tuple-element.20) | non-fusion elementwise | flops 2654208 | bytes 15925248 | tf_op jit(solution)/shard_map/halo_reduction/convert_element_type | solution.py:199
  109.3 0.0 copy-start.4
  109.3 2.2 fusion.8
  111.4 1.3 collective-permute-start.10
  112.7 22.6 %collective-permute-start.11 = (bf16[3,768,384]{2,1,0:T(8,128)(2,1)}, bf16[3,768,384]{2,1,0:T(8,128)(2,1)}, u32[]{:S(2)}, u32[]{:S(2)}) collective-permute-start(bf16[3,768,384]{2,1,0:T(8,128)(2,1)} %get-tuple-element.24), channel_id=1, source_target_pairs={{0,4},{4,8},{8,12},{1,5},{5,9},{9,13},{2,6},{6,10},{10,14},{3,7},{... | collective-permute-start | bytes 5308424 | tf_op jit(solution)/shard_map/halo_reduction/ppermute | solution.py:21
  135.3 1.4 fusion.9
  136.7 0.2 dynamic-slice_convert_fusion.3
  137.0 11.9 %collective-permute-start.4 = (bf16[96,3072]{1,0:T(8,128)(2,1)S(1)}, bf16[96,3072]{1,0:T(8,128)(2,1)S(1)}, u32[]{:S(2)}, u32[]{:S(2)}) collective-permute-start(bf16[96,3072]{1,0:T(8,128)(2,1)S(1)} %get-tuple-element.25), channel_id=1, source_target_pairs={{0,1},{1,2},{2,3},{3,0},{4,5},{5,6},{6,7},{7,4},{8,9},{9,10},{10,1... | collective-permute-start | bytes 1769480 | tf_op jit(solution)/shard_map/output_projection/ppermute | solution.py:26
  148.9 0.7 collective-permute-start.5
  149.6 0.0 collective-permute-done.14
  149.6 0.0 collective-permute-start.6
  149.6 1.5 convert_add_fusion.1
  151.1 0.1 dynamic-slice_convert_fusion.6
  151.2 3.5 %collective-permute-start.15 = (bf16[384,384]{1,0:T(8,128)(2,1)S(1)}, bf16[384,384]{1,0:T(8,128)(2,1)S(1)}, u32[]{:S(2)}, u32[]{:S(2)}) collective-permute-start(bf16[384,384]{1,0:T(8,128)(2,1)S(1)} %get-tuple-element.28), channel_id=1, source_target_pairs={{0,4},{4,8},{8,12},{12,0},{1,5},{5,9},{9,13},{13,1},{2,6},{6,10},{... | collective-permute-start | bytes 884744 | tf_op jit(solution)/shard_map/grad_weight/ppermute | solution.py:26
  154.7 0.0 collective-permute-done.11
  154.7 3.2 %collective-permute-start.16 = (bf16[384,384]{1,0:T(8,128)(2,1)S(1)}, bf16[384,384]{1,0:T(8,128)(2,1)S(1)}, u32[]{:S(2)}, u32[]{:S(2)}) collective-permute-start(bf16[384,384]{1,0:T(8,128)(2,1)S(1)} %get-tuple-element.30), channel_id=1, source_target_pairs={{0,8},{4,12},{8,0},{12,4},{1,9},{5,13},{9,1},{13,5},{2,10},{6,14},... | collective-permute-start | bytes 884744 | tf_op jit(solution)/shard_map/grad_weight/ppermute | solution.py:26
  158.0 3.7 %fusion.7 = (bf16[3,768,384]{2,1,0:T(8,128)(2,1)S(1)}, f32[3,768,384]{2,1,0:T(8,128)S(1)}) fusion(bf16[3,768,384]{2,1,0:T(8,128)(2,1)} %collective-permute-done.11, bf16[3,768,384]{2,1,0:T(8,128)(2,1)} %collective-permute-done.10, f32[9,768,384]{2,1,0:T(8,128)} %get-tuple-element.20), kind=kLoop, calls=%fused_computation.41 | loop fusion | flops 4423680 | bytes 12386304 | tf_op jit(solution)/shard_map/halo_reduction/convert_element_type | solution.py:205
  161.6 0.1 slice_bitcast_fusion.2
  161.8 1.0 collective-permute-done.4
  162.7 38.8 %collective-permute-done.5 = bf16[96,3072]{1,0:T(8,128)(2,1)S(1)} collective-permute-done((bf16[96,3072]{1,0:T(8,128)(2,1)S(1)}, bf16[96,3072]{1,0:T(8,128)(2,1)S(1)}, u32[]{:S(2)}, u32[]{:S(2)}) %collective-permute-start.5) | collective-permute-done | bytes 589856 | tf_op jit(solution)/shard_map/output_projection/ppermute | solution.py:26
  201.5 3.4 %collective-permute-start.12 = (bf16[768,384]{1,0:T(8,128)(2,1)S(1)}, bf16[768,384]{1,0:T(8,128)(2,1)S(1)}, u32[]{:S(2)}, u32[]{:S(2)}) collective-permute-start(bf16[768,384]{1,0:T(8,128)(2,1)S(1)} %get-tuple-element.31), channel_id=1, source_target_pairs={{16,0},{17,1},{18,2},{19,3},{20,4},{21,5},{22,6},{23,7},{24,8},{25... | collective-permute-start | bytes 1769480 | tf_op jit(solution)/shard_map/halo_reduction/ppermute | solution.py:21
  205.0 1.3 collective-permute-start.13
  206.3 1.1 fusion.5
  207.4 0.9 convert_add_fusion.2
  208.3 9.3 %collective-permute-done.12 = bf16[768,384]{1,0:T(8,128)(2,1)S(1)} collective-permute-done((bf16[768,384]{1,0:T(8,128)(2,1)S(1)}, bf16[768,384]{1,0:T(8,128)(2,1)S(1)}, u32[]{:S(2)}, u32[]{:S(2)}) %collective-permute-start.12) | collective-permute-done | bytes 589856 | tf_op jit(solution)/shard_map/halo_reduction/ppermute | solution.py:21
  217.6 4.2 %collective-permute-done.13 = bf16[768,384]{1,0:T(8,128)(2,1)S(1)} collective-permute-done((bf16[768,384]{1,0:T(8,128)(2,1)S(1)}, bf16[768,384]{1,0:T(8,128)(2,1)S(1)}, u32[]{:S(2)}, u32[]{:S(2)}) %collective-permute-start.13) | collective-permute-done | bytes 589856 | tf_op jit(solution)/shard_map/halo_reduction/ppermute | solution.py:21
  221.8 0.2 fusion.3
  222.0 0.9 slice_bitcast_fusion.3
  (29 shorter events, 0.2 us)
Async XLA Ops:
  0.6 50.6 %copy-start = (bf16[384,3072]{1,0:T(8,128)(2,1)S(1)}, bf16[384,3072]{1,0:T(8,128)(2,1)}, u32[]{:S(2)}) copy-start(bf16[384,3072]{1,0:T(8,128)(2,1)} %param.12) | copy-start | bytes 7077892
  0.6 18.5 %collective-permute-start.7 = (bf16[96,3072]{1,0:T(8,128)(2,1)}, bf16[96,3072]{1,0:T(8,128)(2,1)}, u32[]{:S(2)}, u32[]{:S(2)}) collective-permute-start(bf16[96,3072]{1,0:T(8,128)(2,1)} %bitcast.57), channel_id=1, source_target_pairs={{0,3},{1,0},{2,1},{3,2},{4,7},{5,4},{6,5},{7,6},{8,11},{9,8},{10,9... | collective-permute-start | bytes 1769480 | tf_op jit(solution)/shard_map/cotangent_gather/ppermute | solution.py:26
  1.1 42.2 %collective-permute-start.8 = (bf16[96,3072]{1,0:T(8,128)(2,1)}, bf16[96,3072]{1,0:T(8,128)(2,1)}, u32[]{:S(2)}, u32[]{:S(2)}) collective-permute-start(bf16[96,3072]{1,0:T(8,128)(2,1)} %bitcast.58), channel_id=1, source_target_pairs={{0,2},{1,3},{2,0},{3,1},{4,6},{5,7},{6,4},{7,5},{8,10},{9,11},{10,... | collective-permute-start | bytes 1769480 | tf_op jit(solution)/shard_map/cotangent_gather/ppermute | solution.py:26
  1.5 43.0 %collective-permute-start.9 = (bf16[96,3072]{1,0:T(8,128)(2,1)}, bf16[96,3072]{1,0:T(8,128)(2,1)S(1)}, u32[]{:S(2)}, u32[]{:S(2)}) collective-permute-start(bf16[96,3072]{1,0:T(8,128)(2,1)} %bitcast.59), channel_id=1, source_target_pairs={{0,1},{1,2},{2,3},{3,0},{4,5},{5,6},{6,7},{7,4},{8,9},{9,10},{10,1... | collective-permute-start | bytes 1769480 | tf_op jit(solution)/shard_map/cotangent_gather/ppermute | solution.py:26
  7.2 38.5 %collective-permute-start = (bf16[784,384]{1,0:T(8,128)(2,1)}, bf16[784,384]{1,0:T(8,128)(2,1)}, u32[]{:S(2)}, u32[]{:S(2)}) collective-permute-start(bf16[784,384]{1,0:T(8,128)(2,1)} %get-tuple-element.34), channel_id=1, source_target_pairs={{0,16},{1,17},{2,18},{3,19},{4,20},{5,21},{6,22},{7,23},{8,24},{9,... | collective-permute-start | bytes 1806344 | tf_op jit(solution)/shard_map/halo_exchange/ppermute | solution.py:21
  8.5 37.2 %collective-permute-start.1 = (bf16[784,384]{1,0:T(8,128)(2,1)}, bf16[784,384]{1,0:T(8,128)(2,1)}, u32[]{:S(2)}, u32[]{:S(2)}) collective-permute-start(bf16[784,384]{1,0:T(8,128)(2,1)} %get-tuple-element.34), channel_id=1, source_target_pairs={{16,0},{17,1},{18,2},{19,3},{20,4},{21,5},{22,6},{23,7},{24,8},{25... | collective-permute-start | bytes 1806344 | tf_op jit(solution)/shard_map/halo_exchange/ppermute | solution.py:21
  14.7 29.9 %copy-start.5 = (bf16[1,1,96,3072]{3,2,1,0:T(8,128)(2,1)S(1)}, bf16[1,1,96,3072]{3,2,1,0:T(8,128)(2,1)}, u32[]{:S(2)}) copy-start(bf16[1,1,96,3072]{3,2,1,0:T(8,128)(2,1)} %param.13) | copy-start | bytes 1769476
  47.2 6.2 %collective-permute-start.2 = (bf16[3,784,384]{2,1,0:T(8,128)(2,1)S(1)}, bf16[3,784,384]{2,1,0:T(8,128)(2,1)S(1)}, u32[]{:S(2)}, u32[]{:S(2)}) collective-permute-start(bf16[3,784,384]{2,1,0:T(8,128)(2,1)S(1)} %pad_maximum_fusion), channel_id=1, source_target_pairs={{0,4},{4,8},{8,12},{1,5},{5,9},{9,13},{2,6},{6,10},{10,14},{3,7},{... | collective-permute-start | bytes 5419016 | tf_op jit(solution)/shard_map/halo_exchange/ppermute | solution.py:21
  49.7 7.2 %collective-permute-start.3 = (bf16[3,784,384]{2,1,0:T(8,128)(2,1)S(1)}, bf16[3,784,384]{2,1,0:T(8,128)(2,1)S(1)}, u32[]{:S(2)}, u32[]{:S(2)}) collective-permute-start(bf16[3,784,384]{2,1,0:T(8,128)(2,1)S(1)} %pad_maximum_fusion), channel_id=1, source_target_pairs={{4,0},{8,4},{12,8},{5,1},{9,5},{13,9},{6,2},{10,6},{14,10},{7,3},{... | collective-permute-start | bytes 5419016 | tf_op jit(solution)/shard_map/halo_exchange/ppermute | solution.py:21
  51.2 2.2 copy-start.3
  53.4 1.4 copy-start.6
  53.4 1.4 copy-start.7
  57.3 2.3 %copy-start.1 = (bf16[9,784,384]{2,1,0:T(8,128)(2,1)}, bf16[9,784,384]{2,1,0:T(8,128)(2,1)S(1)}, u32[]{:S(2)}) copy-start(bf16[9,784,384]{2,1,0:T(8,128)(2,1)S(1)} %constant_dynamic-update-slice_fusion.k_ref.v_ref) | copy-start | bytes 16257028
  77.6 2.1 copy-start.2
  81.0 68.7 %collective-permute-start.14 = (bf16[1536,384]{1,0:T(8,128)(2,1)}, bf16[1536,384]{1,0:T(8,128)(2,1)}, u32[]{:S(2)}, u32[]{:S(2)}) collective-permute-start(bf16[1536,384]{1,0:T(8,128)(2,1)} %dynamic-slice_convert_fusion), channel_id=1, source_target_pairs={{0,16},{16,0},{1,17},{17,1},{2,18},{18,2},{3,19},{19,3},{4,20},{20... | collective-permute-start | bytes 3538952 | tf_op jit(solution)/shard_map/grad_weight/ppermute | solution.py:26
  109.3 26.1 %copy-start.4 = (bf16[384,384]{1,0:T(8,128)(2,1)S(1)}, bf16[384,384]{1,0:T(8,128)(2,1)}, u32[]{:S(2)}) copy-start(bf16[384,384]{1,0:T(8,128)(2,1)} %tile_attention_forward.1.o_ref) | copy-start | bytes 884740
  109.3 40.4 %slice-start = ((s8[4718592]{0:T(1024)(128)(4,1)}), s8[524288]{0:T(1024)(128)(4,1)S(1)}, s32[]{:S(2)}) async-start(s8[4718592]{0:T(1024)(128)(4,1)} %bitcast.53), calls=%async_computation | async-start | bytes 1048576
  111.4 39.8 %collective-permute-start.10 = (bf16[3,768,384]{2,1,0:T(8,128)(2,1)}, bf16[3,768,384]{2,1,0:T(8,128)(2,1)}, u32[]{:S(2)}, u32[]{:S(2)}) collective-permute-start(bf16[3,768,384]{2,1,0:T(8,128)(2,1)} %get-tuple-element.23), channel_id=1, source_target_pairs={{4,0},{8,4},{12,8},{5,1},{9,5},{13,9},{6,2},{10,6},{14,10},{7,3},{... | collective-permute-start | bytes 5308424 | tf_op jit(solution)/shard_map/halo_reduction/ppermute | solution.py:21
  112.7 42.0 %collective-permute-start.11 = (bf16[3,768,384]{2,1,0:T(8,128)(2,1)}, bf16[3,768,384]{2,1,0:T(8,128)(2,1)}, u32[]{:S(2)}, u32[]{:S(2)}) collective-permute-start(bf16[3,768,384]{2,1,0:T(8,128)(2,1)} %get-tuple-element.24), channel_id=1, source_target_pairs={{0,4},{4,8},{8,12},{1,5},{5,9},{9,13},{2,6},{6,10},{10,14},{3,7},{... | collective-permute-start | bytes 5308424 | tf_op jit(solution)/shard_map/halo_reduction/ppermute | solution.py:21
  135.3 14.3 %slice-start.1 = ((s8[4718592]{0:T(1024)(128)(4,1)}), s8[4194304]{0:T(1024)(128)(4,1)S(1)}, s32[]{:S(2)}) async-start(s8[4718592]{0:T(1024)(128)(4,1)} %bitcast.53), calls=%async_computation.1 | async-start | bytes 8388608
  137.0 25.7 %collective-permute-start.4 = (bf16[96,3072]{1,0:T(8,128)(2,1)S(1)}, bf16[96,3072]{1,0:T(8,128)(2,1)S(1)}, u32[]{:S(2)}, u32[]{:S(2)}) collective-permute-start(bf16[96,3072]{1,0:T(8,128)(2,1)S(1)} %get-tuple-element.25), channel_id=1, source_target_pairs={{0,1},{1,2},{2,3},{3,0},{4,5},{5,6},{6,7},{7,4},{8,9},{9,10},{10,1... | collective-permute-start | bytes 1769480 | tf_op jit(solution)/shard_map/output_projection/ppermute | solution.py:26
  148.9 52.6 %collective-permute-start.5 = (bf16[96,3072]{1,0:T(8,128)(2,1)S(1)}, bf16[96,3072]{1,0:T(8,128)(2,1)S(1)}, u32[]{:S(2)}, u32[]{:S(2)}) collective-permute-start(bf16[96,3072]{1,0:T(8,128)(2,1)S(1)} %get-tuple-element.27), channel_id=1, source_target_pairs={{0,2},{1,3},{2,0},{3,1},{4,6},{5,7},{6,4},{7,5},{8,10},{9,11},{10,... | collective-permute-start | bytes 1769480 | tf_op jit(solution)/shard_map/output_projection/ppermute | solution.py:26
  149.6 55.4 %collective-permute-start.6 = (bf16[96,3072]{1,0:T(8,128)(2,1)S(1)}, bf16[96,3072]{1,0:T(8,128)(2,1)S(1)}, u32[]{:S(2)}, u32[]{:S(2)}) collective-permute-start(bf16[96,3072]{1,0:T(8,128)(2,1)S(1)} %get-tuple-element.26), channel_id=1, source_target_pairs={{0,3},{1,0},{2,1},{3,2},{4,7},{5,4},{6,5},{7,6},{8,11},{9,8},{10,9... | collective-permute-start | bytes 1769480 | tf_op jit(solution)/shard_map/output_projection/ppermute | solution.py:26
  151.2 56.1 %collective-permute-start.15 = (bf16[384,384]{1,0:T(8,128)(2,1)S(1)}, bf16[384,384]{1,0:T(8,128)(2,1)S(1)}, u32[]{:S(2)}, u32[]{:S(2)}) collective-permute-start(bf16[384,384]{1,0:T(8,128)(2,1)S(1)} %get-tuple-element.28), channel_id=1, source_target_pairs={{0,4},{4,8},{8,12},{12,0},{1,5},{5,9},{9,13},{13,1},{2,6},{6,10},{... | collective-permute-start | bytes 884744 | tf_op jit(solution)/shard_map/grad_weight/ppermute | solution.py:26
  154.7 52.7 %collective-permute-start.16 = (bf16[384,384]{1,0:T(8,128)(2,1)S(1)}, bf16[384,384]{1,0:T(8,128)(2,1)S(1)}, u32[]{:S(2)}, u32[]{:S(2)}) collective-permute-start(bf16[384,384]{1,0:T(8,128)(2,1)S(1)} %get-tuple-element.30), channel_id=1, source_target_pairs={{0,8},{4,12},{8,0},{12,4},{1,9},{5,13},{9,1},{13,5},{2,10},{6,14},... | collective-permute-start | bytes 884744 | tf_op jit(solution)/shard_map/grad_weight/ppermute | solution.py:26
  162.7 44.7 %collective-permute-start.17 = (bf16[384,384]{1,0:T(8,128)(2,1)S(1)}, bf16[384,384]{1,0:T(8,128)(2,1)S(1)}, u32[]{:S(2)}, u32[]{:S(2)}) collective-permute-start(bf16[384,384]{1,0:T(8,128)(2,1)S(1)} %get-tuple-element.29), channel_id=1, source_target_pairs={{0,12},{4,0},{8,4},{12,8},{1,13},{5,1},{9,5},{13,9},{2,14},{6,2},{... | collective-permute-start | bytes 884744 | tf_op jit(solution)/shard_map/grad_weight/ppermute | solution.py:26
  201.5 16.1 %collective-permute-start.12 = (bf16[768,384]{1,0:T(8,128)(2,1)S(1)}, bf16[768,384]{1,0:T(8,128)(2,1)S(1)}, u32[]{:S(2)}, u32[]{:S(2)}) collective-permute-start(bf16[768,384]{1,0:T(8,128)(2,1)S(1)} %get-tuple-element.31), channel_id=1, source_target_pairs={{16,0},{17,1},{18,2},{19,3},{20,4},{21,5},{22,6},{23,7},{24,8},{25... | collective-permute-start | bytes 1769480 | tf_op jit(solution)/shard_map/halo_reduction/ppermute | solution.py:21
  205.0 16.8 %collective-permute-start.13 = (bf16[768,384]{1,0:T(8,128)(2,1)S(1)}, bf16[768,384]{1,0:T(8,128)(2,1)S(1)}, u32[]{:S(2)}, u32[]{:S(2)}) collective-permute-start(bf16[768,384]{1,0:T(8,128)(2,1)S(1)} %get-tuple-element.32), channel_id=1, source_target_pairs={{0,16},{1,17},{2,18},{3,19},{4,20},{5,21},{6,22},{7,23},{8,24},{9,... | collective-permute-start | bytes 1769480 | tf_op jit(solution)/shard_map/halo_reduction/ppermute | solution.py:21

commit v2 on v1

--- a/solution.py
+++ b/solution.py
@@ -9,7 +9,8 @@
 
 HD = 128
 MASKED = -1e30
-QCHUNK = 128
+FORWARD_CHUNK = 384
+BACKWARD_CHUNK = 192
 FLAG_ROWS = 16
 
 
@@ -30,8 +31,7 @@
     q = q_ref[...]
     k = k_ref[...].reshape(-1, HD)
     s = lax.dot_general(q, k, (((1,), (1,)), ((), ())), preferred_element_type=jnp.float32)
-    s = s * scale
-    return jnp.where(mask_ref[...] > 0, s, MASKED)
+    return s * scale + mask_ref[...]
 
 
 def forward_kernel(scale, mask_ref, q_ref, k_ref, v_ref, o_ref):
@@ -39,18 +39,18 @@
     m = jnp.max(s, axis=1, keepdims=True)
     e = jnp.exp(s - m)
     total = jnp.sum(e, axis=1, keepdims=True)
-    p = (e / total).astype(jnp.bfloat16)
+    p = (e * (1.0 / total)).astype(jnp.bfloat16)
     v = v_ref[...].reshape(-1, HD)
     o_ref[...] = jnp.dot(p, v, preferred_element_type=jnp.float32).astype(o_ref.dtype)
 
 
-def backward_kernel(scale, mask_ref, q_ref, k_ref, v_ref, o_ref, do_ref, dq_ref, dkv_ref):
+def backward_kernel(scale, mask_ref, q_ref, k_ref, v_ref, o_ref, do_ref, dq_ref, side_ref, mid_ref, acc_ref):
     chunk = pl.program_id(1)
     s = scores_of(mask_ref, q_ref, k_ref, scale)
     m = jnp.max(s, axis=1, keepdims=True)
     e = jnp.exp(s - m)
     total = jnp.sum(e, axis=1, keepdims=True)
-    w = e / total
+    w = e * (1.0 / total)
     p = w.astype(jnp.bfloat16)
     do = do_ref[...]
     row_dot = jnp.sum(
@@ -71,31 +71,38 @@
 
     @pl.when(chunk == 0)
     def _():
-        dkv_ref[:, :tokens, :] = dk
-        dkv_ref[:, tokens:, :] = dv
+        acc_ref[:, :tokens, :] = dk
+        acc_ref[:, tokens:, :] = dv
 
     @pl.when(chunk > 0)
     def _():
-        dkv_ref[:, :tokens, :] += dk
-        dkv_ref[:, tokens:, :] += dv
+        acc_ref[:, :tokens, :] += dk
+        acc_ref[:, tokens:, :] += dv
+
+    @pl.when(chunk == pl.num_programs(1) - 1)
+    def _():
+        side_ref[...] = acc_ref[...].astype(side_ref.dtype)
+        third = tiles // 3
+        mid_ref[...] = acc_ref[third : 2 * third]
 
 
 def attention_forward(mask, queries, window):
     tokens, features = queries.shape
     tiles = window.shape[0]
     heads = features // HD
-    chunks = tokens // QCHUNK
+    chunk = FORWARD_CHUNK
+    chunks = tokens // chunk
     scale = HD ** (-0.5)
     return pl.pallas_call(
         functools.partial(forward_kernel, scale),
         grid=(heads, chunks),
         in_specs=[
             pl.BlockSpec((1, tiles * tokens), lambda h, c: (0, 0)),
-            pl.BlockSpec((QCHUNK, HD), lambda h, c: (c, h)),
+            pl.BlockSpec((chunk, HD), lambda h, c: (c, h)),
             pl.BlockSpec((tiles, tokens, HD), lambda h, c: (0, 0, h)),
             pl.BlockSpec((tiles, tokens, HD), lambda h, c: (0, 1, h)),
         ],
-        out_specs=pl.BlockSpec((QCHUNK, HD), lambda h, c: (c, h)),
+        out_specs=pl.BlockSpec((chunk, HD), lambda h, c: (c, h)),
         out_shape=jax.ShapeDtypeStruct((tokens, features), jnp.bfloat16),
         name="tile_attention_forward",
     )(mask, queries, window, window)
@@ -105,27 +112,31 @@
     tokens, features = queries.shape
     tiles = window.shape[0]
     heads = features // HD
-    chunks = tokens // QCHUNK
+    chunk = BACKWARD_CHUNK
+    chunks = tokens // chunk
     scale = HD ** (-0.5)
     return pl.pallas_call(
         functools.partial(backward_kernel, scale),
         grid=(heads, chunks),
         in_specs=[
             pl.BlockSpec((1, tiles * tokens), lambda h, c: (0, 0)),
-            pl.BlockSpec((QCHUNK, HD), lambda h, c: (c, h)),
+            pl.BlockSpec((chunk, HD), lambda h, c: (c, h)),
             pl.BlockSpec((tiles, tokens, HD), lambda h, c: (0, 0, h)),
             pl.BlockSpec((tiles, tokens, HD), lambda h, c: (0, 1, h)),
-            pl.BlockSpec((QCHUNK, HD), lambda h, c: (c, h)),
-            pl.BlockSpec((QCHUNK, HD), lambda h, c: (c, h)),
+            pl.BlockSpec((chunk, HD), lambda h, c: (c, h)),
+            pl.BlockSpec((chunk, HD), lambda h, c: (c, h)),
         ],
         out_specs=[
-            pl.BlockSpec((QCHUNK, HD), lambda h, c: (c, h)),
+            pl.BlockSpec((chunk, HD), lambda h, c: (c, h)),
             pl.BlockSpec((tiles, 2 * tokens, HD), lambda h, c: (0, 0, h)),
+            pl.BlockSpec((tiles // 3, 2 * tokens, HD), lambda h, c: (0, 0, h)),
         ],
         out_shape=[
             jax.ShapeDtypeStruct((tokens, features), jnp.bfloat16),
-            jax.ShapeDtypeStruct((tiles, 2 * tokens, features), jnp.float32),
-        ],
+            jax.ShapeDtypeStruct((tiles, 2 * tokens, features), jnp.bfloat16),
+            jax.ShapeDtypeStruct((tiles // 3, 2 * tokens, features), jnp.float32),
+        ],
+        scratch_shapes=[pltpu.VMEM((tiles, 2 * tokens, HD), jnp.float32)],
         name="tile_attention_backward",
     )(mask, queries, window, window, attended, grad_attended)
 
@@ -168,18 +179,20 @@
             [shifted(column, "wa", 1), column, shifted(column, "wa", -1)], axis=0
         )
     tiles = window.shape[0]
-    mask = window[:, 2 * tokens, :tokens].reshape(1, tiles * tokens).astype(jnp.float32)
+    flags = window[:, 2 * tokens, :tokens].reshape(1, tiles * tokens)
+    mask = jnp.where(flags > 0, 0.0, MASKED).astype(jnp.float32)
 
     with jax.named_scope("cotangent_gather"):
-        cot_pieces = gather_over(out_cotangent[0, 0], "ha")
-        cot_all = cot_pieces.reshape(-1, model_width)
+        cot_all = lax.all_gather(out_cotangent[0, 0], "ha", axis=0, tiled=True)
 
     with jax.named_scope("attention_forward"):
         attended = attention_forward(mask, q, window)
 
     with jax.named_scope("output_projection"):
         projected = jnp.dot(attended, out_weight, preferred_element_type=jnp.float32)
-        layer_out = scatter_sum(projected, "ha", 0).astype(jnp.bfloat16)
+        layer_out = lax.psum_scatter(
+            projected.astype(jnp.bfloat16), "ha", scatter_dimension=0, tiled=True
+        )
 
     with jax.named_scope("grad_attended"):
         grad_attended = lax.dot_general(
@@ -187,7 +200,7 @@
         ).astype(jnp.bfloat16)
 
     with jax.named_scope("attention_backward"):
-        grad_q, partials = attention_backward(mask, q, window, attended, grad_attended)
+        grad_q, sides, partials = attention_backward(mask, q, window, attended, grad_attended)
 
     with jax.named_scope("grad_weight"):
         weight_part = lax.dot_general(
@@ -196,9 +209,8 @@
         grad_weight = scatter_sum(scatter_sum(weight_part, "fh", 0), "wa", 0)
 
     with jax.named_scope("halo_reduction"):
-        sides = partials.astype(jnp.bfloat16)
         middle = (
-            partials[3:6]
+            partials
             + shifted(sides[0:3], "wa", -1).astype(jnp.float32)
             + shifted(sides[6:9], "wa", 1).astype(jnp.float32)
         )

time: 224 us -> 199 us (0.89)
  the two profiles are of different devices: /device:TPU:28 before, /device:TPU:1 now
where the time goes in v2:
time: 199 us
  waiting for transfers between devices  74.3 us (37%)
  Pallas kernels  36.5 us (18%)
  starting transfers between devices  27.8 us (14%)
  local copies, waits for them, and re-layouts  19.6 us (10%)
  other arithmetic  17.1 us (9%)
  between operations  14.3 us (7%)
  matrix products  8.97 us (5%)
    ppermute x4, waiting for transfers between devices, cyclic(): lax.ppermute(value, axis, [(i, (i + steps) % count) for i in range(count)])  40.5 us
    ppermute x8, waiting for transfers between devices, shifted(): return lax.ppermute(value, axis, shift_pairs(lax.axis_size(axis), steps))  33.7 us
    ppermute x8, starting transfers between devices, shifted(): return lax.ppermute(value, axis, shift_pairs(lax.axis_size(axis), steps))  25 us
    pallas_call x1, Pallas kernels, attention_backward(): pl.pallas_call(functools.partial(backward_kernel, scale), grid=(heads, ch...  22.7 us
    pallas_call x1, Pallas kernels, attention_forward(): pl.pallas_call(functools.partial(forward_kernel, scale), grid=(heads, chu...  13.8 us
    unnamed x26, local copies, waits for them, and re-layouts  10.3 us
    convert_element_type x1, other arithmetic, body(): middle_sides = middle.astype(jnp.bfloat16)  5.4 us
    another operation x2, other arithmetic, body(): jnp.stack([shifted(packed, 'fh', 1), packed, shifted(packed, 'fh', -1)])  4.76 us
  transfers between devices with their start and end apart: 14, of which 7 were waited for; matrix products, arithmetic and copies ran while one was open for 19% of the time, Pallas kernels for 18%

profile of v2, /device:TPU:1, one launch (start us, length us, event | category | flops | bytes accessed | tf_op | source)
XLA Modules:
  0.0 198.6 jit_solution(15501671969512569529)
XLA Ops:
  7.2 0.0 copy-start
  7.2 0.0 all-gather.3.cloned.1.call-start
  7.2 0.8 convert_bitcast_fusion
  8.1 2.0 %fusion.13 = (bf16[1,784,384]{2,1,0:T(8,128)(2,1)S(1)}, bf16[784,384]{1,0:T(8,128)(2,1)}) fusion(bf16[1,384]{1,0:T(2,128)(2,1)S(1)} %convert_bitcast_fusion, bf16[384,384]{1,0:T(8,128)(2,1)} %bitcast.48, bf16[384,384]{1,0:T(8,128)(2,1)} %bitcast.50), kind=kLoop, calls=%fused_computation.33 | loop fusion | flops 2408448 | bytes 1794816 | tf_op jit(solution)/shard_map/halo_exchange/stack | solution.py:177
  10.1 4.8 %collective-permute-start = (bf16[784,384]{1,0:T(8,128)(2,1)}, bf16[784,384]{1,0:T(8,128)(2,1)}, u32[]{:S(2)}, u32[]{:S(2)}) collective-permute-start(bf16[784,384]{1,0:T(8,128)(2,1)} %get-tuple-element.38), channel_id=1, source_target_pairs={{0,16},{1,17},{2,18},{3,19},{4,20},{5,21},{6,22},{7,23},{8,24},{9,... | collective-permute-start | bytes 1806344 | tf_op jit(solution)/shard_map/halo_exchange/ppermute | solution.py:22
  14.9 1.3 collective-permute-start.1
  16.2 0.0 all-gather.3.cloned.1.call-update
  16.2 0.0 reduce-scatter.2.cloned.1.call-start
  16.3 10.3 %collective-permute-done = bf16[784,384]{1,0:T(8,128)(2,1)} collective-permute-done((bf16[784,384]{1,0:T(8,128)(2,1)}, bf16[784,384]{1,0:T(8,128)(2,1)}, u32[]{:S(2)}, u32[]{:S(2)}) %collective-permute-start) | collective-permute-done | bytes 602144 | tf_op jit(solution)/shard_map/halo_exchange/ppermute | solution.py:22
  26.6 4.6 %collective-permute-done.1 = bf16[784,384]{1,0:T(8,128)(2,1)} collective-permute-done((bf16[784,384]{1,0:T(8,128)(2,1)}, bf16[784,384]{1,0:T(8,128)(2,1)}, u32[]{:S(2)}, u32[]{:S(2)}) %collective-permute-start.1) | collective-permute-done | bytes 602144 | tf_op jit(solution)/shard_map/halo_exchange/ppermute | solution.py:22
  31.2 2.8 %pad_maximum_fusion = bf16[3,784,384]{2,1,0:T(8,128)(2,1)} fusion(bf16[1,784,384]{2,1,0:T(8,128)(2,1)} %bitcast.5, bf16[1,784,384]{2,1,0:T(8,128)(2,1)S(1)} %get-tuple-element.37, bf16[1,784,384]{2,1,0:T(8,128)(2,1)} %bitcast.3), kind=kLoop, calls=%fused_computation.8 | loop fusion | flops 1806336 | bytes 3612672 | tf_op jit(solution)/shard_map/halo_exchange/stack | solution.py:177
  34.0 4.9 %collective-permute-start.2 = (bf16[3,784,384]{2,1,0:T(8,128)(2,1)}, bf16[3,784,384]{2,1,0:T(8,128)(2,1)}, u32[]{:S(2)}, u32[]{:S(2)}) collective-permute-start(bf16[3,784,384]{2,1,0:T(8,128)(2,1)} %pad_maximum_fusion), channel_id=1, source_target_pairs={{0,4},{4,8},{8,12},{1,5},{5,9},{9,13},{2,6},{6,10},{10,14},{3,7},{... | collective-permute-start | bytes 5419016 | tf_op jit(solution)/shard_map/halo_exchange/ppermute | solution.py:22
  38.9 1.9 collective-permute-start.3
  40.8 0.0 copy-start.7
  40.8 0.0 copy-start.8
  40.8 18.2 %collective-permute-done.2 = bf16[3,784,384]{2,1,0:T(8,128)(2,1)} collective-permute-done((bf16[3,784,384]{2,1,0:T(8,128)(2,1)}, bf16[3,784,384]{2,1,0:T(8,128)(2,1)}, u32[]{:S(2)}, u32[]{:S(2)}) %collective-permute-start.2) | collective-permute-done | bytes 1806368 | tf_op jit(solution)/shard_map/halo_exchange/ppermute | solution.py:22
  59.0 1.7 constant_dynamic-update-slice_fusion.4
  60.7 1.2 constant_dynamic-update-slice_fusion.3
  61.9 0.0 copy-done.7
  61.9 0.0 copy-done.8
  61.9 0.1 constant_dynamic-update-slice_fusion.2
  62.0 1.2 constant_dynamic-update-slice_fusion.1
  63.2 0.6 collective-permute-done.3
  63.7 1.9 constant_dynamic-update-slice_fusion.k_ref.v_ref
  65.6 0.0 copy-start.1
  65.6 2.3 %copy-done.1 = bf16[9,784,384]{2,1,0:T(8,128)(2,1)} copy-done((bf16[9,784,384]{2,1,0:T(8,128)(2,1)}, bf16[9,784,384]{2,1,0:T(8,128)(2,1)S(1)}, u32[]{:S(2)}) %copy-start.1) | copy-done | bytes 5419032
  67.9 0.6 compare_select_fusion
  68.5 13.8 %tile_attention_forward.1.o_ref = bf16[384,384]{1,0:T(8,128)(2,1)} custom-call(f32[1,3456]{1,0:T(1,128)} %bitcast.52, bf16[384,384]{1,0:T(8,128)(2,1)} %bitcast.46, bf16[9,784,384]{2,1,0:T(8,128)(2,1)} %copy-done.1, bf16[9,784,384]{2,1,0:T(8,128)(2,1)} %copy-done.1), custom_call_target="tpu_custom_call" | custom-call | tf_op jit(solution)/shard_map/attention_forward/tile_attention_forward/pallas_call | solution.py:96
  82.4 0.0 copy-done
  82.4 3.8 %convolution_convert_fusion = bf16[384,3072]{1,0:T(8,128)(2,1)} fusion(bf16[384,384]{1,0:T(8,128)(2,1)} %tile_attention_forward.1.o_ref, bf16[384,3072]{1,0:T(8,128)(2,1)S(1)} %copy-done), kind=kOutput, calls=%fused_computation | convolution fusion | flops 907149312 | bytes 5013504 | tf_op jit(solution)/shard_map/output_projection/dot_general | solution.py:192
  86.1 0.0 reduce-scatter.2.cloned.1.call-update
  86.2 0.0 all-gather.3.cloned.1.call-done
  86.2 3.8 %fusion.4.do_ref = bf16[384,384]{1,0:T(8,128)(2,1)} fusion(bf16[384,3072]{1,0:T(8,128)(2,1)S(1)} %copy-done, bf16[1,1,384,3072]{3,2,1,0:T(8,128)(2,1)} %all-gather.3.cloned.1.call-done), kind=kOutput, calls=%fused_computation.9 | convolution fusion | flops 906117120 | bytes 5013504 | tf_op jit(solution)/shard_map/grad_attended/dot_general | solution.py:198
  90.0 22.7 %tile_attention_backward.1 = (bf16[384,384]{1,0:T(8,128)(2,1)}, bf16[9,768,384]{2,1,0:T(8,128)(2,1)}, f32[3,768,384]{2,1,0:T(8,128)}) custom-call(f32[1,3456]{1,0:T(1,128)} %bitcast.53, bf16[384,384]{1,0:T(8,128)(2,1)} %bitcast.47, bf16[9,784,384]{2,1,0:T(8,128)(2,1)} %copy-done.1, bf16[9,784,384]{2,1,0:T(8,128)(2,1)} %copy-done.1, ...), custom_call_target="tpu_custom_call" | custom-call | tf_op jit(solution)/shard_map/attention_backward/tile_attention_backward/pallas_call | solution.py:118
  112.7 4.3 %fusion.15 = (bf16[3,768,384]{2,1,0:T(8,128)(2,1)}, bf16[3,768,384]{2,1,0:T(8,128)(2,1)}) fusion(bf16[9,768,384]{2,1,0:T(8,128)(2,1)} %get-tuple-element.22), kind=kLoop, calls=%fused_computation.35 | loop fusion | bytes 7077888 | tf_op jit(solution)/shard_map/halo_reduction/slice | solution.py:214
  117.0 1.9 collective-permute-start.4
  118.9 4.0 %collective-permute-start.5 = (bf16[3,768,384]{2,1,0:T(8,128)(2,1)}, bf16[3,768,384]{2,1,0:T(8,128)(2,1)}, u32[]{:S(2)}, u32[]{:S(2)}) collective-permute-start(bf16[3,768,384]{2,1,0:T(8,128)(2,1)} %get-tuple-element.31), channel_id=1, source_target_pairs={{0,4},{4,8},{8,12},{1,5},{5,9},{9,13},{2,6},{6,10},{10,14},{3,7},{... | collective-permute-start | bytes 5308424 | tf_op jit(solution)/shard_map/halo_reduction/ppermute | solution.py:22
  123.0 1.4 fusion
  124.4 2.2 %copy-done.2 = f32[384,3072]{1,0:T(8,128)} copy-done((f32[384,3072]{1,0:T(8,128)}, f32[384,3072]{1,0:T(8,128)S(1)}, u32[]{:S(2)}) %copy-start.2) | copy-done | bytes 4718616
  126.6 0.1 fusion.8
  126.7 0.1 collective-permute-start.8
  126.9 27.9 %collective-permute-done.8 = bf16[1536,384]{0,1:T(8,128)(2,1)} collective-permute-done((bf16[1536,384]{0,1:T(8,128)(2,1)S(1)}, bf16[1536,384]{0,1:T(8,128)(2,1)}, u32[]{:S(2)}, u32[]{:S(2)}) %collective-permute-start.8) | collective-permute-done | bytes 1179680 | tf_op jit(solution)/shard_map/grad_weight/ppermute | solution.py:27
  154.8 2.3 %bitcast_add_fusion = f32[1536,384]{0,1:T(8,128)S(1)} fusion(bf16[1536,384]{0,1:T(8,128)(2,1)} %collective-permute-done.8, f32[384,3072]{1,0:T(8,128)} %copy-done.2, s32[]{:T(128)S(6)} %select_n.45), kind=kLoop, calls=%fused_computation.2 | loop fusion | flops 1179648 | bytes 5898244 | tf_op jit(solution)/shard_map/grad_weight/add | solution.py:163
  157.1 0.0 collective-permute-done.4
  157.1 0.0 collective-permute-done.5
  157.2 5.4 %fusion.14 = (bf16[3,768,384]{2,1,0:T(8,128)(2,1)S(1)}, f32[3,768,384]{2,1,0:T(8,128)}) fusion(bf16[3,768,384]{2,1,0:T(8,128)(2,1)} %collective-permute-done.5, f32[3,768,384]{2,1,0:T(8,128)S(1)} %copy-done.5, bf16[3,768,384]{2,1,0:T(8,128)(2,1)} %collective-permute-done.4), kind=kLoop, calls=%fused_computation.34 | loop fusion | flops 4423680 | bytes 12386304 | tf_op jit(solution)/shard_map/halo_reduction/convert_element_type | solution.py:217
  162.6 1.1 slice_bitcast_fusion.2
  163.7 1.3 collective-permute-start.6
  165.0 4.8 %collective-permute-start.7 = (bf16[768,384]{1,0:T(8,128)(2,1)}, bf16[768,384]{1,0:T(8,128)(2,1)}, u32[]{:S(2)}, u32[]{:S(2)}) collective-permute-start(bf16[768,384]{1,0:T(8,128)(2,1)} %get-tuple-element.36), channel_id=1, source_target_pairs={{0,16},{1,17},{2,18},{3,19},{4,20},{5,21},{6,22},{7,23},{8,24},{9,... | collective-permute-start | bytes 1769480 | tf_op jit(solution)/shard_map/halo_reduction/ppermute | solution.py:22
  169.8 0.0 copy-done.3
  169.8 1.0 dynamic-slice_convert_fusion.3
  170.8 0.0 collective-permute-start.10
  170.8 2.0 %collective-permute-start.11 = (bf16[384,384]{0,1:T(8,128)(2,1)}, bf16[384,384]{0,1:T(8,128)(2,1)S(1)}, u32[]{:S(2)}, u32[]{:S(2)}) collective-permute-start(bf16[384,384]{0,1:T(8,128)(2,1)} %get-tuple-element.33), channel_id=1, source_target_pairs={{0,12},{4,0},{8,4},{12,8},{1,13},{5,1},{9,5},{13,9},{2,14},{6,2},{... | collective-permute-start | bytes 884744 | tf_op jit(solution)/shard_map/grad_weight/ppermute | solution.py:27
  172.8 0.7 collective-permute-start.9
  173.5 5.0 %collective-permute-done.10 = bf16[384,384]{0,1:T(8,128)(2,1)S(1)} collective-permute-done((bf16[384,384]{0,1:T(8,128)(2,1)}, bf16[384,384]{0,1:T(8,128)(2,1)S(1)}, u32[]{:S(2)}, u32[]{:S(2)}) %collective-permute-start.10) | collective-permute-done | bytes 294944 | tf_op jit(solution)/shard_map/grad_weight/ppermute | solution.py:27
  178.5 7.6 %collective-permute-done.11 = bf16[384,384]{0,1:T(8,128)(2,1)S(1)} collective-permute-done((bf16[384,384]{0,1:T(8,128)(2,1)}, bf16[384,384]{0,1:T(8,128)(2,1)S(1)}, u32[]{:S(2)}, u32[]{:S(2)}) %collective-permute-start.11) | collective-permute-done | bytes 294944 | tf_op jit(solution)/shard_map/grad_weight/ppermute | solution.py:27
  186.1 0.7 copy-done.10
  186.8 0.0 collective-permute-done.9
  186.8 1.5 convert_add_fusion.1
  188.2 1.1 copy.11
  189.3 0.0 collective-permute-done.6
  189.3 0.0 collective-permute-done.7
  189.3 1.6 fusion.11
  190.9 0.9 slice_bitcast_fusion.3
  (12 shorter events, 0.0 us)
Async XLA Ops:
  7.2 75.2 %copy-start = (bf16[384,3072]{1,0:T(8,128)(2,1)S(1)}, bf16[384,3072]{1,0:T(8,128)(2,1)}, u32[]{:S(2)}) copy-start(bf16[384,3072]{1,0:T(8,128)(2,1)} %param.12) | copy-start | bytes 7077892
  7.2 79.0 %all-gather.3.cloned.1.call-start = ((), (), s32[]{:S(2)}) async-start(), calls=%async_computation.2 | async-start | bytes 2949120 | tf_op jit(solution)/shard_map/cotangent_gather/all_gather | solution.py:186
  10.1 16.5 %collective-permute-start = (bf16[784,384]{1,0:T(8,128)(2,1)}, bf16[784,384]{1,0:T(8,128)(2,1)}, u32[]{:S(2)}, u32[]{:S(2)}) collective-permute-start(bf16[784,384]{1,0:T(8,128)(2,1)} %get-tuple-element.38), channel_id=1, source_target_pairs={{0,16},{1,17},{2,18},{3,19},{4,20},{5,21},{6,22},{7,23},{8,24},{9,... | collective-permute-start | bytes 1806344 | tf_op jit(solution)/shard_map/halo_exchange/ppermute | solution.py:22
  14.9 16.3 %collective-permute-start.1 = (bf16[784,384]{1,0:T(8,128)(2,1)}, bf16[784,384]{1,0:T(8,128)(2,1)}, u32[]{:S(2)}, u32[]{:S(2)}) collective-permute-start(bf16[784,384]{1,0:T(8,128)(2,1)} %get-tuple-element.38), channel_id=1, source_target_pairs={{16,0},{17,1},{18,2},{19,3},{20,4},{21,5},{22,6},{23,7},{24,8},{25... | collective-permute-start | bytes 1806344 | tf_op jit(solution)/shard_map/halo_exchange/ppermute | solution.py:22
  16.2 175.6 %reduce-scatter.2.cloned.1.call-start = ((), (), s32[]{:S(2)}) async-start(), calls=%async_computation.1 | async-start | bytes 2949120 | tf_op jit(solution)/shard_map/output_projection/reduce_scatter | solution.py:193
  34.0 25.0 %collective-permute-start.2 = (bf16[3,784,384]{2,1,0:T(8,128)(2,1)}, bf16[3,784,384]{2,1,0:T(8,128)(2,1)}, u32[]{:S(2)}, u32[]{:S(2)}) collective-permute-start(bf16[3,784,384]{2,1,0:T(8,128)(2,1)} %pad_maximum_fusion), channel_id=1, source_target_pairs={{0,4},{4,8},{8,12},{1,5},{5,9},{9,13},{2,6},{6,10},{10,14},{3,7},{... | collective-permute-start | bytes 5419016 | tf_op jit(solution)/shard_map/halo_exchange/ppermute | solution.py:22
  38.9 24.8 %collective-permute-start.3 = (bf16[3,784,384]{2,1,0:T(8,128)(2,1)}, bf16[3,784,384]{2,1,0:T(8,128)(2,1)}, u32[]{:S(2)}, u32[]{:S(2)}) collective-permute-start(bf16[3,784,384]{2,1,0:T(8,128)(2,1)} %pad_maximum_fusion), channel_id=1, source_target_pairs={{4,0},{8,4},{12,8},{5,1},{9,5},{13,9},{6,2},{10,6},{14,10},{7,3},{... | collective-permute-start | bytes 5419016 | tf_op jit(solution)/shard_map/halo_exchange/ppermute | solution.py:22
  40.8 21.1 %copy-start.7 = (bf16[1,1,384,384]{3,2,1,0:T(8,128)(2,1)S(1)}, bf16[1,1,384,384]{3,2,1,0:T(8,128)(2,1)}, u32[]{:S(2)}) copy-start(bf16[1,1,384,384]{3,2,1,0:T(8,128)(2,1)} %param.10) | copy-start | bytes 884740
  40.8 21.1 %copy-start.8 = (bf16[1,1,384,384]{3,2,1,0:T(8,128)(2,1)S(1)}, bf16[1,1,384,384]{3,2,1,0:T(8,128)(2,1)}, u32[]{:S(2)}) copy-start(bf16[1,1,384,384]{3,2,1,0:T(8,128)(2,1)} %param.9) | copy-start | bytes 884740
  65.6 2.3 %copy-start.1 = (bf16[9,784,384]{2,1,0:T(8,128)(2,1)}, bf16[9,784,384]{2,1,0:T(8,128)(2,1)S(1)}, u32[]{:S(2)}) copy-start(bf16[9,784,384]{2,1,0:T(8,128)(2,1)S(1)} %constant_dynamic-update-slice_fusion.k_ref.v_ref) | copy-start | bytes 16257028
  112.7 10.3 %copy-start.4 = (bf16[384,384]{1,0:T(8,128)(2,1)S(1)}, bf16[384,384]{1,0:T(8,128)(2,1)}, u32[]{:S(2)}) copy-start(bf16[384,384]{1,0:T(8,128)(2,1)} %tile_attention_forward.1.o_ref) | copy-start | bytes 884740
  112.7 10.3 %copy-start.6 = (bf16[1,1,384,3072]{3,2,1,0:T(8,128)(2,1)S(1)}, bf16[1,1,384,3072]{3,2,1,0:T(8,128)(2,1)}, u32[]{:S(2)}) copy-start(bf16[1,1,384,3072]{3,2,1,0:T(8,128)(2,1)} %all-gather.3.cloned.1.call-done) | copy-start | bytes 7077892
  117.0 40.1 %collective-permute-start.4 = (bf16[3,768,384]{2,1,0:T(8,128)(2,1)}, bf16[3,768,384]{2,1,0:T(8,128)(2,1)}, u32[]{:S(2)}, u32[]{:S(2)}) collective-permute-start(bf16[3,768,384]{2,1,0:T(8,128)(2,1)} %get-tuple-element.30), channel_id=1, source_target_pairs={{4,0},{8,4},{12,8},{5,1},{9,5},{13,9},{6,2},{10,6},{14,10},{7,3},{... | collective-permute-start | bytes 5308424 | tf_op jit(solution)/shard_map/halo_reduction/ppermute | solution.py:22
  118.9 38.2 %collective-permute-start.5 = (bf16[3,768,384]{2,1,0:T(8,128)(2,1)}, bf16[3,768,384]{2,1,0:T(8,128)(2,1)}, u32[]{:S(2)}, u32[]{:S(2)}) collective-permute-start(bf16[3,768,384]{2,1,0:T(8,128)(2,1)} %get-tuple-element.31), channel_id=1, source_target_pairs={{0,4},{4,8},{8,12},{1,5},{5,9},{9,13},{2,6},{6,10},{10,14},{3,7},{... | collective-permute-start | bytes 5308424 | tf_op jit(solution)/shard_map/halo_reduction/ppermute | solution.py:22
  124.4 2.2 %copy-start.2 = (f32[384,3072]{1,0:T(8,128)}, f32[384,3072]{1,0:T(8,128)S(1)}, u32[]{:S(2)}) copy-start(f32[384,3072]{1,0:T(8,128)S(1)} %fusion) | copy-start | bytes 14155780
  126.7 28.1 %collective-permute-start.8 = (bf16[1536,384]{0,1:T(8,128)(2,1)S(1)}, bf16[1536,384]{0,1:T(8,128)(2,1)}, u32[]{:S(2)}, u32[]{:S(2)}) collective-permute-start(bf16[1536,384]{0,1:T(8,128)(2,1)S(1)} %fusion.8), channel_id=1, source_target_pairs={{0,16},{16,0},{1,17},{17,1},{2,18},{18,2},{3,19},{19,3},{4,20},{20... | collective-permute-start | bytes 3538952 | tf_op jit(solution)/shard_map/grad_weight/ppermute | solution.py:27
  126.9 30.3 %copy-start.5 = (f32[3,768,384]{2,1,0:T(8,128)S(1)}, f32[3,768,384]{2,1,0:T(8,128)}, u32[]{:S(2)}) copy-start(f32[3,768,384]{2,1,0:T(8,128)} %get-tuple-element.21) | copy-start | bytes 10616836
  157.1 12.7 %copy-start.3 = (f32[1536,384]{0,1:T(8,128)}, f32[1536,384]{0,1:T(8,128)S(1)}, u32[]{:S(2)}) copy-start(f32[1536,384]{0,1:T(8,128)S(1)} %bitcast_add_fusion) | copy-start | bytes 7077892
  163.7 25.6 %collective-permute-start.6 = (bf16[768,384]{1,0:T(8,128)(2,1)}, bf16[768,384]{1,0:T(8,128)(2,1)S(1)}, u32[]{:S(2)}, u32[]{:S(2)}) collective-permute-start(bf16[768,384]{1,0:T(8,128)(2,1)} %get-tuple-element.35), channel_id=1, source_target_pairs={{16,0},{17,1},{18,2},{19,3},{20,4},{21,5},{22,6},{23,7},{24,8},{25... | collective-permute-start | bytes 1769480 | tf_op jit(solution)/shard_map/halo_reduction/ppermute | solution.py:22
  165.0 24.3 %collective-permute-start.7 = (bf16[768,384]{1,0:T(8,128)(2,1)}, bf16[768,384]{1,0:T(8,128)(2,1)}, u32[]{:S(2)}, u32[]{:S(2)}) collective-permute-start(bf16[768,384]{1,0:T(8,128)(2,1)} %get-tuple-element.36), channel_id=1, source_target_pairs={{0,16},{1,17},{2,18},{3,19},{4,20},{5,21},{6,22},{7,23},{8,24},{9,... | collective-permute-start | bytes 1769480 | tf_op jit(solution)/shard_map/halo_reduction/ppermute | solution.py:22
  170.8 7.7 %collective-permute-start.10 = (bf16[384,384]{0,1:T(8,128)(2,1)}, bf16[384,384]{0,1:T(8,128)(2,1)S(1)}, u32[]{:S(2)}, u32[]{:S(2)}) collective-permute-start(bf16[384,384]{0,1:T(8,128)(2,1)} %get-tuple-element.34), channel_id=1, source_target_pairs={{0,8},{4,12},{8,0},{12,4},{1,9},{5,13},{9,1},{13,5},{2,10},{6,14},... | collective-permute-start | bytes 884744 | tf_op jit(solution)/shard_map/grad_weight/ppermute | solution.py:27
  170.8 15.3 %collective-permute-start.11 = (bf16[384,384]{0,1:T(8,128)(2,1)}, bf16[384,384]{0,1:T(8,128)(2,1)S(1)}, u32[]{:S(2)}, u32[]{:S(2)}) collective-permute-start(bf16[384,384]{0,1:T(8,128)(2,1)} %get-tuple-element.33), channel_id=1, source_target_pairs={{0,12},{4,0},{8,4},{12,8},{1,13},{5,1},{9,5},{13,9},{2,14},{6,2},{... | collective-permute-start | bytes 884744 | tf_op jit(solution)/shard_map/grad_weight/ppermute | solution.py:27
  172.8 14.0 %collective-permute-start.9 = (bf16[384,384]{0,1:T(8,128)(2,1)}, bf16[384,384]{0,1:T(8,128)(2,1)}, u32[]{:S(2)}, u32[]{:S(2)}) collective-permute-start(bf16[384,384]{0,1:T(8,128)(2,1)} %get-tuple-element.32), channel_id=1, source_target_pairs={{0,4},{4,8},{8,12},{12,0},{1,5},{5,9},{9,13},{13,1},{2,6},{6,10},{... | collective-permute-start | bytes 884744 | tf_op jit(solution)/shard_map/grad_weight/ppermute | solution.py:27
  178.5 7.6 %copy-start.9 = (bf16[384,384]{0,1:T(8,128)(2,1)}, bf16[384,384]{0,1:T(8,128)(2,1)S(1)}, u32[]{:S(2)}) copy-start(bf16[384,384]{0,1:T(8,128)(2,1)S(1)} %collective-permute-done.10) | copy-start | bytes 884740
  186.1 0.7 copy-start.10
Sparse Core Ops, SparseCore 0:
  16.3 53.9 all-gather.2
  86.3 48.3 reduce-scatter.1

commit v3 on v2

--- a/solution.py
+++ b/solution.py
@@ -44,7 +44,9 @@
     o_ref[...] = jnp.dot(p, v, preferred_element_type=jnp.float32).astype(o_ref.dtype)
 
 
-def backward_kernel(scale, mask_ref, q_ref, k_ref, v_ref, o_ref, do_ref, dq_ref, side_ref, mid_ref, acc_ref):
+def backward_kernel(
+    scale, mask_ref, q_ref, k_ref, v_ref, o_ref, do_ref, dq_ref, left_ref, mid_ref, right_ref, acc_ref
+):
     chunk = pl.program_id(1)
     s = scores_of(mask_ref, q_ref, k_ref, scale)
     m = jnp.max(s, axis=1, keepdims=True)
@@ -81,9 +83,10 @@
 
     @pl.when(chunk == pl.num_programs(1) - 1)
     def _():
-        side_ref[...] = acc_ref[...].astype(side_ref.dtype)
         third = tiles // 3
+        left_ref[...] = acc_ref[:third].astype(left_ref.dtype)
         mid_ref[...] = acc_ref[third : 2 * third]
+        right_ref[...] = acc_ref[2 * third :].astype(right_ref.dtype)
 
 
 def attention_forward(mask, queries, window):
@@ -128,13 +131,15 @@
         ],
         out_specs=[
             pl.BlockSpec((chunk, HD), lambda h, c: (c, h)),
-            pl.BlockSpec((tiles, 2 * tokens, HD), lambda h, c: (0, 0, h)),
+            pl.BlockSpec((tiles // 3, 2 * tokens, HD), lambda h, c: (0, 0, h)),
+            pl.BlockSpec((tiles // 3, 2 * tokens, HD), lambda h, c: (0, 0, h)),
             pl.BlockSpec((tiles // 3, 2 * tokens, HD), lambda h, c: (0, 0, h)),
         ],
         out_shape=[
             jax.ShapeDtypeStruct((tokens, features), jnp.bfloat16),
-            jax.ShapeDtypeStruct((tiles, 2 * tokens, features), jnp.bfloat16),
+            jax.ShapeDtypeStruct((tiles // 3, 2 * tokens, features), jnp.bfloat16),
             jax.ShapeDtypeStruct((tiles // 3, 2 * tokens, features), jnp.float32),
+            jax.ShapeDtypeStruct((tiles // 3, 2 * tokens, features), jnp.bfloat16),
         ],
         scratch_shapes=[pltpu.VMEM((tiles, 2 * tokens, HD), jnp.float32)],
         name="tile_attention_backward",
@@ -147,6 +152,25 @@
     received = [piece] + [cyclic(piece, axis, steps) for steps in range(1, count)]
     ordered = jnp.stack([received[(-k) % count] for k in range(count)])
     return jnp.roll(ordered, me, axis=0)
+
+
+def scatter_parts(full, axis, dim):
+    count = lax.axis_size(axis)
+    me = lax.axis_index(axis)
+    size = full.shape[dim] // count
+
+    def part(index):
+        return lax.dynamic_slice_in_dim(full, index * size, size, axis=dim)
+
+    sent = [part((me + steps) % count).astype(jnp.bfloat16) for steps in range(1, count)]
+    return part(me).astype(jnp.float32), sent
+
+
+def scatter_finish(own, sent, axis):
+    total = own
+    for steps, piece in enumerate(sent, start=1):
+        total = total + cyclic(piece, axis, steps).astype(jnp.float32)
+    return total
 
 
 def scatter_sum(full, axis, dim):
@@ -199,20 +223,29 @@
             cot_all, out_weight, (((1,), (1,)), ((), ())), preferred_element_type=jnp.float32
         ).astype(jnp.bfloat16)
 
-    with jax.named_scope("attention_backward"):
-        grad_q, sides, partials = attention_backward(mask, q, window, attended, grad_attended)
-
     with jax.named_scope("grad_weight"):
         weight_part = lax.dot_general(
             cot_all, attended, (((0,), (0,)), ((), ())), preferred_element_type=jnp.float32
         )
-        grad_weight = scatter_sum(scatter_sum(weight_part, "fh", 0), "wa", 0)
+        weight_own, weight_sent = scatter_parts(weight_part, "fh", 0)
+        weight_own, weight_sent, grad_attended = lax.optimization_barrier(
+            (weight_own, weight_sent, grad_attended)
+        )
+        weight_rows = scatter_finish(weight_own, weight_sent, "fh")
+
+    with jax.named_scope("attention_backward"):
+        grad_q, left, partials, right = attention_backward(
+            mask, q, window, attended, grad_attended
+        )
+
+    with jax.named_scope("grad_weight"):
+        grad_weight = scatter_sum(weight_rows, "wa", 0)
 
     with jax.named_scope("halo_reduction"):
         middle = (
             partials
-            + shifted(sides[0:3], "wa", -1).astype(jnp.float32)
-            + shifted(sides[6:9], "wa", 1).astype(jnp.float32)
+            + shifted(left, "wa", -1).astype(jnp.float32)
+            + shifted(right, "wa", 1).astype(jnp.float32)
         )
         middle_sides = middle.astype(jnp.bfloat16)
         own = (

time: 199 us -> 184 us (0.925)
  waiting for transfers between devices: 74.3 us -> 62.8 us
  local copies, waits for them, and re-layouts: 19.6 us -> 16.5 us
    ppermute x4, waiting for transfers between devices: 40.5 us -> 11.8 us  [cyclic(): lax.ppermute(value, axis, [(i, (i + steps) % count) for i in range(count)])]
    ppermute x8, waiting for transfers between devices: 33.7 us -> 50.9 us  [shifted(): return lax.ppermute(value, axis, shift_pairs(lax.axis_size(axis), steps))]
    slice x1 -> x0, local copies, waits for them, and re-layouts: 4.33 us -> none  [body(): sides[0:3]]
    add x0 -> x1, other arithmetic: none -> 2.45 us  [scatter_finish(): total = total + cyclic(piece, axis, steps).astype(jnp.float32)]
    add x2 -> x1, other arithmetic: 3.78 us -> 1.45 us  [scatter_sum(): total = total + cyclic(sent, axis, steps).astype(jnp.float32)]
    unnamed x26 -> x24, local copies, waits for them, and re-layouts: 10.3 us -> 9.87 us
  transfers between devices with their start and end apart: 14 -> 14, of which waited for: 7 -> 8; matrix products, arithmetic and copies ran while one was open for 19% -> 19% of each run, Pallas kernels for 18% -> 20%
where the time goes in v3:
time: 184 us
  waiting for transfers between devices  62.8 us (34%)
  Pallas kernels  36.2 us (20%)
  starting transfers between devices  28.4 us (15%)
  local copies, waits for them, and re-layouts  16.5 us (9%)
  other arithmetic  16.4 us (9%)
  between operations  14.3 us (8%)
  matrix products  8.97 us (5%)
    ppermute x8, waiting for transfers between devices, shifted(): return lax.ppermute(value, axis, shift_pairs(lax.axis_size(axis), steps))  50.9 us
    ppermute x8, starting transfers between devices, shifted(): return lax.ppermute(value, axis, shift_pairs(lax.axis_size(axis), steps))  24.8 us
    pallas_call x1, Pallas kernels, attention_backward(): pl.pallas_call(functools.partial(backward_kernel, scale), grid=(heads, ch...  22.4 us
    pallas_call x1, Pallas kernels, attention_forward(): pl.pallas_call(functools.partial(forward_kernel, scale), grid=(heads, chu...  13.8 us
    ppermute x4, waiting for transfers between devices, cyclic(): lax.ppermute(value, axis, [(i, (i + steps) % count) for i in range(count)])  11.8 us
    unnamed x24, local copies, waits for them, and re-layouts  9.87 us
    another operation x2, other arithmetic, body(): jnp.stack([shifted(packed, 'fh', 1), packed, shifted(packed, 'fh', -1)])  4.75 us
    convert_element_type x1, other arithmetic, body(): middle_sides = middle.astype(jnp.bfloat16)  4.56 us
  transfers between devices with their start and end apart: 14, of which 8 were waited for; matrix products, arithmetic and copies ran while one was open for 19% of the time, Pallas kernels for 20%

profile of v3, /device:TPU:1, one launch (start us, length us, event | category | flops | bytes accessed | tf_op | source)
XLA Modules:
  0.0 183.5 jit_solution(17680435018735222391)
XLA Ops:
  7.2 0.0 copy-start
  7.2 0.0 all-gather.3.cloned.1.call-start
  7.2 0.8 convert_bitcast_fusion
  8.1 2.0 %fusion.13 = (bf16[1,784,384]{2,1,0:T(8,128)(2,1)S(1)}, bf16[784,384]{1,0:T(8,128)(2,1)}) fusion(bf16[1,384]{1,0:T(2,128)(2,1)S(1)} %convert_bitcast_fusion, bf16[384,384]{1,0:T(8,128)(2,1)} %bitcast.48, bf16[384,384]{1,0:T(8,128)(2,1)} %bitcast.50), kind=kLoop, calls=%fused_computation.34 | loop fusion | flops 2408448 | bytes 1794816 | tf_op jit(solution)/shard_map/halo_exchange/stack | solution.py:201
  10.0 4.8 %collective-permute-start = (bf16[784,384]{1,0:T(8,128)(2,1)}, bf16[784,384]{1,0:T(8,128)(2,1)}, u32[]{:S(2)}, u32[]{:S(2)}) collective-permute-start(bf16[784,384]{1,0:T(8,128)(2,1)} %get-tuple-element.44), channel_id=1, source_target_pairs={{0,16},{1,17},{2,18},{3,19},{4,20},{5,21},{6,22},{7,23},{8,24},{9,... | collective-permute-start | bytes 1806344 | tf_op jit(solution)/shard_map/halo_exchange/ppermute | solution.py:22
  14.8 1.3 collective-permute-start.1
  16.1 0.0 all-gather.3.cloned.1.call-update
  16.1 0.0 reduce-scatter.2.cloned.1.call-start
  16.2 10.4 %collective-permute-done = bf16[784,384]{1,0:T(8,128)(2,1)} collective-permute-done((bf16[784,384]{1,0:T(8,128)(2,1)}, bf16[784,384]{1,0:T(8,128)(2,1)}, u32[]{:S(2)}, u32[]{:S(2)}) %collective-permute-start) | collective-permute-done | bytes 602144 | tf_op jit(solution)/shard_map/halo_exchange/ppermute | solution.py:22
  26.6 4.6 %collective-permute-done.1 = bf16[784,384]{1,0:T(8,128)(2,1)} collective-permute-done((bf16[784,384]{1,0:T(8,128)(2,1)}, bf16[784,384]{1,0:T(8,128)(2,1)}, u32[]{:S(2)}, u32[]{:S(2)}) %collective-permute-start.1) | collective-permute-done | bytes 602144 | tf_op jit(solution)/shard_map/halo_exchange/ppermute | solution.py:22
  31.2 2.8 %pad_maximum_fusion = bf16[3,784,384]{2,1,0:T(8,128)(2,1)} fusion(bf16[1,784,384]{2,1,0:T(8,128)(2,1)} %bitcast.5, bf16[1,784,384]{2,1,0:T(8,128)(2,1)S(1)} %get-tuple-element.43, bf16[1,784,384]{2,1,0:T(8,128)(2,1)} %bitcast.3), kind=kLoop, calls=%fused_computation.9 | loop fusion | flops 1806336 | bytes 3612672 | tf_op jit(solution)/shard_map/halo_exchange/stack | solution.py:201
  33.9 4.9 %collective-permute-start.2 = (bf16[3,784,384]{2,1,0:T(8,128)(2,1)}, bf16[3,784,384]{2,1,0:T(8,128)(2,1)}, u32[]{:S(2)}, u32[]{:S(2)}) collective-permute-start(bf16[3,784,384]{2,1,0:T(8,128)(2,1)} %pad_maximum_fusion), channel_id=1, source_target_pairs={{0,4},{4,8},{8,12},{1,5},{5,9},{9,13},{2,6},{6,10},{10,14},{3,7},{... | collective-permute-start | bytes 5419016 | tf_op jit(solution)/shard_map/halo_exchange/ppermute | solution.py:22
  38.8 1.9 %collective-permute-start.3 = (bf16[3,784,384]{2,1,0:T(8,128)(2,1)}, bf16[3,784,384]{2,1,0:T(8,128)(2,1)}, u32[]{:S(2)}, u32[]{:S(2)}) collective-permute-start(bf16[3,784,384]{2,1,0:T(8,128)(2,1)} %pad_maximum_fusion), channel_id=1, source_target_pairs={{4,0},{8,4},{12,8},{5,1},{9,5},{13,9},{6,2},{10,6},{14,10},{7,3},{... | collective-permute-start | bytes 5419016 | tf_op jit(solution)/shard_map/halo_exchange/ppermute | solution.py:22
  40.8 0.0 copy-start.6
  40.8 0.0 copy-start.7
  40.8 18.2 %collective-permute-done.2 = bf16[3,784,384]{2,1,0:T(8,128)(2,1)} collective-permute-done((bf16[3,784,384]{2,1,0:T(8,128)(2,1)}, bf16[3,784,384]{2,1,0:T(8,128)(2,1)}, u32[]{:S(2)}, u32[]{:S(2)}) %collective-permute-start.2) | collective-permute-done | bytes 1806368 | tf_op jit(solution)/shard_map/halo_exchange/ppermute | solution.py:22
  59.0 1.7 constant_dynamic-update-slice_fusion.4
  60.6 1.2 constant_dynamic-update-slice_fusion.3
  61.8 0.0 copy-done.6
  61.8 0.0 copy-done.7
  61.8 0.1 constant_dynamic-update-slice_fusion.2
  61.9 1.2 constant_dynamic-update-slice_fusion.1
  63.1 0.6 collective-permute-done.3
  63.7 1.9 %constant_dynamic-update-slice_fusion.k_ref.v_ref = bf16[9,784,384]{2,1,0:T(8,128)(2,1)S(1)} fusion(bf16[9,784,384]{2,1,0:T(8,128)(2,1)S(1)} %constant_dynamic-update-slice_fusion.1, bf16[3,784,384]{2,1,0:T(8,128)(2,1)} %collective-permute-done.3), kind=kLoop, calls=%fused_computation.28 | loop fusion | bytes 3612672 | tf_op jit(solution)/shard_map/halo_exchange/concatenate | solution.py:202
  65.5 0.0 copy-start.1
  65.5 2.3 %copy-done.1 = bf16[9,784,384]{2,1,0:T(8,128)(2,1)} copy-done((bf16[9,784,384]{2,1,0:T(8,128)(2,1)}, bf16[9,784,384]{2,1,0:T(8,128)(2,1)S(1)}, u32[]{:S(2)}) %copy-start.1) | copy-done | bytes 5419032
  67.9 0.6 compare_select_fusion
  68.5 13.8 %tile_attention_forward.1.o_ref = bf16[384,384]{1,0:T(8,128)(2,1)} custom-call(f32[1,3456]{1,0:T(1,128)} %bitcast.52, bf16[384,384]{1,0:T(8,128)(2,1)} %bitcast.46, bf16[9,784,384]{2,1,0:T(8,128)(2,1)} %copy-done.1, bf16[9,784,384]{2,1,0:T(8,128)(2,1)} %copy-done.1), custom_call_target="tpu_custom_call" | custom-call | tf_op jit(solution)/shard_map/attention_forward/tile_attention_forward/pallas_call | solution.py:99
  82.3 3.8 %convolution_convert_fusion = bf16[384,3072]{1,0:T(8,128)(2,1)} fusion(bf16[384,384]{1,0:T(8,128)(2,1)} %tile_attention_forward.1.o_ref, bf16[384,3072]{1,0:T(8,128)(2,1)S(1)} %copy-done), kind=kOutput, calls=%fused_computation | convolution fusion | flops 907149312 | bytes 5013504 | tf_op jit(solution)/shard_map/output_projection/dot_general | solution.py:216
  86.1 0.0 reduce-scatter.2.cloned.1.call-update
  86.1 0.0 all-gather.3.cloned.1.call-done
  86.1 0.9 copy-done.3
  87.0 3.1 %fusion.2 = f32[384,3072]{1,0:T(8,128)S(1)} fusion(bf16[384,384]{1,0:T(8,128)(2,1)S(1)} %copy-done.3, bf16[1,1,384,3072]{3,2,1,0:T(8,128)(2,1)} %all-gather.3.cloned.1.call-done), kind=kOutput, calls=%fused_computation.4 | convolution fusion | flops 905969664 | bytes 7372800 | tf_op jit(solution)/shard_map/grad_weight/dot_general | solution.py:227
  90.1 0.1 fusion.8
  90.3 0.0 copy-start.5
  90.3 1.7 dynamic-slice_bitcast_fusion
  92.0 0.8 copy-done.5
  92.8 2.1 %fusion.4.do_ref = bf16[384,384]{1,0:T(8,128)(2,1)} fusion(bf16[384,3072]{1,0:T(8,128)(2,1)S(1)} %copy-done, bf16[1,1,384,3072]{3,2,1,0:T(8,128)(2,1)S(1)} %copy-done.5), kind=kOutput, calls=%fused_computation.10 | convolution fusion | flops 906117120 | bytes 5013504 | tf_op jit(solution)/shard_map/grad_attended/dot_general | solution.py:222
  94.9 0.0 collective-permute-start.8
  94.9 22.4 %tile_attention_backward.1 = (bf16[384,384]{1,0:T(8,128)(2,1)}, bf16[3,768,384]{2,1,0:T(8,128)(2,1)}, f32[3,768,384]{2,1,0:T(8,128)}, bf16[3,768,384]{2,1,0:T(8,128)(2,1)}) custom-call(f32[1,3456]{1,0:T(1,128)} %bitcast.53, bf16[384,384]{1,0:T(8,128)(2,1)} %bitcast.47, bf16[9,784,384]{2,1,0:T(8,128)(2,1)} %copy-done.1, bf16[9,784,384]{2,1,0:T(8,128)(2,1)} %copy-done.1, ...), custom_call_target="tpu_custom_call" | custom-call | tf_op jit(solution)/shard_map/attention_backward/tile_attention_backward/pallas_call | solution.py:121
  117.3 1.9 %collective-permute-start.4 = (bf16[3,768,384]{2,1,0:T(8,128)(2,1)}, bf16[3,768,384]{2,1,0:T(8,128)(2,1)}, u32[]{:S(2)}, u32[]{:S(2)}) collective-permute-start(bf16[3,768,384]{2,1,0:T(8,128)(2,1)} %get-tuple-element.27), channel_id=1, source_target_pairs={{4,0},{8,4},{12,8},{5,1},{9,5},{13,9},{6,2},{10,6},{14,10},{7,3},{... | collective-permute-start | bytes 5308424 | tf_op jit(solution)/shard_map/halo_reduction/ppermute | solution.py:22
  119.2 3.9 %collective-permute-start.5 = (bf16[3,768,384]{2,1,0:T(8,128)(2,1)}, bf16[3,768,384]{2,1,0:T(8,128)(2,1)}, u32[]{:S(2)}, u32[]{:S(2)}) collective-permute-start(bf16[3,768,384]{2,1,0:T(8,128)(2,1)} %get-tuple-element.28), channel_id=1, source_target_pairs={{0,4},{4,8},{8,12},{1,5},{5,9},{9,13},{2,6},{6,10},{10,14},{3,7},{... | collective-permute-start | bytes 5308424 | tf_op jit(solution)/shard_map/halo_reduction/ppermute | solution.py:22
  123.1 0.0 collective-permute-done.8
  123.2 2.5 %convert_add_fusion.1 = f32[1536,384]{0,1:T(8,128)S(1)} fusion(f32[1536,384]{0,1:T(8,128)} %dynamic-slice_bitcast_fusion, bf16[1536,384]{0,1:T(8,128)(2,1)} %collective-permute-done.8), kind=kLoop, calls=%fused_computation.6 | loop fusion | flops 1179648 | bytes 5898240 | tf_op jit(solution)/shard_map/grad_weight/add | solution.py:172
  125.6 16.2 %collective-permute-done.4 = bf16[3,768,384]{2,1,0:T(8,128)(2,1)} collective-permute-done((bf16[3,768,384]{2,1,0:T(8,128)(2,1)}, bf16[3,768,384]{2,1,0:T(8,128)(2,1)}, u32[]{:S(2)}, u32[]{:S(2)}) %collective-permute-start.4) | collective-permute-done | bytes 1769504 | tf_op jit(solution)/shard_map/halo_reduction/ppermute | solution.py:22
  141.9 1.0 collective-permute-done.5
  142.8 4.6 %fusion.14 = (bf16[3,768,384]{2,1,0:T(8,128)(2,1)S(1)}, f32[3,768,384]{2,1,0:T(8,128)}) fusion(bf16[3,768,384]{2,1,0:T(8,128)(2,1)} %collective-permute-done.5, f32[3,768,384]{2,1,0:T(8,128)S(1)} %copy-done.4, bf16[3,768,384]{2,1,0:T(8,128)(2,1)} %collective-permute-done.4), kind=kLoop, calls=%fused_computation.35 | loop fusion | flops 4423680 | bytes 12386304 | tf_op jit(solution)/shard_map/halo_reduction/convert_element_type | solution.py:250
  147.4 1.1 slice_bitcast_fusion.2
  148.5 1.3 collective-permute-start.6
  149.8 4.9 %collective-permute-start.7 = (bf16[768,384]{1,0:T(8,128)(2,1)}, bf16[768,384]{1,0:T(8,128)(2,1)}, u32[]{:S(2)}, u32[]{:S(2)}) collective-permute-start(bf16[768,384]{1,0:T(8,128)(2,1)} %get-tuple-element.42), channel_id=1, source_target_pairs={{0,16},{1,17},{2,18},{3,19},{4,20},{5,21},{6,22},{7,23},{8,24},{9,... | collective-permute-start | bytes 1769480 | tf_op jit(solution)/shard_map/halo_reduction/ppermute | solution.py:22
  154.7 1.0 dynamic-slice_convert_fusion.3
  155.7 0.0 collective-permute-start.10
  155.7 3.4 %collective-permute-start.11 = (bf16[384,384]{0,1:T(8,128)(2,1)}, bf16[384,384]{0,1:T(8,128)(2,1)S(1)}, u32[]{:S(2)}, u32[]{:S(2)}) collective-permute-start(bf16[384,384]{0,1:T(8,128)(2,1)} %get-tuple-element.39), channel_id=1, source_target_pairs={{0,12},{4,0},{8,4},{12,8},{1,13},{5,1},{9,5},{13,9},{2,14},{6,2},{... | collective-permute-start | bytes 884744 | tf_op jit(solution)/shard_map/grad_weight/ppermute | solution.py:27
  159.1 0.0 collective-permute-start.9
  159.1 3.9 %collective-permute-done.10 = bf16[384,384]{0,1:T(8,128)(2,1)S(1)} collective-permute-done((bf16[384,384]{0,1:T(8,128)(2,1)}, bf16[384,384]{0,1:T(8,128)(2,1)S(1)}, u32[]{:S(2)}, u32[]{:S(2)}) %collective-permute-start.10) | collective-permute-done | bytes 294944 | tf_op jit(solution)/shard_map/grad_weight/ppermute | solution.py:27
  163.0 8.0 %collective-permute-done.11 = bf16[384,384]{0,1:T(8,128)(2,1)S(1)} collective-permute-done((bf16[384,384]{0,1:T(8,128)(2,1)}, bf16[384,384]{0,1:T(8,128)(2,1)S(1)}, u32[]{:S(2)}, u32[]{:S(2)}) %collective-permute-start.11) | collective-permute-done | bytes 294944 | tf_op jit(solution)/shard_map/grad_weight/ppermute | solution.py:27
  171.0 0.7 copy-done.9
  171.7 0.0 collective-permute-done.9
  171.7 1.5 convert_add_fusion.2
  173.1 1.1 copy.11
  174.2 0.0 collective-permute-done.6
  174.2 0.0 collective-permute-done.7
  174.2 1.6 fusion.11
  175.8 0.9 slice_bitcast_fusion.3
  (10 shorter events, 0.0 us)
Async XLA Ops:
  7.2 75.1 %copy-start = (bf16[384,3072]{1,0:T(8,128)(2,1)S(1)}, bf16[384,3072]{1,0:T(8,128)(2,1)}, u32[]{:S(2)}) copy-start(bf16[384,3072]{1,0:T(8,128)(2,1)} %param.12) | copy-start | bytes 7077892
  7.2 79.0 %all-gather.3.cloned.1.call-start = ((), (), s32[]{:S(2)}) async-start(), calls=%async_computation.2 | async-start | bytes 2949120 | tf_op jit(solution)/shard_map/cotangent_gather/all_gather | solution.py:210
  10.0 16.5 %collective-permute-start = (bf16[784,384]{1,0:T(8,128)(2,1)}, bf16[784,384]{1,0:T(8,128)(2,1)}, u32[]{:S(2)}, u32[]{:S(2)}) collective-permute-start(bf16[784,384]{1,0:T(8,128)(2,1)} %get-tuple-element.44), channel_id=1, source_target_pairs={{0,16},{1,17},{2,18},{3,19},{4,20},{5,21},{6,22},{7,23},{8,24},{9,... | collective-permute-start | bytes 1806344 | tf_op jit(solution)/shard_map/halo_exchange/ppermute | solution.py:22
  14.8 16.3 %collective-permute-start.1 = (bf16[784,384]{1,0:T(8,128)(2,1)}, bf16[784,384]{1,0:T(8,128)(2,1)}, u32[]{:S(2)}, u32[]{:S(2)}) collective-permute-start(bf16[784,384]{1,0:T(8,128)(2,1)} %get-tuple-element.44), channel_id=1, source_target_pairs={{16,0},{17,1},{18,2},{19,3},{20,4},{21,5},{22,6},{23,7},{24,8},{25... | collective-permute-start | bytes 1806344 | tf_op jit(solution)/shard_map/halo_exchange/ppermute | solution.py:22
  16.1 160.5 %reduce-scatter.2.cloned.1.call-start = ((), (), s32[]{:S(2)}) async-start(), calls=%async_computation.1 | async-start | bytes 2949120 | tf_op jit(solution)/shard_map/output_projection/reduce_scatter | solution.py:217
  33.9 25.0 %collective-permute-start.2 = (bf16[3,784,384]{2,1,0:T(8,128)(2,1)}, bf16[3,784,384]{2,1,0:T(8,128)(2,1)}, u32[]{:S(2)}, u32[]{:S(2)}) collective-permute-start(bf16[3,784,384]{2,1,0:T(8,128)(2,1)} %pad_maximum_fusion), channel_id=1, source_target_pairs={{0,4},{4,8},{8,12},{1,5},{5,9},{9,13},{2,6},{6,10},{10,14},{3,7},{... | collective-permute-start | bytes 5419016 | tf_op jit(solution)/shard_map/halo_exchange/ppermute | solution.py:22
  38.8 24.8 %collective-permute-start.3 = (bf16[3,784,384]{2,1,0:T(8,128)(2,1)}, bf16[3,784,384]{2,1,0:T(8,128)(2,1)}, u32[]{:S(2)}, u32[]{:S(2)}) collective-permute-start(bf16[3,784,384]{2,1,0:T(8,128)(2,1)} %pad_maximum_fusion), channel_id=1, source_target_pairs={{4,0},{8,4},{12,8},{5,1},{9,5},{13,9},{6,2},{10,6},{14,10},{7,3},{... | collective-permute-start | bytes 5419016 | tf_op jit(solution)/shard_map/halo_exchange/ppermute | solution.py:22
  40.8 21.1 %copy-start.6 = (bf16[1,1,384,384]{3,2,1,0:T(8,128)(2,1)S(1)}, bf16[1,1,384,384]{3,2,1,0:T(8,128)(2,1)}, u32[]{:S(2)}) copy-start(bf16[1,1,384,384]{3,2,1,0:T(8,128)(2,1)} %param.10) | copy-start | bytes 884740
  40.8 21.1 %copy-start.7 = (bf16[1,1,384,384]{3,2,1,0:T(8,128)(2,1)S(1)}, bf16[1,1,384,384]{3,2,1,0:T(8,128)(2,1)}, u32[]{:S(2)}) copy-start(bf16[1,1,384,384]{3,2,1,0:T(8,128)(2,1)} %param.9) | copy-start | bytes 884740
  65.5 2.3 %copy-start.1 = (bf16[9,784,384]{2,1,0:T(8,128)(2,1)}, bf16[9,784,384]{2,1,0:T(8,128)(2,1)S(1)}, u32[]{:S(2)}) copy-start(bf16[9,784,384]{2,1,0:T(8,128)(2,1)S(1)} %constant_dynamic-update-slice_fusion.k_ref.v_ref) | copy-start | bytes 16257028
  86.1 1.0 copy-start.3
  90.3 2.5 %copy-start.5 = (bf16[1,1,384,3072]{3,2,1,0:T(8,128)(2,1)S(1)}, bf16[1,1,384,3072]{3,2,1,0:T(8,128)(2,1)}, u32[]{:S(2)}) copy-start(bf16[1,1,384,3072]{3,2,1,0:T(8,128)(2,1)} %all-gather.3.cloned.1.call-done) | copy-start | bytes 7077892
  94.9 28.2 %collective-permute-start.8 = (bf16[1536,384]{0,1:T(8,128)(2,1)S(1)}, bf16[1536,384]{0,1:T(8,128)(2,1)}, u32[]{:S(2)}, u32[]{:S(2)}) collective-permute-start(bf16[1536,384]{0,1:T(8,128)(2,1)S(1)} %fusion.8), channel_id=1, source_target_pairs={{0,16},{16,0},{1,17},{17,1},{2,18},{18,2},{3,19},{19,3},{4,20},{20... | collective-permute-start | bytes 3538952 | tf_op jit(solution)/shard_map/grad_weight/ppermute | solution.py:27
  117.3 24.6 %collective-permute-start.4 = (bf16[3,768,384]{2,1,0:T(8,128)(2,1)}, bf16[3,768,384]{2,1,0:T(8,128)(2,1)}, u32[]{:S(2)}, u32[]{:S(2)}) collective-permute-start(bf16[3,768,384]{2,1,0:T(8,128)(2,1)} %get-tuple-element.27), channel_id=1, source_target_pairs={{4,0},{8,4},{12,8},{5,1},{9,5},{13,9},{6,2},{10,6},{14,10},{7,3},{... | collective-permute-start | bytes 5308424 | tf_op jit(solution)/shard_map/halo_reduction/ppermute | solution.py:22
  119.2 23.6 %collective-permute-start.5 = (bf16[3,768,384]{2,1,0:T(8,128)(2,1)}, bf16[3,768,384]{2,1,0:T(8,128)(2,1)}, u32[]{:S(2)}, u32[]{:S(2)}) collective-permute-start(bf16[3,768,384]{2,1,0:T(8,128)(2,1)} %get-tuple-element.28), channel_id=1, source_target_pairs={{0,4},{4,8},{8,12},{1,5},{5,9},{9,13},{2,6},{6,10},{10,14},{3,7},{... | collective-permute-start | bytes 5308424 | tf_op jit(solution)/shard_map/halo_reduction/ppermute | solution.py:22
  123.1 19.7 %copy-start.4 = (f32[3,768,384]{2,1,0:T(8,128)S(1)}, f32[3,768,384]{2,1,0:T(8,128)}, u32[]{:S(2)}) copy-start(f32[3,768,384]{2,1,0:T(8,128)} %get-tuple-element.26) | copy-start | bytes 10616836
  125.6 29.1 %copy-start.2 = (f32[1536,384]{0,1:T(8,128)}, f32[1536,384]{0,1:T(8,128)S(1)}, u32[]{:S(2)}) copy-start(f32[1536,384]{0,1:T(8,128)S(1)} %convert_add_fusion.1) | copy-start | bytes 7077892
  148.5 25.7 %collective-permute-start.6 = (bf16[768,384]{1,0:T(8,128)(2,1)}, bf16[768,384]{1,0:T(8,128)(2,1)S(1)}, u32[]{:S(2)}, u32[]{:S(2)}) collective-permute-start(bf16[768,384]{1,0:T(8,128)(2,1)} %get-tuple-element.41), channel_id=1, source_target_pairs={{16,0},{17,1},{18,2},{19,3},{20,4},{21,5},{22,6},{23,7},{24,8},{25... | collective-permute-start | bytes 1769480 | tf_op jit(solution)/shard_map/halo_reduction/ppermute | solution.py:22
  149.8 24.4 %collective-permute-start.7 = (bf16[768,384]{1,0:T(8,128)(2,1)}, bf16[768,384]{1,0:T(8,128)(2,1)}, u32[]{:S(2)}, u32[]{:S(2)}) collective-permute-start(bf16[768,384]{1,0:T(8,128)(2,1)} %get-tuple-element.42), channel_id=1, source_target_pairs={{0,16},{1,17},{2,18},{3,19},{4,20},{5,21},{6,22},{7,23},{8,24},{9,... | collective-permute-start | bytes 1769480 | tf_op jit(solution)/shard_map/halo_reduction/ppermute | solution.py:22
  155.7 7.3 %collective-permute-start.10 = (bf16[384,384]{0,1:T(8,128)(2,1)}, bf16[384,384]{0,1:T(8,128)(2,1)S(1)}, u32[]{:S(2)}, u32[]{:S(2)}) collective-permute-start(bf16[384,384]{0,1:T(8,128)(2,1)} %get-tuple-element.40), channel_id=1, source_target_pairs={{0,8},{4,12},{8,0},{12,4},{1,9},{5,13},{9,1},{13,5},{2,10},{6,14},... | collective-permute-start | bytes 884744 | tf_op jit(solution)/shard_map/grad_weight/ppermute | solution.py:27
  155.7 15.3 %collective-permute-start.11 = (bf16[384,384]{0,1:T(8,128)(2,1)}, bf16[384,384]{0,1:T(8,128)(2,1)S(1)}, u32[]{:S(2)}, u32[]{:S(2)}) collective-permute-start(bf16[384,384]{0,1:T(8,128)(2,1)} %get-tuple-element.39), channel_id=1, source_target_pairs={{0,12},{4,0},{8,4},{12,8},{1,13},{5,1},{9,5},{13,9},{2,14},{6,2},{... | collective-permute-start | bytes 884744 | tf_op jit(solution)/shard_map/grad_weight/ppermute | solution.py:27
  159.1 12.5 %collective-permute-start.9 = (bf16[384,384]{0,1:T(8,128)(2,1)}, bf16[384,384]{0,1:T(8,128)(2,1)}, u32[]{:S(2)}, u32[]{:S(2)}) collective-permute-start(bf16[384,384]{0,1:T(8,128)(2,1)} %get-tuple-element.38), channel_id=1, source_target_pairs={{0,4},{4,8},{8,12},{12,0},{1,5},{5,9},{9,13},{13,1},{2,6},{6,10},{... | collective-permute-start | bytes 884744 | tf_op jit(solution)/shard_map/grad_weight/ppermute | solution.py:27
  163.0 8.0 %copy-start.8 = (bf16[384,384]{0,1:T(8,128)(2,1)}, bf16[384,384]{0,1:T(8,128)(2,1)S(1)}, u32[]{:S(2)}) copy-start(bf16[384,384]{0,1:T(8,128)(2,1)S(1)} %collective-permute-done.10) | copy-start | bytes 884740
  171.0 0.7 copy-start.9
Sparse Core Ops, SparseCore 0:
  16.3 53.9 all-gather.2
  86.2 48.3 reduce-scatter.1

commit v4 on v3

--- a/solution.py
+++ b/solution.py
@@ -227,11 +227,14 @@
         weight_part = lax.dot_general(
             cot_all, attended, (((0,), (0,)), ((), ())), preferred_element_type=jnp.float32
         )
-        weight_own, weight_sent = scatter_parts(weight_part, "fh", 0)
+        row_blocks = weight_part.reshape(
+            lax.axis_size("fh"), lax.axis_size("wa"), -1, weight_part.shape[1]
+        )
+        weight_own, weight_sent = scatter_parts(row_blocks, "wa", 1)
         weight_own, weight_sent, grad_attended = lax.optimization_barrier(
             (weight_own, weight_sent, grad_attended)
         )
-        weight_rows = scatter_finish(weight_own, weight_sent, "fh")
+        weight_rows = scatter_finish(weight_own, weight_sent, "wa")
 
     with jax.named_scope("attention_backward"):
         grad_q, left, partials, right = attention_backward(
@@ -239,7 +242,7 @@
         )
 
     with jax.named_scope("grad_weight"):
-        grad_weight = scatter_sum(weight_rows, "wa", 0)
+        grad_weight = scatter_sum(weight_rows, "fh", 0).reshape(-1, weight_part.shape[1])
 
     with jax.named_scope("halo_reduction"):
         middle = (

time: 184 us -> 219 us (1.19)
  the two profiles are of different devices: /device:TPU:1 before, /device:TPU:31 now
where the time goes in v4:
time: 219 us; the launch traced here: 218 us
  waiting for transfers between devices  75 us (34%)
  starting transfers between devices  42.9 us (20%)
  Pallas kernels  36.2 us (17%)
  local copies, waits for them, and re-layouts  22.5 us (10%)
  other arithmetic  16.4 us (7%)
  between operations  14.2 us (6%)
  matrix products  11.2 us (5%)
    ppermute x4, waiting for transfers between devices, cyclic(): lax.ppermute(value, axis, [(i, (i + steps) % count) for i in range(count)])  59.5 us
    ppermute x8, starting transfers between devices, shifted(): return lax.ppermute(value, axis, shift_pairs(lax.axis_size(axis), steps))  37.5 us
    pallas_call x1, Pallas kernels, attention_backward(): pl.pallas_call(functools.partial(backward_kernel, scale), grid=(heads, ch...  22.3 us
    ppermute x8, waiting for transfers between devices, shifted(): return lax.ppermute(value, axis, shift_pairs(lax.axis_size(axis), steps))  15.4 us
    pallas_call x1, Pallas kernels, attention_forward(): pl.pallas_call(functools.partial(forward_kernel, scale), grid=(heads, chu...  13.9 us
    unnamed x19, local copies, waits for them, and re-layouts  7.23 us
    reshape x1, local copies, waits for them, and re-layouts, body(): weight_part.reshape(lax.axis_size('fh'), lax.axis_size('wa'), -1, weight_...  6.07 us
    ppermute x4, starting transfers between devices, cyclic(): lax.ppermute(value, axis, [(i, (i + steps) % count) for i in range(count)])  5.4 us
  transfers between devices with their start and end apart: 14, of which 7 were waited for; matrix products, arithmetic and copies ran while one was open for 20% of the time, Pallas kernels for 17%

profile of v4, /device:TPU:31, one launch (start us, length us, event | category | flops | bytes accessed | tf_op | source)
XLA Modules:
  0.0 218.5 jit_solution(3839789690557279848)
XLA Ops:
  7.2 0.0 copy-start
  7.2 0.0 all-gather.3.cloned.1.call-start
  7.2 0.8 convert_bitcast_fusion
  8.1 2.0 fusion.11
  10.0 3.0 %collective-permute-start.1 = (bf16[784,384]{1,0:T(8,128)(2,1)}, bf16[784,384]{1,0:T(8,128)(2,1)}, u32[]{:S(2)}, u32[]{:S(2)}) collective-permute-start(bf16[784,384]{1,0:T(8,128)(2,1)} %get-tuple-element.43), channel_id=1, source_target_pairs={{16,0},{17,1},{18,2},{19,3},{20,4},{21,5},{22,6},{23,7},{24,8},{25... | collective-permute-start | bytes 1806344 | tf_op jit(solution)/shard_map/halo_exchange/ppermute | solution.py:22
  13.0 1.3 collective-permute-start
  14.3 0.0 all-gather.3.cloned.1.call-update
  14.3 0.0 reduce-scatter.2.cloned.1.call-start
  14.4 10.4 %collective-permute-done.1 = bf16[784,384]{1,0:T(8,128)(2,1)} collective-permute-done((bf16[784,384]{1,0:T(8,128)(2,1)}, bf16[784,384]{1,0:T(8,128)(2,1)}, u32[]{:S(2)}, u32[]{:S(2)}) %collective-permute-start.1) | collective-permute-done | bytes 602144 | tf_op jit(solution)/shard_map/halo_exchange/ppermute | solution.py:22
  24.7 4.6 %collective-permute-done = bf16[784,384]{1,0:T(8,128)(2,1)} collective-permute-done((bf16[784,384]{1,0:T(8,128)(2,1)}, bf16[784,384]{1,0:T(8,128)(2,1)}, u32[]{:S(2)}, u32[]{:S(2)}) %collective-permute-start) | collective-permute-done | bytes 602144 | tf_op jit(solution)/shard_map/halo_exchange/ppermute | solution.py:22
  29.3 2.7 %pad_maximum_fusion = bf16[3,784,384]{2,1,0:T(8,128)(2,1)} fusion(bf16[1,784,384]{2,1,0:T(8,128)(2,1)} %bitcast.5, bf16[1,784,384]{2,1,0:T(8,128)(2,1)S(1)} %get-tuple-element.42, bf16[1,784,384]{2,1,0:T(8,128)(2,1)} %bitcast.3), kind=kLoop, calls=%fused_computation.6 | loop fusion | flops 1806336 | bytes 3612672 | tf_op jit(solution)/shard_map/halo_exchange/stack | solution.py:201
  32.1 1.3 collective-permute-start.2
  33.4 5.6 %collective-permute-start.3 = (bf16[3,784,384]{2,1,0:T(8,128)(2,1)}, bf16[3,784,384]{2,1,0:T(8,128)(2,1)}, u32[]{:S(2)}, u32[]{:S(2)}) collective-permute-start(bf16[3,784,384]{2,1,0:T(8,128)(2,1)} %pad_maximum_fusion), channel_id=1, source_target_pairs={{4,0},{8,4},{12,8},{5,1},{9,5},{13,9},{6,2},{10,6},{14,10},{7,3},{... | collective-permute-start | bytes 5419016 | tf_op jit(solution)/shard_map/halo_exchange/ppermute | solution.py:22
  39.0 0.4 collective-permute-done.2
  39.4 1.7 constant_dynamic-update-slice_fusion.4
  41.1 1.2 constant_dynamic-update-slice_fusion.3
  42.3 0.0 copy-done.6
  42.3 0.0 copy-done.7
  42.3 0.1 constant_dynamic-update-slice_fusion.2
  42.4 1.2 constant_dynamic-update-slice_fusion.1
  43.6 0.0 collective-permute-done.3
  43.6 1.9 constant_dynamic-update-slice_fusion.k_ref.v_ref
  45.4 0.0 copy-start.1
  45.4 2.4 %copy-done.1 = bf16[9,784,384]{2,1,0:T(8,128)(2,1)} copy-done((bf16[9,784,384]{2,1,0:T(8,128)(2,1)}, bf16[9,784,384]{2,1,0:T(8,128)(2,1)S(1)}, u32[]{:S(2)}) %copy-start.1) | copy-done | bytes 5419032
  47.8 0.6 compare_select_fusion
  48.4 13.9 %tile_attention_forward.1.o_ref = bf16[384,384]{1,0:T(8,128)(2,1)} custom-call(f32[1,3456]{1,0:T(1,128)} %bitcast.55, bf16[384,384]{1,0:T(8,128)(2,1)} %bitcast.49, bf16[9,784,384]{2,1,0:T(8,128)(2,1)} %copy-done.1, bf16[9,784,384]{2,1,0:T(8,128)(2,1)} %copy-done.1), custom_call_target="tpu_custom_call" | custom-call | tf_op jit(solution)/shard_map/attention_forward/tile_attention_forward/pallas_call | solution.py:99
  62.3 0.0 copy-done
  62.3 3.7 %convolution_convert_fusion = bf16[384,3072]{1,0:T(8,128)(2,1)} fusion(bf16[384,384]{1,0:T(8,128)(2,1)} %tile_attention_forward.1.o_ref, bf16[384,3072]{1,0:T(8,128)(2,1)S(1)} %copy-done), kind=kOutput, calls=%fused_computation.1 | convolution fusion | flops 907149312 | bytes 5013504 | tf_op jit(solution)/shard_map/output_projection/dot_general | solution.py:216
  66.0 0.0 reduce-scatter.2.cloned.1.call-update
  66.0 0.1 all-gather.3.cloned.1.call-done
  66.1 0.8 copy-done.2
  67.0 5.3 %convolution_bitcast_fusion = f32[3072,384]{0,1:T(8,128)} fusion(bf16[384,384]{1,0:T(8,128)(2,1)S(1)} %copy-done.2, bf16[1,1,384,3072]{3,2,1,0:T(8,128)(2,1)} %all-gather.3.cloned.1.call-done), kind=kOutput, calls=%fused_computation | convolution fusion | flops 905969664 | bytes 7372800 | tf_op jit(solution)/shard_map/grad_weight/dot_general | solution.py:227
  72.3 6.1 %copy.15 = f32[3072,384]{1,0:T(8,128)} copy(f32[3072,384]{0,1:T(8,128)} %convolution_bitcast_fusion) | data formatting | bytes 9437184 | tf_op jit(solution)/shard_map/grad_weight/reshape | solution.py:230
  78.4 1.3 constant_dynamic-slice_fusion
  79.7 0.0 copy-start.5
  79.7 3.4 %dynamic-slice_convert_fusion = (bf16[2,1,384,384]{3,2,1,0:T(8,128)(2,1)}, bf16[2,1,384,384]{3,2,1,0:T(8,128)(2,1)}, bf16[2,1,384,384]{3,2,1,0:T(8,128)(2,1)}) fusion(f32[2,4,384,384]{3,2,1,0:T(8,128)} %bitcast.48, s32[]{:T(128)S(6)} %select_n.51, s32[]{:T(128)S(6)} %select_n.49, s32[]{:T(128)S(6)} %select_n.47), kind=kLoop, calls=%fused_computation.15 | loop fusion | bytes 3538956 | tf_op jit(solution)/shard_map/grad_weight/convert_element_type | solution.py:165
  83.2 0.0 copy-done.5
  83.2 2.1 fusion.3.do_ref
  85.3 22.3 %tile_attention_backward.1 = (bf16[384,384]{1,0:T(8,128)(2,1)}, bf16[3,768,384]{2,1,0:T(8,128)(2,1)}, f32[3,768,384]{2,1,0:T(8,128)}, bf16[3,768,384]{2,1,0:T(8,128)(2,1)}) custom-call(f32[1,3456]{1,0:T(1,128)} %bitcast.56, bf16[384,384]{1,0:T(8,128)(2,1)} %bitcast.50, bf16[9,784,384]{2,1,0:T(8,128)(2,1)} %copy-done.1, bf16[9,784,384]{2,1,0:T(8,128)(2,1)} %copy-done.1, ...), custom_call_target="tpu_custom_call" | custom-call | tf_op jit(solution)/shard_map/attention_backward/tile_attention_backward/pallas_call | solution.py:121
  107.6 22.5 %collective-permute-start.4 = (bf16[3,768,384]{2,1,0:T(8,128)(2,1)}, bf16[3,768,384]{2,1,0:T(8,128)(2,1)}, u32[]{:S(2)}, u32[]{:S(2)}) collective-permute-start(bf16[3,768,384]{2,1,0:T(8,128)(2,1)} %get-tuple-element.29), channel_id=1, source_target_pairs={{4,0},{8,4},{12,8},{5,1},{9,5},{13,9},{6,2},{10,6},{14,10},{7,3},{... | collective-permute-start | bytes 5308424 | tf_op jit(solution)/shard_map/halo_reduction/ppermute | solution.py:22
  130.1 1.3 collective-permute-start.5
  131.3 0.2 collective-permute-start.8
  131.6 2.3 %collective-permute-start.9 = (bf16[2,1,384,384]{3,2,1,0:T(8,128)(2,1)}, bf16[2,1,384,384]{3,2,1,0:T(8,128)(2,1)}, u32[]{:S(2)}, u32[]{:S(2)}) collective-permute-start(bf16[2,1,384,384]{3,2,1,0:T(8,128)(2,1)} %get-tuple-element.33), channel_id=1, source_target_pairs={{0,8},{4,12},{8,0},{12,4},{1,9},{5,13},{9,1},{13,5},{2,10},{6,14},... | collective-permute-start | bytes 1769480 | tf_op jit(solution)/shard_map/grad_weight/ppermute | solution.py:27
  133.9 0.0 collective-permute-start.10
  133.9 11.2 %collective-permute-done.8 = bf16[2,1,384,384]{3,2,1,0:T(8,128)(2,1)} collective-permute-done((bf16[2,1,384,384]{3,2,1,0:T(8,128)(2,1)}, bf16[2,1,384,384]{3,2,1,0:T(8,128)(2,1)}, u32[]{:S(2)}, u32[]{:S(2)}) %collective-permute-start.8) | collective-permute-done | bytes 589856 | tf_op jit(solution)/shard_map/grad_weight/ppermute | solution.py:27
  145.1 32.5 %collective-permute-done.9 = bf16[2,1,384,384]{3,2,1,0:T(8,128)(2,1)} collective-permute-done((bf16[2,1,384,384]{3,2,1,0:T(8,128)(2,1)}, bf16[2,1,384,384]{3,2,1,0:T(8,128)(2,1)}, u32[]{:S(2)}, u32[]{:S(2)}) %collective-permute-start.9) | collective-permute-done | bytes 589856 | tf_op jit(solution)/shard_map/grad_weight/ppermute | solution.py:27
  177.6 0.0 collective-permute-done.10
  177.6 1.7 convert_add_fusion.1
  179.3 0.0 copy-start.3
  179.3 0.0 collective-permute-done.4
  179.3 0.0 collective-permute-done.5
  179.3 0.0 copy-done.4
  179.3 4.9 %fusion.12 = (bf16[3,768,384]{2,1,0:T(8,128)(2,1)S(1)}, f32[3,768,384]{2,1,0:T(8,128)}) fusion(bf16[3,768,384]{2,1,0:T(8,128)(2,1)} %collective-permute-done.5, f32[3,768,384]{2,1,0:T(8,128)S(1)} %copy-done.4, bf16[3,768,384]{2,1,0:T(8,128)(2,1)} %collective-permute-done.4), kind=kLoop, calls=%fused_computation.34 | loop fusion | flops 4423680 | bytes 12386304 | tf_op jit(solution)/shard_map/halo_reduction/convert_element_type | solution.py:253
  184.2 0.9 slice_bitcast_fusion.2
  185.1 1.3 collective-permute-start.6
  186.4 1.3 collective-permute-start.7
  187.7 0.8 dynamic-slice_convert_fusion.3
  188.5 2.9 %collective-permute-start.11 = (bf16[1,1,384,384]{3,2,1,0:T(8,128)(2,1)}, bf16[1,1,384,384]{3,2,1,0:T(8,128)(2,1)}, u32[]{:S(2)}, u32[]{:S(2)}) collective-permute-start(bf16[1,1,384,384]{3,2,1,0:T(8,128)(2,1)} %dynamic-slice_convert_fusion.3), channel_id=1, source_target_pairs={{0,16},{16,0},{1,17},{17,1},{2,18},{18,2},{3,19},{19,3},{4,20},{20... | collective-permute-start | bytes 884744 | tf_op jit(solution)/shard_map/grad_weight/ppermute | solution.py:27
  191.4 15.8 %collective-permute-done.11 = bf16[1,1,384,384]{3,2,1,0:T(8,128)(2,1)} collective-permute-done((bf16[1,1,384,384]{3,2,1,0:T(8,128)(2,1)}, bf16[1,1,384,384]{3,2,1,0:T(8,128)(2,1)}, u32[]{:S(2)}, u32[]{:S(2)}) %collective-permute-start.11) | collective-permute-done | bytes 294944 | tf_op jit(solution)/shard_map/grad_weight/ppermute | solution.py:27
  207.1 2.0 add_bitcast_fusion
  209.2 0.0 collective-permute-done.6
  209.2 0.0 collective-permute-done.7
  209.2 1.6 fusion.9
  210.8 0.9 slice_bitcast_fusion.3
  (6 shorter events, 0.0 us)
Async XLA Ops:
  7.2 55.1 %copy-start = (bf16[384,3072]{1,0:T(8,128)(2,1)S(1)}, bf16[384,3072]{1,0:T(8,128)(2,1)}, u32[]{:S(2)}) copy-start(bf16[384,3072]{1,0:T(8,128)(2,1)} %param.12) | copy-start | bytes 7077892
  7.2 59.0 %all-gather.3.cloned.1.call-start = ((), (), s32[]{:S(2)}) async-start(), calls=%async_computation.2 | async-start | bytes 2949120 | tf_op jit(solution)/shard_map/cotangent_gather/all_gather | solution.py:210
  10.0 14.7 %collective-permute-start.1 = (bf16[784,384]{1,0:T(8,128)(2,1)}, bf16[784,384]{1,0:T(8,128)(2,1)}, u32[]{:S(2)}, u32[]{:S(2)}) collective-permute-start(bf16[784,384]{1,0:T(8,128)(2,1)} %get-tuple-element.43), channel_id=1, source_target_pairs={{16,0},{17,1},{18,2},{19,3},{20,4},{21,5},{22,6},{23,7},{24,8},{25... | collective-permute-start | bytes 1806344 | tf_op jit(solution)/shard_map/halo_exchange/ppermute | solution.py:22
  13.0 16.3 %collective-permute-start = (bf16[784,384]{1,0:T(8,128)(2,1)}, bf16[784,384]{1,0:T(8,128)(2,1)}, u32[]{:S(2)}, u32[]{:S(2)}) collective-permute-start(bf16[784,384]{1,0:T(8,128)(2,1)} %get-tuple-element.43), channel_id=1, source_target_pairs={{0,16},{1,17},{2,18},{3,19},{4,20},{5,21},{6,22},{7,23},{8,24},{9,... | collective-permute-start | bytes 1806344 | tf_op jit(solution)/shard_map/halo_exchange/ppermute | solution.py:22
  14.3 197.3 %reduce-scatter.2.cloned.1.call-start = ((), (), s32[]{:S(2)}) async-start(), calls=%async_computation.1 | async-start | bytes 2949120 | tf_op jit(solution)/shard_map/output_projection/reduce_scatter | solution.py:217
  32.1 7.3 %collective-permute-start.2 = (bf16[3,784,384]{2,1,0:T(8,128)(2,1)}, bf16[3,784,384]{2,1,0:T(8,128)(2,1)}, u32[]{:S(2)}, u32[]{:S(2)}) collective-permute-start(bf16[3,784,384]{2,1,0:T(8,128)(2,1)} %pad_maximum_fusion), channel_id=1, source_target_pairs={{0,4},{4,8},{8,12},{1,5},{5,9},{9,13},{2,6},{6,10},{10,14},{3,7},{... | collective-permute-start | bytes 5419016 | tf_op jit(solution)/shard_map/halo_exchange/ppermute | solution.py:22
  33.4 10.2 %collective-permute-start.3 = (bf16[3,784,384]{2,1,0:T(8,128)(2,1)}, bf16[3,784,384]{2,1,0:T(8,128)(2,1)}, u32[]{:S(2)}, u32[]{:S(2)}) collective-permute-start(bf16[3,784,384]{2,1,0:T(8,128)(2,1)} %pad_maximum_fusion), channel_id=1, source_target_pairs={{4,0},{8,4},{12,8},{5,1},{9,5},{13,9},{6,2},{10,6},{14,10},{7,3},{... | collective-permute-start | bytes 5419016 | tf_op jit(solution)/shard_map/halo_exchange/ppermute | solution.py:22
  39.0 3.3 %copy-start.6 = (bf16[1,1,384,384]{3,2,1,0:T(8,128)(2,1)S(1)}, bf16[1,1,384,384]{3,2,1,0:T(8,128)(2,1)}, u32[]{:S(2)}) copy-start(bf16[1,1,384,384]{3,2,1,0:T(8,128)(2,1)} %param.10) | copy-start | bytes 884740
  39.0 3.3 %copy-start.7 = (bf16[1,1,384,384]{3,2,1,0:T(8,128)(2,1)S(1)}, bf16[1,1,384,384]{3,2,1,0:T(8,128)(2,1)}, u32[]{:S(2)}) copy-start(bf16[1,1,384,384]{3,2,1,0:T(8,128)(2,1)} %param.9) | copy-start | bytes 884740
  45.4 2.4 %copy-start.1 = (bf16[9,784,384]{2,1,0:T(8,128)(2,1)}, bf16[9,784,384]{2,1,0:T(8,128)(2,1)S(1)}, u32[]{:S(2)}) copy-start(bf16[9,784,384]{2,1,0:T(8,128)(2,1)S(1)} %constant_dynamic-update-slice_fusion.k_ref.v_ref) | copy-start | bytes 16257028
  66.0 1.0 copy-start.2
  79.7 3.4 %copy-start.5 = (bf16[1,1,384,3072]{3,2,1,0:T(8,128)(2,1)S(1)}, bf16[1,1,384,3072]{3,2,1,0:T(8,128)(2,1)}, u32[]{:S(2)}) copy-start(bf16[1,1,384,3072]{3,2,1,0:T(8,128)(2,1)} %all-gather.3.cloned.1.call-done) | copy-start | bytes 7077892
  107.6 71.7 %collective-permute-start.4 = (bf16[3,768,384]{2,1,0:T(8,128)(2,1)}, bf16[3,768,384]{2,1,0:T(8,128)(2,1)}, u32[]{:S(2)}, u32[]{:S(2)}) collective-permute-start(bf16[3,768,384]{2,1,0:T(8,128)(2,1)} %get-tuple-element.29), channel_id=1, source_target_pairs={{4,0},{8,4},{12,8},{5,1},{9,5},{13,9},{6,2},{10,6},{14,10},{7,3},{... | collective-permute-start | bytes 5308424 | tf_op jit(solution)/shard_map/halo_reduction/ppermute | solution.py:22
  130.1 49.2 %collective-permute-start.5 = (bf16[3,768,384]{2,1,0:T(8,128)(2,1)}, bf16[3,768,384]{2,1,0:T(8,128)(2,1)}, u32[]{:S(2)}, u32[]{:S(2)}) collective-permute-start(bf16[3,768,384]{2,1,0:T(8,128)(2,1)} %get-tuple-element.30), channel_id=1, source_target_pairs={{0,4},{4,8},{8,12},{1,5},{5,9},{9,13},{2,6},{6,10},{10,14},{3,7},{... | collective-permute-start | bytes 5308424 | tf_op jit(solution)/shard_map/halo_reduction/ppermute | solution.py:22
  131.3 13.8 %collective-permute-start.8 = (bf16[2,1,384,384]{3,2,1,0:T(8,128)(2,1)}, bf16[2,1,384,384]{3,2,1,0:T(8,128)(2,1)}, u32[]{:S(2)}, u32[]{:S(2)}) collective-permute-start(bf16[2,1,384,384]{3,2,1,0:T(8,128)(2,1)} %get-tuple-element.32), channel_id=1, source_target_pairs={{0,4},{4,8},{8,12},{12,0},{1,5},{5,9},{9,13},{13,1},{2,6},{6,10},{... | collective-permute-start | bytes 1769480 | tf_op jit(solution)/shard_map/grad_weight/ppermute | solution.py:27
  131.6 46.0 %collective-permute-start.9 = (bf16[2,1,384,384]{3,2,1,0:T(8,128)(2,1)}, bf16[2,1,384,384]{3,2,1,0:T(8,128)(2,1)}, u32[]{:S(2)}, u32[]{:S(2)}) collective-permute-start(bf16[2,1,384,384]{3,2,1,0:T(8,128)(2,1)} %get-tuple-element.33), channel_id=1, source_target_pairs={{0,8},{4,12},{8,0},{12,4},{1,9},{5,13},{9,1},{13,5},{2,10},{6,14},... | collective-permute-start | bytes 1769480 | tf_op jit(solution)/shard_map/grad_weight/ppermute | solution.py:27
  133.9 43.7 %collective-permute-start.10 = (bf16[2,1,384,384]{3,2,1,0:T(8,128)(2,1)}, bf16[2,1,384,384]{3,2,1,0:T(8,128)(2,1)}, u32[]{:S(2)}, u32[]{:S(2)}) collective-permute-start(bf16[2,1,384,384]{3,2,1,0:T(8,128)(2,1)} %get-tuple-element.34), channel_id=1, source_target_pairs={{0,12},{4,0},{8,4},{12,8},{1,13},{5,1},{9,5},{13,9},{2,14},{6,2},{... | collective-permute-start | bytes 1769480 | tf_op jit(solution)/shard_map/grad_weight/ppermute | solution.py:27
  133.9 45.4 %copy-start.4 = (f32[3,768,384]{2,1,0:T(8,128)S(1)}, f32[3,768,384]{2,1,0:T(8,128)}, u32[]{:S(2)}) copy-start(f32[3,768,384]{2,1,0:T(8,128)} %get-tuple-element.28) | copy-start | bytes 10616836
  179.3 8.5 %copy-start.3 = (f32[2,1,384,384]{3,2,1,0:T(8,128)}, f32[2,1,384,384]{3,2,1,0:T(8,128)S(1)}, u32[]{:S(2)}) copy-start(f32[2,1,384,384]{3,2,1,0:T(8,128)S(1)} %convert_add_fusion.1) | copy-start | bytes 3538948
  185.1 24.0 %collective-permute-start.6 = (bf16[768,384]{1,0:T(8,128)(2,1)}, bf16[768,384]{1,0:T(8,128)(2,1)S(1)}, u32[]{:S(2)}, u32[]{:S(2)}) collective-permute-start(bf16[768,384]{1,0:T(8,128)(2,1)} %get-tuple-element.40), channel_id=1, source_target_pairs={{16,0},{17,1},{18,2},{19,3},{20,4},{21,5},{22,6},{23,7},{24,8},{25... | collective-permute-start | bytes 1769480 | tf_op jit(solution)/shard_map/halo_reduction/ppermute | solution.py:22
  186.4 22.7 %collective-permute-start.7 = (bf16[768,384]{1,0:T(8,128)(2,1)S(1)}, bf16[768,384]{1,0:T(8,128)(2,1)}, u32[]{:S(2)}, u32[]{:S(2)}) collective-permute-start(bf16[768,384]{1,0:T(8,128)(2,1)S(1)} %get-tuple-element.41), channel_id=1, source_target_pairs={{0,16},{1,17},{2,18},{3,19},{4,20},{5,21},{6,22},{7,23},{8,24},{9,... | collective-permute-start | bytes 1769480 | tf_op jit(solution)/shard_map/halo_reduction/ppermute | solution.py:22
  188.5 18.6 %collective-permute-start.11 = (bf16[1,1,384,384]{3,2,1,0:T(8,128)(2,1)}, bf16[1,1,384,384]{3,2,1,0:T(8,128)(2,1)}, u32[]{:S(2)}, u32[]{:S(2)}) collective-permute-start(bf16[1,1,384,384]{3,2,1,0:T(8,128)(2,1)} %dynamic-slice_convert_fusion.3), channel_id=1, source_target_pairs={{0,16},{16,0},{1,17},{17,1},{2,18},{18,2},{3,19},{19,3},{4,20},{20... | collective-permute-start | bytes 884744 | tf_op jit(solution)/shard_map/grad_weight/ppermute | solution.py:27
Sparse Core Ops, SparseCore 0:
  14.4 51.6 all-gather.2
  69.0 62.9 reduce-scatter.1

commit v5 on v3

--- a/solution.py
+++ b/solution.py
@@ -111,39 +111,53 @@
     )(mask, queries, window, window)
 
 
-def attention_backward(mask, queries, window, attended, grad_attended):
+def attention_backward(mask, queries, window, attended, grad_attended, head):
     tokens, features = queries.shape
     tiles = window.shape[0]
-    heads = features // HD
     chunk = BACKWARD_CHUNK
     chunks = tokens // chunk
     scale = HD ** (-0.5)
+    third = tiles // 3
     return pl.pallas_call(
         functools.partial(backward_kernel, scale),
-        grid=(heads, chunks),
+        grid=(1, chunks),
         in_specs=[
             pl.BlockSpec((1, tiles * tokens), lambda h, c: (0, 0)),
-            pl.BlockSpec((chunk, HD), lambda h, c: (c, h)),
-            pl.BlockSpec((tiles, tokens, HD), lambda h, c: (0, 0, h)),
-            pl.BlockSpec((tiles, tokens, HD), lambda h, c: (0, 1, h)),
-            pl.BlockSpec((chunk, HD), lambda h, c: (c, h)),
-            pl.BlockSpec((chunk, HD), lambda h, c: (c, h)),
+            pl.BlockSpec((chunk, HD), lambda h, c: (c, head)),
+            pl.BlockSpec((tiles, tokens, HD), lambda h, c: (0, 0, head)),
+            pl.BlockSpec((tiles, tokens, HD), lambda h, c: (0, 1, head)),
+            pl.BlockSpec((chunk, HD), lambda h, c: (c, head)),
+            pl.BlockSpec((chunk, HD), lambda h, c: (c, head)),
         ],
         out_specs=[
-            pl.BlockSpec((chunk, HD), lambda h, c: (c, h)),
-            pl.BlockSpec((tiles // 3, 2 * tokens, HD), lambda h, c: (0, 0, h)),
-            pl.BlockSpec((tiles // 3, 2 * tokens, HD), lambda h, c: (0, 0, h)),
-            pl.BlockSpec((tiles // 3, 2 * tokens, HD), lambda h, c: (0, 0, h)),
+            pl.BlockSpec((chunk, HD), lambda h, c: (c, 0)),
+            pl.BlockSpec((third, 2 * tokens, HD), lambda h, c: (0, 0, 0)),
+            pl.BlockSpec((third, 2 * tokens, HD), lambda h, c: (0, 0, 0)),
+            pl.BlockSpec((third, 2 * tokens, HD), lambda h, c: (0, 0, 0)),
         ],
         out_shape=[
-            jax.ShapeDtypeStruct((tokens, features), jnp.bfloat16),
-            jax.ShapeDtypeStruct((tiles // 3, 2 * tokens, features), jnp.bfloat16),
-            jax.ShapeDtypeStruct((tiles // 3, 2 * tokens, features), jnp.float32),
-            jax.ShapeDtypeStruct((tiles // 3, 2 * tokens, features), jnp.bfloat16),
+            jax.ShapeDtypeStruct((tokens, HD), jnp.bfloat16),
+            jax.ShapeDtypeStruct((third, 2 * tokens, HD), jnp.bfloat16),
+            jax.ShapeDtypeStruct((third, 2 * tokens, HD), jnp.float32),
+            jax.ShapeDtypeStruct((third, 2 * tokens, HD), jnp.bfloat16),
         ],
         scratch_shapes=[pltpu.VMEM((tiles, 2 * tokens, HD), jnp.float32)],
         name="tile_attention_backward",
     )(mask, queries, window, window, attended, grad_attended)
+
+
+def return_halo(left, partials, right):
+    middle = (
+        partials
+        + shifted(left, "wa", -1).astype(jnp.float32)
+        + shifted(right, "wa", 1).astype(jnp.float32)
+    )
+    middle_sides = middle.astype(jnp.bfloat16)
+    return (
+        middle[1]
+        + shifted(middle_sides[0], "fh", -1).astype(jnp.float32)
+        + shifted(middle_sides[2], "fh", 1).astype(jnp.float32)
+    )
 
 
 def gather_over(piece, axis):
@@ -233,26 +247,21 @@
         )
         weight_rows = scatter_finish(weight_own, weight_sent, "fh")
 
-    with jax.named_scope("attention_backward"):
-        grad_q, left, partials, right = attention_backward(
-            mask, q, window, attended, grad_attended
-        )
+    grad_q_heads, own_heads = [], []
+    for head in range(features // HD):
+        with jax.named_scope("attention_backward"):
+            grad_q, left, partials, right = attention_backward(
+                mask, q, window, attended, grad_attended, head
+            )
+        with jax.named_scope("halo_reduction"):
+            own_heads.append(return_halo(left, partials, right))
+        grad_q_heads.append(grad_q)
+    grad_q = jnp.concatenate(grad_q_heads, axis=1)
+    own = jnp.concatenate(own_heads, axis=1)
 
     with jax.named_scope("grad_weight"):
         grad_weight = scatter_sum(weight_rows, "wa", 0)
 
-    with jax.named_scope("halo_reduction"):
-        middle = (
-            partials
-            + shifted(left, "wa", -1).astype(jnp.float32)
-            + shifted(right, "wa", 1).astype(jnp.float32)
-        )
-        middle_sides = middle.astype(jnp.bfloat16)
-        own = (
-            middle[1]
-            + shifted(middle_sides[0], "fh", -1).astype(jnp.float32)
-            + shifted(middle_sides[2], "fh", 1).astype(jnp.float32)
-        )
     grad_keys = own[:tokens].astype(jnp.bfloat16)
     grad_values = own[tokens:].astype(jnp.bfloat16)
     expand = lambda x: x[None, None]

time: 184 us -> 196 us (1.065)
  starting transfers between devices: 28.4 us -> 48.3 us
  waiting for transfers between devices: 62.8 us -> 56.5 us
  Pallas kernels: 36.2 us -> 42 us
  other arithmetic: 16.4 us -> 11.1 us
  local copies, waits for them, and re-layouts: 16.5 us -> 14 us
    ppermute x8 -> x16, starting transfers between devices: 24.8 us -> 45.9 us  [shifted(): return lax.ppermute(value, axis, shift_pairs(lax.axis_size(axis), steps))]
    ppermute x8 -> x16, waiting for transfers between devices: 50.9 us -> 43.8 us  [shifted(): return lax.ppermute(value, axis, shift_pairs(lax.axis_size(axis), steps))]
    pallas_call x1 -> x3, Pallas kernels: 22.4 us -> 28.2 us  [attention_backward(): pl.pallas_call(functools.partial(backward_kernel, scale), grid=(1, chunks...]
    convert_element_type x1 -> x3, other arithmetic: 4.56 us -> 2.3 us  [return_halo(): middle_sides = middle.astype(jnp.bfloat16)]
    add x1, other arithmetic: 2.45 us -> 0.31 us  [scatter_finish(): total = total + cyclic(piece, axis, steps).astype(jnp.float32)]
    unnamed x24 -> x22, local copies, waits for them, and re-layouts: 9.87 us -> 9.24 us
  transfers between devices with their start and end apart: 14 -> 22, of which waited for: 8 -> 10; matrix products, arithmetic and copies ran while one was open for 19% -> 14% of each run, Pallas kernels for 20% -> 22%
where the time goes in v5:
time: 196 us; the launch traced here: 195 us
  waiting for transfers between devices  56.5 us (29%)
  starting transfers between devices  48.3 us (25%)
  Pallas kernels  42 us (21%)
  between operations  14.5 us (7%)
  local copies, waits for them, and re-layouts  14 us (7%)
  other arithmetic  11.1 us (6%)
  matrix products  8.99 us (5%)
    ppermute x16, starting transfers between devices, shifted(): return lax.ppermute(value, axis, shift_pairs(lax.axis_size(axis), steps))  45.9 us
    ppermute x16, waiting for transfers between devices, shifted(): return lax.ppermute(value, axis, shift_pairs(lax.axis_size(axis), steps))  43.8 us
    pallas_call x3, Pallas kernels, attention_backward(): pl.pallas_call(functools.partial(backward_kernel, scale), grid=(1, chunks...  28.2 us
    pallas_call x1, Pallas kernels, attention_forward(): pl.pallas_call(functools.partial(forward_kernel, scale), grid=(heads, chu...  13.8 us
    ppermute x4, waiting for transfers between devices, cyclic(): lax.ppermute(value, axis, [(i, (i + steps) % count) for i in range(count)])  12.6 us
    unnamed x22, local copies, waits for them, and re-layouts  9.24 us
    another operation x2, other arithmetic, body(): jnp.stack([shifted(packed, 'fh', 1), packed, shifted(packed, 'fh', -1)])  4.69 us
  transfers between devices with their start and end apart: 22, of which 10 were waited for; matrix products, arithmetic and copies ran while one was open for 14% of the time, Pallas kernels for 22%

profile of v5, /device:TPU:1, one launch (start us, length us, event | category | flops | bytes accessed | tf_op | source)
XLA Modules:
  0.0 195.4 jit_solution(13928671792378359568)
XLA Ops:
  7.2 0.0 all-gather.3.cloned.1.call-start
  7.2 0.8 convert_bitcast_fusion
  8.1 2.0 %fusion.16 = (bf16[1,784,384]{2,1,0:T(8,128)(2,1)S(1)}, bf16[784,384]{1,0:T(8,128)(2,1)}) fusion(bf16[1,384]{1,0:T(2,128)(2,1)S(1)} %convert_bitcast_fusion, bf16[384,384]{1,0:T(8,128)(2,1)} %bitcast.69, bf16[384,384]{1,0:T(8,128)(2,1)} %bitcast.71), kind=kLoop, calls=%fused_computation.47 | loop fusion | flops 2408448 | bytes 1794816 | tf_op jit(solution)/shard_map/halo_exchange/stack | solution.py:215
  10.0 4.8 %collective-permute-start = (bf16[784,384]{1,0:T(8,128)(2,1)}, bf16[784,384]{1,0:T(8,128)(2,1)}, u32[]{:S(2)}, u32[]{:S(2)}) collective-permute-start(bf16[784,384]{1,0:T(8,128)(2,1)} %get-tuple-element.62), channel_id=1, source_target_pairs={{0,16},{1,17},{2,18},{3,19},{4,20},{5,21},{6,22},{7,23},{8,24},{9,... | collective-permute-start | bytes 1806344 | tf_op jit(solution)/shard_map/halo_exchange/ppermute | solution.py:22
  14.8 1.3 collective-permute-start.1
  16.1 0.0 reduce-scatter.2.cloned.1.call-start
  16.2 10.4 %collective-permute-done = bf16[784,384]{1,0:T(8,128)(2,1)} collective-permute-done((bf16[784,384]{1,0:T(8,128)(2,1)}, bf16[784,384]{1,0:T(8,128)(2,1)}, u32[]{:S(2)}, u32[]{:S(2)}) %collective-permute-start) | collective-permute-done | bytes 602144 | tf_op jit(solution)/shard_map/halo_exchange/ppermute | solution.py:22
  26.6 4.6 %collective-permute-done.1 = bf16[784,384]{1,0:T(8,128)(2,1)} collective-permute-done((bf16[784,384]{1,0:T(8,128)(2,1)}, bf16[784,384]{1,0:T(8,128)(2,1)}, u32[]{:S(2)}, u32[]{:S(2)}) %collective-permute-start.1) | collective-permute-done | bytes 602144 | tf_op jit(solution)/shard_map/halo_exchange/ppermute | solution.py:22
  31.2 2.7 %pad_maximum_fusion = bf16[3,784,384]{2,1,0:T(8,128)(2,1)} fusion(bf16[1,784,384]{2,1,0:T(8,128)(2,1)} %bitcast.5, bf16[1,784,384]{2,1,0:T(8,128)(2,1)S(1)} %get-tuple-element.61, bf16[1,784,384]{2,1,0:T(8,128)(2,1)} %bitcast.3), kind=kLoop, calls=%fused_computation.8 | loop fusion | flops 1806336 | bytes 3612672 | tf_op jit(solution)/shard_map/halo_exchange/stack | solution.py:215
  33.9 4.9 %collective-permute-start.2 = (bf16[3,784,384]{2,1,0:T(8,128)(2,1)}, bf16[3,784,384]{2,1,0:T(8,128)(2,1)}, u32[]{:S(2)}, u32[]{:S(2)}) collective-permute-start(bf16[3,784,384]{2,1,0:T(8,128)(2,1)} %pad_maximum_fusion), channel_id=1, source_target_pairs={{0,4},{4,8},{8,12},{1,5},{5,9},{9,13},{2,6},{6,10},{10,14},{3,7},{... | collective-permute-start | bytes 5419016 | tf_op jit(solution)/shard_map/halo_exchange/ppermute | solution.py:22
  38.8 1.9 collective-permute-start.3
  40.7 18.2 %collective-permute-done.2 = bf16[3,784,384]{2,1,0:T(8,128)(2,1)} collective-permute-done((bf16[3,784,384]{2,1,0:T(8,128)(2,1)}, bf16[3,784,384]{2,1,0:T(8,128)(2,1)}, u32[]{:S(2)}, u32[]{:S(2)}) %collective-permute-start.2) | collective-permute-done | bytes 1806368 | tf_op jit(solution)/shard_map/halo_exchange/ppermute | solution.py:22
  58.9 1.7 constant_dynamic-update-slice_fusion.4
  60.6 1.2 constant_dynamic-update-slice_fusion.3
  61.8 0.1 constant_dynamic-update-slice_fusion.2
  61.9 1.2 constant_dynamic-update-slice_fusion.1
  63.1 0.6 collective-permute-done.3
  63.6 1.9 constant_dynamic-update-slice_fusion.k_ref.v_ref
  65.5 2.4 %copy-done.1 = bf16[9,784,384]{2,1,0:T(8,128)(2,1)} copy-done((bf16[9,784,384]{2,1,0:T(8,128)(2,1)}, bf16[9,784,384]{2,1,0:T(8,128)(2,1)S(1)}, u32[]{:S(2)}) %copy-start.1) | copy-done | bytes 5419032
  67.9 0.6 compare_select_fusion
  68.5 13.8 %tile_attention_forward.1.o_ref = bf16[384,384]{1,0:T(8,128)(2,1)} custom-call(f32[1,3456]{1,0:T(1,128)} %bitcast.73, bf16[384,384]{1,0:T(8,128)(2,1)} %bitcast.65, bf16[9,784,384]{2,1,0:T(8,128)(2,1)} %copy-done.1, bf16[9,784,384]{2,1,0:T(8,128)(2,1)} %copy-done.1), custom_call_target="tpu_custom_call" | custom-call | tf_op jit(solution)/shard_map/attention_forward/tile_attention_forward/pallas_call | solution.py:99
  82.3 3.8 %convolution_convert_fusion = bf16[384,3072]{1,0:T(8,128)(2,1)} fusion(bf16[384,384]{1,0:T(8,128)(2,1)} %tile_attention_forward.1.o_ref, bf16[384,3072]{1,0:T(8,128)(2,1)S(1)} %copy-done), kind=kOutput, calls=%fused_computation | convolution fusion | flops 907149312 | bytes 5013504 | tf_op jit(solution)/shard_map/output_projection/dot_general | solution.py:230
  86.2 0.9 copy-done.2
  87.1 3.1 %fusion.2 = f32[384,3072]{1,0:T(8,128)S(1)} fusion(bf16[384,384]{1,0:T(8,128)(2,1)S(1)} %copy-done.2, bf16[1,1,384,3072]{3,2,1,0:T(8,128)(2,1)} %all-gather.3.cloned.1.call-done), kind=kOutput, calls=%fused_computation.3 | convolution fusion | flops 905969664 | bytes 7372800 | tf_op jit(solution)/shard_map/grad_weight/dot_general | solution.py:241
  90.2 1.6 dynamic-slice_bitcast_fusion
  91.8 0.9 copy-done.4
  92.7 2.1 %fusion.4.do_ref = bf16[384,384]{1,0:T(8,128)(2,1)} fusion(bf16[384,3072]{1,0:T(8,128)(2,1)S(1)} %copy-done, bf16[1,1,384,3072]{3,2,1,0:T(8,128)(2,1)S(1)} %copy-done.4), kind=kOutput, calls=%fused_computation.9 | convolution fusion | flops 906117120 | bytes 5013504 | tf_op jit(solution)/shard_map/grad_attended/dot_general | solution.py:236
  94.8 0.1 fusion.8
  94.9 9.4 %tile_attention_backward.3 = (bf16[384,128]{1,0:T(8,128)(2,1)}, bf16[3,768,128]{2,1,0:T(8,128)(2,1)}, f32[3,768,128]{2,1,0:T(8,128)}, bf16[3,768,128]{2,1,0:T(8,128)(2,1)}) custom-call(f32[1,3456]{1,0:T(1,128)} %bitcast.74, bf16[384,384]{1,0:T(8,128)(2,1)} %bitcast.66, bf16[9,784,384]{2,1,0:T(8,128)(2,1)} %copy-done.1, bf16[9,784,384]{2,1,0:T(8,128)(2,1)} %copy-done.1, ...), custom_call_target="tpu_custom_call" | custom-call | tf_op jit(solution)/shard_map/attention_backward/tile_attention_backward/pallas_call | solution.py:121
  104.3 1.9 collective-permute-start.4
  106.2 4.0 %collective-permute-start.5 = (bf16[3,768,128]{2,1,0:T(8,128)(2,1)}, bf16[3,768,128]{2,1,0:T(8,128)(2,1)}, u32[]{:S(2)}, u32[]{:S(2)}) collective-permute-start(bf16[3,768,128]{2,1,0:T(8,128)(2,1)} %get-tuple-element.38), channel_id=1, source_target_pairs={{0,4},{4,8},{8,12},{1,5},{5,9},{9,13},{2,6},{6,10},{10,14},{3,7},{... | collective-permute-start | bytes 1769480 | tf_op jit(solution)/shard_map/halo_reduction/ppermute | solution.py:22
  110.3 9.4 %tile_attention_backward.4 = (bf16[384,128]{1,0:T(8,128)(2,1)}, bf16[3,768,128]{2,1,0:T(8,128)(2,1)}, f32[3,768,128]{2,1,0:T(8,128)}, bf16[3,768,128]{2,1,0:T(8,128)(2,1)}) custom-call(f32[1,3456]{1,0:T(1,128)} %bitcast.75, bf16[384,384]{1,0:T(8,128)(2,1)} %bitcast.67, bf16[9,784,384]{2,1,0:T(8,128)(2,1)} %copy-done.1, bf16[9,784,384]{2,1,0:T(8,128)(2,1)} %copy-done.1, ...), custom_call_target="tpu_custom_call" | custom-call | tf_op jit(solution)/shard_map/attention_backward/tile_attention_backward/pallas_call | solution.py:121
  119.7 9.4 %tile_attention_backward.5 = (bf16[384,128]{1,0:T(8,128)(2,1)}, bf16[3,768,128]{2,1,0:T(8,128)(2,1)}, f32[3,768,128]{2,1,0:T(8,128)}, bf16[3,768,128]{2,1,0:T(8,128)(2,1)}) custom-call(f32[1,3456]{1,0:T(1,128)} %bitcast.76, bf16[384,384]{1,0:T(8,128)(2,1)} %bitcast.68, bf16[9,784,384]{2,1,0:T(8,128)(2,1)} %copy-done.1, bf16[9,784,384]{2,1,0:T(8,128)(2,1)} %copy-done.1, ...), custom_call_target="tpu_custom_call" | custom-call | tf_op jit(solution)/shard_map/attention_backward/tile_attention_backward/pallas_call | solution.py:121
  129.2 1.9 collective-permute-start.8
  131.1 3.6 %collective-permute-start.9 = (bf16[3,768,128]{2,1,0:T(8,128)(2,1)}, bf16[3,768,128]{2,1,0:T(8,128)(2,1)S(1)}, u32[]{:S(2)}, u32[]{:S(2)}) collective-permute-start(bf16[3,768,128]{2,1,0:T(8,128)(2,1)} %get-tuple-element.41), channel_id=1, source_target_pairs={{0,4},{4,8},{8,12},{1,5},{5,9},{9,13},{2,6},{6,10},{10,14},{3,7},{... | collective-permute-start | bytes 1769480 | tf_op jit(solution)/shard_map/halo_reduction/ppermute | solution.py:22
  134.7 1.7 maximum_bitcast_fusion
  136.5 1.9 collective-permute-start.12
  138.4 3.6 %collective-permute-start.13 = (bf16[3,768,128]{2,1,0:T(8,128)(2,1)}, bf16[3,768,128]{2,1,0:T(8,128)(2,1)S(1)}, u32[]{:S(2)}, u32[]{:S(2)}) collective-permute-start(bf16[3,768,128]{2,1,0:T(8,128)(2,1)} %get-tuple-element.44), channel_id=1, source_target_pairs={{0,4},{4,8},{8,12},{1,5},{5,9},{9,13},{2,6},{6,10},{10,14},{3,7},{... | collective-permute-start | bytes 1769480 | tf_op jit(solution)/shard_map/halo_reduction/ppermute | solution.py:22
  142.1 1.9 fusion.17
  144.0 1.3 collective-permute-start.6
  145.3 4.0 %collective-permute-start.7 = (bf16[768,128]{1,0:T(8,128)(2,1)S(1)}, bf16[768,128]{1,0:T(8,128)(2,1)S(1)}, u32[]{:S(2)}, u32[]{:S(2)}) collective-permute-start(bf16[768,128]{1,0:T(8,128)(2,1)S(1)} %get-tuple-element.66), channel_id=1, source_target_pairs={{0,16},{1,17},{2,18},{3,19},{4,20},{5,21},{6,22},{7,23},{8,24},{9,... | collective-permute-start | bytes 589832 | tf_op jit(solution)/shard_map/halo_reduction/ppermute | solution.py:22
  149.3 0.2 fusion.18
  149.6 1.4 collective-permute-start.10
  151.0 4.0 %collective-permute-start.11 = (bf16[768,128]{1,0:T(8,128)(2,1)S(1)}, bf16[768,128]{1,0:T(8,128)(2,1)S(1)}, u32[]{:S(2)}, u32[]{:S(2)}) collective-permute-start(bf16[768,128]{1,0:T(8,128)(2,1)S(1)} %get-tuple-element.68), channel_id=1, source_target_pairs={{0,16},{1,17},{2,18},{3,19},{4,20},{5,21},{6,22},{7,23},{8,24},{9,... | collective-permute-start | bytes 589832 | tf_op jit(solution)/shard_map/halo_reduction/ppermute | solution.py:22
  155.1 0.2 fusion.19
  155.3 6.0 %collective-permute-done.6 = bf16[768,128]{1,0:T(8,128)(2,1)S(1)} collective-permute-done((bf16[768,128]{1,0:T(8,128)(2,1)S(1)}, bf16[768,128]{1,0:T(8,128)(2,1)S(1)}, u32[]{:S(2)}, u32[]{:S(2)}) %collective-permute-start.6) | collective-permute-done | bytes 196640 | tf_op jit(solution)/shard_map/halo_reduction/ppermute | solution.py:22
  161.3 1.3 collective-permute-start.14
  162.6 4.0 %collective-permute-start.15 = (bf16[768,128]{1,0:T(8,128)(2,1)S(1)}, bf16[768,128]{1,0:T(8,128)(2,1)S(1)}, u32[]{:S(2)}, u32[]{:S(2)}) collective-permute-start(bf16[768,128]{1,0:T(8,128)(2,1)S(1)} %get-tuple-element.70), channel_id=1, source_target_pairs={{0,16},{1,17},{2,18},{3,19},{4,20},{5,21},{6,22},{7,23},{8,24},{9,... | collective-permute-start | bytes 589832 | tf_op jit(solution)/shard_map/halo_reduction/ppermute | solution.py:22
  166.7 0.1 fusion.15
  166.8 0.1 fusion.13
  166.8 3.0 %collective-permute-done.14 = bf16[768,128]{1,0:T(8,128)(2,1)S(1)} collective-permute-done((bf16[768,128]{1,0:T(8,128)(2,1)S(1)}, bf16[768,128]{1,0:T(8,128)(2,1)S(1)}, u32[]{:S(2)}, u32[]{:S(2)}) %collective-permute-start.14) | collective-permute-done | bytes 196640 | tf_op jit(solution)/shard_map/halo_reduction/ppermute | solution.py:22
  169.9 1.0 collective-permute-done.15
  170.9 0.1 fusion.11
  171.0 0.3 convert_add_fusion
  171.3 0.2 dynamic-slice_convert_fusion.3
  171.5 1.8 collective-permute-start.17
  173.3 0.5 collective-permute-start.18
  173.7 0.1 maximum_convert_fusion
  173.8 0.9 slice_bitcast_fusion.3
  174.7 4.8 %collective-permute-done.17 = bf16[384,384]{0,1:T(8,128)(2,1)S(1)} collective-permute-done((bf16[384,384]{0,1:T(8,128)(2,1)S(1)}, bf16[384,384]{0,1:T(8,128)(2,1)S(1)}, u32[]{:S(2)}, u32[]{:S(2)}) %collective-permute-start.17) | collective-permute-done | bytes 294944 | tf_op jit(solution)/shard_map/grad_weight/ppermute | solution.py:27
  179.5 7.2 %collective-permute-done.18 = bf16[384,384]{0,1:T(8,128)(2,1)S(1)} collective-permute-done((bf16[384,384]{0,1:T(8,128)(2,1)S(1)}, bf16[384,384]{0,1:T(8,128)(2,1)S(1)}, u32[]{:S(2)}, u32[]{:S(2)}) %collective-permute-start.18) | collective-permute-done | bytes 294944 | tf_op jit(solution)/shard_map/grad_weight/ppermute | solution.py:27
  186.7 0.6 collective-permute-done.19
  187.3 0.2 convert_add_fusion.4
  187.5 1.1 copy.11
  (34 shorter events, 0.2 us)
Async XLA Ops:
  7.2 75.1 %copy-start = (bf16[384,3072]{1,0:T(8,128)(2,1)S(1)}, bf16[384,3072]{1,0:T(8,128)(2,1)}, u32[]{:S(2)}) copy-start(bf16[384,3072]{1,0:T(8,128)(2,1)} %param.12) | copy-start | bytes 7077892
  7.2 79.0 %all-gather.3.cloned.1.call-start = ((), (), s32[]{:S(2)}) async-start(), calls=%async_computation.2 | async-start | bytes 2949120 | tf_op jit(solution)/shard_map/cotangent_gather/all_gather | solution.py:224
  10.0 16.5 %collective-permute-start = (bf16[784,384]{1,0:T(8,128)(2,1)}, bf16[784,384]{1,0:T(8,128)(2,1)}, u32[]{:S(2)}, u32[]{:S(2)}) collective-permute-start(bf16[784,384]{1,0:T(8,128)(2,1)} %get-tuple-element.62), channel_id=1, source_target_pairs={{0,16},{1,17},{2,18},{3,19},{4,20},{5,21},{6,22},{7,23},{8,24},{9,... | collective-permute-start | bytes 1806344 | tf_op jit(solution)/shard_map/halo_exchange/ppermute | solution.py:22
  14.8 16.3 %collective-permute-start.1 = (bf16[784,384]{1,0:T(8,128)(2,1)}, bf16[784,384]{1,0:T(8,128)(2,1)}, u32[]{:S(2)}, u32[]{:S(2)}) collective-permute-start(bf16[784,384]{1,0:T(8,128)(2,1)} %get-tuple-element.62), channel_id=1, source_target_pairs={{16,0},{17,1},{18,2},{19,3},{20,4},{21,5},{22,6},{23,7},{24,8},{25... | collective-permute-start | bytes 1806344 | tf_op jit(solution)/shard_map/halo_exchange/ppermute | solution.py:22
  16.1 172.4 %reduce-scatter.2.cloned.1.call-start = ((), (), s32[]{:S(2)}) async-start(), calls=%async_computation.1 | async-start | bytes 2949120 | tf_op jit(solution)/shard_map/output_projection/reduce_scatter | solution.py:231
  33.9 25.0 %collective-permute-start.2 = (bf16[3,784,384]{2,1,0:T(8,128)(2,1)}, bf16[3,784,384]{2,1,0:T(8,128)(2,1)}, u32[]{:S(2)}, u32[]{:S(2)}) collective-permute-start(bf16[3,784,384]{2,1,0:T(8,128)(2,1)} %pad_maximum_fusion), channel_id=1, source_target_pairs={{0,4},{4,8},{8,12},{1,5},{5,9},{9,13},{2,6},{6,10},{10,14},{3,7},{... | collective-permute-start | bytes 5419016 | tf_op jit(solution)/shard_map/halo_exchange/ppermute | solution.py:22
  38.8 24.8 %collective-permute-start.3 = (bf16[3,784,384]{2,1,0:T(8,128)(2,1)}, bf16[3,784,384]{2,1,0:T(8,128)(2,1)}, u32[]{:S(2)}, u32[]{:S(2)}) collective-permute-start(bf16[3,784,384]{2,1,0:T(8,128)(2,1)} %pad_maximum_fusion), channel_id=1, source_target_pairs={{4,0},{8,4},{12,8},{5,1},{9,5},{13,9},{6,2},{10,6},{14,10},{7,3},{... | collective-permute-start | bytes 5419016 | tf_op jit(solution)/shard_map/halo_exchange/ppermute | solution.py:22
  40.7 21.1 %copy-start.5 = (bf16[1,1,384,384]{3,2,1,0:T(8,128)(2,1)S(1)}, bf16[1,1,384,384]{3,2,1,0:T(8,128)(2,1)}, u32[]{:S(2)}) copy-start(bf16[1,1,384,384]{3,2,1,0:T(8,128)(2,1)} %param.10) | copy-start | bytes 884740
  40.7 21.1 %copy-start.6 = (bf16[1,1,384,384]{3,2,1,0:T(8,128)(2,1)S(1)}, bf16[1,1,384,384]{3,2,1,0:T(8,128)(2,1)}, u32[]{:S(2)}) copy-start(bf16[1,1,384,384]{3,2,1,0:T(8,128)(2,1)} %param.9) | copy-start | bytes 884740
  65.5 2.4 %copy-start.1 = (bf16[9,784,384]{2,1,0:T(8,128)(2,1)}, bf16[9,784,384]{2,1,0:T(8,128)(2,1)S(1)}, u32[]{:S(2)}) copy-start(bf16[9,784,384]{2,1,0:T(8,128)(2,1)S(1)} %constant_dynamic-update-slice_fusion.k_ref.v_ref) | copy-start | bytes 16257028
  86.1 1.0 copy-start.2
  90.1 2.5 %copy-start.4 = (bf16[1,1,384,3072]{3,2,1,0:T(8,128)(2,1)S(1)}, bf16[1,1,384,3072]{3,2,1,0:T(8,128)(2,1)}, u32[]{:S(2)}) copy-start(bf16[1,1,384,3072]{3,2,1,0:T(8,128)(2,1)} %all-gather.3.cloned.1.call-done) | copy-start | bytes 7077892
  104.3 32.2 %collective-permute-start.4 = (bf16[3,768,128]{2,1,0:T(8,128)(2,1)}, bf16[3,768,128]{2,1,0:T(8,128)(2,1)}, u32[]{:S(2)}, u32[]{:S(2)}) collective-permute-start(bf16[3,768,128]{2,1,0:T(8,128)(2,1)} %get-tuple-element.37), channel_id=1, source_target_pairs={{4,0},{8,4},{12,8},{5,1},{9,5},{13,9},{6,2},{10,6},{14,10},{7,3},{... | collective-permute-start | bytes 1769480 | tf_op jit(solution)/shard_map/halo_reduction/ppermute | solution.py:22
  106.2 32.2 %collective-permute-start.5 = (bf16[3,768,128]{2,1,0:T(8,128)(2,1)}, bf16[3,768,128]{2,1,0:T(8,128)(2,1)}, u32[]{:S(2)}, u32[]{:S(2)}) collective-permute-start(bf16[3,768,128]{2,1,0:T(8,128)(2,1)} %get-tuple-element.38), channel_id=1, source_target_pairs={{0,4},{4,8},{8,12},{1,5},{5,9},{9,13},{2,6},{6,10},{10,14},{3,7},{... | collective-permute-start | bytes 1769480 | tf_op jit(solution)/shard_map/halo_reduction/ppermute | solution.py:22
  129.1 41.8 %collective-permute-start.16 = (bf16[1536,384]{0,1:T(8,128)(2,1)S(1)}, bf16[1536,384]{0,1:T(8,128)(2,1)S(1)}, u32[]{:S(2)}, u32[]{:S(2)}) collective-permute-start(bf16[1536,384]{0,1:T(8,128)(2,1)S(1)} %fusion.8), channel_id=1, source_target_pairs={{0,16},{16,0},{1,17},{17,1},{2,18},{18,2},{3,19},{19,3},{4,20},{20... | collective-permute-start | bytes 3538952 | tf_op jit(solution)/shard_map/grad_weight/ppermute | solution.py:27
  129.2 14.8 %collective-permute-start.8 = (bf16[3,768,128]{2,1,0:T(8,128)(2,1)}, bf16[3,768,128]{2,1,0:T(8,128)(2,1)S(1)}, u32[]{:S(2)}, u32[]{:S(2)}) collective-permute-start(bf16[3,768,128]{2,1,0:T(8,128)(2,1)} %get-tuple-element.40), channel_id=1, source_target_pairs={{4,0},{8,4},{12,8},{5,1},{9,5},{13,9},{6,2},{10,6},{14,10},{7,3},{... | collective-permute-start | bytes 1769480 | tf_op jit(solution)/shard_map/halo_reduction/ppermute | solution.py:22
  131.1 14.2 %collective-permute-start.9 = (bf16[3,768,128]{2,1,0:T(8,128)(2,1)}, bf16[3,768,128]{2,1,0:T(8,128)(2,1)S(1)}, u32[]{:S(2)}, u32[]{:S(2)}) collective-permute-start(bf16[3,768,128]{2,1,0:T(8,128)(2,1)} %get-tuple-element.41), channel_id=1, source_target_pairs={{0,4},{4,8},{8,12},{1,5},{5,9},{9,13},{2,6},{6,10},{10,14},{3,7},{... | collective-permute-start | bytes 1769480 | tf_op jit(solution)/shard_map/halo_reduction/ppermute | solution.py:22
  136.5 13.1 %collective-permute-start.12 = (bf16[3,768,128]{2,1,0:T(8,128)(2,1)}, bf16[3,768,128]{2,1,0:T(8,128)(2,1)S(1)}, u32[]{:S(2)}, u32[]{:S(2)}) collective-permute-start(bf16[3,768,128]{2,1,0:T(8,128)(2,1)} %get-tuple-element.43), channel_id=1, source_target_pairs={{4,0},{8,4},{12,8},{5,1},{9,5},{13,9},{6,2},{10,6},{14,10},{7,3},{... | collective-permute-start | bytes 1769480 | tf_op jit(solution)/shard_map/halo_reduction/ppermute | solution.py:22
  138.4 12.6 %collective-permute-start.13 = (bf16[3,768,128]{2,1,0:T(8,128)(2,1)}, bf16[3,768,128]{2,1,0:T(8,128)(2,1)S(1)}, u32[]{:S(2)}, u32[]{:S(2)}) collective-permute-start(bf16[3,768,128]{2,1,0:T(8,128)(2,1)} %get-tuple-element.44), channel_id=1, source_target_pairs={{0,4},{4,8},{8,12},{1,5},{5,9},{9,13},{2,6},{6,10},{10,14},{3,7},{... | collective-permute-start | bytes 1769480 | tf_op jit(solution)/shard_map/halo_reduction/ppermute | solution.py:22
  142.1 7.3 %copy-start.8 = (f32[3,768,128]{2,1,0:T(8,128)S(1)}, f32[3,768,128]{2,1,0:T(8,128)}, u32[]{:S(2)}) copy-start(f32[3,768,128]{2,1,0:T(8,128)} %get-tuple-element.39) | copy-start | bytes 3538948
  144.0 17.3 %collective-permute-start.6 = (bf16[768,128]{1,0:T(8,128)(2,1)S(1)}, bf16[768,128]{1,0:T(8,128)(2,1)S(1)}, u32[]{:S(2)}, u32[]{:S(2)}) collective-permute-start(bf16[768,128]{1,0:T(8,128)(2,1)S(1)} %get-tuple-element.65), channel_id=1, source_target_pairs={{16,0},{17,1},{18,2},{19,3},{20,4},{21,5},{22,6},{23,7},{24,8},{25... | collective-permute-start | bytes 589832 | tf_op jit(solution)/shard_map/halo_reduction/ppermute | solution.py:22
  145.3 17.3 %collective-permute-start.7 = (bf16[768,128]{1,0:T(8,128)(2,1)S(1)}, bf16[768,128]{1,0:T(8,128)(2,1)S(1)}, u32[]{:S(2)}, u32[]{:S(2)}) collective-permute-start(bf16[768,128]{1,0:T(8,128)(2,1)S(1)} %get-tuple-element.66), channel_id=1, source_target_pairs={{0,16},{1,17},{2,18},{3,19},{4,20},{5,21},{6,22},{7,23},{8,24},{9,... | collective-permute-start | bytes 589832 | tf_op jit(solution)/shard_map/halo_reduction/ppermute | solution.py:22
  149.3 5.7 %copy-start.7 = (f32[3,768,128]{2,1,0:T(8,128)S(1)}, f32[3,768,128]{2,1,0:T(8,128)}, u32[]{:S(2)}) copy-start(f32[3,768,128]{2,1,0:T(8,128)} %get-tuple-element.42) | copy-start | bytes 3538948
  149.6 17.1 %collective-permute-start.10 = (bf16[768,128]{1,0:T(8,128)(2,1)S(1)}, bf16[768,128]{1,0:T(8,128)(2,1)S(1)}, u32[]{:S(2)}, u32[]{:S(2)}) collective-permute-start(bf16[768,128]{1,0:T(8,128)(2,1)S(1)} %get-tuple-element.67), channel_id=1, source_target_pairs={{16,0},{17,1},{18,2},{19,3},{20,4},{21,5},{22,6},{23,7},{24,8},{25... | collective-permute-start | bytes 589832 | tf_op jit(solution)/shard_map/halo_reduction/ppermute | solution.py:22
  151.0 15.7 %collective-permute-start.11 = (bf16[768,128]{1,0:T(8,128)(2,1)S(1)}, bf16[768,128]{1,0:T(8,128)(2,1)S(1)}, u32[]{:S(2)}, u32[]{:S(2)}) collective-permute-start(bf16[768,128]{1,0:T(8,128)(2,1)S(1)} %get-tuple-element.68), channel_id=1, source_target_pairs={{0,16},{1,17},{2,18},{3,19},{4,20},{5,21},{6,22},{7,23},{8,24},{9,... | collective-permute-start | bytes 589832 | tf_op jit(solution)/shard_map/halo_reduction/ppermute | solution.py:22
  155.3 15.7 %copy-start.3 = (f32[1536,384]{0,1:T(8,128)S(1)}, f32[1536,384]{0,1:T(8,128)}, u32[]{:S(2)}) copy-start(f32[1536,384]{0,1:T(8,128)} %dynamic-slice_bitcast_fusion) | copy-start | bytes 7077892
  161.3 8.6 %collective-permute-start.14 = (bf16[768,128]{1,0:T(8,128)(2,1)S(1)}, bf16[768,128]{1,0:T(8,128)(2,1)S(1)}, u32[]{:S(2)}, u32[]{:S(2)}) collective-permute-start(bf16[768,128]{1,0:T(8,128)(2,1)S(1)} %get-tuple-element.69), channel_id=1, source_target_pairs={{16,0},{17,1},{18,2},{19,3},{20,4},{21,5},{22,6},{23,7},{24,8},{25... | collective-permute-start | bytes 589832 | tf_op jit(solution)/shard_map/halo_reduction/ppermute | solution.py:22
  162.6 8.2 %collective-permute-start.15 = (bf16[768,128]{1,0:T(8,128)(2,1)S(1)}, bf16[768,128]{1,0:T(8,128)(2,1)S(1)}, u32[]{:S(2)}, u32[]{:S(2)}) collective-permute-start(bf16[768,128]{1,0:T(8,128)(2,1)S(1)} %get-tuple-element.70), channel_id=1, source_target_pairs={{0,16},{1,17},{2,18},{3,19},{4,20},{5,21},{6,22},{7,23},{8,24},{9,... | collective-permute-start | bytes 589832 | tf_op jit(solution)/shard_map/halo_reduction/ppermute | solution.py:22
  171.5 8.0 %collective-permute-start.17 = (bf16[384,384]{0,1:T(8,128)(2,1)S(1)}, bf16[384,384]{0,1:T(8,128)(2,1)S(1)}, u32[]{:S(2)}, u32[]{:S(2)}) collective-permute-start(bf16[384,384]{0,1:T(8,128)(2,1)S(1)} %get-tuple-element.58), channel_id=1, source_target_pairs={{0,4},{4,8},{8,12},{12,0},{1,5},{5,9},{9,13},{13,1},{2,6},{6,10},{... | collective-permute-start | bytes 884744 | tf_op jit(solution)/shard_map/grad_weight/ppermute | solution.py:27
  173.3 13.4 %collective-permute-start.18 = (bf16[384,384]{0,1:T(8,128)(2,1)S(1)}, bf16[384,384]{0,1:T(8,128)(2,1)S(1)}, u32[]{:S(2)}, u32[]{:S(2)}) collective-permute-start(bf16[384,384]{0,1:T(8,128)(2,1)S(1)} %get-tuple-element.60), channel_id=1, source_target_pairs={{0,8},{4,12},{8,0},{12,4},{1,9},{5,13},{9,1},{13,5},{2,10},{6,14},... | collective-permute-start | bytes 884744 | tf_op jit(solution)/shard_map/grad_weight/ppermute | solution.py:27
  173.7 13.6 %collective-permute-start.19 = (bf16[384,384]{0,1:T(8,128)(2,1)S(1)}, bf16[384,384]{0,1:T(8,128)(2,1)S(1)}, u32[]{:S(2)}, u32[]{:S(2)}) collective-permute-start(bf16[384,384]{0,1:T(8,128)(2,1)S(1)} %get-tuple-element.59), channel_id=1, source_target_pairs={{0,12},{4,0},{8,4},{12,8},{1,13},{5,1},{9,5},{13,9},{2,14},{6,2},{... | collective-permute-start | bytes 884744 | tf_op jit(solution)/shard_map/grad_weight/ppermute | solution.py:27
Sparse Core Ops, SparseCore 0:
  16.3 53.9 all-gather.2
  86.2 48.3 reduce-scatter.1

commit v6 on v3

--- a/solution.py
+++ b/solution.py
@@ -214,9 +214,7 @@
 
     with jax.named_scope("output_projection"):
         projected = jnp.dot(attended, out_weight, preferred_element_type=jnp.float32)
-        layer_out = lax.psum_scatter(
-            projected.astype(jnp.bfloat16), "ha", scatter_dimension=0, tiled=True
-        )
+        out_own, out_sent = scatter_parts(projected, "ha", 0)
 
     with jax.named_scope("grad_attended"):
         grad_attended = lax.dot_general(
@@ -227,11 +225,14 @@
         weight_part = lax.dot_general(
             cot_all, attended, (((0,), (0,)), ((), ())), preferred_element_type=jnp.float32
         )
-        weight_own, weight_sent = scatter_parts(weight_part, "fh", 0)
-        weight_own, weight_sent, grad_attended = lax.optimization_barrier(
-            (weight_own, weight_sent, grad_attended)
-        )
-        weight_rows = scatter_finish(weight_own, weight_sent, "fh")
+        weight_bf16 = weight_part.astype(jnp.bfloat16)
+        out_own, out_sent, weight_bf16, grad_attended = lax.optimization_barrier(
+            (out_own, out_sent, weight_bf16, grad_attended)
+        )
+        layer_out = scatter_finish(out_own, out_sent, "ha").astype(jnp.bfloat16)
+        weight_summed = lax.psum_scatter(
+            weight_bf16, ("fh", "wa"), scatter_dimension=0, tiled=True
+        )
 
     with jax.named_scope("attention_backward"):
         grad_q, left, partials, right = attention_backward(
@@ -239,7 +240,7 @@
         )
 
     with jax.named_scope("grad_weight"):
-        grad_weight = scatter_sum(weight_rows, "wa", 0)
+        grad_weight = weight_summed.astype(jnp.float32)
 
     with jax.named_scope("halo_reduction"):
         middle = (

time: 184 us -> 189 us (1.027)
  waiting for transfers between devices: 62.8 us -> 77.5 us
  other arithmetic: 16.4 us -> 9.55 us
  starting transfers between devices: 28.4 us -> 25 us
    ppermute x4 -> x3, waiting for transfers between devices: 11.8 us -> 25.7 us  [cyclic(): lax.ppermute(value, axis, [(i, (i + steps) % count) for i in range(count)])]
    add x2 -> x0, other arithmetic: 3.9 us -> none  [the longest x1 2.45 us: scatter_finish(): total = total + cyclic(piece, axis, steps).astype(jnp.float32)]
    all_gather x1, waiting for transfers between devices: 0.02 us -> 3.15 us  [body(): cot_all = lax.all_gather(out_cotangent[0, 0], 'ha', axis=0, tiled=True)]
    ppermute x8, waiting for transfers between devices: 50.9 us -> 48.6 us  [shifted(): return lax.ppermute(value, axis, shift_pairs(lax.axis_size(axis), steps))]
    ppermute x8, starting transfers between devices: 24.8 us -> 22.6 us  [shifted(): return lax.ppermute(value, axis, shift_pairs(lax.axis_size(axis), steps))]
    another operation x2, other arithmetic: 4.75 us -> 2.65 us  [body(): jnp.stack([shifted(packed, 'fh', 1), packed, shifted(packed, 'fh', -1)])]
    unnamed x24 -> x26, local copies, waits for them, and re-layouts: 9.87 us -> 10.9 us
  transfers between devices with their start and end apart: 14 -> 13, of which waited for: 8 -> 8; matrix products, arithmetic and copies ran while one was open for 19% -> 11% of each run, Pallas kernels for 20% -> 7%
where the time goes in v6:
time: 189 us; the launch traced here: 188 us
  waiting for transfers between devices  77.5 us (41%)
  Pallas kernels  36.2 us (19%)
  starting transfers between devices  25 us (13%)
  local copies, waits for them, and re-layouts  16.1 us (9%)
  between operations  14.3 us (8%)
  other arithmetic  9.55 us (5%)
  matrix products  9.17 us (5%)
    ppermute x8, waiting for transfers between devices, shifted(): return lax.ppermute(value, axis, shift_pairs(lax.axis_size(axis), steps))  48.6 us
    ppermute x3, waiting for transfers between devices, cyclic(): lax.ppermute(value, axis, [(i, (i + steps) % count) for i in range(count)])  25.7 us
    ppermute x8, starting transfers between devices, shifted(): return lax.ppermute(value, axis, shift_pairs(lax.axis_size(axis), steps))  22.6 us
    pallas_call x1, Pallas kernels, attention_backward(): pl.pallas_call(functools.partial(backward_kernel, scale), grid=(heads, ch...  22.3 us
    pallas_call x1, Pallas kernels, attention_forward(): pl.pallas_call(functools.partial(forward_kernel, scale), grid=(heads, chu...  13.9 us
    unnamed x26, local copies, waits for them, and re-layouts  10.9 us
    dot_general x1, matrix products, body(): lax.dot_general(cot_all, attended, (((0,), (0,)), ((), ())), preferred_el...  4.69 us
    convert_element_type x1, other arithmetic, body(): middle_sides = middle.astype(jnp.bfloat16)  4 us
  transfers between devices with their start and end apart: 13, of which 8 were waited for; matrix products, arithmetic and copies ran while one was open for 11% of the time, Pallas kernels for 7%

profile of v6, /device:TPU:1, one launch (start us, length us, event | category | flops | bytes accessed | tf_op | source)
XLA Modules:
  0.0 187.7 jit_solution(7741495237597329273)
XLA Ops:
  7.2 0.0 copy-start
  7.2 0.0 all-gather.3.cloned.1.call-start
  7.2 0.8 convert_bitcast_fusion
  8.1 1.2 fusion.13
  9.2 1.3 collective-permute-start.1
  10.5 4.1 %collective-permute-start = (bf16[784,384]{1,0:T(8,128)(2,1)S(1)}, bf16[784,384]{1,0:T(8,128)(2,1)S(1)}, u32[]{:S(2)}, u32[]{:S(2)}) collective-permute-start(bf16[784,384]{1,0:T(8,128)(2,1)S(1)} %get-tuple-element.55), channel_id=1, source_target_pairs={{0,16},{1,17},{2,18},{3,19},{4,20},{5,21},{6,22},{7,23},{8,24},{9,... | collective-permute-start | bytes 1806344 | tf_op jit(solution)/shard_map/halo_exchange/ppermute | solution.py:22
  14.6 11.3 %collective-permute-done.1 = bf16[784,384]{1,0:T(8,128)(2,1)S(1)} collective-permute-done((bf16[784,384]{1,0:T(8,128)(2,1)S(1)}, bf16[784,384]{1,0:T(8,128)(2,1)S(1)}, u32[]{:S(2)}, u32[]{:S(2)}) %collective-permute-start.1) | collective-permute-done | bytes 602144 | tf_op jit(solution)/shard_map/halo_exchange/ppermute | solution.py:22
  25.9 0.9 collective-permute-done
  26.8 1.5 pad_maximum_fusion
  28.3 0.0 copy-done.4
  28.3 5.4 %collective-permute-start.2 = (bf16[3,784,384]{2,1,0:T(8,128)(2,1)}, bf16[3,784,384]{2,1,0:T(8,128)(2,1)}, u32[]{:S(2)}, u32[]{:S(2)}) collective-permute-start(bf16[3,784,384]{2,1,0:T(8,128)(2,1)} %pad_maximum_fusion), channel_id=1, source_target_pairs={{0,4},{4,8},{8,12},{1,5},{5,9},{9,13},{2,6},{6,10},{10,14},{3,7},{... | collective-permute-start | bytes 5419016 | tf_op jit(solution)/shard_map/halo_exchange/ppermute | solution.py:22
  33.7 0.0 all-gather.3.cloned.1.call-update
  33.7 0.0 reduce-scatter.4.cloned.1.call-start
  33.7 1.9 %collective-permute-start.3 = (bf16[3,784,384]{2,1,0:T(8,128)(2,1)}, bf16[3,784,384]{2,1,0:T(8,128)(2,1)}, u32[]{:S(2)}, u32[]{:S(2)}) collective-permute-start(bf16[3,784,384]{2,1,0:T(8,128)(2,1)} %pad_maximum_fusion), channel_id=1, source_target_pairs={{4,0},{8,4},{12,8},{5,1},{9,5},{13,9},{6,2},{10,6},{14,10},{7,3},{... | collective-permute-start | bytes 5419016 | tf_op jit(solution)/shard_map/halo_exchange/ppermute | solution.py:22
  35.7 0.0 copy-start.5
  35.7 0.0 copy-start.7
  35.7 0.0 copy-start.8
  35.8 18.1 %collective-permute-done.2 = bf16[3,784,384]{2,1,0:T(8,128)(2,1)} collective-permute-done((bf16[3,784,384]{2,1,0:T(8,128)(2,1)}, bf16[3,784,384]{2,1,0:T(8,128)(2,1)}, u32[]{:S(2)}, u32[]{:S(2)}) %collective-permute-start.2) | collective-permute-done | bytes 1806368 | tf_op jit(solution)/shard_map/halo_exchange/ppermute | solution.py:22
  53.8 1.7 constant_dynamic-update-slice_fusion.4
  55.5 0.0 copy-done.5
  55.5 0.1 constant_dynamic-update-slice_fusion.3
  55.6 0.0 copy-done.7
  55.6 0.0 copy-done.8
  55.6 0.1 constant_dynamic-update-slice_fusion.2
  55.7 0.1 constant_dynamic-update-slice_fusion.1
  55.9 2.7 %collective-permute-done.3 = bf16[3,784,384]{2,1,0:T(8,128)(2,1)} collective-permute-done((bf16[3,784,384]{2,1,0:T(8,128)(2,1)}, bf16[3,784,384]{2,1,0:T(8,128)(2,1)}, u32[]{:S(2)}, u32[]{:S(2)}) %collective-permute-start.3) | collective-permute-done | bytes 1806368 | tf_op jit(solution)/shard_map/halo_exchange/ppermute | solution.py:22
  58.6 1.9 constant_dynamic-update-slice_fusion.k_ref.v_ref
  60.4 0.0 copy-start.1
  60.5 2.3 %copy-done.1 = bf16[9,784,384]{2,1,0:T(8,128)(2,1)} copy-done((bf16[9,784,384]{2,1,0:T(8,128)(2,1)}, bf16[9,784,384]{2,1,0:T(8,128)(2,1)S(1)}, u32[]{:S(2)}) %copy-start.1) | copy-done | bytes 5419032
  62.8 0.6 compare_select_fusion
  63.4 13.9 %tile_attention_forward.1.o_ref = bf16[384,384]{1,0:T(8,128)(2,1)} custom-call(f32[1,3456]{1,0:T(1,128)} %bitcast.54, bf16[384,384]{1,0:T(8,128)(2,1)} %bitcast.48, bf16[9,784,384]{2,1,0:T(8,128)(2,1)} %copy-done.1, bf16[9,784,384]{2,1,0:T(8,128)(2,1)} %copy-done.1), custom_call_target="tpu_custom_call" | custom-call | tf_op jit(solution)/shard_map/attention_forward/tile_attention_forward/pallas_call | solution.py:99
  77.2 0.0 copy-done
  77.2 2.3 %fusion.15 = f32[384,3072]{1,0:T(8,128)S(1)} fusion(bf16[384,384]{1,0:T(8,128)(2,1)} %tile_attention_forward.1.o_ref, bf16[384,3072]{1,0:T(8,128)(2,1)S(1)} %copy-done), kind=kOutput, calls=%fused_computation.34 | convolution fusion | flops 905969664 | bytes 7372800 | tf_op jit(solution)/shard_map/output_projection/dot_general | solution.py:216
  79.6 1.1 constant_dynamic-slice_fusion
  80.7 1.2 dynamic-slice_convert_fusion
  81.9 3.2 %all-gather.3.cloned.1.call-done = bf16[1,1,384,3072]{3,2,1,0:T(8,128)(2,1)} async-done(((bf16[1,1,96,3072]{3,2,1,0:T(8,128)(2,1)}), bf16[1,1,384,3072]{3,2,1,0:T(8,128)(2,1)}) %all-gather.3.cloned.1.call-update) | async-done | bytes 2359312 | tf_op jit(solution)/shard_map/cotangent_gather/all_gather | solution.py:210
  85.1 4.7 %fusion = bf16[3072,384]{0,1:T(8,128)(2,1)} fusion(bf16[384,384]{1,0:T(8,128)(2,1)S(1)} %copy-done.2, bf16[1,1,384,3072]{3,2,1,0:T(8,128)(2,1)} %all-gather.3.cloned.1.call-done), kind=kOutput, calls=%fused_computation.1 | convolution fusion | flops 907149312 | bytes 5013504 | tf_op jit(solution)/shard_map/grad_weight/dot_general | solution.py:225
  89.8 0.0 copy-done.6
  89.8 2.1 %fusion.4.do_ref = bf16[384,384]{1,0:T(8,128)(2,1)} fusion(bf16[384,3072]{1,0:T(8,128)(2,1)S(1)} %copy-done, bf16[1,1,384,3072]{3,2,1,0:T(8,128)(2,1)S(1)} %copy-done.6), kind=kOutput, calls=%fused_computation.7 | convolution fusion | flops 906117120 | bytes 5013504 | tf_op jit(solution)/shard_map/grad_attended/dot_general | solution.py:220
  91.9 22.3 %tile_attention_backward.1 = (bf16[384,384]{1,0:T(8,128)(2,1)}, bf16[3,768,384]{2,1,0:T(8,128)(2,1)}, f32[3,768,384]{2,1,0:T(8,128)}, bf16[3,768,384]{2,1,0:T(8,128)(2,1)}) custom-call(f32[1,3456]{1,0:T(1,128)} %bitcast.55, bf16[384,384]{1,0:T(8,128)(2,1)} %bitcast.49, bf16[9,784,384]{2,1,0:T(8,128)(2,1)} %copy-done.1, bf16[9,784,384]{2,1,0:T(8,128)(2,1)} %copy-done.1, ...), custom_call_target="tpu_custom_call" | custom-call | tf_op jit(solution)/shard_map/attention_backward/tile_attention_backward/pallas_call | solution.py:121
  114.2 3.7 %collective-permute-start.8 = (bf16[3,768,384]{2,1,0:T(8,128)(2,1)}, bf16[3,768,384]{2,1,0:T(8,128)(2,1)}, u32[]{:S(2)}, u32[]{:S(2)}) collective-permute-start(bf16[3,768,384]{2,1,0:T(8,128)(2,1)} %get-tuple-element.35), channel_id=1, source_target_pairs={{0,4},{4,8},{8,12},{1,5},{5,9},{9,13},{2,6},{6,10},{10,14},{3,7},{... | collective-permute-start | bytes 5308424 | tf_op jit(solution)/shard_map/halo_reduction/ppermute | solution.py:22
  117.9 1.9 %collective-permute-start.7 = (bf16[3,768,384]{2,1,0:T(8,128)(2,1)}, bf16[3,768,384]{2,1,0:T(8,128)(2,1)}, u32[]{:S(2)}, u32[]{:S(2)}) collective-permute-start(bf16[3,768,384]{2,1,0:T(8,128)(2,1)} %get-tuple-element.34), channel_id=1, source_target_pairs={{4,0},{8,4},{12,8},{5,1},{9,5},{13,9},{6,2},{10,6},{14,10},{7,3},{... | collective-permute-start | bytes 5308424 | tf_op jit(solution)/shard_map/halo_reduction/ppermute | solution.py:22
  119.9 4.3 %copy.13 = bf16[3072,384]{1,0:T(8,128)(2,1)} copy(bf16[3072,384]{0,1:T(8,128)(2,1)} %fusion) | data formatting | bytes 4718592
  124.2 0.0 reduce-scatter.4.cloned.1.call-update
  124.2 0.9 collective-permute-start.6
  125.1 0.2 copy-done.9
  125.3 0.9 collective-permute-start.5
  126.2 0.5 collective-permute-start.4
  126.7 11.0 %collective-permute-done.8 = bf16[3,768,384]{2,1,0:T(8,128)(2,1)} collective-permute-done((bf16[3,768,384]{2,1,0:T(8,128)(2,1)}, bf16[3,768,384]{2,1,0:T(8,128)(2,1)}, u32[]{:S(2)}, u32[]{:S(2)}) %collective-permute-start.8) | collective-permute-done | bytes 1769504 | tf_op jit(solution)/shard_map/halo_reduction/ppermute | solution.py:22
  137.7 4.6 %collective-permute-done.7 = bf16[3,768,384]{2,1,0:T(8,128)(2,1)} collective-permute-done((bf16[3,768,384]{2,1,0:T(8,128)(2,1)}, bf16[3,768,384]{2,1,0:T(8,128)(2,1)}, u32[]{:S(2)}, u32[]{:S(2)}) %collective-permute-start.7) | collective-permute-done | bytes 1769504 | tf_op jit(solution)/shard_map/halo_reduction/ppermute | solution.py:22
  142.3 4.0 %fusion.14 = (bf16[3,768,384]{2,1,0:T(8,128)(2,1)S(1)}, f32[3,768,384]{2,1,0:T(8,128)S(1)}) fusion(bf16[3,768,384]{2,1,0:T(8,128)(2,1)} %collective-permute-done.8, f32[3,768,384]{2,1,0:T(8,128)} %get-tuple-element.33, bf16[3,768,384]{2,1,0:T(8,128)(2,1)} %collective-permute-done.7), kind=kLoop, calls=%fused_computation.33 | loop fusion | flops 4423680 | bytes 12386304 | tf_op jit(solution)/shard_map/halo_reduction/convert_element_type | solution.py:251
  146.3 0.1 slice_bitcast_fusion.2
  146.4 3.0 %collective-permute-start.10 = (bf16[768,384]{1,0:T(8,128)(2,1)S(1)}, bf16[768,384]{1,0:T(8,128)(2,1)S(1)}, u32[]{:S(2)}, u32[]{:S(2)}) collective-permute-start(bf16[768,384]{1,0:T(8,128)(2,1)S(1)} %get-tuple-element.53), channel_id=1, source_target_pairs={{0,16},{1,17},{2,18},{3,19},{4,20},{5,21},{6,22},{7,23},{8,24},{9,... | collective-permute-start | bytes 1769480 | tf_op jit(solution)/shard_map/halo_reduction/ppermute | solution.py:22
  149.5 1.3 collective-permute-start.9
  150.8 0.0 collective-permute-done.6
  150.8 25.7 %collective-permute-done.5 = bf16[96,3072]{1,0:T(8,128)(2,1)S(1)} collective-permute-done((bf16[96,3072]{1,0:T(8,128)(2,1)S(1)}, bf16[96,3072]{1,0:T(8,128)(2,1)S(1)}, u32[]{:S(2)}, u32[]{:S(2)}) %collective-permute-start.5) | collective-permute-done | bytes 589856 | tf_op jit(solution)/shard_map/grad_weight/ppermute | solution.py:27
  176.5 0.0 collective-permute-done.4
  176.5 1.1 fusion.12
  177.6 0.0 collective-permute-done.10
  177.6 0.0 collective-permute-done.9
  177.6 0.2 fusion.10
  177.8 0.9 slice_bitcast_fusion.3
  178.7 1.2 copy.14
  179.9 1.0 copy.12
  (8 shorter events, 0.0 us)
Async XLA Ops:
  7.2 70.1 %copy-start = (bf16[384,3072]{1,0:T(8,128)(2,1)S(1)}, bf16[384,3072]{1,0:T(8,128)(2,1)}, u32[]{:S(2)}) copy-start(bf16[384,3072]{1,0:T(8,128)(2,1)} %param.12) | copy-start | bytes 7077892
  7.2 77.9 %all-gather.3.cloned.1.call-start = ((), (), s32[]{:S(2)}) async-start(), calls=%async_computation.1 | async-start | bytes 2949120 | tf_op jit(solution)/shard_map/cotangent_gather/all_gather | solution.py:210
  9.2 16.7 %collective-permute-start.1 = (bf16[784,384]{1,0:T(8,128)(2,1)S(1)}, bf16[784,384]{1,0:T(8,128)(2,1)S(1)}, u32[]{:S(2)}, u32[]{:S(2)}) collective-permute-start(bf16[784,384]{1,0:T(8,128)(2,1)S(1)} %get-tuple-element.55), channel_id=1, source_target_pairs={{16,0},{17,1},{18,2},{19,3},{20,4},{21,5},{22,6},{23,7},{24,8},{25... | collective-permute-start | bytes 1806344 | tf_op jit(solution)/shard_map/halo_exchange/ppermute | solution.py:22
  10.5 16.3 %collective-permute-start = (bf16[784,384]{1,0:T(8,128)(2,1)S(1)}, bf16[784,384]{1,0:T(8,128)(2,1)S(1)}, u32[]{:S(2)}, u32[]{:S(2)}) collective-permute-start(bf16[784,384]{1,0:T(8,128)(2,1)S(1)} %get-tuple-element.55), channel_id=1, source_target_pairs={{0,16},{1,17},{2,18},{3,19},{4,20},{5,21},{6,22},{7,23},{8,24},{9,... | collective-permute-start | bytes 1806344 | tf_op jit(solution)/shard_map/halo_exchange/ppermute | solution.py:22
  26.8 1.5 copy-start.4
  28.3 25.5 %collective-permute-start.2 = (bf16[3,784,384]{2,1,0:T(8,128)(2,1)}, bf16[3,784,384]{2,1,0:T(8,128)(2,1)}, u32[]{:S(2)}, u32[]{:S(2)}) collective-permute-start(bf16[3,784,384]{2,1,0:T(8,128)(2,1)} %pad_maximum_fusion), channel_id=1, source_target_pairs={{0,4},{4,8},{8,12},{1,5},{5,9},{9,13},{2,6},{6,10},{10,14},{3,7},{... | collective-permute-start | bytes 5419016 | tf_op jit(solution)/shard_map/halo_exchange/ppermute | solution.py:22
  33.7 145.0 %reduce-scatter.4.cloned.1.call-start = ((), (), s32[]{:S(2)}) async-start(), calls=%async_computation.2 | async-start | bytes 2654208
  33.7 24.8 %collective-permute-start.3 = (bf16[3,784,384]{2,1,0:T(8,128)(2,1)}, bf16[3,784,384]{2,1,0:T(8,128)(2,1)}, u32[]{:S(2)}, u32[]{:S(2)}) collective-permute-start(bf16[3,784,384]{2,1,0:T(8,128)(2,1)} %pad_maximum_fusion), channel_id=1, source_target_pairs={{4,0},{8,4},{12,8},{5,1},{9,5},{13,9},{6,2},{10,6},{14,10},{7,3},{... | collective-permute-start | bytes 5419016 | tf_op jit(solution)/shard_map/halo_exchange/ppermute | solution.py:22
  35.7 19.8 %copy-start.5 = (bf16[784,384]{1,0:T(8,128)(2,1)S(1)}, bf16[784,384]{1,0:T(8,128)(2,1)}, u32[]{:S(2)}) copy-start(bf16[784,384]{1,0:T(8,128)(2,1)} %copy-done.4) | copy-start | bytes 1806340
  35.7 19.9 %copy-start.7 = (bf16[1,1,384,384]{3,2,1,0:T(8,128)(2,1)S(1)}, bf16[1,1,384,384]{3,2,1,0:T(8,128)(2,1)}, u32[]{:S(2)}) copy-start(bf16[1,1,384,384]{3,2,1,0:T(8,128)(2,1)} %param.10) | copy-start | bytes 884740
  35.7 19.9 %copy-start.8 = (bf16[1,1,384,384]{3,2,1,0:T(8,128)(2,1)S(1)}, bf16[1,1,384,384]{3,2,1,0:T(8,128)(2,1)}, u32[]{:S(2)}) copy-start(bf16[1,1,384,384]{3,2,1,0:T(8,128)(2,1)} %param.9) | copy-start | bytes 884740
  60.4 2.3 %copy-start.1 = (bf16[9,784,384]{2,1,0:T(8,128)(2,1)}, bf16[9,784,384]{2,1,0:T(8,128)(2,1)S(1)}, u32[]{:S(2)}) copy-start(bf16[9,784,384]{2,1,0:T(8,128)(2,1)S(1)} %constant_dynamic-update-slice_fusion.k_ref.v_ref) | copy-start | bytes 16257028
  80.7 4.4 %copy-start.2 = (bf16[384,384]{1,0:T(8,128)(2,1)S(1)}, bf16[384,384]{1,0:T(8,128)(2,1)}, u32[]{:S(2)}) copy-start(bf16[384,384]{1,0:T(8,128)(2,1)} %tile_attention_forward.1.o_ref) | copy-start | bytes 884740
  85.1 4.7 %copy-start.6 = (bf16[1,1,384,3072]{3,2,1,0:T(8,128)(2,1)S(1)}, bf16[1,1,384,3072]{3,2,1,0:T(8,128)(2,1)}, u32[]{:S(2)}) copy-start(bf16[1,1,384,3072]{3,2,1,0:T(8,128)(2,1)} %all-gather.3.cloned.1.call-done) | copy-start | bytes 7077892
  114.2 23.5 %collective-permute-start.8 = (bf16[3,768,384]{2,1,0:T(8,128)(2,1)}, bf16[3,768,384]{2,1,0:T(8,128)(2,1)}, u32[]{:S(2)}, u32[]{:S(2)}) collective-permute-start(bf16[3,768,384]{2,1,0:T(8,128)(2,1)} %get-tuple-element.35), channel_id=1, source_target_pairs={{0,4},{4,8},{8,12},{1,5},{5,9},{9,13},{2,6},{6,10},{10,14},{3,7},{... | collective-permute-start | bytes 5308424 | tf_op jit(solution)/shard_map/halo_reduction/ppermute | solution.py:22
  117.9 24.3 %collective-permute-start.7 = (bf16[3,768,384]{2,1,0:T(8,128)(2,1)}, bf16[3,768,384]{2,1,0:T(8,128)(2,1)}, u32[]{:S(2)}, u32[]{:S(2)}) collective-permute-start(bf16[3,768,384]{2,1,0:T(8,128)(2,1)} %get-tuple-element.34), channel_id=1, source_target_pairs={{4,0},{8,4},{12,8},{5,1},{9,5},{13,9},{6,2},{10,6},{14,10},{7,3},{... | collective-permute-start | bytes 5308424 | tf_op jit(solution)/shard_map/halo_reduction/ppermute | solution.py:22
  124.2 1.1 copy-start.9
  124.2 26.5 %collective-permute-start.6 = (bf16[96,3072]{1,0:T(8,128)(2,1)}, bf16[96,3072]{1,0:T(8,128)(2,1)S(1)}, u32[]{:S(2)}, u32[]{:S(2)}) collective-permute-start(bf16[96,3072]{1,0:T(8,128)(2,1)} %get-tuple-element.30), channel_id=1, source_target_pairs={{0,3},{1,0},{2,1},{3,2},{4,7},{5,4},{6,5},{7,6},{8,11},{9,8},{10,9... | collective-permute-start | bytes 1769480 | tf_op jit(solution)/shard_map/grad_weight/ppermute | solution.py:27
  125.3 51.2 %collective-permute-start.5 = (bf16[96,3072]{1,0:T(8,128)(2,1)S(1)}, bf16[96,3072]{1,0:T(8,128)(2,1)S(1)}, u32[]{:S(2)}, u32[]{:S(2)}) collective-permute-start(bf16[96,3072]{1,0:T(8,128)(2,1)S(1)} %copy-done.9), channel_id=1, source_target_pairs={{0,2},{1,3},{2,0},{3,1},{4,6},{5,7},{6,4},{7,5},{8,10},{9,11},{10,... | collective-permute-start | bytes 1769480 | tf_op jit(solution)/shard_map/grad_weight/ppermute | solution.py:27
  126.2 50.2 %collective-permute-start.4 = (bf16[96,3072]{1,0:T(8,128)(2,1)S(1)}, bf16[96,3072]{1,0:T(8,128)(2,1)S(1)}, u32[]{:S(2)}, u32[]{:S(2)}) collective-permute-start(bf16[96,3072]{1,0:T(8,128)(2,1)S(1)} %get-tuple-element.28), channel_id=1, source_target_pairs={{0,1},{1,2},{2,3},{3,0},{4,5},{5,6},{6,7},{7,4},{8,9},{9,10},{10,1... | collective-permute-start | bytes 1769480 | tf_op jit(solution)/shard_map/grad_weight/ppermute | solution.py:27
  146.3 30.2 %copy-start.3 = (f32[96,3072]{1,0:T(8,128)S(1)}, f32[96,3072]{1,0:T(8,128)}, u32[]{:S(2)}) copy-start(f32[96,3072]{1,0:T(8,128)} %constant_dynamic-slice_fusion) | copy-start | bytes 3538948
  146.4 31.2 %collective-permute-start.10 = (bf16[768,384]{1,0:T(8,128)(2,1)S(1)}, bf16[768,384]{1,0:T(8,128)(2,1)S(1)}, u32[]{:S(2)}, u32[]{:S(2)}) collective-permute-start(bf16[768,384]{1,0:T(8,128)(2,1)S(1)} %get-tuple-element.53), channel_id=1, source_target_pairs={{0,16},{1,17},{2,18},{3,19},{4,20},{5,21},{6,22},{7,23},{8,24},{9,... | collective-permute-start | bytes 1769480 | tf_op jit(solution)/shard_map/halo_reduction/ppermute | solution.py:22
  149.5 28.1 %collective-permute-start.9 = (bf16[768,384]{1,0:T(8,128)(2,1)S(1)}, bf16[768,384]{1,0:T(8,128)(2,1)S(1)}, u32[]{:S(2)}, u32[]{:S(2)}) collective-permute-start(bf16[768,384]{1,0:T(8,128)(2,1)S(1)} %get-tuple-element.52), channel_id=1, source_target_pairs={{16,0},{17,1},{18,2},{19,3},{20,4},{21,5},{22,6},{23,7},{24,8},{25... | collective-permute-start | bytes 1769480 | tf_op jit(solution)/shard_map/halo_reduction/ppermute | solution.py:22
Sparse Core Ops, SparseCore 0:
  33.8 51.2 all-gather.2
  124.4 43.6 reduce-scatter.3

commit v7 on v3

--- a/solution.py
+++ b/solution.py
@@ -27,28 +27,34 @@
     return lax.ppermute(value, axis, [(i, (i + steps) % count) for i in range(count)])
 
 
-def scores_of(mask_ref, q_ref, k_ref, scale):
+def joined(refs):
+    return jnp.concatenate([ref[...].reshape(-1, HD) for ref in refs], axis=0)
+
+
+def scores_of(mask_ref, q_ref, k, scale):
     q = q_ref[...]
-    k = k_ref[...].reshape(-1, HD)
     s = lax.dot_general(q, k, (((1,), (1,)), ((), ())), preferred_element_type=jnp.float32)
     return s * scale + mask_ref[...]
 
 
-def forward_kernel(scale, mask_ref, q_ref, k_ref, v_ref, o_ref):
-    s = scores_of(mask_ref, q_ref, k_ref, scale)
+def forward_kernel(scale, mask_ref, q_ref, kl, km, kr, vl, vm, vr, o_ref):
+    s = scores_of(mask_ref, q_ref, joined((kl, km, kr)), scale)
     m = jnp.max(s, axis=1, keepdims=True)
     e = jnp.exp(s - m)
     total = jnp.sum(e, axis=1, keepdims=True)
     p = (e * (1.0 / total)).astype(jnp.bfloat16)
-    v = v_ref[...].reshape(-1, HD)
+    v = joined((vl, vm, vr))
     o_ref[...] = jnp.dot(p, v, preferred_element_type=jnp.float32).astype(o_ref.dtype)
 
 
 def backward_kernel(
-    scale, mask_ref, q_ref, k_ref, v_ref, o_ref, do_ref, dq_ref, left_ref, mid_ref, right_ref, acc_ref
+    scale, mask_ref, q_ref, kl, km, kr, vl, vm, vr, o_ref, do_ref, dq_ref, left_ref, mid_ref,
+    right_ref, acc_ref
 ):
     chunk = pl.program_id(1)
-    s = scores_of(mask_ref, q_ref, k_ref, scale)
+    k = joined((kl, km, kr))
+    v = joined((vl, vm, vr))
+    s = scores_of(mask_ref, q_ref, k, scale)
     m = jnp.max(s, axis=1, keepdims=True)
     e = jnp.exp(s - m)
     total = jnp.sum(e, axis=1, keepdims=True)
@@ -58,8 +64,6 @@
     row_dot = jnp.sum(
         do.astype(jnp.float32) * o_ref[...].astype(jnp.float32), axis=1, keepdims=True
     )
-    k = k_ref[...].reshape(-1, HD)
-    v = v_ref[...].reshape(-1, HD)
     dp = lax.dot_general(do, v, (((1,), (1,)), ((), ())), preferred_element_type=jnp.float32)
     ds = (w * (dp - row_dot)).astype(jnp.bfloat16)
     dq = jnp.dot(ds, k, preferred_element_type=jnp.float32) * scale
@@ -67,7 +71,7 @@
     contract0 = (((0,), (0,)), ((), ()))
     dk = lax.dot_general(ds, q_ref[...], contract0, preferred_element_type=jnp.float32) * scale
     dv = lax.dot_general(p, do, contract0, preferred_element_type=jnp.float32)
-    tiles, tokens = k_ref.shape[0], k_ref.shape[1]
+    tiles, tokens = 3 * kl.shape[0], kl.shape[1]
     dk = dk.reshape(tiles, tokens, HD)
     dv = dv.reshape(tiles, tokens, HD)
 
@@ -89,9 +93,9 @@
         right_ref[...] = acc_ref[2 * third :].astype(right_ref.dtype)
 
 
-def attention_forward(mask, queries, window):
+def attention_forward(mask, queries, columns):
     tokens, features = queries.shape
-    tiles = window.shape[0]
+    tiles = 3 * columns[0].shape[0]
     heads = features // HD
     chunk = FORWARD_CHUNK
     chunks = tokens // chunk
@@ -102,18 +106,18 @@
         in_specs=[
             pl.BlockSpec((1, tiles * tokens), lambda h, c: (0, 0)),
             pl.BlockSpec((chunk, HD), lambda h, c: (c, h)),
-            pl.BlockSpec((tiles, tokens, HD), lambda h, c: (0, 0, h)),
-            pl.BlockSpec((tiles, tokens, HD), lambda h, c: (0, 1, h)),
+            *[pl.BlockSpec((tiles // 3, tokens, HD), lambda h, c: (0, 0, h))] * 3,
+            *[pl.BlockSpec((tiles // 3, tokens, HD), lambda h, c: (0, 1, h))] * 3,
         ],
         out_specs=pl.BlockSpec((chunk, HD), lambda h, c: (c, h)),
         out_shape=jax.ShapeDtypeStruct((tokens, features), jnp.bfloat16),
         name="tile_attention_forward",
-    )(mask, queries, window, window)
-
-
-def attention_backward(mask, queries, window, attended, grad_attended):
+    )(mask, queries, *columns, *columns)
+
+
+def attention_backward(mask, queries, columns, attended, grad_attended):
     tokens, features = queries.shape
-    tiles = window.shape[0]
+    tiles = 3 * columns[0].shape[0]
     heads = features // HD
     chunk = BACKWARD_CHUNK
     chunks = tokens // chunk
@@ -124,8 +128,8 @@
         in_specs=[
             pl.BlockSpec((1, tiles * tokens), lambda h, c: (0, 0)),
             pl.BlockSpec((chunk, HD), lambda h, c: (c, h)),
-            pl.BlockSpec((tiles, tokens, HD), lambda h, c: (0, 0, h)),
-            pl.BlockSpec((tiles, tokens, HD), lambda h, c: (0, 1, h)),
+            *[pl.BlockSpec((tiles // 3, tokens, HD), lambda h, c: (0, 0, h))] * 3,
+            *[pl.BlockSpec((tiles // 3, tokens, HD), lambda h, c: (0, 1, h))] * 3,
             pl.BlockSpec((chunk, HD), lambda h, c: (c, h)),
             pl.BlockSpec((chunk, HD), lambda h, c: (c, h)),
         ],
@@ -143,7 +147,7 @@
         ],
         scratch_shapes=[pltpu.VMEM((tiles, 2 * tokens, HD), jnp.float32)],
         name="tile_attention_backward",
-    )(mask, queries, window, window, attended, grad_attended)
+    )(mask, queries, *columns, *columns, attended, grad_attended)
 
 
 def gather_over(piece, axis):
@@ -199,18 +203,16 @@
 
     with jax.named_scope("halo_exchange"):
         column = jnp.stack([shifted(packed, "fh", 1), packed, shifted(packed, "fh", -1)])
-        window = jnp.concatenate(
-            [shifted(column, "wa", 1), column, shifted(column, "wa", -1)], axis=0
-        )
-    tiles = window.shape[0]
-    flags = window[:, 2 * tokens, :tokens].reshape(1, tiles * tokens)
+        columns = (shifted(column, "wa", 1), column, shifted(column, "wa", -1))
+    flags = jnp.concatenate([side[:, 2 * tokens, :tokens] for side in columns], axis=0)
+    flags = flags.reshape(1, -1)
     mask = jnp.where(flags > 0, 0.0, MASKED).astype(jnp.float32)
 
     with jax.named_scope("cotangent_gather"):
         cot_all = lax.all_gather(out_cotangent[0, 0], "ha", axis=0, tiled=True)
 
     with jax.named_scope("attention_forward"):
-        attended = attention_forward(mask, q, window)
+        attended = attention_forward(mask, q, columns)
 
     with jax.named_scope("output_projection"):
         projected = jnp.dot(attended, out_weight, preferred_element_type=jnp.float32)
@@ -235,7 +237,7 @@
 
     with jax.named_scope("attention_backward"):
         grad_q, left, partials, right = attention_backward(
-            mask, q, window, attended, grad_attended
+            mask, q, columns, attended, grad_attended
         )
 
     with jax.named_scope("grad_weight"):

time: 184 us -> 176 us (0.957)
  local copies, waits for them, and re-layouts: 16.5 us -> 11.2 us
  waiting for transfers between devices: 62.8 us -> 59 us
  other arithmetic: 16.4 us -> 13.4 us
  starting transfers between devices: 28.4 us -> 30.9 us
    unnamed x24 -> x19, local copies, waits for them, and re-layouts: 9.87 us -> 4.18 us
    ppermute x8, waiting for transfers between devices: 50.9 us -> 48 us  [shifted(): return lax.ppermute(value, axis, shift_pairs(lax.axis_size(axis), steps))]
    slice x0 -> x3, local copies, waits for them, and re-layouts: none -> 2.21 us  [body(): side[:, 2 * tokens, :tokens]]
    another operation x2, other arithmetic: 4.75 us -> 2.67 us  [body(): jnp.stack([shifted(packed, 'fh', 1), packed, shifted(packed, 'fh', -1)])]
    ppermute x4, starting transfers between devices: 3.44 us -> 5.36 us  [cyclic(): lax.ppermute(value, axis, [(i, (i + steps) % count) for i in range(count)])]
    concatenate x1 -> x0, local copies, waits for them, and re-layouts: 1.85 us -> none  [body(): jnp.concatenate([shifted(column, 'wa', 1), column, shifted(column, 'wa',...]
  transfers between devices with their start and end apart: 14 -> 14, of which waited for: 8 -> 9; matrix products, arithmetic and copies ran while one was open for 19% -> 18% of each run, Pallas kernels for 20% -> 21%
where the time goes in v7:
time: 176 us; the launch traced here: 174 us
  waiting for transfers between devices  59 us (34%)
  Pallas kernels  36.3 us (21%)
  starting transfers between devices  30.9 us (18%)
  between operations  14.3 us (8%)
  other arithmetic  13.4 us (8%)
  local copies, waits for them, and re-layouts  11.2 us (6%)
  matrix products  8.95 us (5%)
    ppermute x8, waiting for transfers between devices, shifted(): return lax.ppermute(value, axis, shift_pairs(lax.axis_size(axis), steps))  48 us
    ppermute x8, starting transfers between devices, shifted(): return lax.ppermute(value, axis, shift_pairs(lax.axis_size(axis), steps))  25.4 us
    pallas_call x1, Pallas kernels, attention_backward(): pl.pallas_call(functools.partial(backward_kernel, scale), grid=(heads, ch...  22.5 us
    pallas_call x1, Pallas kernels, attention_forward(): pl.pallas_call(functools.partial(forward_kernel, scale), grid=(heads, chu...  13.8 us
    ppermute x4, waiting for transfers between devices, cyclic(): lax.ppermute(value, axis, [(i, (i + steps) % count) for i in range(count)])  10.3 us
    ppermute x4, starting transfers between devices, cyclic(): lax.ppermute(value, axis, [(i, (i + steps) % count) for i in range(count)])  5.36 us
    convert_element_type x1, other arithmetic, body(): middle_sides = middle.astype(jnp.bfloat16)  4.46 us
    unnamed x19, local copies, waits for them, and re-layouts  4.18 us
  transfers between devices with their start and end apart: 14, of which 9 were waited for; matrix products, arithmetic and copies ran while one was open for 18% of the time, Pallas kernels for 21%

profile of v7, /device:TPU:1, one launch (start us, length us, event | category | flops | bytes accessed | tf_op | source)
XLA Modules:
  0.0 174.0 jit_solution(2030247196606057909)
XLA Ops:
  7.2 0.0 copy-start
  7.2 0.0 all-gather.3.cloned.1.call-start
  7.2 0.7 all-gather.3.cloned.1.call-update
  7.9 0.0 reduce-scatter.2.cloned.1.call-start
  8.0 0.7 convert_bitcast_fusion
  8.6 1.2 fusion.13
  9.8 1.3 collective-permute-start.1
  11.1 4.1 %collective-permute-start = (bf16[784,384]{1,0:T(8,128)(2,1)S(1)}, bf16[784,384]{1,0:T(8,128)(2,1)S(1)}, u32[]{:S(2)}, u32[]{:S(2)}) collective-permute-start(bf16[784,384]{1,0:T(8,128)(2,1)S(1)} %get-tuple-element.59), channel_id=1, source_target_pairs={{0,16},{1,17},{2,18},{3,19},{4,20},{5,21},{6,22},{7,23},{8,24},{9,... | collective-permute-start | bytes 1806344 | tf_op jit(solution)/shard_map/halo_exchange/ppermute | solution.py:22
  15.2 11.4 %collective-permute-done.1 = bf16[784,384]{1,0:T(8,128)(2,1)S(1)} collective-permute-done((bf16[784,384]{1,0:T(8,128)(2,1)S(1)}, bf16[784,384]{1,0:T(8,128)(2,1)S(1)}, u32[]{:S(2)}, u32[]{:S(2)}) %collective-permute-start.1) | collective-permute-done | bytes 602144 | tf_op jit(solution)/shard_map/halo_exchange/ppermute | solution.py:22
  26.6 0.8 collective-permute-done
  27.4 1.5 pad_maximum_fusion.km.vm
  28.9 3.4 %collective-permute-start.3 = (bf16[3,784,384]{2,1,0:T(8,128)(2,1)}, bf16[3,784,384]{2,1,0:T(8,128)(2,1)}, u32[]{:S(2)}, u32[]{:S(2)}) collective-permute-start(bf16[3,784,384]{2,1,0:T(8,128)(2,1)} %pad_maximum_fusion.km.vm), channel_id=1, source_target_pairs={{4,0},{8,4},{12,8},{5,1},{9,5},{13,9},{6,2},{10,6},{14,10},{7,3},{... | collective-permute-start | bytes 5419016 | tf_op jit(solution)/shard_map/halo_exchange/ppermute | solution.py:22
  32.3 3.8 %collective-permute-start.2 = (bf16[3,784,384]{2,1,0:T(8,128)(2,1)}, bf16[3,784,384]{2,1,0:T(8,128)(2,1)}, u32[]{:S(2)}, u32[]{:S(2)}) collective-permute-start(bf16[3,784,384]{2,1,0:T(8,128)(2,1)} %pad_maximum_fusion.km.vm), channel_id=1, source_target_pairs={{0,4},{4,8},{8,12},{1,5},{5,9},{9,13},{2,6},{6,10},{10,14},{3,7},{... | collective-permute-start | bytes 5419016 | tf_op jit(solution)/shard_map/halo_exchange/ppermute | solution.py:22
  36.2 0.8 slice.49
  37.0 18.5 %collective-permute-done.3.kr.vr = bf16[3,784,384]{2,1,0:T(8,128)(2,1)} collective-permute-done((bf16[3,784,384]{2,1,0:T(8,128)(2,1)}, bf16[3,784,384]{2,1,0:T(8,128)(2,1)}, u32[]{:S(2)}, u32[]{:S(2)}) %collective-permute-start.3) | collective-permute-done | bytes 1806368 | tf_op jit(solution)/shard_map/halo_exchange/ppermute | solution.py:22
  55.5 0.7 slice.50
  56.2 0.2 collective-permute-done.2.kl.vl
  56.4 0.7 slice.48
  57.1 0.6 copy.34
  57.7 13.8 %tile_attention_forward.1.o_ref = bf16[384,384]{1,0:T(8,128)(2,1)} custom-call(f32[1,3456]{1,0:T(1,128)} %bitcast.61, bf16[384,384]{1,0:T(8,128)(2,1)} %bitcast.55, bf16[3,784,384]{2,1,0:T(8,128)(2,1)} %collective-permute-done.2.kl.vl, bf16[3,784,384]{2,1,0:T(8,128)(2,1)} %pad_maximum_fusion.km.vm, bf16[3,784,384]{2,1,0:T(8,128)(2,1)} %collective-permute-done.3.kr.vr, ...), custom_call_target="tpu_custom_call" | custom-call | tf_op jit(solution)/shard_map/attention_forward/tile_attention_forward/pallas_call | solution.py:103
  71.5 0.0 copy-done
  71.5 3.8 %convolution_convert_fusion = bf16[384,3072]{1,0:T(8,128)(2,1)} fusion(bf16[384,384]{1,0:T(8,128)(2,1)} %tile_attention_forward.1.o_ref, bf16[384,3072]{1,0:T(8,128)(2,1)S(1)} %copy-done), kind=kOutput, calls=%fused_computation | convolution fusion | flops 907149312 | bytes 5013504 | tf_op jit(solution)/shard_map/output_projection/dot_general | solution.py:218
  75.3 0.0 copy-start.2
  75.3 0.0 reduce-scatter.2.cloned.1.call-update
  75.3 0.0 all-gather.3.cloned.1.call-done
  75.3 0.9 copy-done.2
  76.2 3.1 %fusion.2 = f32[384,3072]{1,0:T(8,128)S(1)} fusion(bf16[384,384]{1,0:T(8,128)(2,1)S(1)} %copy-done.2, bf16[1,1,384,3072]{3,2,1,0:T(8,128)(2,1)} %all-gather.3.cloned.1.call-done), kind=kOutput, calls=%fused_computation.4 | convolution fusion | flops 905969664 | bytes 7372800 | tf_op jit(solution)/shard_map/grad_weight/dot_general | solution.py:229
  79.3 0.1 fusion.8
  79.5 0.0 copy-start.4
  79.5 1.7 dynamic-slice_bitcast_fusion
  81.1 0.9 copy-done.4
  82.0 2.1 %fusion.4.do_ref = bf16[384,384]{1,0:T(8,128)(2,1)} fusion(bf16[384,3072]{1,0:T(8,128)(2,1)S(1)} %copy-done, bf16[1,1,384,3072]{3,2,1,0:T(8,128)(2,1)S(1)} %copy-done.4), kind=kOutput, calls=%fused_computation.10 | convolution fusion | flops 906117120 | bytes 5013504 | tf_op jit(solution)/shard_map/grad_attended/dot_general | solution.py:224
  84.1 2.2 %collective-permute-start.8 = (bf16[1536,384]{0,1:T(8,128)(2,1)S(1)}, bf16[1536,384]{0,1:T(8,128)(2,1)}, u32[]{:S(2)}, u32[]{:S(2)}) collective-permute-start(bf16[1536,384]{0,1:T(8,128)(2,1)S(1)} %fusion.8), channel_id=1, source_target_pairs={{0,16},{16,0},{1,17},{17,1},{2,18},{18,2},{3,19},{19,3},{4,20},{20... | collective-permute-start | bytes 3538952 | tf_op jit(solution)/shard_map/grad_weight/ppermute | solution.py:27
  86.3 22.5 %tile_attention_backward.1 = (bf16[384,384]{1,0:T(8,128)(2,1)}, bf16[3,768,384]{2,1,0:T(8,128)(2,1)}, f32[3,768,384]{2,1,0:T(8,128)}, bf16[3,768,384]{2,1,0:T(8,128)(2,1)}) custom-call(f32[1,3456]{1,0:T(1,128)} %bitcast.62, bf16[384,384]{1,0:T(8,128)(2,1)} %bitcast.56, bf16[3,784,384]{2,1,0:T(8,128)(2,1)} %collective-permute-done.2.kl.vl, ...), custom_call_target="tpu_custom_call" | custom-call | tf_op jit(solution)/shard_map/attention_backward/tile_attention_backward/pallas_call | solution.py:125
  108.8 1.9 %collective-permute-start.4 = (bf16[3,768,384]{2,1,0:T(8,128)(2,1)}, bf16[3,768,384]{2,1,0:T(8,128)(2,1)}, u32[]{:S(2)}, u32[]{:S(2)}) collective-permute-start(bf16[3,768,384]{2,1,0:T(8,128)(2,1)} %get-tuple-element.27), channel_id=1, source_target_pairs={{4,0},{8,4},{12,8},{5,1},{9,5},{13,9},{6,2},{10,6},{14,10},{7,3},{... | collective-permute-start | bytes 5308424 | tf_op jit(solution)/shard_map/halo_reduction/ppermute | solution.py:22
  110.7 4.7 %collective-permute-start.5 = (bf16[3,768,384]{2,1,0:T(8,128)(2,1)}, bf16[3,768,384]{2,1,0:T(8,128)(2,1)}, u32[]{:S(2)}, u32[]{:S(2)}) collective-permute-start(bf16[3,768,384]{2,1,0:T(8,128)(2,1)} %get-tuple-element.28), channel_id=1, source_target_pairs={{0,4},{4,8},{8,12},{1,5},{5,9},{9,13},{2,6},{6,10},{10,14},{3,7},{... | collective-permute-start | bytes 5308424 | tf_op jit(solution)/shard_map/halo_reduction/ppermute | solution.py:22
  115.5 0.0 copy-start.3
  115.5 0.0 collective-permute-done.8
  115.5 2.5 %convert_add_fusion.1 = f32[1536,384]{0,1:T(8,128)S(1)} fusion(f32[1536,384]{0,1:T(8,128)} %dynamic-slice_bitcast_fusion, bf16[1536,384]{0,1:T(8,128)(2,1)} %collective-permute-done.8), kind=kLoop, calls=%fused_computation.6 | loop fusion | flops 1179648 | bytes 5898240 | tf_op jit(solution)/shard_map/grad_weight/add | solution.py:176
  118.0 0.0 copy-start.1
  118.0 16.2 %collective-permute-done.4 = bf16[3,768,384]{2,1,0:T(8,128)(2,1)} collective-permute-done((bf16[3,768,384]{2,1,0:T(8,128)(2,1)}, bf16[3,768,384]{2,1,0:T(8,128)(2,1)}, u32[]{:S(2)}, u32[]{:S(2)}) %collective-permute-start.4) | collective-permute-done | bytes 1769504 | tf_op jit(solution)/shard_map/halo_reduction/ppermute | solution.py:22
  134.2 1.0 collective-permute-done.5
  135.2 0.0 copy-done.3
  135.2 4.5 %fusion.14 = (bf16[3,768,384]{2,1,0:T(8,128)(2,1)S(1)}, f32[3,768,384]{2,1,0:T(8,128)}) fusion(bf16[3,768,384]{2,1,0:T(8,128)(2,1)} %collective-permute-done.5, f32[3,768,384]{2,1,0:T(8,128)S(1)} %copy-done.3, bf16[3,768,384]{2,1,0:T(8,128)(2,1)} %collective-permute-done.4), kind=kLoop, calls=%fused_computation.33 | loop fusion | flops 4423680 | bytes 12386304 | tf_op jit(solution)/shard_map/halo_reduction/convert_element_type | solution.py:252
  139.6 1.1 slice_bitcast_fusion.2
  140.8 1.3 collective-permute-start.6
  142.1 4.9 %collective-permute-start.7 = (bf16[768,384]{1,0:T(8,128)(2,1)}, bf16[768,384]{1,0:T(8,128)(2,1)}, u32[]{:S(2)}, u32[]{:S(2)}) collective-permute-start(bf16[768,384]{1,0:T(8,128)(2,1)} %get-tuple-element.57), channel_id=1, source_target_pairs={{0,16},{1,17},{2,18},{3,19},{4,20},{5,21},{6,22},{7,23},{8,24},{9,... | collective-permute-start | bytes 1769480 | tf_op jit(solution)/shard_map/halo_reduction/ppermute | solution.py:22
  147.0 0.0 copy-done.1
  147.0 1.0 dynamic-slice_convert_fusion.3
  148.0 3.0 %collective-permute-start.9 = (bf16[384,384]{0,1:T(8,128)(2,1)}, bf16[384,384]{0,1:T(8,128)(2,1)S(1)}, u32[]{:S(2)}, u32[]{:S(2)}) collective-permute-start(bf16[384,384]{0,1:T(8,128)(2,1)} %get-tuple-element.53), channel_id=1, source_target_pairs={{0,4},{4,8},{8,12},{12,0},{1,5},{5,9},{9,13},{13,1},{2,6},{6,10},{... | collective-permute-start | bytes 884744 | tf_op jit(solution)/shard_map/grad_weight/ppermute | solution.py:27
  151.0 0.0 collective-permute-start.11
  151.0 0.1 collective-permute-start.10
  151.1 6.3 %collective-permute-done.9 = bf16[384,384]{0,1:T(8,128)(2,1)S(1)} collective-permute-done((bf16[384,384]{0,1:T(8,128)(2,1)}, bf16[384,384]{0,1:T(8,128)(2,1)S(1)}, u32[]{:S(2)}, u32[]{:S(2)}) %collective-permute-start.9) | collective-permute-done | bytes 294944 | tf_op jit(solution)/shard_map/grad_weight/ppermute | solution.py:27
  157.4 0.0 copy-start.5
  157.4 2.6 %collective-permute-done.11 = bf16[384,384]{0,1:T(8,128)(2,1)S(1)} collective-permute-done((bf16[384,384]{0,1:T(8,128)(2,1)}, bf16[384,384]{0,1:T(8,128)(2,1)S(1)}, u32[]{:S(2)}, u32[]{:S(2)}) %collective-permute-start.11) | collective-permute-done | bytes 294944 | tf_op jit(solution)/shard_map/grad_weight/ppermute | solution.py:27
  160.0 0.0 copy-done.5
  160.0 0.7 copy-done.6
  160.7 1.4 collective-permute-done.10
  162.1 1.5 convert_add_fusion.2
  163.6 1.1 copy.30
  164.7 0.0 collective-permute-done.6
  164.7 0.0 collective-permute-done.7
  164.7 1.6 fusion.11
  166.3 0.9 slice_bitcast_fusion.3
  (6 shorter events, 0.0 us)
Async XLA Ops:
  7.2 64.3 %copy-start = (bf16[384,3072]{1,0:T(8,128)(2,1)S(1)}, bf16[384,3072]{1,0:T(8,128)(2,1)}, u32[]{:S(2)}) copy-start(bf16[384,3072]{1,0:T(8,128)(2,1)} %param.12) | copy-start | bytes 7077892
  7.2 68.1 %all-gather.3.cloned.1.call-start = ((), (), s32[]{:S(2)}) async-start(), calls=%async_computation.2 | async-start | bytes 2949120 | tf_op jit(solution)/shard_map/cotangent_gather/all_gather | solution.py:212
  7.9 159.2 %reduce-scatter.2.cloned.1.call-start = ((), (), s32[]{:S(2)}) async-start(), calls=%async_computation.1 | async-start | bytes 2949120 | tf_op jit(solution)/shard_map/output_projection/reduce_scatter | solution.py:219
  9.8 16.8 %collective-permute-start.1 = (bf16[784,384]{1,0:T(8,128)(2,1)S(1)}, bf16[784,384]{1,0:T(8,128)(2,1)S(1)}, u32[]{:S(2)}, u32[]{:S(2)}) collective-permute-start(bf16[784,384]{1,0:T(8,128)(2,1)S(1)} %get-tuple-element.59), channel_id=1, source_target_pairs={{16,0},{17,1},{18,2},{19,3},{20,4},{21,5},{22,6},{23,7},{24,8},{25... | collective-permute-start | bytes 1806344 | tf_op jit(solution)/shard_map/halo_exchange/ppermute | solution.py:22
  11.1 16.3 %collective-permute-start = (bf16[784,384]{1,0:T(8,128)(2,1)S(1)}, bf16[784,384]{1,0:T(8,128)(2,1)S(1)}, u32[]{:S(2)}, u32[]{:S(2)}) collective-permute-start(bf16[784,384]{1,0:T(8,128)(2,1)S(1)} %get-tuple-element.59), channel_id=1, source_target_pairs={{0,16},{1,17},{2,18},{3,19},{4,20},{5,21},{6,22},{7,23},{8,24},{9,... | collective-permute-start | bytes 1806344 | tf_op jit(solution)/shard_map/halo_exchange/ppermute | solution.py:22
  28.9 26.6 %collective-permute-start.3 = (bf16[3,784,384]{2,1,0:T(8,128)(2,1)}, bf16[3,784,384]{2,1,0:T(8,128)(2,1)}, u32[]{:S(2)}, u32[]{:S(2)}) collective-permute-start(bf16[3,784,384]{2,1,0:T(8,128)(2,1)} %pad_maximum_fusion.km.vm), channel_id=1, source_target_pairs={{4,0},{8,4},{12,8},{5,1},{9,5},{13,9},{6,2},{10,6},{14,10},{7,3},{... | collective-permute-start | bytes 5419016 | tf_op jit(solution)/shard_map/halo_exchange/ppermute | solution.py:22
  32.3 24.0 %collective-permute-start.2 = (bf16[3,784,384]{2,1,0:T(8,128)(2,1)}, bf16[3,784,384]{2,1,0:T(8,128)(2,1)}, u32[]{:S(2)}, u32[]{:S(2)}) collective-permute-start(bf16[3,784,384]{2,1,0:T(8,128)(2,1)} %pad_maximum_fusion.km.vm), channel_id=1, source_target_pairs={{0,4},{4,8},{8,12},{1,5},{5,9},{9,13},{2,6},{6,10},{10,14},{3,7},{... | collective-permute-start | bytes 5419016 | tf_op jit(solution)/shard_map/halo_exchange/ppermute | solution.py:22
  75.3 1.0 copy-start.2
  79.5 2.5 %copy-start.4 = (bf16[1,1,384,3072]{3,2,1,0:T(8,128)(2,1)S(1)}, bf16[1,1,384,3072]{3,2,1,0:T(8,128)(2,1)}, u32[]{:S(2)}) copy-start(bf16[1,1,384,3072]{3,2,1,0:T(8,128)(2,1)} %all-gather.3.cloned.1.call-done) | copy-start | bytes 7077892
  84.1 31.4 %collective-permute-start.8 = (bf16[1536,384]{0,1:T(8,128)(2,1)S(1)}, bf16[1536,384]{0,1:T(8,128)(2,1)}, u32[]{:S(2)}, u32[]{:S(2)}) collective-permute-start(bf16[1536,384]{0,1:T(8,128)(2,1)S(1)} %fusion.8), channel_id=1, source_target_pairs={{0,16},{16,0},{1,17},{17,1},{2,18},{18,2},{3,19},{19,3},{4,20},{20... | collective-permute-start | bytes 3538952 | tf_op jit(solution)/shard_map/grad_weight/ppermute | solution.py:27
  108.8 25.4 %collective-permute-start.4 = (bf16[3,768,384]{2,1,0:T(8,128)(2,1)}, bf16[3,768,384]{2,1,0:T(8,128)(2,1)}, u32[]{:S(2)}, u32[]{:S(2)}) collective-permute-start(bf16[3,768,384]{2,1,0:T(8,128)(2,1)} %get-tuple-element.27), channel_id=1, source_target_pairs={{4,0},{8,4},{12,8},{5,1},{9,5},{13,9},{6,2},{10,6},{14,10},{7,3},{... | collective-permute-start | bytes 5308424 | tf_op jit(solution)/shard_map/halo_reduction/ppermute | solution.py:22
  110.7 24.4 %collective-permute-start.5 = (bf16[3,768,384]{2,1,0:T(8,128)(2,1)}, bf16[3,768,384]{2,1,0:T(8,128)(2,1)}, u32[]{:S(2)}, u32[]{:S(2)}) collective-permute-start(bf16[3,768,384]{2,1,0:T(8,128)(2,1)} %get-tuple-element.28), channel_id=1, source_target_pairs={{0,4},{4,8},{8,12},{1,5},{5,9},{9,13},{2,6},{6,10},{10,14},{3,7},{... | collective-permute-start | bytes 5308424 | tf_op jit(solution)/shard_map/halo_reduction/ppermute | solution.py:22
  115.5 19.7 %copy-start.3 = (f32[3,768,384]{2,1,0:T(8,128)S(1)}, f32[3,768,384]{2,1,0:T(8,128)}, u32[]{:S(2)}) copy-start(f32[3,768,384]{2,1,0:T(8,128)} %get-tuple-element.26) | copy-start | bytes 10616836
  118.0 29.0 %copy-start.1 = (f32[1536,384]{0,1:T(8,128)}, f32[1536,384]{0,1:T(8,128)S(1)}, u32[]{:S(2)}) copy-start(f32[1536,384]{0,1:T(8,128)S(1)} %convert_add_fusion.1) | copy-start | bytes 7077892
  140.8 23.9 %collective-permute-start.6 = (bf16[768,384]{1,0:T(8,128)(2,1)}, bf16[768,384]{1,0:T(8,128)(2,1)S(1)}, u32[]{:S(2)}, u32[]{:S(2)}) collective-permute-start(bf16[768,384]{1,0:T(8,128)(2,1)} %get-tuple-element.56), channel_id=1, source_target_pairs={{16,0},{17,1},{18,2},{19,3},{20,4},{21,5},{22,6},{23,7},{24,8},{25... | collective-permute-start | bytes 1769480 | tf_op jit(solution)/shard_map/halo_reduction/ppermute | solution.py:22
  142.1 22.6 %collective-permute-start.7 = (bf16[768,384]{1,0:T(8,128)(2,1)}, bf16[768,384]{1,0:T(8,128)(2,1)}, u32[]{:S(2)}, u32[]{:S(2)}) collective-permute-start(bf16[768,384]{1,0:T(8,128)(2,1)} %get-tuple-element.57), channel_id=1, source_target_pairs={{0,16},{1,17},{2,18},{3,19},{4,20},{5,21},{6,22},{7,23},{8,24},{9,... | collective-permute-start | bytes 1769480 | tf_op jit(solution)/shard_map/halo_reduction/ppermute | solution.py:22
  148.0 9.4 %collective-permute-start.9 = (bf16[384,384]{0,1:T(8,128)(2,1)}, bf16[384,384]{0,1:T(8,128)(2,1)S(1)}, u32[]{:S(2)}, u32[]{:S(2)}) collective-permute-start(bf16[384,384]{0,1:T(8,128)(2,1)} %get-tuple-element.53), channel_id=1, source_target_pairs={{0,4},{4,8},{8,12},{12,0},{1,5},{5,9},{9,13},{13,1},{2,6},{6,10},{... | collective-permute-start | bytes 884744 | tf_op jit(solution)/shard_map/grad_weight/ppermute | solution.py:27
  151.0 9.0 %collective-permute-start.11 = (bf16[384,384]{0,1:T(8,128)(2,1)}, bf16[384,384]{0,1:T(8,128)(2,1)S(1)}, u32[]{:S(2)}, u32[]{:S(2)}) collective-permute-start(bf16[384,384]{0,1:T(8,128)(2,1)} %get-tuple-element.54), channel_id=1, source_target_pairs={{0,12},{4,0},{8,4},{12,8},{1,13},{5,1},{9,5},{13,9},{2,14},{6,2},{... | collective-permute-start | bytes 884744 | tf_op jit(solution)/shard_map/grad_weight/ppermute | solution.py:27
  151.0 11.1 %collective-permute-start.10 = (bf16[384,384]{0,1:T(8,128)(2,1)}, bf16[384,384]{0,1:T(8,128)(2,1)}, u32[]{:S(2)}, u32[]{:S(2)}) collective-permute-start(bf16[384,384]{0,1:T(8,128)(2,1)} %get-tuple-element.55), channel_id=1, source_target_pairs={{0,8},{4,12},{8,0},{12,4},{1,9},{5,13},{9,1},{13,5},{2,10},{6,14},... | collective-permute-start | bytes 884744 | tf_op jit(solution)/shard_map/grad_weight/ppermute | solution.py:27
  157.4 2.6 %copy-start.5 = (bf16[384,384]{0,1:T(8,128)(2,1)}, bf16[384,384]{0,1:T(8,128)(2,1)S(1)}, u32[]{:S(2)}) copy-start(bf16[384,384]{0,1:T(8,128)(2,1)S(1)} %collective-permute-done.9) | copy-start | bytes 884740
  160.0 0.7 copy-start.6
Sparse Core Ops, SparseCore 0:
  9.6 52.5 all-gather.2
  75.4 50.7 reduce-scatter.1

commit v8 on v7

v8 whole, which is shorter than its diff:
```python
import functools

import jax
import jax.numpy as jnp
from jax import lax
from jax.experimental import pallas as pl
from jax.experimental.pallas import tpu as pltpu
from jax.sharding import PartitionSpec as P

HD = 128
MASKED = -1e30
FORWARD_CHUNK = 384
BACKWARD_CHUNK = 192
FLAG_ROWS = 16


def shift_pairs(count, steps):
    return [(source, source + steps) for source in range(count) if 0 <= source + steps < count]


def shifted(value, axis, steps):
    return lax.ppermute(value, axis, shift_pairs(lax.axis_size(axis), steps))


def cyclic(value, axis, steps):
    count = lax.axis_size(axis)
    return lax.ppermute(value, axis, [(i, (i + steps) % count) for i in range(count)])


def softmax_rows(scale, present_ref, mask_ref, q, k_cols, s_scr, m_scr, l_scr):
    tiles = s_scr.shape[0]
    rows = tiles // len(k_cols)
    m_scr[...] = jnp.full(m_scr.shape, -jnp.inf, jnp.float32)
    l_scr[...] = jnp.zeros(l_scr.shape, jnp.float32)
    for t in range(tiles):

        @pl.when(present_ref[t] > 0)
        def _():
            k = k_cols[t // rows][t % rows]
            s = lax.dot_general(q, k, (((1,), (1,)), ((), ())), preferred_element_type=jnp.float32)
            s = s * scale + mask_ref[t]
            s_scr[t] = s
            m_scr[...] = jnp.maximum(m_scr[...], jnp.max(s, axis=1, keepdims=True))

    for t in range(tiles):

        @pl.when(present_ref[t] > 0)
        def _():
            e = jnp.exp(s_scr[t] - m_scr[...])
            s_scr[t] = e
            l_scr[...] += jnp.sum(e, axis=1, keepdims=True)


def forward_kernel(
    scale, present_ref, mask_ref, q_ref, kl, km, kr, vl, vm, vr, o_ref, s_scr, m_scr, l_scr, acc_scr
):
    q = q_ref[...]
    softmax_rows(scale, present_ref, mask_ref, q, (kl, km, kr), s_scr, m_scr, l_scr)
    inverse = 1.0 / l_scr[...]
    v_cols = (vl, vm, vr)
    tiles = s_scr.shape[0]
    rows = tiles // 3
    acc_scr[...] = jnp.zeros(acc_scr.shape, jnp.float32)
    for t in range(tiles):

        @pl.when(present_ref[t] > 0)
        def _():
            p = (s_scr[t] * inverse).astype(jnp.bfloat16)
            v = v_cols[t // rows][t % rows]
            acc_scr[...] += jnp.dot(p, v, preferred_element_type=jnp.float32)

    o_ref[...] = acc_scr[...].astype(o_ref.dtype)


def backward_kernel(
    scale, present_ref, mask_ref, q_ref, kl, km, kr, vl, vm, vr, o_ref, do_ref,
    dq_ref, left_ref, mid_ref, right_ref, s_scr, m_scr, l_scr, dq_scr, acc_ref
):
    chunk = pl.program_id(1)
    tiles = s_scr.shape[0]
    rows = tiles // 3
    tokens = kl.shape[1]

    @pl.when(chunk == 0)
    def _():
        acc_ref[...] = jnp.zeros(acc_ref.shape, jnp.float32)

    q = q_ref[...]
    k_cols = (kl, km, kr)
    v_cols = (vl, vm, vr)
    softmax_rows(scale, present_ref, mask_ref, q, k_cols, s_scr, m_scr, l_scr)
    inverse = 1.0 / l_scr[...]
    do = do_ref[...]
    row_dot = jnp.sum(
        do.astype(jnp.float32) * o_ref[...].astype(jnp.float32), axis=1, keepdims=True
    )
    dq_scr[...] = jnp.zeros(dq_scr.shape, jnp.float32)
    contract0 = (((0,), (0,)), ((), ()))
    for t in range(tiles):

        @pl.when(present_ref[t] > 0)
        def _():
            k = k_cols[t // rows][t % rows]
            v = v_cols[t // rows][t % rows]
            w = s_scr[t] * inverse
            p = w.astype(jnp.bfloat16)
            dp = lax.dot_general(
                do, v, (((1,), (1,)), ((), ())), preferred_element_type=jnp.float32
            )
            ds = (w * (dp - row_dot)).astype(jnp.bfloat16)
            dq_scr[...] += jnp.dot(ds, k, preferred_element_type=jnp.float32)
            dk = lax.dot_general(ds, q, contract0, preferred_element_type=jnp.float32) * scale
            dv = lax.dot_general(p, do, contract0, preferred_element_type=jnp.float32)
            acc_ref[t, :tokens, :] += dk
            acc_ref[t, tokens:, :] += dv

    dq_ref[...] = (dq_scr[...] * scale).astype(dq_ref.dtype)

    @pl.when(chunk == pl.num_programs(1) - 1)
    def _():
        left_ref[...] = acc_ref[:rows].astype(left_ref.dtype)
        mid_ref[...] = acc_ref[rows : 2 * rows]
        right_ref[...] = acc_ref[2 * rows :].astype(right_ref.dtype)


def attention_forward(present, mask, queries, columns):
    tokens, features = queries.shape
    rows = columns[0].shape[0]
    tiles = 3 * rows
    heads = features // HD
    chunk = FORWARD_CHUNK
    chunks = tokens // chunk
    scale = HD ** (-0.5)
    return pl.pallas_call(
        functools.partial(forward_kernel, scale),
        grid_spec=pltpu.PrefetchScalarGridSpec(
            num_scalar_prefetch=1,
            grid=(heads, chunks),
            in_specs=[
                pl.BlockSpec((tiles, 1, tokens), lambda h, c, flags: (0, 0, 0)),
                pl.BlockSpec((chunk, HD), lambda h, c, flags: (c, h)),
                *[pl.BlockSpec((rows, tokens, HD), lambda h, c, flags: (0, 0, h))] * 3,
                *[pl.BlockSpec((rows, tokens, HD), lambda h, c, flags: (0, 1, h))] * 3,
            ],
            out_specs=pl.BlockSpec((chunk, HD), lambda h, c, flags: (c, h)),
            scratch_shapes=[
                pltpu.VMEM((tiles, chunk, tokens), jnp.float32),
                pltpu.VMEM((chunk, 1), jnp.float32),
                pltpu.VMEM((chunk, 1), jnp.float32),
                pltpu.VMEM((chunk, HD), jnp.float32),
            ],
        ),
        out_shape=jax.ShapeDtypeStruct((tokens, features), jnp.bfloat16),
        name="tile_attention_forward",
    )(present, mask, queries, *columns, *columns)


def attention_backward(present, mask, queries, columns, attended, grad_attended):
    tokens, features = queries.shape
    rows = columns[0].shape[0]
    tiles = 3 * rows
    heads = features // HD
    chunk = BACKWARD_CHUNK
    chunks = tokens // chunk
    scale = HD ** (-0.5)
    return pl.pallas_call(
        functools.partial(backward_kernel, scale),
        grid_spec=pltpu.PrefetchScalarGridSpec(
            num_scalar_prefetch=1,
            grid=(heads, chunks),
            in_specs=[
                pl.BlockSpec((tiles, 1, tokens), lambda h, c, flags: (0, 0, 0)),
                pl.BlockSpec((chunk, HD), lambda h, c, flags: (c, h)),
                *[pl.BlockSpec((rows, tokens, HD), lambda h, c, flags: (0, 0, h))] * 3,
                *[pl.BlockSpec((rows, tokens, HD), lambda h, c, flags: (0, 1, h))] * 3,
                pl.BlockSpec((chunk, HD), lambda h, c, flags: (c, h)),
                pl.BlockSpec((chunk, HD), lambda h, c, flags: (c, h)),
            ],
            out_specs=[
                pl.BlockSpec((chunk, HD), lambda h, c, flags: (c, h)),
                *[pl.BlockSpec((rows, 2 * tokens, HD), lambda h, c, flags: (0, 0, h))] * 3,
            ],
            scratch_shapes=[
                pltpu.VMEM((tiles, chunk, tokens), jnp.float32),
                pltpu.VMEM((chunk, 1), jnp.float32),
                pltpu.VMEM((chunk, 1), jnp.float32),
                pltpu.VMEM((chunk, HD), jnp.float32),
                pltpu.VMEM((tiles, 2 * tokens, HD), jnp.float32),
            ],
        ),
        out_shape=[
            jax.ShapeDtypeStruct((tokens, features), jnp.bfloat16),
            jax.ShapeDtypeStruct((rows, 2 * tokens, features), jnp.bfloat16),
            jax.ShapeDtypeStruct((rows, 2 * tokens, features), jnp.float32),
            jax.ShapeDtypeStruct((rows, 2 * tokens, features), jnp.bfloat16),
        ],
        name="tile_attention_backward",
    )(present, mask, queries, *columns, *columns, attended, grad_attended)


def gather_over(piece, axis):
    count = lax.axis_size(axis)
    me = lax.axis_index(axis)
    received = [piece] + [cyclic(piece, axis, steps) for steps in range(1, count)]
    ordered = jnp.stack([received[(-k) % count] for k in range(count)])
    return jnp.roll(ordered, me, axis=0)


def scatter_parts(full, axis, dim):
    count = lax.axis_size(axis)
    me = lax.axis_index(axis)
    size = full.shape[dim] // count

    def part(index):
        return lax.dynamic_slice_in_dim(full, index * size, size, axis=dim)

    sent = [part((me + steps) % count).astype(jnp.bfloat16) for steps in range(1, count)]
    return part(me).astype(jnp.float32), sent


def scatter_finish(own, sent, axis):
    total = own
    for steps, piece in enumerate(sent, start=1):
        total = total + cyclic(piece, axis, steps).astype(jnp.float32)
    return total


def scatter_sum(full, axis, dim):
    count = lax.axis_size(axis)
    me = lax.axis_index(axis)
    size = full.shape[dim] // count

    def part(index):
        return lax.dynamic_slice_in_dim(full, index * size, size, axis=dim)

    total = part(me).astype(jnp.float32)
    for steps in range(1, count):
        sent = part((me + steps) % count).astype(jnp.bfloat16)
        total = total + cyclic(sent, axis, steps).astype(jnp.float32)
    return total


def body(queries, key_states, value_states, valid_mask, out_weight, out_cotangent):
    tile_rows, tile_columns, tokens, features = queries.shape
    assert tile_rows == 1 and tile_columns == 1
    model_width = out_weight.shape[1]
    q = queries[0, 0]
    flag_rows = jnp.zeros((FLAG_ROWS, features), jnp.bfloat16)
    flag_rows = flag_rows.at[0, :tokens].set(valid_mask[0, 0].astype(jnp.bfloat16))
    packed = jnp.concatenate([key_states[0, 0], value_states[0, 0], flag_rows], axis=0)

    with jax.named_scope("halo_exchange"):
        column = jnp.stack([shifted(packed, "fh", 1), packed, shifted(packed, "fh", -1)])
        columns = (shifted(column, "wa", 1), column, shifted(column, "wa", -1))
    mask = jnp.concatenate(
        [jnp.where(side[:, 2 * tokens : 2 * tokens + 1, :tokens] > 0, 0.0, MASKED) for side in columns]
    ).astype(jnp.float32)
    row_at = lax.axis_index("fh") + jnp.arange(3) - 1
    column_at = lax.axis_index("wa") + jnp.arange(3) - 1
    present = (
        ((column_at >= 0) & (column_at < lax.axis_size("wa")))[:, None]
        & ((row_at >= 0) & (row_at < lax.axis_size("fh")))[None, :]
    ).reshape(-1).astype(jnp.int32)

    with jax.named_scope("cotangent_gather"):
        cot_all = lax.all_gather(out_cotangent[0, 0], "ha", axis=0, tiled=True)

    with jax.named_scope("attention_forward"):
        attended = attention_forward(present, mask, q, columns)

    with jax.named_scope("output_projection"):
        projected = jnp.dot(attended, out_weight, preferred_element_type=jnp.float32)
        layer_out = lax.psum_scatter(
            projected.astype(jnp.bfloat16), "ha", scatter_dimension=0, tiled=True
        )

    with jax.named_scope("grad_attended"):
        grad_attended = lax.dot_general(
            cot_all, out_weight, (((1,), (1,)), ((), ())), preferred_element_type=jnp.float32
        ).astype(jnp.bfloat16)

    with jax.named_scope("grad_weight"):
        weight_part = lax.dot_general(
            cot_all, attended, (((0,), (0,)), ((), ())), preferred_element_type=jnp.float32
        )
        weight_own, weight_sent = scatter_parts(weight_part, "fh", 0)
        weight_own, weight_sent, grad_attended = lax.optimization_barrier(
            (weight_own, weight_sent, grad_attended)
        )
        weight_rows = scatter_finish(weight_own, weight_sent, "fh")

    with jax.named_scope("attention_backward"):
        grad_q, left, partials, right = attention_backward(
            present, mask, q, columns, attended, grad_attended
        )

    with jax.named_scope("grad_weight"):
        grad_weight = scatter_sum(weight_rows, "wa", 0)

    with jax.named_scope("halo_reduction"):
        middle = (
            partials
            + shifted(left, "wa", -1).astype(jnp.float32)
            + shifted(right, "wa", 1).astype(jnp.float32)
        )
        middle_sides = middle.astype(jnp.bfloat16)
        own = (
            middle[1]
            + shifted(middle_sides[0], "fh", -1).astype(jnp.float32)
            + shifted(middle_sides[2], "fh", 1).astype(jnp.float32)
        )
    grad_keys = own[:tokens].astype(jnp.bfloat16)
    grad_values = own[tokens:].astype(jnp.bfloat16)
    expand = lambda x: x[None, None]
    return (
        expand(layer_out),
        expand(grad_q),
        expand(grad_keys),
        expand(grad_values),
        grad_weight,
    )


def solution(mesh):
    return jax.shard_map(
        body,
        mesh=mesh,
        in_specs=(
            P("fh", "wa", None, "ha"),
            P("fh", "wa", None, "ha"),
            P("fh", "wa", None, "ha"),
            P("fh", "wa", None),
            P("ha", None),
            P("fh", "wa", "ha", None),
        ),
        out_specs=(
            P("fh", "wa", "ha", None),
            P("fh", "wa", None, "ha"),
            P("fh", "wa", None, "ha"),
            P("fh", "wa", None, "ha"),
            P(("fh", "wa"), "ha"),
        ),
        check_vma=False,
    )
```

time: 176 us -> 201 us (1.14)
  Pallas kernels: 36.3 us -> 61.4 us
  other arithmetic: 13.4 us -> 16.2 us
  local copies, waits for them, and re-layouts: 11.2 us -> 8.92 us
    pallas_call x2, Pallas kernels: 36.3 us -> 61.4 us  [the longest x1 42.8 us: attention_backward(): pl.pallas_call(functools.partial(backward_kernel, scale), grid_spec=pltpu...]
    slice x3 -> x0, local copies, waits for them, and re-layouts: 2.21 us -> none  [body(): side[:, 2 * tokens, :tokens]]
    select_n x0 -> x3, other arithmetic: none -> 2.18 us  [body(): jnp.where(side[:, 2 * tokens:2 * tokens + 1, :tokens] > 0, 0.0, MASKED)]
    unnamed x19 -> x15, local copies, waits for them, and re-layouts: 4.18 us -> 3.54 us
  transfers between devices with their start and end apart: 14 -> 14, of which waited for: 9 -> 9; matrix products, arithmetic and copies ran while one was open for 18% -> 16% of each run, Pallas kernels for 21% -> 31%
where the time goes in v8:
time: 201 us; the launch traced here: 199 us
  Pallas kernels  61.4 us (31%)
  waiting for transfers between devices  58.5 us (29%)
  starting transfers between devices  30.8 us (15%)
  other arithmetic  16.2 us (8%)
  between operations  14.3 us (7%)
  matrix products  8.94 us (4%)
  local copies, waits for them, and re-layouts  8.92 us (4%)
    ppermute x8, waiting for transfers between devices, shifted(): return lax.ppermute(value, axis, shift_pairs(lax.axis_size(axis), steps))  47.5 us
    pallas_call x1, Pallas kernels, attention_backward(): pl.pallas_call(functools.partial(backward_kernel, scale), grid_spec=pltpu...  42.8 us
    ppermute x8, starting transfers between devices, shifted(): return lax.ppermute(value, axis, shift_pairs(lax.axis_size(axis), steps))  25.4 us
    pallas_call x1, Pallas kernels, attention_forward(): pl.pallas_call(functools.partial(forward_kernel, scale), grid_spec=pltpu....  18.7 us
    ppermute x4, waiting for transfers between devices, cyclic(): lax.ppermute(value, axis, [(i, (i + steps) % count) for i in range(count)])  10.3 us
    ppermute x4, starting transfers between devices, cyclic(): lax.ppermute(value, axis, [(i, (i + steps) % count) for i in range(count)])  5.29 us
    convert_element_type x1, other arithmetic, body(): middle_sides = middle.astype(jnp.bfloat16)  4.47 us
  transfers between devices with their start and end apart: 14, of which 9 were waited for; matrix products, arithmetic and copies ran while one was open for 16% of the time, Pallas kernels for 31%

profile of v8, /device:TPU:1, one launch (start us, length us, event | category | flops | bytes accessed | tf_op | source)
XLA Modules:
  0.0 199.0 jit_solution(12343026168141058275)
XLA Ops:
  7.2 0.0 copy-start
  7.2 0.0 all-gather.3.cloned.1.call-start
  7.2 0.7 all-gather.3.cloned.1.call-update
  7.9 0.0 reduce-scatter.2.cloned.1.call-start
  8.0 0.7 convert_bitcast_fusion
  8.6 1.2 fusion.13
  9.8 1.3 collective-permute-start.1
  11.1 4.1 %collective-permute-start = (bf16[784,384]{1,0:T(8,128)(2,1)S(1)}, bf16[784,384]{1,0:T(8,128)(2,1)S(1)}, u32[]{:S(2)}, u32[]{:S(2)}) collective-permute-start(bf16[784,384]{1,0:T(8,128)(2,1)S(1)} %get-tuple-element.44), channel_id=1, source_target_pairs={{0,16},{1,17},{2,18},{3,19},{4,20},{5,21},{6,22},{7,23},{8,24},{9,... | collective-permute-start | bytes 1806344 | tf_op jit(solution)/shard_map/halo_exchange/ppermute | solution.py:22
  15.2 11.4 %collective-permute-done.1 = bf16[784,384]{1,0:T(8,128)(2,1)S(1)} collective-permute-done((bf16[784,384]{1,0:T(8,128)(2,1)S(1)}, bf16[784,384]{1,0:T(8,128)(2,1)S(1)}, u32[]{:S(2)}, u32[]{:S(2)}) %collective-permute-start.1) | collective-permute-done | bytes 602144 | tf_op jit(solution)/shard_map/halo_exchange/ppermute | solution.py:22
  26.6 0.8 collective-permute-done
  27.4 1.5 pad_maximum_fusion.km.vm
  28.9 3.4 %collective-permute-start.3 = (bf16[3,784,384]{2,1,0:T(8,128)(2,1)}, bf16[3,784,384]{2,1,0:T(8,128)(2,1)}, u32[]{:S(2)}, u32[]{:S(2)}) collective-permute-start(bf16[3,784,384]{2,1,0:T(8,128)(2,1)} %pad_maximum_fusion.km.vm), channel_id=1, source_target_pairs={{4,0},{8,4},{12,8},{5,1},{9,5},{13,9},{6,2},{10,6},{14,10},{7,3},{... | collective-permute-start | bytes 5419016 | tf_op jit(solution)/shard_map/halo_exchange/ppermute | solution.py:22
  32.3 3.8 %collective-permute-start.2 = (bf16[3,784,384]{2,1,0:T(8,128)(2,1)}, bf16[3,784,384]{2,1,0:T(8,128)(2,1)}, u32[]{:S(2)}, u32[]{:S(2)}) collective-permute-start(bf16[3,784,384]{2,1,0:T(8,128)(2,1)} %pad_maximum_fusion.km.vm), channel_id=1, source_target_pairs={{0,4},{4,8},{8,12},{1,5},{5,9},{9,13},{2,6},{6,10},{10,14},{3,7},{... | collective-permute-start | bytes 5419016 | tf_op jit(solution)/shard_map/halo_exchange/ppermute | solution.py:22
  36.2 0.1 and_convert_fusion
  36.3 0.6 reshape.66.present_ref
  36.9 0.7 compare_select_fusion.1
  37.6 17.8 %collective-permute-done.3.kr.vr = bf16[3,784,384]{2,1,0:T(8,128)(2,1)} collective-permute-done((bf16[3,784,384]{2,1,0:T(8,128)(2,1)}, bf16[3,784,384]{2,1,0:T(8,128)(2,1)}, u32[]{:S(2)}, u32[]{:S(2)}) %collective-permute-start.3) | collective-permute-done | bytes 1806368 | tf_op jit(solution)/shard_map/halo_exchange/ppermute | solution.py:22
  55.5 0.7 compare_select_fusion
  56.2 0.2 collective-permute-done.2.kl.vl
  56.3 0.7 compare_select_fusion.2
  57.1 0.6 pad_maximum_fusion.1.mask_ref
  57.7 18.7 %tile_attention_forward.1.o_ref = bf16[384,384]{1,0:T(8,128)(2,1)} custom-call(s32[9]{0:T(128)} %reshape.66.present_ref, f32[9,1,384]{2,1,0:T(1,128)} %pad_maximum_fusion.1.mask_ref, bf16[384,384]{1,0:T(8,128)(2,1)} %bitcast.42, bf16[3,784,384]{2,1,0:T(8,128)(2,1)} %collective-permute-done.2.kl.vl, bf16[3,784,384]{2,1,0:T(8,128)(2,1)} %pad_maximum_fusion.km.vm, ...), custom_call_target="tpu_custom_call" | custom-call | tf_op jit(solution)/shard_map/attention_forward/tile_attention_forward/pallas_call | solution.py:134
  76.3 0.0 copy-done
  76.3 3.7 %convolution_convert_fusion = bf16[384,3072]{1,0:T(8,128)(2,1)} fusion(bf16[384,384]{1,0:T(8,128)(2,1)} %tile_attention_forward.1.o_ref, bf16[384,3072]{1,0:T(8,128)(2,1)S(1)} %copy-done), kind=kOutput, calls=%fused_computation | convolution fusion | flops 907149312 | bytes 5013504 | tf_op jit(solution)/shard_map/output_projection/dot_general | solution.py:272
  80.1 0.0 reduce-scatter.2.cloned.1.call-update
  80.1 0.0 all-gather.3.cloned.1.call-done
  80.2 0.9 copy-done.2
  81.1 3.1 %fusion.2 = f32[384,3072]{1,0:T(8,128)S(1)} fusion(bf16[384,384]{1,0:T(8,128)(2,1)S(1)} %copy-done.2, bf16[1,1,384,3072]{3,2,1,0:T(8,128)(2,1)} %all-gather.3.cloned.1.call-done), kind=kOutput, calls=%fused_computation.4 | convolution fusion | flops 905969664 | bytes 7372800 | tf_op jit(solution)/shard_map/grad_weight/dot_general | solution.py:283
  84.1 0.1 fusion.8
  84.3 0.0 copy-start.4
  84.3 1.7 dynamic-slice_bitcast_fusion
  86.0 0.8 copy-done.4
  86.8 2.1 %fusion.4.do_ref = bf16[384,384]{1,0:T(8,128)(2,1)} fusion(bf16[384,3072]{1,0:T(8,128)(2,1)S(1)} %copy-done, bf16[1,1,384,3072]{3,2,1,0:T(8,128)(2,1)S(1)} %copy-done.4), kind=kOutput, calls=%fused_computation.10 | convolution fusion | flops 906117120 | bytes 5013504 | tf_op jit(solution)/shard_map/grad_attended/dot_general | solution.py:278
  88.9 2.1 %collective-permute-start.8 = (bf16[1536,384]{0,1:T(8,128)(2,1)S(1)}, bf16[1536,384]{0,1:T(8,128)(2,1)}, u32[]{:S(2)}, u32[]{:S(2)}) collective-permute-start(bf16[1536,384]{0,1:T(8,128)(2,1)S(1)} %fusion.8), channel_id=1, source_target_pairs={{0,16},{16,0},{1,17},{17,1},{2,18},{18,2},{3,19},{19,3},{4,20},{20... | collective-permute-start | bytes 3538952 | tf_op jit(solution)/shard_map/grad_weight/ppermute | solution.py:27
  91.1 42.8 %tile_attention_backward.1 = (bf16[384,384]{1,0:T(8,128)(2,1)}, bf16[3,768,384]{2,1,0:T(8,128)(2,1)}, f32[3,768,384]{2,1,0:T(8,128)}, bf16[3,768,384]{2,1,0:T(8,128)(2,1)}) custom-call(s32[9]{0:T(128)} %reshape.66.present_ref, f32[9,1,384]{2,1,0:T(1,128)} %pad_maximum_fusion.1.mask_ref, bf16[384,384]{1,0:T(8,128)(2,1)} %bitcast.43, ...), custom_call_target="tpu_custom_call" | custom-call | tf_op jit(solution)/shard_map/attention_backward/tile_attention_backward/pallas_call | solution.py:166
  133.8 1.9 collective-permute-start.4
  135.8 4.7 %collective-permute-start.5 = (bf16[3,768,384]{2,1,0:T(8,128)(2,1)}, bf16[3,768,384]{2,1,0:T(8,128)(2,1)}, u32[]{:S(2)}, u32[]{:S(2)}) collective-permute-start(bf16[3,768,384]{2,1,0:T(8,128)(2,1)} %get-tuple-element.28), channel_id=1, source_target_pairs={{0,4},{4,8},{8,12},{1,5},{5,9},{9,13},{2,6},{6,10},{10,14},{3,7},{... | collective-permute-start | bytes 5308424 | tf_op jit(solution)/shard_map/halo_reduction/ppermute | solution.py:22
  140.5 0.0 copy-start.3
  140.5 0.0 collective-permute-done.8
  140.5 2.4 %convert_add_fusion.1 = f32[1536,384]{0,1:T(8,128)S(1)} fusion(f32[1536,384]{0,1:T(8,128)} %dynamic-slice_bitcast_fusion, bf16[1536,384]{0,1:T(8,128)(2,1)} %collective-permute-done.8), kind=kLoop, calls=%fused_computation.6 | loop fusion | flops 1179648 | bytes 5898240 | tf_op jit(solution)/shard_map/grad_weight/add | solution.py:224
  143.0 0.0 copy-start.1
  143.0 16.3 %collective-permute-done.4 = bf16[3,768,384]{2,1,0:T(8,128)(2,1)} collective-permute-done((bf16[3,768,384]{2,1,0:T(8,128)(2,1)}, bf16[3,768,384]{2,1,0:T(8,128)(2,1)}, u32[]{:S(2)}, u32[]{:S(2)}) %collective-permute-start.4) | collective-permute-done | bytes 1769504 | tf_op jit(solution)/shard_map/halo_reduction/ppermute | solution.py:22
  159.2 1.0 collective-permute-done.5
  160.2 0.0 copy-done.3
  160.2 4.5 %fusion.14 = (bf16[3,768,384]{2,1,0:T(8,128)(2,1)S(1)}, f32[3,768,384]{2,1,0:T(8,128)}) fusion(bf16[3,768,384]{2,1,0:T(8,128)(2,1)} %collective-permute-done.5, f32[3,768,384]{2,1,0:T(8,128)S(1)} %copy-done.3, bf16[3,768,384]{2,1,0:T(8,128)(2,1)} %collective-permute-done.4), kind=kLoop, calls=%fused_computation.36 | loop fusion | flops 4423680 | bytes 12386304 | tf_op jit(solution)/shard_map/halo_reduction/convert_element_type | solution.py:306
  164.7 1.1 slice_bitcast_fusion.2
  165.8 1.3 collective-permute-start.6
  167.1 4.9 %collective-permute-start.7 = (bf16[768,384]{1,0:T(8,128)(2,1)}, bf16[768,384]{1,0:T(8,128)(2,1)}, u32[]{:S(2)}, u32[]{:S(2)}) collective-permute-start(bf16[768,384]{1,0:T(8,128)(2,1)} %get-tuple-element.42), channel_id=1, source_target_pairs={{0,16},{1,17},{2,18},{3,19},{4,20},{5,21},{6,22},{7,23},{8,24},{9,... | collective-permute-start | bytes 1769480 | tf_op jit(solution)/shard_map/halo_reduction/ppermute | solution.py:22
  172.0 0.0 copy-done.1
  172.0 1.0 dynamic-slice_convert_fusion.3
  173.0 3.0 %collective-permute-start.9 = (bf16[384,384]{0,1:T(8,128)(2,1)}, bf16[384,384]{0,1:T(8,128)(2,1)S(1)}, u32[]{:S(2)}, u32[]{:S(2)}) collective-permute-start(bf16[384,384]{0,1:T(8,128)(2,1)} %get-tuple-element.38), channel_id=1, source_target_pairs={{0,4},{4,8},{8,12},{12,0},{1,5},{5,9},{9,13},{13,1},{2,6},{6,10},{... | collective-permute-start | bytes 884744 | tf_op jit(solution)/shard_map/grad_weight/ppermute | solution.py:27
  176.0 0.0 collective-permute-start.11
  176.0 0.1 collective-permute-start.10
  176.1 6.3 %collective-permute-done.9 = bf16[384,384]{0,1:T(8,128)(2,1)S(1)} collective-permute-done((bf16[384,384]{0,1:T(8,128)(2,1)}, bf16[384,384]{0,1:T(8,128)(2,1)S(1)}, u32[]{:S(2)}, u32[]{:S(2)}) %collective-permute-start.9) | collective-permute-done | bytes 294944 | tf_op jit(solution)/shard_map/grad_weight/ppermute | solution.py:27
  182.4 2.6 %collective-permute-done.11 = bf16[384,384]{0,1:T(8,128)(2,1)S(1)} collective-permute-done((bf16[384,384]{0,1:T(8,128)(2,1)}, bf16[384,384]{0,1:T(8,128)(2,1)S(1)}, u32[]{:S(2)}, u32[]{:S(2)}) %collective-permute-start.11) | collective-permute-done | bytes 294944 | tf_op jit(solution)/shard_map/grad_weight/ppermute | solution.py:27
  185.0 0.0 copy-done.5
  185.0 0.7 copy-done.6
  185.7 1.4 collective-permute-done.10
  187.1 1.5 convert_add_fusion.2
  188.6 1.1 copy.11
  189.6 0.0 collective-permute-done.6
  189.6 0.0 collective-permute-done.7
  189.7 1.6 fusion.11
  191.3 0.9 slice_bitcast_fusion.3
  (5 shorter events, 0.0 us)
Async XLA Ops:
  7.2 69.2 %copy-start = (bf16[384,3072]{1,0:T(8,128)(2,1)S(1)}, bf16[384,3072]{1,0:T(8,128)(2,1)}, u32[]{:S(2)}) copy-start(bf16[384,3072]{1,0:T(8,128)(2,1)} %param.12) | copy-start | bytes 7077892
  7.2 73.0 %all-gather.3.cloned.1.call-start = ((), (), s32[]{:S(2)}) async-start(), calls=%async_computation.2 | async-start | bytes 2949120 | tf_op jit(solution)/shard_map/cotangent_gather/all_gather | solution.py:266
  7.9 184.2 %reduce-scatter.2.cloned.1.call-start = ((), (), s32[]{:S(2)}) async-start(), calls=%async_computation.1 | async-start | bytes 2949120 | tf_op jit(solution)/shard_map/output_projection/reduce_scatter | solution.py:273
  9.8 16.8 %collective-permute-start.1 = (bf16[784,384]{1,0:T(8,128)(2,1)S(1)}, bf16[784,384]{1,0:T(8,128)(2,1)S(1)}, u32[]{:S(2)}, u32[]{:S(2)}) collective-permute-start(bf16[784,384]{1,0:T(8,128)(2,1)S(1)} %get-tuple-element.44), channel_id=1, source_target_pairs={{16,0},{17,1},{18,2},{19,3},{20,4},{21,5},{22,6},{23,7},{24,8},{25... | collective-permute-start | bytes 1806344 | tf_op jit(solution)/shard_map/halo_exchange/ppermute | solution.py:22
  11.1 16.3 %collective-permute-start = (bf16[784,384]{1,0:T(8,128)(2,1)S(1)}, bf16[784,384]{1,0:T(8,128)(2,1)S(1)}, u32[]{:S(2)}, u32[]{:S(2)}) collective-permute-start(bf16[784,384]{1,0:T(8,128)(2,1)S(1)} %get-tuple-element.44), channel_id=1, source_target_pairs={{0,16},{1,17},{2,18},{3,19},{4,20},{5,21},{6,22},{7,23},{8,24},{9,... | collective-permute-start | bytes 1806344 | tf_op jit(solution)/shard_map/halo_exchange/ppermute | solution.py:22
  28.9 26.6 %collective-permute-start.3 = (bf16[3,784,384]{2,1,0:T(8,128)(2,1)}, bf16[3,784,384]{2,1,0:T(8,128)(2,1)}, u32[]{:S(2)}, u32[]{:S(2)}) collective-permute-start(bf16[3,784,384]{2,1,0:T(8,128)(2,1)} %pad_maximum_fusion.km.vm), channel_id=1, source_target_pairs={{4,0},{8,4},{12,8},{5,1},{9,5},{13,9},{6,2},{10,6},{14,10},{7,3},{... | collective-permute-start | bytes 5419016 | tf_op jit(solution)/shard_map/halo_exchange/ppermute | solution.py:22
  32.3 24.0 %collective-permute-start.2 = (bf16[3,784,384]{2,1,0:T(8,128)(2,1)}, bf16[3,784,384]{2,1,0:T(8,128)(2,1)}, u32[]{:S(2)}, u32[]{:S(2)}) collective-permute-start(bf16[3,784,384]{2,1,0:T(8,128)(2,1)} %pad_maximum_fusion.km.vm), channel_id=1, source_target_pairs={{0,4},{4,8},{8,12},{1,5},{5,9},{9,13},{2,6},{6,10},{10,14},{3,7},{... | collective-permute-start | bytes 5419016 | tf_op jit(solution)/shard_map/halo_exchange/ppermute | solution.py:22
  80.1 1.0 copy-start.2
  84.3 2.5 %copy-start.4 = (bf16[1,1,384,3072]{3,2,1,0:T(8,128)(2,1)S(1)}, bf16[1,1,384,3072]{3,2,1,0:T(8,128)(2,1)}, u32[]{:S(2)}) copy-start(bf16[1,1,384,3072]{3,2,1,0:T(8,128)(2,1)} %all-gather.3.cloned.1.call-done) | copy-start | bytes 7077892
  88.9 51.6 %collective-permute-start.8 = (bf16[1536,384]{0,1:T(8,128)(2,1)S(1)}, bf16[1536,384]{0,1:T(8,128)(2,1)}, u32[]{:S(2)}, u32[]{:S(2)}) collective-permute-start(bf16[1536,384]{0,1:T(8,128)(2,1)S(1)} %fusion.8), channel_id=1, source_target_pairs={{0,16},{16,0},{1,17},{17,1},{2,18},{18,2},{3,19},{19,3},{4,20},{20... | collective-permute-start | bytes 3538952 | tf_op jit(solution)/shard_map/grad_weight/ppermute | solution.py:27
  133.8 25.4 %collective-permute-start.4 = (bf16[3,768,384]{2,1,0:T(8,128)(2,1)}, bf16[3,768,384]{2,1,0:T(8,128)(2,1)}, u32[]{:S(2)}, u32[]{:S(2)}) collective-permute-start(bf16[3,768,384]{2,1,0:T(8,128)(2,1)} %get-tuple-element.27), channel_id=1, source_target_pairs={{4,0},{8,4},{12,8},{5,1},{9,5},{13,9},{6,2},{10,6},{14,10},{7,3},{... | collective-permute-start | bytes 5308424 | tf_op jit(solution)/shard_map/halo_reduction/ppermute | solution.py:22
  135.8 24.4 %collective-permute-start.5 = (bf16[3,768,384]{2,1,0:T(8,128)(2,1)}, bf16[3,768,384]{2,1,0:T(8,128)(2,1)}, u32[]{:S(2)}, u32[]{:S(2)}) collective-permute-start(bf16[3,768,384]{2,1,0:T(8,128)(2,1)} %get-tuple-element.28), channel_id=1, source_target_pairs={{0,4},{4,8},{8,12},{1,5},{5,9},{9,13},{2,6},{6,10},{10,14},{3,7},{... | collective-permute-start | bytes 5308424 | tf_op jit(solution)/shard_map/halo_reduction/ppermute | solution.py:22
  140.5 19.7 %copy-start.3 = (f32[3,768,384]{2,1,0:T(8,128)S(1)}, f32[3,768,384]{2,1,0:T(8,128)}, u32[]{:S(2)}) copy-start(f32[3,768,384]{2,1,0:T(8,128)} %get-tuple-element.26) | copy-start | bytes 10616836
  143.0 29.1 %copy-start.1 = (f32[1536,384]{0,1:T(8,128)}, f32[1536,384]{0,1:T(8,128)S(1)}, u32[]{:S(2)}) copy-start(f32[1536,384]{0,1:T(8,128)S(1)} %convert_add_fusion.1) | copy-start | bytes 7077892
  165.8 23.8 %collective-permute-start.6 = (bf16[768,384]{1,0:T(8,128)(2,1)}, bf16[768,384]{1,0:T(8,128)(2,1)S(1)}, u32[]{:S(2)}, u32[]{:S(2)}) collective-permute-start(bf16[768,384]{1,0:T(8,128)(2,1)} %get-tuple-element.41), channel_id=1, source_target_pairs={{16,0},{17,1},{18,2},{19,3},{20,4},{21,5},{22,6},{23,7},{24,8},{25... | collective-permute-start | bytes 1769480 | tf_op jit(solution)/shard_map/halo_reduction/ppermute | solution.py:22
  167.1 22.6 %collective-permute-start.7 = (bf16[768,384]{1,0:T(8,128)(2,1)}, bf16[768,384]{1,0:T(8,128)(2,1)}, u32[]{:S(2)}, u32[]{:S(2)}) collective-permute-start(bf16[768,384]{1,0:T(8,128)(2,1)} %get-tuple-element.42), channel_id=1, source_target_pairs={{0,16},{1,17},{2,18},{3,19},{4,20},{5,21},{6,22},{7,23},{8,24},{9,... | collective-permute-start | bytes 1769480 | tf_op jit(solution)/shard_map/halo_reduction/ppermute | solution.py:22
  173.0 9.4 %collective-permute-start.9 = (bf16[384,384]{0,1:T(8,128)(2,1)}, bf16[384,384]{0,1:T(8,128)(2,1)S(1)}, u32[]{:S(2)}, u32[]{:S(2)}) collective-permute-start(bf16[384,384]{0,1:T(8,128)(2,1)} %get-tuple-element.38), channel_id=1, source_target_pairs={{0,4},{4,8},{8,12},{12,0},{1,5},{5,9},{9,13},{13,1},{2,6},{6,10},{... | collective-permute-start | bytes 884744 | tf_op jit(solution)/shard_map/grad_weight/ppermute | solution.py:27
  176.0 9.0 %collective-permute-start.11 = (bf16[384,384]{0,1:T(8,128)(2,1)}, bf16[384,384]{0,1:T(8,128)(2,1)S(1)}, u32[]{:S(2)}, u32[]{:S(2)}) collective-permute-start(bf16[384,384]{0,1:T(8,128)(2,1)} %get-tuple-element.39), channel_id=1, source_target_pairs={{0,12},{4,0},{8,4},{12,8},{1,13},{5,1},{9,5},{13,9},{2,14},{6,2},{... | collective-permute-start | bytes 884744 | tf_op jit(solution)/shard_map/grad_weight/ppermute | solution.py:27
  176.0 11.1 %collective-permute-start.10 = (bf16[384,384]{0,1:T(8,128)(2,1)}, bf16[384,384]{0,1:T(8,128)(2,1)}, u32[]{:S(2)}, u32[]{:S(2)}) collective-permute-start(bf16[384,384]{0,1:T(8,128)(2,1)} %get-tuple-element.40), channel_id=1, source_target_pairs={{0,8},{4,12},{8,0},{12,4},{1,9},{5,13},{9,1},{13,5},{2,10},{6,14},... | collective-permute-start | bytes 884744 | tf_op jit(solution)/shard_map/grad_weight/ppermute | solution.py:27
  182.4 2.6 %copy-start.5 = (bf16[384,384]{0,1:T(8,128)(2,1)}, bf16[384,384]{0,1:T(8,128)(2,1)S(1)}, u32[]{:S(2)}) copy-start(bf16[384,384]{0,1:T(8,128)(2,1)S(1)} %collective-permute-done.9) | copy-start | bytes 884740
  185.0 0.7 copy-start.6
Sparse Core Ops, SparseCore 0:
  9.6 52.5 all-gather.2
  80.2 50.7 reduce-scatter.1

commit v9 on v7

--- a/solution.py
+++ b/solution.py
@@ -12,6 +12,7 @@
 FORWARD_CHUNK = 384
 BACKWARD_CHUNK = 192
 FLAG_ROWS = 16
+LOG2E = 1.4426950408889634
 
 
 def shift_pairs(count, steps):
@@ -31,34 +32,32 @@
     return jnp.concatenate([ref[...].reshape(-1, HD) for ref in refs], axis=0)
 
 
-def scores_of(mask_ref, q_ref, k, scale):
-    q = q_ref[...]
-    s = lax.dot_general(q, k, (((1,), (1,)), ((), ())), preferred_element_type=jnp.float32)
-    return s * scale + mask_ref[...]
-
-
-def forward_kernel(scale, mask_ref, q_ref, kl, km, kr, vl, vm, vr, o_ref):
-    s = scores_of(mask_ref, q_ref, joined((kl, km, kr)), scale)
+def raw_scores(mask_ref, q_ref, k):
+    s = lax.dot_general(q_ref[...], k, (((1,), (1,)), ((), ())), preferred_element_type=jnp.float32)
+    return s + mask_ref[...]
+
+
+def forward_kernel(exp_scale, mask_ref, q_ref, kl, km, kr, vl, vm, vr, o_ref, m_ref, r_ref):
+    s = raw_scores(mask_ref, q_ref, joined((kl, km, kr)))
     m = jnp.max(s, axis=1, keepdims=True)
-    e = jnp.exp(s - m)
-    total = jnp.sum(e, axis=1, keepdims=True)
-    p = (e * (1.0 / total)).astype(jnp.bfloat16)
+    e = jnp.exp2((s - m) * exp_scale)
+    inverse = 1.0 / jnp.sum(e, axis=1, keepdims=True)
+    p = (e * inverse).astype(jnp.bfloat16)
     v = joined((vl, vm, vr))
     o_ref[...] = jnp.dot(p, v, preferred_element_type=jnp.float32).astype(o_ref.dtype)
+    m_ref[...] = jnp.broadcast_to(m, m_ref.shape)
+    r_ref[...] = jnp.broadcast_to(inverse, r_ref.shape)
 
 
 def backward_kernel(
-    scale, mask_ref, q_ref, kl, km, kr, vl, vm, vr, o_ref, do_ref, dq_ref, left_ref, mid_ref,
-    right_ref, acc_ref
+    scale, exp_scale, mask_ref, q_ref, kl, km, kr, vl, vm, vr, o_ref, m_ref, r_ref, do_ref,
+    dq_ref, left_ref, mid_ref, right_ref, acc_ref
 ):
     chunk = pl.program_id(1)
     k = joined((kl, km, kr))
     v = joined((vl, vm, vr))
-    s = scores_of(mask_ref, q_ref, k, scale)
-    m = jnp.max(s, axis=1, keepdims=True)
-    e = jnp.exp(s - m)
-    total = jnp.sum(e, axis=1, keepdims=True)
-    w = e * (1.0 / total)
+    s = raw_scores(mask_ref, q_ref, k)
+    w = jnp.exp2((s - m_ref[:, :1]) * exp_scale) * r_ref[:, :1]
     p = w.astype(jnp.bfloat16)
     do = do_ref[...]
     row_dot = jnp.sum(
@@ -101,7 +100,7 @@
     chunks = tokens // chunk
     scale = HD ** (-0.5)
     return pl.pallas_call(
-        functools.partial(forward_kernel, scale),
+        functools.partial(forward_kernel, scale * LOG2E),
         grid=(heads, chunks),
         in_specs=[
             pl.BlockSpec((1, tiles * tokens), lambda h, c: (0, 0)),
@@ -109,13 +108,17 @@
             *[pl.BlockSpec((tiles // 3, tokens, HD), lambda h, c: (0, 0, h))] * 3,
             *[pl.BlockSpec((tiles // 3, tokens, HD), lambda h, c: (0, 1, h))] * 3,
         ],
-        out_specs=pl.BlockSpec((chunk, HD), lambda h, c: (c, h)),
-        out_shape=jax.ShapeDtypeStruct((tokens, features), jnp.bfloat16),
+        out_specs=[pl.BlockSpec((chunk, HD), lambda h, c: (c, h))] * 3,
+        out_shape=[
+            jax.ShapeDtypeStruct((tokens, features), jnp.bfloat16),
+            jax.ShapeDtypeStruct((tokens, features), jnp.float32),
+            jax.ShapeDtypeStruct((tokens, features), jnp.float32),
+        ],
         name="tile_attention_forward",
     )(mask, queries, *columns, *columns)
 
 
-def attention_backward(mask, queries, columns, attended, grad_attended):
+def attention_backward(mask, queries, columns, attended, row_max, row_inverse, grad_attended):
     tokens, features = queries.shape
     tiles = 3 * columns[0].shape[0]
     heads = features // HD
@@ -123,13 +126,15 @@
     chunks = tokens // chunk
     scale = HD ** (-0.5)
     return pl.pallas_call(
-        functools.partial(backward_kernel, scale),
+        functools.partial(backward_kernel, scale, scale * LOG2E),
         grid=(heads, chunks),
         in_specs=[
             pl.BlockSpec((1, tiles * tokens), lambda h, c: (0, 0)),
             pl.BlockSpec((chunk, HD), lambda h, c: (c, h)),
             *[pl.BlockSpec((tiles // 3, tokens, HD), lambda h, c: (0, 0, h))] * 3,
             *[pl.BlockSpec((tiles // 3, tokens, HD), lambda h, c: (0, 1, h))] * 3,
+            pl.BlockSpec((chunk, HD), lambda h, c: (c, h)),
+            pl.BlockSpec((chunk, HD), lambda h, c: (c, h)),
             pl.BlockSpec((chunk, HD), lambda h, c: (c, h)),
             pl.BlockSpec((chunk, HD), lambda h, c: (c, h)),
         ],
@@ -147,7 +152,7 @@
         ],
         scratch_shapes=[pltpu.VMEM((tiles, 2 * tokens, HD), jnp.float32)],
         name="tile_attention_backward",
-    )(mask, queries, *columns, *columns, attended, grad_attended)
+    )(mask, queries, *columns, *columns, attended, row_max, row_inverse, grad_attended)
 
 
 def gather_over(piece, axis):
@@ -206,13 +211,13 @@
         columns = (shifted(column, "wa", 1), column, shifted(column, "wa", -1))
     flags = jnp.concatenate([side[:, 2 * tokens, :tokens] for side in columns], axis=0)
     flags = flags.reshape(1, -1)
-    mask = jnp.where(flags > 0, 0.0, MASKED).astype(jnp.float32)
+    mask = jnp.where(flags > 0, 0.0, MASKED / HD ** (-0.5)).astype(jnp.float32)
 
     with jax.named_scope("cotangent_gather"):
         cot_all = lax.all_gather(out_cotangent[0, 0], "ha", axis=0, tiled=True)
 
     with jax.named_scope("attention_forward"):
-        attended = attention_forward(mask, q, columns)
+        attended, row_max, row_inverse = attention_forward(mask, q, columns)
 
     with jax.named_scope("output_projection"):
         projected = jnp.dot(attended, out_weight, preferred_element_type=jnp.float32)
@@ -237,7 +242,7 @@
 
     with jax.named_scope("attention_backward"):
         grad_q, left, partials, right = attention_backward(
-            mask, q, columns, attended, grad_attended
+            mask, q, columns, attended, row_max, row_inverse, grad_attended
         )
 
     with jax.named_scope("grad_weight"):

time: 176 us -> 174 us (0.989)
  waiting for transfers between devices: 59 us -> 63.3 us
  starting transfers between devices: 30.9 us -> 28 us
  Pallas kernels: 36.3 us -> 34.4 us
    ppermute x8, waiting for transfers between devices: 48 us -> 50.7 us  [shifted(): return lax.ppermute(value, axis, shift_pairs(lax.axis_size(axis), steps))]
    ppermute x4, starting transfers between devices: 5.36 us -> 3.44 us  [cyclic(): lax.ppermute(value, axis, [(i, (i + steps) % count) for i in range(count)])]
    pallas_call x2, Pallas kernels: 36.3 us -> 34.4 us  [the longest x1 20.6 us: attention_backward(): pl.pallas_call(functools.partial(backward_kernel, scale, scale * LOG2E),...]
  transfers between devices with their start and end apart: 14 -> 14, of which waited for: 9 -> 8; matrix products, arithmetic and copies ran while one was open for 18% -> 18% of each run, Pallas kernels for 21% -> 20%
where the time goes in v9:
time: 174 us; the launch traced here: 173 us
  waiting for transfers between devices  63.3 us (36%)
  Pallas kernels  34.4 us (20%)
  starting transfers between devices  28 us (16%)
  between operations  14.3 us (8%)
  other arithmetic  13.3 us (8%)
  local copies, waits for them, and re-layouts  11.2 us (6%)
  matrix products  8.95 us (5%)
    ppermute x8, waiting for transfers between devices, shifted(): return lax.ppermute(value, axis, shift_pairs(lax.axis_size(axis), steps))  50.7 us
    ppermute x8, starting transfers between devices, shifted(): return lax.ppermute(value, axis, shift_pairs(lax.axis_size(axis), steps))  24.5 us
    pallas_call x1, Pallas kernels, attention_backward(): pl.pallas_call(functools.partial(backward_kernel, scale, scale * LOG2E),...  20.6 us
    pallas_call x1, Pallas kernels, attention_forward(): pl.pallas_call(functools.partial(forward_kernel, scale * LOG2E), grid=(he...  13.8 us
    ppermute x4, waiting for transfers between devices, cyclic(): lax.ppermute(value, axis, [(i, (i + steps) % count) for i in range(count)])  11.8 us
    convert_element_type x1, other arithmetic, body(): middle_sides = middle.astype(jnp.bfloat16)  4.47 us
    unnamed x19, local copies, waits for them, and re-layouts  4.17 us
    dot_general x1, matrix products, body(): jnp.dot(attended, out_weight, preferred_element_type=jnp.float32)  3.75 us
  transfers between devices with their start and end apart: 14, of which 8 were waited for; matrix products, arithmetic and copies ran while one was open for 18% of the time, Pallas kernels for 20%

profile of v9, /device:TPU:1, one launch (start us, length us, event | category | flops | bytes accessed | tf_op | source)
XLA Modules:
  0.0 173.4 jit_solution(14645691721301438880)
XLA Ops:
  7.2 0.0 copy-start
  7.2 0.0 all-gather.3.cloned.1.call-start
  7.2 0.7 all-gather.3.cloned.1.call-update
  7.9 0.0 reduce-scatter.2.cloned.1.call-start
  8.0 0.7 convert_bitcast_fusion
  8.6 1.2 fusion.13
  9.8 4.0 %collective-permute-start = (bf16[784,384]{1,0:T(8,128)(2,1)S(1)}, bf16[784,384]{1,0:T(8,128)(2,1)S(1)}, u32[]{:S(2)}, u32[]{:S(2)}) collective-permute-start(bf16[784,384]{1,0:T(8,128)(2,1)S(1)} %get-tuple-element.65), channel_id=1, source_target_pairs={{0,16},{1,17},{2,18},{3,19},{4,20},{5,21},{6,22},{7,23},{8,24},{9,... | collective-permute-start | bytes 1806344 | tf_op jit(solution)/shard_map/halo_exchange/ppermute | solution.py:23
  13.8 1.3 collective-permute-start.1
  15.1 10.9 %collective-permute-done = bf16[784,384]{1,0:T(8,128)(2,1)S(1)} collective-permute-done((bf16[784,384]{1,0:T(8,128)(2,1)S(1)}, bf16[784,384]{1,0:T(8,128)(2,1)S(1)}, u32[]{:S(2)}, u32[]{:S(2)}) %collective-permute-start) | collective-permute-done | bytes 602144 | tf_op jit(solution)/shard_map/halo_exchange/ppermute | solution.py:23
  26.0 3.9 %collective-permute-done.1 = bf16[784,384]{1,0:T(8,128)(2,1)S(1)} collective-permute-done((bf16[784,384]{1,0:T(8,128)(2,1)S(1)}, bf16[784,384]{1,0:T(8,128)(2,1)S(1)}, u32[]{:S(2)}, u32[]{:S(2)}) %collective-permute-start.1) | collective-permute-done | bytes 602144 | tf_op jit(solution)/shard_map/halo_exchange/ppermute | solution.py:23
  30.0 1.5 pad_maximum_fusion.km.vm
  31.5 3.7 %collective-permute-start.3 = (bf16[3,784,384]{2,1,0:T(8,128)(2,1)}, bf16[3,784,384]{2,1,0:T(8,128)(2,1)}, u32[]{:S(2)}, u32[]{:S(2)}) collective-permute-start(bf16[3,784,384]{2,1,0:T(8,128)(2,1)} %pad_maximum_fusion.km.vm), channel_id=1, source_target_pairs={{4,0},{8,4},{12,8},{5,1},{9,5},{13,9},{6,2},{10,6},{14,10},{7,3},{... | collective-permute-start | bytes 5419016 | tf_op jit(solution)/shard_map/halo_exchange/ppermute | solution.py:23
  35.1 3.0 %collective-permute-start.2 = (bf16[3,784,384]{2,1,0:T(8,128)(2,1)}, bf16[3,784,384]{2,1,0:T(8,128)(2,1)}, u32[]{:S(2)}, u32[]{:S(2)}) collective-permute-start(bf16[3,784,384]{2,1,0:T(8,128)(2,1)} %pad_maximum_fusion.km.vm), channel_id=1, source_target_pairs={{0,4},{4,8},{8,12},{1,5},{5,9},{9,13},{2,6},{6,10},{10,14},{3,7},{... | collective-permute-start | bytes 5419016 | tf_op jit(solution)/shard_map/halo_exchange/ppermute | solution.py:23
  38.2 0.8 slice.49
  38.9 18.5 %collective-permute-done.3.kr.vr = bf16[3,784,384]{2,1,0:T(8,128)(2,1)} collective-permute-done((bf16[3,784,384]{2,1,0:T(8,128)(2,1)}, bf16[3,784,384]{2,1,0:T(8,128)(2,1)}, u32[]{:S(2)}, u32[]{:S(2)}) %collective-permute-start.3) | collective-permute-done | bytes 1806368 | tf_op jit(solution)/shard_map/halo_exchange/ppermute | solution.py:23
  57.4 0.7 slice.50
  58.2 0.2 collective-permute-done.2.kl.vl
  58.3 0.7 slice.48
  59.1 0.6 copy.34
  59.7 13.8 %tile_attention_forward.1 = (bf16[384,384]{1,0:T(8,128)(2,1)}, f32[384,384]{1,0:T(8,128)}, f32[384,384]{1,0:T(8,128)}) custom-call(f32[1,3456]{1,0:T(1,128)} %bitcast.61, bf16[384,384]{1,0:T(8,128)(2,1)} %bitcast.55, bf16[3,784,384]{2,1,0:T(8,128)(2,1)} %collective-permute-done.2.kl.vl, bf16[3,784,384]{2,1,0:T(8,128)(2,1)} %pad_maximum_fusion.km.vm, ...), custom_call_target="tpu_custom_call" | custom-call | tf_op jit(solution)/shard_map/attention_forward/tile_attention_forward/pallas_call | solution.py:102
  73.5 0.0 copy-done
  73.5 3.7 %convolution_convert_fusion = bf16[384,3072]{1,0:T(8,128)(2,1)} fusion(bf16[384,384]{1,0:T(8,128)(2,1)} %get-tuple-element.27.o_ref, bf16[384,3072]{1,0:T(8,128)(2,1)S(1)} %copy-done), kind=kOutput, calls=%fused_computation | convolution fusion | flops 907149312 | bytes 5013504 | tf_op jit(solution)/shard_map/output_projection/dot_general | solution.py:223
  77.2 0.0 copy-start.3
  77.2 0.0 reduce-scatter.2.cloned.1.call-update
  77.3 0.0 all-gather.3.cloned.1.call-done
  77.3 0.9 copy-done.3
  78.2 3.1 %fusion.2 = f32[384,3072]{1,0:T(8,128)S(1)} fusion(bf16[384,384]{1,0:T(8,128)(2,1)S(1)} %copy-done.3, bf16[1,1,384,3072]{3,2,1,0:T(8,128)(2,1)} %all-gather.3.cloned.1.call-done), kind=kOutput, calls=%fused_computation.4 | convolution fusion | flops 905969664 | bytes 7372800 | tf_op jit(solution)/shard_map/grad_weight/dot_general | solution.py:234
  81.3 0.1 fusion.8
  81.4 0.0 copy-start.4
  81.4 1.7 dynamic-slice_bitcast_fusion
  83.1 0.8 copy-done.4
  84.0 2.1 %fusion.4.do_ref = bf16[384,384]{1,0:T(8,128)(2,1)} fusion(bf16[384,3072]{1,0:T(8,128)(2,1)S(1)} %copy-done, bf16[1,1,384,3072]{3,2,1,0:T(8,128)(2,1)S(1)} %copy-done.4), kind=kOutput, calls=%fused_computation.10 | convolution fusion | flops 906117120 | bytes 5013504 | tf_op jit(solution)/shard_map/grad_attended/dot_general | solution.py:229
  86.1 0.0 collective-permute-start.8
  86.1 20.6 %tile_attention_backward.1 = (bf16[384,384]{1,0:T(8,128)(2,1)}, bf16[3,768,384]{2,1,0:T(8,128)(2,1)}, f32[3,768,384]{2,1,0:T(8,128)}, bf16[3,768,384]{2,1,0:T(8,128)(2,1)}) custom-call(f32[1,3456]{1,0:T(1,128)} %bitcast.62, bf16[384,384]{1,0:T(8,128)(2,1)} %bitcast.56, bf16[3,784,384]{2,1,0:T(8,128)(2,1)} %collective-permute-done.2.kl.vl, ...), custom_call_target="tpu_custom_call" | custom-call | tf_op jit(solution)/shard_map/attention_backward/tile_attention_backward/pallas_call | solution.py:128
  106.7 1.9 %collective-permute-start.4 = (bf16[3,768,384]{2,1,0:T(8,128)(2,1)}, bf16[3,768,384]{2,1,0:T(8,128)(2,1)}, u32[]{:S(2)}, u32[]{:S(2)}) collective-permute-start(bf16[3,768,384]{2,1,0:T(8,128)(2,1)} %get-tuple-element.33), channel_id=1, source_target_pairs={{4,0},{8,4},{12,8},{5,1},{9,5},{13,9},{6,2},{10,6},{14,10},{7,3},{... | collective-permute-start | bytes 5308424 | tf_op jit(solution)/shard_map/halo_reduction/ppermute | solution.py:23
  108.7 4.4 %collective-permute-start.5 = (bf16[3,768,384]{2,1,0:T(8,128)(2,1)}, bf16[3,768,384]{2,1,0:T(8,128)(2,1)}, u32[]{:S(2)}, u32[]{:S(2)}) collective-permute-start(bf16[3,768,384]{2,1,0:T(8,128)(2,1)} %get-tuple-element.34), channel_id=1, source_target_pairs={{0,4},{4,8},{8,12},{1,5},{5,9},{9,13},{2,6},{6,10},{10,14},{3,7},{... | collective-permute-start | bytes 5308424 | tf_op jit(solution)/shard_map/halo_reduction/ppermute | solution.py:23
  113.1 0.0 copy-start.2
  113.1 0.0 collective-permute-done.8
  113.1 2.4 %convert_add_fusion.1 = f32[1536,384]{0,1:T(8,128)S(1)} fusion(f32[1536,384]{0,1:T(8,128)} %dynamic-slice_bitcast_fusion, bf16[1536,384]{0,1:T(8,128)(2,1)} %collective-permute-done.8), kind=kLoop, calls=%fused_computation.6 | loop fusion | flops 1179648 | bytes 5898240 | tf_op jit(solution)/shard_map/grad_weight/add | solution.py:181
  115.6 0.0 copy-start.1
  115.6 16.3 %collective-permute-done.4 = bf16[3,768,384]{2,1,0:T(8,128)(2,1)} collective-permute-done((bf16[3,768,384]{2,1,0:T(8,128)(2,1)}, bf16[3,768,384]{2,1,0:T(8,128)(2,1)}, u32[]{:S(2)}, u32[]{:S(2)}) %collective-permute-start.4) | collective-permute-done | bytes 1769504 | tf_op jit(solution)/shard_map/halo_reduction/ppermute | solution.py:23
  131.8 1.0 collective-permute-done.5
  132.8 0.0 copy-done.2
  132.8 4.5 %fusion.14 = (bf16[3,768,384]{2,1,0:T(8,128)(2,1)S(1)}, f32[3,768,384]{2,1,0:T(8,128)}) fusion(bf16[3,768,384]{2,1,0:T(8,128)(2,1)} %collective-permute-done.5, f32[3,768,384]{2,1,0:T(8,128)S(1)} %copy-done.2, bf16[3,768,384]{2,1,0:T(8,128)(2,1)} %collective-permute-done.4), kind=kLoop, calls=%fused_computation.33 | loop fusion | flops 4423680 | bytes 12386304 | tf_op jit(solution)/shard_map/halo_reduction/convert_element_type | solution.py:257
  137.3 1.1 slice_bitcast_fusion.2
  138.4 1.3 collective-permute-start.6
  139.7 4.9 %collective-permute-start.7 = (bf16[768,384]{1,0:T(8,128)(2,1)}, bf16[768,384]{1,0:T(8,128)(2,1)}, u32[]{:S(2)}, u32[]{:S(2)}) collective-permute-start(bf16[768,384]{1,0:T(8,128)(2,1)} %get-tuple-element.63), channel_id=1, source_target_pairs={{0,16},{1,17},{2,18},{3,19},{4,20},{5,21},{6,22},{7,23},{8,24},{9,... | collective-permute-start | bytes 1769480 | tf_op jit(solution)/shard_map/halo_reduction/ppermute | solution.py:23
  144.6 0.0 copy-done.1
  144.6 1.0 dynamic-slice_convert_fusion.3
  145.6 0.0 collective-permute-start.10
  145.6 3.4 %collective-permute-start.11 = (bf16[384,384]{0,1:T(8,128)(2,1)}, bf16[384,384]{0,1:T(8,128)(2,1)S(1)}, u32[]{:S(2)}, u32[]{:S(2)}) collective-permute-start(bf16[384,384]{0,1:T(8,128)(2,1)} %get-tuple-element.60), channel_id=1, source_target_pairs={{0,12},{4,0},{8,4},{12,8},{1,13},{5,1},{9,5},{13,9},{2,14},{6,2},{... | collective-permute-start | bytes 884744 | tf_op jit(solution)/shard_map/grad_weight/ppermute | solution.py:28
  149.0 0.0 collective-permute-start.9
  149.0 3.9 %collective-permute-done.10 = bf16[384,384]{0,1:T(8,128)(2,1)S(1)} collective-permute-done((bf16[384,384]{0,1:T(8,128)(2,1)}, bf16[384,384]{0,1:T(8,128)(2,1)S(1)}, u32[]{:S(2)}, u32[]{:S(2)}) %collective-permute-start.10) | collective-permute-done | bytes 294944 | tf_op jit(solution)/shard_map/grad_weight/ppermute | solution.py:28
  152.9 0.0 copy-start.5
  152.9 8.0 %collective-permute-done.11 = bf16[384,384]{0,1:T(8,128)(2,1)S(1)} collective-permute-done((bf16[384,384]{0,1:T(8,128)(2,1)}, bf16[384,384]{0,1:T(8,128)(2,1)S(1)}, u32[]{:S(2)}, u32[]{:S(2)}) %collective-permute-start.11) | collective-permute-done | bytes 294944 | tf_op jit(solution)/shard_map/grad_weight/ppermute | solution.py:28
  160.9 0.0 copy-done.5
  160.9 0.7 copy-done.6
  161.6 0.0 collective-permute-done.9
  161.6 1.5 convert_add_fusion.2
  163.0 1.1 copy.30
  164.1 0.0 collective-permute-done.6
  164.1 0.0 collective-permute-done.7
  164.1 1.6 fusion.11
  165.7 0.9 slice_bitcast_fusion.3
  (6 shorter events, 0.0 us)
Async XLA Ops:
  7.2 66.3 %copy-start = (bf16[384,3072]{1,0:T(8,128)(2,1)S(1)}, bf16[384,3072]{1,0:T(8,128)(2,1)}, u32[]{:S(2)}) copy-start(bf16[384,3072]{1,0:T(8,128)(2,1)} %param.12) | copy-start | bytes 7077892
  7.2 70.1 %all-gather.3.cloned.1.call-start = ((), (), s32[]{:S(2)}) async-start(), calls=%async_computation.2 | async-start | bytes 2949120 | tf_op jit(solution)/shard_map/cotangent_gather/all_gather | solution.py:217
  7.9 158.7 %reduce-scatter.2.cloned.1.call-start = ((), (), s32[]{:S(2)}) async-start(), calls=%async_computation.1 | async-start | bytes 2949120 | tf_op jit(solution)/shard_map/output_projection/reduce_scatter | solution.py:224
  9.8 16.2 %collective-permute-start = (bf16[784,384]{1,0:T(8,128)(2,1)S(1)}, bf16[784,384]{1,0:T(8,128)(2,1)S(1)}, u32[]{:S(2)}, u32[]{:S(2)}) collective-permute-start(bf16[784,384]{1,0:T(8,128)(2,1)S(1)} %get-tuple-element.65), channel_id=1, source_target_pairs={{0,16},{1,17},{2,18},{3,19},{4,20},{5,21},{6,22},{7,23},{8,24},{9,... | collective-permute-start | bytes 1806344 | tf_op jit(solution)/shard_map/halo_exchange/ppermute | solution.py:23
  13.8 16.1 %collective-permute-start.1 = (bf16[784,384]{1,0:T(8,128)(2,1)S(1)}, bf16[784,384]{1,0:T(8,128)(2,1)S(1)}, u32[]{:S(2)}, u32[]{:S(2)}) collective-permute-start(bf16[784,384]{1,0:T(8,128)(2,1)S(1)} %get-tuple-element.65), channel_id=1, source_target_pairs={{16,0},{17,1},{18,2},{19,3},{20,4},{21,5},{22,6},{23,7},{24,8},{25... | collective-permute-start | bytes 1806344 | tf_op jit(solution)/shard_map/halo_exchange/ppermute | solution.py:23
  31.5 26.0 %collective-permute-start.3 = (bf16[3,784,384]{2,1,0:T(8,128)(2,1)}, bf16[3,784,384]{2,1,0:T(8,128)(2,1)}, u32[]{:S(2)}, u32[]{:S(2)}) collective-permute-start(bf16[3,784,384]{2,1,0:T(8,128)(2,1)} %pad_maximum_fusion.km.vm), channel_id=1, source_target_pairs={{4,0},{8,4},{12,8},{5,1},{9,5},{13,9},{6,2},{10,6},{14,10},{7,3},{... | collective-permute-start | bytes 5419016 | tf_op jit(solution)/shard_map/halo_exchange/ppermute | solution.py:23
  35.1 23.2 %collective-permute-start.2 = (bf16[3,784,384]{2,1,0:T(8,128)(2,1)}, bf16[3,784,384]{2,1,0:T(8,128)(2,1)}, u32[]{:S(2)}, u32[]{:S(2)}) collective-permute-start(bf16[3,784,384]{2,1,0:T(8,128)(2,1)} %pad_maximum_fusion.km.vm), channel_id=1, source_target_pairs={{0,4},{4,8},{8,12},{1,5},{5,9},{9,13},{2,6},{6,10},{10,14},{3,7},{... | collective-permute-start | bytes 5419016 | tf_op jit(solution)/shard_map/halo_exchange/ppermute | solution.py:23
  77.2 1.0 copy-start.3
  81.4 2.5 %copy-start.4 = (bf16[1,1,384,3072]{3,2,1,0:T(8,128)(2,1)S(1)}, bf16[1,1,384,3072]{3,2,1,0:T(8,128)(2,1)}, u32[]{:S(2)}) copy-start(bf16[1,1,384,3072]{3,2,1,0:T(8,128)(2,1)} %all-gather.3.cloned.1.call-done) | copy-start | bytes 7077892
  86.1 27.1 %collective-permute-start.8 = (bf16[1536,384]{0,1:T(8,128)(2,1)S(1)}, bf16[1536,384]{0,1:T(8,128)(2,1)}, u32[]{:S(2)}, u32[]{:S(2)}) collective-permute-start(bf16[1536,384]{0,1:T(8,128)(2,1)S(1)} %fusion.8), channel_id=1, source_target_pairs={{0,16},{16,0},{1,17},{17,1},{2,18},{18,2},{3,19},{19,3},{4,20},{20... | collective-permute-start | bytes 3538952 | tf_op jit(solution)/shard_map/grad_weight/ppermute | solution.py:28
  106.7 25.1 %collective-permute-start.4 = (bf16[3,768,384]{2,1,0:T(8,128)(2,1)}, bf16[3,768,384]{2,1,0:T(8,128)(2,1)}, u32[]{:S(2)}, u32[]{:S(2)}) collective-permute-start(bf16[3,768,384]{2,1,0:T(8,128)(2,1)} %get-tuple-element.33), channel_id=1, source_target_pairs={{4,0},{8,4},{12,8},{5,1},{9,5},{13,9},{6,2},{10,6},{14,10},{7,3},{... | collective-permute-start | bytes 5308424 | tf_op jit(solution)/shard_map/halo_reduction/ppermute | solution.py:23
  108.7 24.2 %collective-permute-start.5 = (bf16[3,768,384]{2,1,0:T(8,128)(2,1)}, bf16[3,768,384]{2,1,0:T(8,128)(2,1)}, u32[]{:S(2)}, u32[]{:S(2)}) collective-permute-start(bf16[3,768,384]{2,1,0:T(8,128)(2,1)} %get-tuple-element.34), channel_id=1, source_target_pairs={{0,4},{4,8},{8,12},{1,5},{5,9},{9,13},{2,6},{6,10},{10,14},{3,7},{... | collective-permute-start | bytes 5308424 | tf_op jit(solution)/shard_map/halo_reduction/ppermute | solution.py:23
  113.1 19.7 %copy-start.2 = (f32[3,768,384]{2,1,0:T(8,128)S(1)}, f32[3,768,384]{2,1,0:T(8,128)}, u32[]{:S(2)}) copy-start(f32[3,768,384]{2,1,0:T(8,128)} %get-tuple-element.32) | copy-start | bytes 10616836
  115.6 29.1 %copy-start.1 = (f32[1536,384]{0,1:T(8,128)}, f32[1536,384]{0,1:T(8,128)S(1)}, u32[]{:S(2)}) copy-start(f32[1536,384]{0,1:T(8,128)S(1)} %convert_add_fusion.1) | copy-start | bytes 7077892
  138.4 25.7 %collective-permute-start.6 = (bf16[768,384]{1,0:T(8,128)(2,1)}, bf16[768,384]{1,0:T(8,128)(2,1)S(1)}, u32[]{:S(2)}, u32[]{:S(2)}) collective-permute-start(bf16[768,384]{1,0:T(8,128)(2,1)} %get-tuple-element.62), channel_id=1, source_target_pairs={{16,0},{17,1},{18,2},{19,3},{20,4},{21,5},{22,6},{23,7},{24,8},{25... | collective-permute-start | bytes 1769480 | tf_op jit(solution)/shard_map/halo_reduction/ppermute | solution.py:23
  139.7 24.4 %collective-permute-start.7 = (bf16[768,384]{1,0:T(8,128)(2,1)}, bf16[768,384]{1,0:T(8,128)(2,1)}, u32[]{:S(2)}, u32[]{:S(2)}) collective-permute-start(bf16[768,384]{1,0:T(8,128)(2,1)} %get-tuple-element.63), channel_id=1, source_target_pairs={{0,16},{1,17},{2,18},{3,19},{4,20},{5,21},{6,22},{7,23},{8,24},{9,... | collective-permute-start | bytes 1769480 | tf_op jit(solution)/shard_map/halo_reduction/ppermute | solution.py:23
  145.6 7.3 %collective-permute-start.10 = (bf16[384,384]{0,1:T(8,128)(2,1)}, bf16[384,384]{0,1:T(8,128)(2,1)S(1)}, u32[]{:S(2)}, u32[]{:S(2)}) collective-permute-start(bf16[384,384]{0,1:T(8,128)(2,1)} %get-tuple-element.61), channel_id=1, source_target_pairs={{0,8},{4,12},{8,0},{12,4},{1,9},{5,13},{9,1},{13,5},{2,10},{6,14},... | collective-permute-start | bytes 884744 | tf_op jit(solution)/shard_map/grad_weight/ppermute | solution.py:28
  145.6 15.3 %collective-permute-start.11 = (bf16[384,384]{0,1:T(8,128)(2,1)}, bf16[384,384]{0,1:T(8,128)(2,1)S(1)}, u32[]{:S(2)}, u32[]{:S(2)}) collective-permute-start(bf16[384,384]{0,1:T(8,128)(2,1)} %get-tuple-element.60), channel_id=1, source_target_pairs={{0,12},{4,0},{8,4},{12,8},{1,13},{5,1},{9,5},{13,9},{2,14},{6,2},{... | collective-permute-start | bytes 884744 | tf_op jit(solution)/shard_map/grad_weight/ppermute | solution.py:28
  149.0 12.5 %collective-permute-start.9 = (bf16[384,384]{0,1:T(8,128)(2,1)}, bf16[384,384]{0,1:T(8,128)(2,1)}, u32[]{:S(2)}, u32[]{:S(2)}) collective-permute-start(bf16[384,384]{0,1:T(8,128)(2,1)} %get-tuple-element.59), channel_id=1, source_target_pairs={{0,4},{4,8},{8,12},{12,0},{1,5},{5,9},{9,13},{13,1},{2,6},{6,10},{... | collective-permute-start | bytes 884744 | tf_op jit(solution)/shard_map/grad_weight/ppermute | solution.py:28
  152.9 8.0 %copy-start.5 = (bf16[384,384]{0,1:T(8,128)(2,1)}, bf16[384,384]{0,1:T(8,128)(2,1)S(1)}, u32[]{:S(2)}) copy-start(bf16[384,384]{0,1:T(8,128)(2,1)S(1)} %collective-permute-done.10) | copy-start | bytes 884740
  160.9 0.7 copy-start.6
Sparse Core Ops, SparseCore 0:
  9.6 52.5 all-gather.2
  77.4 48.8 reduce-scatter.1

commit v10 on v9

--- a/solution.py
+++ b/solution.py
@@ -207,7 +207,10 @@
     packed = jnp.concatenate([key_states[0, 0], value_states[0, 0], flag_rows], axis=0)
 
     with jax.named_scope("halo_exchange"):
-        column = jnp.stack([shifted(packed, "fh", 1), packed, shifted(packed, "fh", -1)])
+        if lax.axis_size("fh") == 2:
+            column = jnp.stack([cyclic(packed, "fh", 1), packed])
+        else:
+            column = jnp.stack([shifted(packed, "fh", 1), packed, shifted(packed, "fh", -1)])
         columns = (shifted(column, "wa", 1), column, shifted(column, "wa", -1))
     flags = jnp.concatenate([side[:, 2 * tokens, :tokens] for side in columns], axis=0)
     flags = flags.reshape(1, -1)
@@ -255,11 +258,14 @@
             + shifted(right, "wa", 1).astype(jnp.float32)
         )
         middle_sides = middle.astype(jnp.bfloat16)
-        own = (
-            middle[1]
-            + shifted(middle_sides[0], "fh", -1).astype(jnp.float32)
-            + shifted(middle_sides[2], "fh", 1).astype(jnp.float32)
-        )
+        if lax.axis_size("fh") == 2:
+            own = middle[1] + cyclic(middle_sides[0], "fh", 1).astype(jnp.float32)
+        else:
+            own = (
+                middle[1]
+                + shifted(middle_sides[0], "fh", -1).astype(jnp.float32)
+                + shifted(middle_sides[2], "fh", 1).astype(jnp.float32)
+            )
     grad_keys = own[:tokens].astype(jnp.bfloat16)
     grad_values = own[tokens:].astype(jnp.bfloat16)
     expand = lambda x: x[None, None]

time: 174 us -> 154 us (0.89)
  Pallas kernels: 34.4 us -> 25.3 us
  starting transfers between devices: 28 us -> 19.1 us
  other arithmetic: 13.3 us -> 10.9 us
    ppermute x8 -> x4, waiting for transfers between devices: 50.7 us -> 24.4 us  [shifted(): return lax.ppermute(value, axis, shift_pairs(lax.axis_size(axis), steps))]
    ppermute x4 -> x6, waiting for transfers between devices: 11.8 us -> 36.9 us  [cyclic(): lax.ppermute(value, axis, [(i, (i + steps) % count) for i in range(count)])]
    ppermute x8 -> x4, starting transfers between devices: 24.5 us -> 12.6 us  [shifted(): return lax.ppermute(value, axis, shift_pairs(lax.axis_size(axis), steps))]
    pallas_call x1, Pallas kernels: 20.6 us -> 15.2 us  [attention_backward(): pl.pallas_call(functools.partial(backward_kernel, scale, scale * LOG2E),...]
    convert_element_type x1 -> x0, other arithmetic: 4.47 us -> none  [body(): middle_sides = middle.astype(jnp.bfloat16)]
    pallas_call x1, Pallas kernels: 13.8 us -> 10.1 us  [attention_forward(): pl.pallas_call(functools.partial(forward_kernel, scale * LOG2E), grid=(he...]
    ppermute x4 -> x6, starting transfers between devices: 3.44 us -> 6.44 us  [cyclic(): lax.ppermute(value, axis, [(i, (i + steps) % count) for i in range(count)])]
    add x0 -> x1, other arithmetic: none -> 2.48 us  [body(): partials + shifted(left, 'wa', -1).astype(jnp.float32)]
  transfers between devices with their start and end apart: 14 -> 12, of which waited for: 8 -> 9; matrix products, arithmetic and copies ran while one was open for 18% -> 18% of each run, Pallas kernels for 20% -> 17%
where the time goes in v10:
time: 154 us; the launch traced here: 152 us
  waiting for transfers between devices  62 us (40%)
  Pallas kernels  25.3 us (16%)
  starting transfers between devices  19.1 us (12%)
  between operations  14.2 us (9%)
  local copies, waits for them, and re-layouts  12 us (8%)
  other arithmetic  10.9 us (7%)
  matrix products  8.99 us (6%)
    ppermute x6, waiting for transfers between devices, cyclic(): lax.ppermute(value, axis, [(i, (i + steps) % count) for i in range(count)])  36.9 us
    ppermute x4, waiting for transfers between devices, shifted(): return lax.ppermute(value, axis, shift_pairs(lax.axis_size(axis), steps))  24.4 us
    pallas_call x1, Pallas kernels, attention_backward(): pl.pallas_call(functools.partial(backward_kernel, scale, scale * LOG2E),...  15.2 us
    ppermute x4, starting transfers between devices, shifted(): return lax.ppermute(value, axis, shift_pairs(lax.axis_size(axis), steps))  12.6 us
    pallas_call x1, Pallas kernels, attention_forward(): pl.pallas_call(functools.partial(forward_kernel, scale * LOG2E), grid=(he...  10.1 us
    ppermute x6, starting transfers between devices, cyclic(): lax.ppermute(value, axis, [(i, (i + steps) % count) for i in range(count)])  6.44 us
    unnamed x23, local copies, waits for them, and re-layouts  5.63 us
    dot_general x1, matrix products, body(): jnp.dot(attended, out_weight, preferred_element_type=jnp.float32)  3.79 us
  transfers between devices with their start and end apart: 12, of which 9 were waited for; matrix products, arithmetic and copies ran while one was open for 18% of the time, Pallas kernels for 17%

profile of v10, /device:TPU:1, one launch (start us, length us, event | category | flops | bytes accessed | tf_op | source)
XLA Modules:
  0.0 152.4 jit_solution(12008684160204850311)
XLA Ops:
  7.2 0.0 copy-start
  7.2 0.0 all-gather.3.cloned.1.call-start
  7.2 0.7 all-gather.3.cloned.1.call-update
  7.9 0.0 reduce-scatter.2.cloned.1.call-start
  8.0 0.7 convert_bitcast_fusion
  8.6 1.2 fusion.11
  9.8 2.1 %collective-permute-start = (bf16[784,384]{1,0:T(8,128)(2,1)S(1)}, bf16[784,384]{1,0:T(8,128)(2,1)S(1)}, u32[]{:S(2)}, u32[]{:S(2)}) collective-permute-start(bf16[784,384]{1,0:T(8,128)(2,1)S(1)} %get-tuple-element.60), channel_id=1, source_target_pairs={{0,16},{16,0},{1,17},{17,1},{2,18},{18,2},{3,19},{19,3},{4,20},{20... | collective-permute-start | bytes 1806344 | tf_op jit(solution)/shard_map/halo_exchange/ppermute | solution.py:28
  11.9 13.4 %collective-permute-done = bf16[784,384]{1,0:T(8,128)(2,1)S(1)} collective-permute-done((bf16[784,384]{1,0:T(8,128)(2,1)S(1)}, bf16[784,384]{1,0:T(8,128)(2,1)S(1)}, u32[]{:S(2)}, u32[]{:S(2)}) %collective-permute-start) | collective-permute-done | bytes 602144 | tf_op jit(solution)/shard_map/halo_exchange/ppermute | solution.py:28
  25.4 0.0 copy-start.5
  25.4 0.8 copy-done.5
  26.2 1.2 pad_maximum_fusion.km.vm
  27.5 3.0 %collective-permute-start.2 = (bf16[2,784,384]{2,1,0:T(8,128)(2,1)}, bf16[2,784,384]{2,1,0:T(8,128)(2,1)}, u32[]{:S(2)}, u32[]{:S(2)}) collective-permute-start(bf16[2,784,384]{2,1,0:T(8,128)(2,1)} %pad_maximum_fusion.km.vm), channel_id=1, source_target_pairs={{4,0},{8,4},{12,8},{5,1},{9,5},{13,9},{6,2},{10,6},{14,10},{7,3},{... | collective-permute-start | bytes 3612680 | tf_op jit(solution)/shard_map/halo_exchange/ppermute | solution.py:23
  30.5 3.2 %collective-permute-start.1 = (bf16[2,784,384]{2,1,0:T(8,128)(2,1)}, bf16[2,784,384]{2,1,0:T(8,128)(2,1)}, u32[]{:S(2)}, u32[]{:S(2)}) collective-permute-start(bf16[2,784,384]{2,1,0:T(8,128)(2,1)} %pad_maximum_fusion.km.vm), channel_id=1, source_target_pairs={{0,4},{4,8},{8,12},{1,5},{5,9},{9,13},{2,6},{6,10},{10,14},{3,7},{... | collective-permute-start | bytes 3612680 | tf_op jit(solution)/shard_map/halo_exchange/ppermute | solution.py:23
  33.7 0.7 fusion.13
  34.5 12.1 %collective-permute-done.2.kr.vr = bf16[2,784,384]{2,1,0:T(8,128)(2,1)} collective-permute-done((bf16[2,784,384]{2,1,0:T(8,128)(2,1)}, bf16[2,784,384]{2,1,0:T(8,128)(2,1)}, u32[]{:S(2)}, u32[]{:S(2)}) %collective-permute-start.2) | collective-permute-done | bytes 1204256 | tf_op jit(solution)/shard_map/halo_exchange/ppermute | solution.py:23
  46.5 0.7 slice.47
  47.3 0.2 collective-permute-done.1.kl.vl
  47.4 0.7 slice.44
  48.2 0.6 copy.33
  48.8 10.1 %tile_attention_forward.1 = (bf16[384,384]{1,0:T(8,128)(2,1)}, f32[384,384]{1,0:T(8,128)}, f32[384,384]{1,0:T(8,128)}) custom-call(f32[1,2304]{1,0:T(1,128)} %bitcast.56, bf16[384,384]{1,0:T(8,128)(2,1)} %bitcast.52, bf16[2,784,384]{2,1,0:T(8,128)(2,1)} %collective-permute-done.1.kl.vl, bf16[2,784,384]{2,1,0:T(8,128)(2,1)} %pad_maximum_fusion.km.vm, ...), custom_call_target="tpu_custom_call" | custom-call | tf_op jit(solution)/shard_map/attention_forward/tile_attention_forward/pallas_call | solution.py:102
  58.9 0.0 copy-done
  58.9 3.8 %convolution_convert_fusion = bf16[384,3072]{1,0:T(8,128)(2,1)} fusion(bf16[384,384]{1,0:T(8,128)(2,1)} %get-tuple-element.27.o_ref, bf16[384,3072]{1,0:T(8,128)(2,1)S(1)} %copy-done), kind=kOutput, calls=%fused_computation | convolution fusion | flops 907149312 | bytes 5013504 | tf_op jit(solution)/shard_map/output_projection/dot_general | solution.py:226
  62.7 0.0 copy-start.4
  62.7 0.0 reduce-scatter.2.cloned.1.call-update
  62.7 0.0 all-gather.3.cloned.1.call-done
  62.7 0.9 copy-done.4
  63.6 3.1 %fusion.2 = f32[384,3072]{1,0:T(8,128)S(1)} fusion(bf16[384,384]{1,0:T(8,128)(2,1)S(1)} %copy-done.4, bf16[1,1,384,3072]{3,2,1,0:T(8,128)(2,1)} %all-gather.3.cloned.1.call-done), kind=kOutput, calls=%fused_computation.3 | convolution fusion | flops 905969664 | bytes 7372800 | tf_op jit(solution)/shard_map/grad_weight/dot_general | solution.py:237
  66.7 1.2 fusion.8
  67.9 0.0 copy-start.6
  67.9 1.6 %dynamic-slice_bitcast_fusion = f32[1536,384]{0,1:T(8,128)} fusion(f32[384,3072]{1,0:T(8,128)S(1)} %fusion.2, s32[]{:T(128)S(6)} %select_n.45), kind=kLoop, calls=%fused_computation.8 | loop fusion | bytes 4718596 | tf_op jit(solution)/shard_map/grad_weight/dynamic_slice | solution.py:172
  69.5 0.9 copy-done.6
  70.4 2.1 %fusion.4.do_ref = bf16[384,384]{1,0:T(8,128)(2,1)} fusion(bf16[384,3072]{1,0:T(8,128)(2,1)S(1)} %copy-done, bf16[1,1,384,3072]{3,2,1,0:T(8,128)(2,1)S(1)} %copy-done.6), kind=kOutput, calls=%fused_computation.12 | convolution fusion | flops 906117120 | bytes 5013504 | tf_op jit(solution)/shard_map/grad_attended/dot_general | solution.py:232
  72.5 15.2 %tile_attention_backward.1 = (bf16[384,384]{1,0:T(8,128)(2,1)}, bf16[2,768,384]{2,1,0:T(8,128)(2,1)}, f32[2,768,384]{2,1,0:T(8,128)}, bf16[2,768,384]{2,1,0:T(8,128)(2,1)}) custom-call(f32[1,2304]{1,0:T(1,128)} %bitcast.57, bf16[384,384]{1,0:T(8,128)(2,1)} %bitcast.53, bf16[2,784,384]{2,1,0:T(8,128)(2,1)} %collective-permute-done.1.kl.vl, ...), custom_call_target="tpu_custom_call" | custom-call | tf_op jit(solution)/shard_map/attention_backward/tile_attention_backward/pallas_call | solution.py:128
  87.7 1.9 %collective-permute-start.3 = (bf16[2,768,384]{2,1,0:T(8,128)(2,1)}, bf16[2,768,384]{2,1,0:T(8,128)(2,1)S(1)}, u32[]{:S(2)}, u32[]{:S(2)}) collective-permute-start(bf16[2,768,384]{2,1,0:T(8,128)(2,1)} %get-tuple-element.33), channel_id=1, source_target_pairs={{4,0},{8,4},{12,8},{5,1},{9,5},{13,9},{6,2},{10,6},{14,10},{7,3},{... | collective-permute-start | bytes 3538952 | tf_op jit(solution)/shard_map/halo_reduction/ppermute | solution.py:23
  89.6 4.4 %collective-permute-start.4 = (bf16[2,768,384]{2,1,0:T(8,128)(2,1)}, bf16[2,768,384]{2,1,0:T(8,128)(2,1)}, u32[]{:S(2)}, u32[]{:S(2)}) collective-permute-start(bf16[2,768,384]{2,1,0:T(8,128)(2,1)} %get-tuple-element.34), channel_id=1, source_target_pairs={{0,4},{4,8},{8,12},{1,5},{5,9},{9,13},{2,6},{6,10},{10,14},{3,7},{... | collective-permute-start | bytes 3538952 | tf_op jit(solution)/shard_map/halo_reduction/ppermute | solution.py:23
  94.1 1.3 collective-permute-start.6
  95.4 11.2 %collective-permute-done.3 = bf16[2,768,384]{2,1,0:T(8,128)(2,1)S(1)} collective-permute-done((bf16[2,768,384]{2,1,0:T(8,128)(2,1)}, bf16[2,768,384]{2,1,0:T(8,128)(2,1)S(1)}, u32[]{:S(2)}, u32[]{:S(2)}) %collective-permute-start.3) | collective-permute-done | bytes 1179680 | tf_op jit(solution)/shard_map/halo_reduction/ppermute | solution.py:23
  106.6 0.9 collective-permute-done.4
  107.5 0.0 copy-start.1
  107.5 2.5 %convert_add_fusion.1 = f32[2,768,384]{2,1,0:T(8,128)S(1)} fusion(bf16[2,768,384]{2,1,0:T(8,128)(2,1)} %collective-permute-done.4, f32[2,768,384]{2,1,0:T(8,128)} %get-tuple-element.32, bf16[2,768,384]{2,1,0:T(8,128)(2,1)S(1)} %collective-permute-done.3), kind=kLoop, calls=%fused_computation.6 | loop fusion | flops 2359296 | bytes 7077888 | tf_op jit(solution)/shard_map/halo_reduction/add | solution.py:256
  110.0 0.0 copy-start.2
  110.0 0.1 fusion.12
  110.1 1.3 collective-permute-start.5
  111.4 11.0 %collective-permute-done.6 = bf16[1536,384]{0,1:T(8,128)(2,1)} collective-permute-done((bf16[1536,384]{0,1:T(8,128)(2,1)}, bf16[1536,384]{0,1:T(8,128)(2,1)}, u32[]{:S(2)}, u32[]{:S(2)}) %collective-permute-start.6) | collective-permute-done | bytes 1179680 | tf_op jit(solution)/shard_map/grad_weight/ppermute | solution.py:28
  122.4 0.0 copy-done.1
  122.4 1.6 %convert_add_fusion = f32[1536,384]{0,1:T(8,128)S(1)} fusion(f32[1536,384]{0,1:T(8,128)S(1)} %copy-done.1, bf16[1536,384]{0,1:T(8,128)(2,1)} %collective-permute-done.6), kind=kLoop, calls=%fused_computation.5 | loop fusion | flops 1179648 | bytes 5898240 | tf_op jit(solution)/shard_map/grad_weight/add | solution.py:181
  124.0 0.0 copy-done.2
  124.0 0.0 copy-start.3
  124.0 1.1 dynamic-slice_convert_fusion.3
  125.2 0.6 copy-done.3
  125.8 1.6 %collective-permute-start.7 = (bf16[384,384]{0,1:T(8,128)(2,1)}, bf16[384,384]{0,1:T(8,128)(2,1)S(1)}, u32[]{:S(2)}, u32[]{:S(2)}) collective-permute-start(bf16[384,384]{0,1:T(8,128)(2,1)} %get-tuple-element.57), channel_id=1, source_target_pairs={{0,4},{4,8},{8,12},{12,0},{1,5},{5,9},{9,13},{13,1},{2,6},{6,10},{... | collective-permute-start | bytes 884744 | tf_op jit(solution)/shard_map/grad_weight/ppermute | solution.py:28
  127.3 0.0 collective-permute-start.9
  127.3 0.1 collective-permute-start.8
  127.4 7.0 %collective-permute-done.7 = bf16[384,384]{0,1:T(8,128)(2,1)S(1)} collective-permute-done((bf16[384,384]{0,1:T(8,128)(2,1)}, bf16[384,384]{0,1:T(8,128)(2,1)S(1)}, u32[]{:S(2)}, u32[]{:S(2)}) %collective-permute-start.7) | collective-permute-done | bytes 294944 | tf_op jit(solution)/shard_map/grad_weight/ppermute | solution.py:28
  134.5 0.0 copy-start.7
  134.5 2.4 %collective-permute-done.9 = bf16[384,384]{0,1:T(8,128)(2,1)S(1)} collective-permute-done((bf16[384,384]{0,1:T(8,128)(2,1)}, bf16[384,384]{0,1:T(8,128)(2,1)S(1)}, u32[]{:S(2)}, u32[]{:S(2)}) %collective-permute-start.9) | collective-permute-done | bytes 294944 | tf_op jit(solution)/shard_map/grad_weight/ppermute | solution.py:28
  136.9 0.0 copy-done.7
  136.9 0.7 copy-done.8
  137.6 3.1 %collective-permute-done.8 = bf16[384,384]{0,1:T(8,128)(2,1)} collective-permute-done((bf16[384,384]{0,1:T(8,128)(2,1)}, bf16[384,384]{0,1:T(8,128)(2,1)}, u32[]{:S(2)}, u32[]{:S(2)}) %collective-permute-start.8) | collective-permute-done | bytes 294944 | tf_op jit(solution)/shard_map/grad_weight/ppermute | solution.py:28
  140.7 1.5 convert_add_fusion.2
  142.1 1.1 copy.29
  143.2 0.0 collective-permute-done.5
  143.2 1.5 %fusion.10 = bf16[768,384]{1,0:T(8,128)(2,1)S(1)} fusion(f32[2,768,384]{2,1,0:T(8,128)} %copy-done.2, bf16[768,384]{1,0:T(8,128)(2,1)} %collective-permute-done.5), kind=kLoop, calls=%fused_computation.19 | loop fusion | flops 884736 | bytes 2359296 | tf_op jit(solution)/shard_map/convert.1
  144.7 0.9 slice_bitcast_fusion.1
  (6 shorter events, 0.0 us)
Async XLA Ops:
  7.2 51.7 %copy-start = (bf16[384,3072]{1,0:T(8,128)(2,1)S(1)}, bf16[384,3072]{1,0:T(8,128)(2,1)}, u32[]{:S(2)}) copy-start(bf16[384,3072]{1,0:T(8,128)(2,1)} %param.12) | copy-start | bytes 7077892
  7.2 55.5 %all-gather.3.cloned.1.call-start = ((), (), s32[]{:S(2)}) async-start(), calls=%async_computation.2 | async-start | bytes 2949120 | tf_op jit(solution)/shard_map/cotangent_gather/all_gather | solution.py:220
  7.9 137.7 %reduce-scatter.2.cloned.1.call-start = ((), (), s32[]{:S(2)}) async-start(), calls=%async_computation.1 | async-start | bytes 2949120 | tf_op jit(solution)/shard_map/output_projection/reduce_scatter | solution.py:227
  9.8 15.6 %collective-permute-start = (bf16[784,384]{1,0:T(8,128)(2,1)S(1)}, bf16[784,384]{1,0:T(8,128)(2,1)S(1)}, u32[]{:S(2)}, u32[]{:S(2)}) collective-permute-start(bf16[784,384]{1,0:T(8,128)(2,1)S(1)} %get-tuple-element.60), channel_id=1, source_target_pairs={{0,16},{16,0},{1,17},{17,1},{2,18},{18,2},{3,19},{19,3},{4,20},{20... | collective-permute-start | bytes 1806344 | tf_op jit(solution)/shard_map/halo_exchange/ppermute | solution.py:28
  25.4 0.8 copy-start.5
  27.5 19.1 %collective-permute-start.2 = (bf16[2,784,384]{2,1,0:T(8,128)(2,1)}, bf16[2,784,384]{2,1,0:T(8,128)(2,1)}, u32[]{:S(2)}, u32[]{:S(2)}) collective-permute-start(bf16[2,784,384]{2,1,0:T(8,128)(2,1)} %pad_maximum_fusion.km.vm), channel_id=1, source_target_pairs={{4,0},{8,4},{12,8},{5,1},{9,5},{13,9},{6,2},{10,6},{14,10},{7,3},{... | collective-permute-start | bytes 3612680 | tf_op jit(solution)/shard_map/halo_exchange/ppermute | solution.py:23
  30.5 17.0 %collective-permute-start.1 = (bf16[2,784,384]{2,1,0:T(8,128)(2,1)}, bf16[2,784,384]{2,1,0:T(8,128)(2,1)}, u32[]{:S(2)}, u32[]{:S(2)}) collective-permute-start(bf16[2,784,384]{2,1,0:T(8,128)(2,1)} %pad_maximum_fusion.km.vm), channel_id=1, source_target_pairs={{0,4},{4,8},{8,12},{1,5},{5,9},{9,13},{2,6},{6,10},{10,14},{3,7},{... | collective-permute-start | bytes 3612680 | tf_op jit(solution)/shard_map/halo_exchange/ppermute | solution.py:23
  62.7 1.0 copy-start.4
  67.9 2.5 %copy-start.6 = (bf16[1,1,384,3072]{3,2,1,0:T(8,128)(2,1)S(1)}, bf16[1,1,384,3072]{3,2,1,0:T(8,128)(2,1)}, u32[]{:S(2)}) copy-start(bf16[1,1,384,3072]{3,2,1,0:T(8,128)(2,1)} %all-gather.3.cloned.1.call-done) | copy-start | bytes 7077892
  87.7 18.9 %collective-permute-start.3 = (bf16[2,768,384]{2,1,0:T(8,128)(2,1)}, bf16[2,768,384]{2,1,0:T(8,128)(2,1)S(1)}, u32[]{:S(2)}, u32[]{:S(2)}) collective-permute-start(bf16[2,768,384]{2,1,0:T(8,128)(2,1)} %get-tuple-element.33), channel_id=1, source_target_pairs={{4,0},{8,4},{12,8},{5,1},{9,5},{13,9},{6,2},{10,6},{14,10},{7,3},{... | collective-permute-start | bytes 3538952 | tf_op jit(solution)/shard_map/halo_reduction/ppermute | solution.py:23
  89.6 17.9 %collective-permute-start.4 = (bf16[2,768,384]{2,1,0:T(8,128)(2,1)}, bf16[2,768,384]{2,1,0:T(8,128)(2,1)}, u32[]{:S(2)}, u32[]{:S(2)}) collective-permute-start(bf16[2,768,384]{2,1,0:T(8,128)(2,1)} %get-tuple-element.34), channel_id=1, source_target_pairs={{0,4},{4,8},{8,12},{1,5},{5,9},{9,13},{2,6},{6,10},{10,14},{3,7},{... | collective-permute-start | bytes 3538952 | tf_op jit(solution)/shard_map/halo_reduction/ppermute | solution.py:23
  94.1 28.3 %collective-permute-start.6 = (bf16[1536,384]{0,1:T(8,128)(2,1)}, bf16[1536,384]{0,1:T(8,128)(2,1)}, u32[]{:S(2)}, u32[]{:S(2)}) collective-permute-start(bf16[1536,384]{0,1:T(8,128)(2,1)} %fusion.8), channel_id=1, source_target_pairs={{0,16},{16,0},{1,17},{17,1},{2,18},{18,2},{3,19},{19,3},{4,20},{20... | collective-permute-start | bytes 3538952 | tf_op jit(solution)/shard_map/grad_weight/ppermute | solution.py:28
  107.5 14.9 %copy-start.1 = (f32[1536,384]{0,1:T(8,128)S(1)}, f32[1536,384]{0,1:T(8,128)}, u32[]{:S(2)}) copy-start(f32[1536,384]{0,1:T(8,128)} %dynamic-slice_bitcast_fusion) | copy-start | bytes 7077892
  110.0 14.0 %copy-start.2 = (f32[2,768,384]{2,1,0:T(8,128)}, f32[2,768,384]{2,1,0:T(8,128)S(1)}, u32[]{:S(2)}) copy-start(f32[2,768,384]{2,1,0:T(8,128)S(1)} %convert_add_fusion.1) | copy-start | bytes 7077892
  110.1 33.1 %collective-permute-start.5 = (bf16[768,384]{1,0:T(8,128)(2,1)S(1)}, bf16[768,384]{1,0:T(8,128)(2,1)}, u32[]{:S(2)}, u32[]{:S(2)}) collective-permute-start(bf16[768,384]{1,0:T(8,128)(2,1)S(1)} %fusion.12), channel_id=1, source_target_pairs={{0,16},{16,0},{1,17},{17,1},{2,18},{18,2},{3,19},{19,3},{4,20},{20... | collective-permute-start | bytes 1769480 | tf_op jit(solution)/shard_map/halo_reduction/ppermute | solution.py:28
  124.0 1.8 %copy-start.3 = (f32[1536,384]{0,1:T(8,128)}, f32[1536,384]{0,1:T(8,128)S(1)}, u32[]{:S(2)}) copy-start(f32[1536,384]{0,1:T(8,128)S(1)} %convert_add_fusion) | copy-start | bytes 7077892
  125.8 8.7 %collective-permute-start.7 = (bf16[384,384]{0,1:T(8,128)(2,1)}, bf16[384,384]{0,1:T(8,128)(2,1)S(1)}, u32[]{:S(2)}, u32[]{:S(2)}) collective-permute-start(bf16[384,384]{0,1:T(8,128)(2,1)} %get-tuple-element.57), channel_id=1, source_target_pairs={{0,4},{4,8},{8,12},{12,0},{1,5},{5,9},{9,13},{13,1},{2,6},{6,10},{... | collective-permute-start | bytes 884744 | tf_op jit(solution)/shard_map/grad_weight/ppermute | solution.py:28
  127.3 9.6 %collective-permute-start.9 = (bf16[384,384]{0,1:T(8,128)(2,1)}, bf16[384,384]{0,1:T(8,128)(2,1)S(1)}, u32[]{:S(2)}, u32[]{:S(2)}) collective-permute-start(bf16[384,384]{0,1:T(8,128)(2,1)} %get-tuple-element.58), channel_id=1, source_target_pairs={{0,12},{4,0},{8,4},{12,8},{1,13},{5,1},{9,5},{13,9},{2,14},{6,2},{... | collective-permute-start | bytes 884744 | tf_op jit(solution)/shard_map/grad_weight/ppermute | solution.py:28
  127.3 13.4 %collective-permute-start.8 = (bf16[384,384]{0,1:T(8,128)(2,1)}, bf16[384,384]{0,1:T(8,128)(2,1)}, u32[]{:S(2)}, u32[]{:S(2)}) collective-permute-start(bf16[384,384]{0,1:T(8,128)(2,1)} %get-tuple-element.59), channel_id=1, source_target_pairs={{0,8},{4,12},{8,0},{12,4},{1,9},{5,13},{9,1},{13,5},{2,10},{6,14},... | collective-permute-start | bytes 884744 | tf_op jit(solution)/shard_map/grad_weight/ppermute | solution.py:28
  134.5 2.4 %copy-start.7 = (bf16[384,384]{0,1:T(8,128)(2,1)}, bf16[384,384]{0,1:T(8,128)(2,1)S(1)}, u32[]{:S(2)}) copy-start(bf16[384,384]{0,1:T(8,128)(2,1)S(1)} %collective-permute-done.7) | copy-start | bytes 884740
  136.9 0.7 copy-start.8
Sparse Core Ops, SparseCore 0:
  9.6 52.5 all-gather.2
  65.0 47.6 reduce-scatter.1

commit v11 on v10

--- a/solution.py
+++ b/solution.py
@@ -21,6 +21,11 @@
 
 def shifted(value, axis, steps):
     return lax.ppermute(value, axis, shift_pairs(lax.axis_size(axis), steps))
+
+
+def partner(value, axis, bit):
+    count = lax.axis_size(axis)
+    return lax.ppermute(value, axis, [(i, i ^ bit) for i in range(count)])
 
 
 def cyclic(value, axis, steps):
@@ -233,15 +238,32 @@
             cot_all, out_weight, (((1,), (1,)), ((), ())), preferred_element_type=jnp.float32
         ).astype(jnp.bfloat16)
 
+    halving = lax.axis_size("fh") == 2 and lax.axis_size("wa") == 4
     with jax.named_scope("grad_weight"):
-        weight_part = lax.dot_general(
-            cot_all, attended, (((0,), (0,)), ((), ())), preferred_element_type=jnp.float32
-        )
-        weight_own, weight_sent = scatter_parts(weight_part, "fh", 0)
-        weight_own, weight_sent, grad_attended = lax.optimization_barrier(
-            (weight_own, weight_sent, grad_attended)
-        )
-        weight_rows = scatter_finish(weight_own, weight_sent, "fh")
+        if halving:
+            rows = model_width // 8
+            cot_blocks = cot_all.reshape(-1, 2, 2, 2, rows)
+            weight_blocks = lax.dot_general(
+                cot_blocks, attended, (((0,), (0,)), ((), ())), preferred_element_type=jnp.float32
+            )
+            weight_blocks = jnp.transpose(weight_blocks, (2, 1, 0, 3, 4))
+            core = lax.axis_index("wa") % 2
+            weight_own = lax.dynamic_index_in_dim(weight_blocks, core, 0, keepdims=False)
+            weight_sent = lax.dynamic_index_in_dim(weight_blocks, 1 - core, 0, keepdims=False)
+            weight_sent = weight_sent.astype(jnp.bfloat16)
+            weight_own, weight_sent, grad_attended = lax.optimization_barrier(
+                (weight_own, weight_sent, grad_attended)
+            )
+            weight_x = weight_own + partner(weight_sent, "wa", 1).astype(jnp.float32)
+        else:
+            weight_part = lax.dot_general(
+                cot_all, attended, (((0,), (0,)), ((), ())), preferred_element_type=jnp.float32
+            )
+            weight_own, weight_sent = scatter_parts(weight_part, "fh", 0)
+            weight_own, weight_sent, grad_attended = lax.optimization_barrier(
+                (weight_own, weight_sent, grad_attended)
+            )
+            weight_rows = scatter_finish(weight_own, weight_sent, "fh")
 
     with jax.named_scope("attention_backward"):
         grad_q, left, partials, right = attention_backward(
@@ -249,7 +271,17 @@
         )
 
     with jax.named_scope("grad_weight"):
-        grad_weight = scatter_sum(weight_rows, "wa", 0)
+        if halving:
+            column = lax.axis_index("wa") // 2
+            kept = lax.dynamic_index_in_dim(weight_x, column, 0, keepdims=False)
+            sent = lax.dynamic_index_in_dim(weight_x, 1 - column, 0, keepdims=False)
+            weight_f = kept + partner(sent.astype(jnp.bfloat16), "wa", 2).astype(jnp.float32)
+            row = lax.axis_index("fh")
+            kept = lax.dynamic_index_in_dim(weight_f, row, 0, keepdims=False)
+            sent = lax.dynamic_index_in_dim(weight_f, 1 - row, 0, keepdims=False)
+            grad_weight = kept + partner(sent.astype(jnp.bfloat16), "fh", 1).astype(jnp.float32)
+        else:
+            grad_weight = scatter_sum(weight_rows, "wa", 0)
 
     with jax.named_scope("halo_reduction"):
         middle = (

time: 154 us -> 145 us (0.942)
  waiting for transfers between devices: 62 us -> 52.7 us
  local copies, waits for them, and re-layouts: 12 us -> 15.4 us
  starting transfers between devices: 19.1 us -> 17.4 us
    ppermute x6 -> x2, waiting for transfers between devices: 36.9 us -> 18 us  [cyclic(): lax.ppermute(value, axis, [(i, (i + steps) % count) for i in range(count)])]
    ppermute x0 -> x3, waiting for transfers between devices: none -> 5.34 us  [partner(): return lax.ppermute(value, axis, [(i, i ^ bit) for i in range(count)])]
    all_gather x0 -> x1, local copies, waits for them, and re-layouts: none -> 4.33 us  [body(): cot_all = lax.all_gather(out_cotangent[0, 0], 'ha', axis=0, tiled=True)]
    ppermute x4, waiting for transfers between devices: 24.4 us -> 28.7 us  [shifted(): return lax.ppermute(value, axis, shift_pairs(lax.axis_size(axis), steps))]
    ppermute x6 -> x2, starting transfers between devices: 6.44 us -> 3.45 us  [cyclic(): lax.ppermute(value, axis, [(i, (i + steps) % count) for i in range(count)])]
    dynamic_slice x1 -> x0, local copies, waits for them, and re-layouts: 1.65 us -> none  [part(): return lax.dynamic_slice_in_dim(full, index * size, size, axis=dim)]
    squeeze x0 -> x1, local copies, waits for them, and re-layouts: none -> 1.58 us  [body(): lax.dynamic_index_in_dim(weight_blocks, core, 0, keepdims=False)]
    add x2 -> x3, other arithmetic: 3.06 us -> 3.94 us  [the longest x1 2.33 us: body(): weight_x = weight_own + partner(weight_sent, 'wa', 1).astype(jnp.float32)]
  transfers between devices with their start and end apart: 12 -> 11, of which waited for: 9 -> 8; matrix products, arithmetic and copies ran while one was open for 18% -> 21% of each run, Pallas kernels for 17% -> 18%
where the time goes in v11:
time: 145 us; the launch traced here: 144 us
  waiting for transfers between devices  52.7 us (36%)
  Pallas kernels  25.3 us (17%)
  starting transfers between devices  17.4 us (12%)
  local copies, waits for them, and re-layouts  15.4 us (11%)
  between operations  14.2 us (10%)
  other arithmetic  9.49 us (7%)
  matrix products  9 us (6%)
    ppermute x4, waiting for transfers between devices, shifted(): return lax.ppermute(value, axis, shift_pairs(lax.axis_size(axis), steps))  28.7 us
    ppermute x2, waiting for transfers between devices, cyclic(): lax.ppermute(value, axis, [(i, (i + steps) % count) for i in range(count)])  18 us
    pallas_call x1, Pallas kernels, attention_backward(): pl.pallas_call(functools.partial(backward_kernel, scale, scale * LOG2E),...  15.2 us
    ppermute x4, starting transfers between devices, shifted(): return lax.ppermute(value, axis, shift_pairs(lax.axis_size(axis), steps))  12.5 us
    pallas_call x1, Pallas kernels, attention_forward(): pl.pallas_call(functools.partial(forward_kernel, scale * LOG2E), grid=(he...  10.1 us
    ppermute x3, waiting for transfers between devices, partner(): return lax.ppermute(value, axis, [(i, i ^ bit) for i in range(count)])  5.34 us
    unnamed x21, local copies, waits for them, and re-layouts  4.93 us
    all_gather x1, local copies, waits for them, and re-layouts, body(): cot_all = lax.all_gather(out_cotangent[0, 0], 'ha', axis=0, tiled=True)  4.33 us
  transfers between devices with their start and end apart: 11, of which 8 were waited for; matrix products, arithmetic and copies ran while one was open for 21% of the time, Pallas kernels for 18%

profile of v11, /device:TPU:1, one launch (start us, length us, event | category | flops | bytes accessed | tf_op | source)
XLA Modules:
  0.0 143.5 jit_solution(2906909228223402456)
XLA Ops:
  7.2 0.0 copy-start
  7.2 0.0 all-gather.3.cloned.1.call-start
  7.2 0.7 all-gather.3.cloned.1.call-update
  7.9 0.0 reduce-scatter.2.cloned.1.call-start
  8.0 0.7 convert_bitcast_fusion
  8.6 1.2 fusion.9
  9.8 2.1 %collective-permute-start = (bf16[784,384]{1,0:T(8,128)(2,1)S(1)}, bf16[784,384]{1,0:T(8,128)(2,1)S(1)}, u32[]{:S(2)}, u32[]{:S(2)}) collective-permute-start(bf16[784,384]{1,0:T(8,128)(2,1)S(1)} %get-tuple-element.62), channel_id=1, source_target_pairs={{0,16},{16,0},{1,17},{17,1},{2,18},{18,2},{3,19},{19,3},{4,20},{20... | collective-permute-start | bytes 1806344 | tf_op jit(solution)/shard_map/halo_exchange/ppermute | solution.py:33
  11.9 13.4 %collective-permute-done = bf16[784,384]{1,0:T(8,128)(2,1)S(1)} collective-permute-done((bf16[784,384]{1,0:T(8,128)(2,1)S(1)}, bf16[784,384]{1,0:T(8,128)(2,1)S(1)}, u32[]{:S(2)}, u32[]{:S(2)}) %collective-permute-start) | collective-permute-done | bytes 602144 | tf_op jit(solution)/shard_map/halo_exchange/ppermute | solution.py:33
  25.4 0.0 copy-start.5
  25.4 0.8 copy-done.5
  26.2 1.2 pad_maximum_fusion.km.vm
  27.4 3.0 %collective-permute-start.2 = (bf16[2,784,384]{2,1,0:T(8,128)(2,1)}, bf16[2,784,384]{2,1,0:T(8,128)(2,1)}, u32[]{:S(2)}, u32[]{:S(2)}) collective-permute-start(bf16[2,784,384]{2,1,0:T(8,128)(2,1)} %pad_maximum_fusion.km.vm), channel_id=1, source_target_pairs={{4,0},{8,4},{12,8},{5,1},{9,5},{13,9},{6,2},{10,6},{14,10},{7,3},{... | collective-permute-start | bytes 3612680 | tf_op jit(solution)/shard_map/halo_exchange/ppermute | solution.py:23
  30.5 3.2 %collective-permute-start.1 = (bf16[2,784,384]{2,1,0:T(8,128)(2,1)}, bf16[2,784,384]{2,1,0:T(8,128)(2,1)}, u32[]{:S(2)}, u32[]{:S(2)}) collective-permute-start(bf16[2,784,384]{2,1,0:T(8,128)(2,1)} %pad_maximum_fusion.km.vm), channel_id=1, source_target_pairs={{0,4},{4,8},{8,12},{1,5},{5,9},{9,13},{2,6},{6,10},{10,14},{3,7},{... | collective-permute-start | bytes 3612680 | tf_op jit(solution)/shard_map/halo_exchange/ppermute | solution.py:23
  33.7 0.7 fusion.15
  34.4 12.1 %collective-permute-done.2.kr.vr = bf16[2,784,384]{2,1,0:T(8,128)(2,1)} collective-permute-done((bf16[2,784,384]{2,1,0:T(8,128)(2,1)}, bf16[2,784,384]{2,1,0:T(8,128)(2,1)}, u32[]{:S(2)}, u32[]{:S(2)}) %collective-permute-start.2) | collective-permute-done | bytes 1204256 | tf_op jit(solution)/shard_map/halo_exchange/ppermute | solution.py:23
  46.5 0.7 slice.47
  47.2 0.2 collective-permute-done.1.kl.vl
  47.4 0.7 slice.44
  48.1 0.6 copy.50
  48.8 10.1 %tile_attention_forward.1 = (bf16[384,384]{1,0:T(8,128)(2,1)}, f32[384,384]{1,0:T(8,128)}, f32[384,384]{1,0:T(8,128)}) custom-call(f32[1,2304]{1,0:T(1,128)} %bitcast.75, bf16[384,384]{1,0:T(8,128)(2,1)} %bitcast.71, bf16[2,784,384]{2,1,0:T(8,128)(2,1)} %collective-permute-done.1.kl.vl, bf16[2,784,384]{2,1,0:T(8,128)(2,1)} %pad_maximum_fusion.km.vm, ...), custom_call_target="tpu_custom_call" | custom-call | tf_op jit(solution)/shard_map/attention_forward/tile_attention_forward/pallas_call | solution.py:107
  58.9 0.0 copy-done
  58.9 3.8 %convolution_convert_fusion = bf16[384,3072]{1,0:T(8,128)(2,1)} fusion(bf16[384,384]{1,0:T(8,128)(2,1)} %get-tuple-element.27.o_ref, bf16[384,3072]{1,0:T(8,128)(2,1)S(1)} %copy-done), kind=kOutput, calls=%fused_computation | convolution fusion | flops 907149312 | bytes 5013504 | tf_op jit(solution)/shard_map/output_projection/dot_general | solution.py:231
  62.7 0.0 reduce-scatter.2.cloned.1.call-update
  62.7 0.0 copy-start.4
  62.7 0.0 all-gather.3.cloned.1.call-done
  62.7 4.3 %copy.40 = bf16[1,1,384,3072]{2,3,1,0:T(8,128)(2,1)} copy(bf16[1,1,384,3072]{3,2,1,0:T(8,128)(2,1)} %all-gather.3.cloned.1.call-done) | data formatting | bytes 4718592 | tf_op jit(solution)/shard_map/cotangent_gather/all_gather | solution.py:225
  67.1 0.0 copy-done.4
  67.1 3.1 %fusion.13 = f32[384,2,2,2,384]{4,0,3,2,1:T(8,128)S(1)} fusion(bf16[384,2,2,2,384]{0,4,3,2,1:T(8,128)(2,1)} %bitcast.68, bf16[384,384]{1,0:T(8,128)(2,1)S(1)} %copy-done.4), kind=kOutput, calls=%fused_computation.28 | convolution fusion | flops 905969664 | bytes 7372800 | tf_op jit(solution)/shard_map/grad_weight/dot_general | solution.py:246
  70.2 1.1 fusion.6
  71.3 0.0 copy-start.7
  71.3 1.6 %dynamic-slice_bitcast_fusion = f32[2,2,384,384]{2,3,0,1:T(8,128)} fusion(f32[384,2,2,2,384]{4,0,3,2,1:T(8,128)S(1)} %fusion.13, s32[]{:T(128)S(6)} %select_n.41), kind=kLoop, calls=%fused_computation.6 | loop fusion | bytes 4718596 | tf_op jit(solution)/shard_map/grad_weight/jit(dynamic_index_in_dim)/squeeze | solution.py:251
  72.9 1.0 copy-done.7
  73.8 2.1 %fusion.2.do_ref = bf16[384,384]{1,0:T(8,128)(2,1)} fusion(bf16[384,3072]{1,0:T(8,128)(2,1)S(1)} %copy-done, bf16[1,1,384,3072]{3,2,1,0:T(8,128)(2,1)S(1)} %copy-done.7), kind=kOutput, calls=%fused_computation.10 | convolution fusion | flops 906117120 | bytes 5013504 | tf_op jit(solution)/shard_map/grad_attended/dot_general | solution.py:237
  76.0 0.1 collective-permute-start.6
  76.1 15.2 %tile_attention_backward.1 = (bf16[384,384]{1,0:T(8,128)(2,1)}, bf16[2,768,384]{2,1,0:T(8,128)(2,1)}, f32[2,768,384]{2,1,0:T(8,128)}, bf16[2,768,384]{2,1,0:T(8,128)(2,1)}) custom-call(f32[1,2304]{1,0:T(1,128)} %bitcast.76, bf16[384,384]{1,0:T(8,128)(2,1)} %bitcast.72, bf16[2,784,384]{2,1,0:T(8,128)(2,1)} %collective-permute-done.1.kl.vl, ...), custom_call_target="tpu_custom_call" | custom-call | tf_op jit(solution)/shard_map/attention_backward/tile_attention_backward/pallas_call | solution.py:133
  91.3 2.3 %collective-permute-start.3 = (bf16[2,768,384]{2,1,0:T(8,128)(2,1)}, bf16[2,768,384]{2,1,0:T(8,128)(2,1)S(1)}, u32[]{:S(2)}, u32[]{:S(2)}) collective-permute-start(bf16[2,768,384]{2,1,0:T(8,128)(2,1)} %get-tuple-element.33), channel_id=1, source_target_pairs={{4,0},{8,4},{12,8},{5,1},{9,5},{13,9},{6,2},{10,6},{14,10},{7,3},{... | collective-permute-start | bytes 3538952 | tf_op jit(solution)/shard_map/halo_reduction/ppermute | solution.py:23
  93.6 3.9 %collective-permute-start.4 = (bf16[2,768,384]{2,1,0:T(8,128)(2,1)}, bf16[2,768,384]{2,1,0:T(8,128)(2,1)}, u32[]{:S(2)}, u32[]{:S(2)}) collective-permute-start(bf16[2,768,384]{2,1,0:T(8,128)(2,1)} %get-tuple-element.34), channel_id=1, source_target_pairs={{0,4},{4,8},{8,12},{1,5},{5,9},{9,13},{2,6},{6,10},{10,14},{3,7},{... | collective-permute-start | bytes 3538952 | tf_op jit(solution)/shard_map/halo_reduction/ppermute | solution.py:23
  97.5 0.0 copy-start.6
  97.5 0.0 collective-permute-done.6
  97.6 2.3 %convert_add_fusion = f32[2,2,384,384]{2,3,0,1:T(8,128)S(1)} fusion(f32[2,2,384,384]{2,3,0,1:T(8,128)} %dynamic-slice_bitcast_fusion, bf16[2,2,384,384]{2,3,0,1:T(8,128)(2,1)} %collective-permute-done.6), kind=kLoop, calls=%fused_computation.3 | loop fusion | flops 1179648 | bytes 5898240 | tf_op jit(solution)/shard_map/grad_weight/add | solution.py:257
  99.9 0.0 copy-start.3
  99.9 1.0 fusion.10
  100.9 0.0 collective-permute-start.7
  100.9 14.9 %collective-permute-done.3 = bf16[2,768,384]{2,1,0:T(8,128)(2,1)S(1)} collective-permute-done((bf16[2,768,384]{2,1,0:T(8,128)(2,1)}, bf16[2,768,384]{2,1,0:T(8,128)(2,1)S(1)}, u32[]{:S(2)}, u32[]{:S(2)}) %collective-permute-start.3) | collective-permute-done | bytes 1179680 | tf_op jit(solution)/shard_map/halo_reduction/ppermute | solution.py:23
  115.8 1.5 %collective-permute-done.4 = bf16[2,768,384]{2,1,0:T(8,128)(2,1)} collective-permute-done((bf16[2,768,384]{2,1,0:T(8,128)(2,1)}, bf16[2,768,384]{2,1,0:T(8,128)(2,1)}, u32[]{:S(2)}, u32[]{:S(2)}) %collective-permute-start.4) | collective-permute-done | bytes 1179680 | tf_op jit(solution)/shard_map/halo_reduction/ppermute | solution.py:23
  117.3 0.0 copy-done.3
  117.3 0.0 copy-done.6
  117.3 1.7 %convert_add_fusion.1 = f32[2,768,384]{2,1,0:T(8,128)S(1)} fusion(bf16[2,768,384]{2,1,0:T(8,128)(2,1)} %collective-permute-done.4, f32[2,768,384]{2,1,0:T(8,128)S(1)} %copy-done.6, bf16[2,768,384]{2,1,0:T(8,128)(2,1)S(1)} %collective-permute-done.3), kind=kLoop, calls=%fused_computation.4 | loop fusion | flops 2359296 | bytes 7077888 | tf_op jit(solution)/shard_map/halo_reduction/add | solution.py:288
  118.9 0.0 copy-start.1
  119.0 1.4 copy-done.1
  120.4 0.1 fusion.11
  120.4 1.3 collective-permute-start.5
  121.8 0.0 copy-start.2
  121.8 1.8 %collective-permute-done.7 = bf16[2,384,384]{1,2,0:T(8,128)(2,1)} collective-permute-done((bf16[2,384,384]{1,2,0:T(8,128)(2,1)}, bf16[2,384,384]{1,2,0:T(8,128)(2,1)}, u32[]{:S(2)}, u32[]{:S(2)}) %collective-permute-start.7) | collective-permute-done | bytes 589856 | tf_op jit(solution)/shard_map/grad_weight/ppermute | solution.py:28
  123.6 1.6 %bitcast_add_fusion = f32[2,384,384]{1,2,0:T(8,128)S(1)} fusion(bf16[2,384,384]{1,2,0:T(8,128)(2,1)} %collective-permute-done.7, f32[2,2,384,384]{2,3,0,1:T(8,128)} %copy-done.3, s32[]{:T(128)S(6)} %select_n.44), kind=kLoop, calls=%fused_computation.18 | loop fusion | flops 589824 | bytes 2949124 | tf_op jit(solution)/shard_map/grad_weight/add | solution.py:278
  125.2 1.3 collective-permute-start.8
  126.5 4.5 %collective-permute-done.5 = bf16[768,384]{1,0:T(8,128)(2,1)S(1)} collective-permute-done((bf16[768,384]{1,0:T(8,128)(2,1)S(1)}, bf16[768,384]{1,0:T(8,128)(2,1)S(1)}, u32[]{:S(2)}, u32[]{:S(2)}) %collective-permute-start.5) | collective-permute-done | bytes 589856 | tf_op jit(solution)/shard_map/halo_reduction/ppermute | solution.py:33
  131.1 0.0 copy-done.2
  131.1 0.1 fusion.8
  131.2 0.9 slice_bitcast_fusion.1
  132.1 3.5 %collective-permute-done.8 = bf16[384,384]{0,1:T(8,128)(2,1)S(1)} collective-permute-done((bf16[384,384]{0,1:T(8,128)(2,1)S(1)}, bf16[384,384]{0,1:T(8,128)(2,1)S(1)}, u32[]{:S(2)}, u32[]{:S(2)}) %collective-permute-start.8) | collective-permute-done | bytes 294944 | tf_op jit(solution)/shard_map/grad_weight/ppermute | solution.py:28
  135.6 0.1 bitcast_add_fusion.1
  135.6 1.1 copy.43
  136.7 0.0 reduce-scatter.2.cloned.1.call-done
  (5 shorter events, 0.1 us)
Async XLA Ops:
  7.2 51.7 %copy-start = (bf16[384,3072]{1,0:T(8,128)(2,1)S(1)}, bf16[384,3072]{1,0:T(8,128)(2,1)}, u32[]{:S(2)}) copy-start(bf16[384,3072]{1,0:T(8,128)(2,1)} %param.12) | copy-start | bytes 7077892
  7.2 55.5 %all-gather.3.cloned.1.call-start = ((), (), s32[]{:S(2)}) async-start(), calls=%async_computation.2 | async-start | bytes 2949120 | tf_op jit(solution)/shard_map/cotangent_gather/all_gather | solution.py:225
  7.9 128.8 %reduce-scatter.2.cloned.1.call-start = ((), (), s32[]{:S(2)}) async-start(), calls=%async_computation.1 | async-start | bytes 2949120 | tf_op jit(solution)/shard_map/output_projection/reduce_scatter | solution.py:232
  9.8 15.6 %collective-permute-start = (bf16[784,384]{1,0:T(8,128)(2,1)S(1)}, bf16[784,384]{1,0:T(8,128)(2,1)S(1)}, u32[]{:S(2)}, u32[]{:S(2)}) collective-permute-start(bf16[784,384]{1,0:T(8,128)(2,1)S(1)} %get-tuple-element.62), channel_id=1, source_target_pairs={{0,16},{16,0},{1,17},{17,1},{2,18},{18,2},{3,19},{19,3},{4,20},{20... | collective-permute-start | bytes 1806344 | tf_op jit(solution)/shard_map/halo_exchange/ppermute | solution.py:33
  25.4 0.8 copy-start.5
  27.4 19.1 %collective-permute-start.2 = (bf16[2,784,384]{2,1,0:T(8,128)(2,1)}, bf16[2,784,384]{2,1,0:T(8,128)(2,1)}, u32[]{:S(2)}, u32[]{:S(2)}) collective-permute-start(bf16[2,784,384]{2,1,0:T(8,128)(2,1)} %pad_maximum_fusion.km.vm), channel_id=1, source_target_pairs={{4,0},{8,4},{12,8},{5,1},{9,5},{13,9},{6,2},{10,6},{14,10},{7,3},{... | collective-permute-start | bytes 3612680 | tf_op jit(solution)/shard_map/halo_exchange/ppermute | solution.py:23
  30.5 17.0 %collective-permute-start.1 = (bf16[2,784,384]{2,1,0:T(8,128)(2,1)}, bf16[2,784,384]{2,1,0:T(8,128)(2,1)}, u32[]{:S(2)}, u32[]{:S(2)}) collective-permute-start(bf16[2,784,384]{2,1,0:T(8,128)(2,1)} %pad_maximum_fusion.km.vm), channel_id=1, source_target_pairs={{0,4},{4,8},{8,12},{1,5},{5,9},{9,13},{2,6},{6,10},{10,14},{3,7},{... | collective-permute-start | bytes 3612680 | tf_op jit(solution)/shard_map/halo_exchange/ppermute | solution.py:23
  62.7 4.4 %copy-start.4 = (bf16[384,384]{1,0:T(8,128)(2,1)S(1)}, bf16[384,384]{1,0:T(8,128)(2,1)}, u32[]{:S(2)}) copy-start(bf16[384,384]{1,0:T(8,128)(2,1)} %get-tuple-element.27.o_ref) | copy-start | bytes 884740
  71.3 2.5 %copy-start.7 = (bf16[1,1,384,3072]{3,2,1,0:T(8,128)(2,1)S(1)}, bf16[1,1,384,3072]{3,2,1,0:T(8,128)(2,1)}, u32[]{:S(2)}) copy-start(bf16[1,1,384,3072]{3,2,1,0:T(8,128)(2,1)} %all-gather.3.cloned.1.call-done) | copy-start | bytes 7077892
  76.0 21.6 %collective-permute-start.6 = (bf16[2,2,384,384]{2,3,0,1:T(8,128)(2,1)}, bf16[2,2,384,384]{2,3,0,1:T(8,128)(2,1)}, u32[]{:S(2)}, u32[]{:S(2)}) collective-permute-start(bf16[2,2,384,384]{2,3,0,1:T(8,128)(2,1)} %fusion.6), channel_id=1, source_target_pairs={{0,4},{4,0},{8,12},{12,8},{1,5},{5,1},{9,13},{13,9},{2,6},{6,2},{1... | collective-permute-start | bytes 3538952 | tf_op jit(solution)/shard_map/grad_weight/ppermute | solution.py:28
  91.3 24.5 %collective-permute-start.3 = (bf16[2,768,384]{2,1,0:T(8,128)(2,1)}, bf16[2,768,384]{2,1,0:T(8,128)(2,1)S(1)}, u32[]{:S(2)}, u32[]{:S(2)}) collective-permute-start(bf16[2,768,384]{2,1,0:T(8,128)(2,1)} %get-tuple-element.33), channel_id=1, source_target_pairs={{4,0},{8,4},{12,8},{5,1},{9,5},{13,9},{6,2},{10,6},{14,10},{7,3},{... | collective-permute-start | bytes 3538952 | tf_op jit(solution)/shard_map/halo_reduction/ppermute | solution.py:23
  93.6 23.7 %collective-permute-start.4 = (bf16[2,768,384]{2,1,0:T(8,128)(2,1)}, bf16[2,768,384]{2,1,0:T(8,128)(2,1)}, u32[]{:S(2)}, u32[]{:S(2)}) collective-permute-start(bf16[2,768,384]{2,1,0:T(8,128)(2,1)} %get-tuple-element.34), channel_id=1, source_target_pairs={{0,4},{4,8},{8,12},{1,5},{5,9},{9,13},{2,6},{6,10},{10,14},{3,7},{... | collective-permute-start | bytes 3538952 | tf_op jit(solution)/shard_map/halo_reduction/ppermute | solution.py:23
  97.5 19.7 %copy-start.6 = (f32[2,768,384]{2,1,0:T(8,128)S(1)}, f32[2,768,384]{2,1,0:T(8,128)}, u32[]{:S(2)}) copy-start(f32[2,768,384]{2,1,0:T(8,128)} %get-tuple-element.32) | copy-start | bytes 7077892
  99.9 17.4 %copy-start.3 = (f32[2,2,384,384]{2,3,0,1:T(8,128)}, f32[2,2,384,384]{2,3,0,1:T(8,128)S(1)}, u32[]{:S(2)}) copy-start(f32[2,2,384,384]{2,3,0,1:T(8,128)S(1)} %convert_add_fusion) | copy-start | bytes 7077892
  100.9 22.7 %collective-permute-start.7 = (bf16[2,384,384]{1,2,0:T(8,128)(2,1)}, bf16[2,384,384]{1,2,0:T(8,128)(2,1)}, u32[]{:S(2)}, u32[]{:S(2)}) collective-permute-start(bf16[2,384,384]{1,2,0:T(8,128)(2,1)} %fusion.10), channel_id=1, source_target_pairs={{0,8},{4,12},{8,0},{12,4},{1,9},{5,13},{9,1},{13,5},{2,10},{6,14},... | collective-permute-start | bytes 1769480 | tf_op jit(solution)/shard_map/grad_weight/ppermute | solution.py:28
  118.9 1.4 copy-start.1
  120.4 10.6 %collective-permute-start.5 = (bf16[768,384]{1,0:T(8,128)(2,1)S(1)}, bf16[768,384]{1,0:T(8,128)(2,1)S(1)}, u32[]{:S(2)}, u32[]{:S(2)}) collective-permute-start(bf16[768,384]{1,0:T(8,128)(2,1)S(1)} %fusion.11), channel_id=1, source_target_pairs={{0,16},{16,0},{1,17},{17,1},{2,18},{18,2},{3,19},{19,3},{4,20},{20... | collective-permute-start | bytes 1769480 | tf_op jit(solution)/shard_map/halo_reduction/ppermute | solution.py:33
  121.8 9.3 %copy-start.2 = (f32[2,768,384]{2,1,0:T(8,128)S(1)}, f32[2,768,384]{2,1,0:T(8,128)}, u32[]{:S(2)}) copy-start(f32[2,768,384]{2,1,0:T(8,128)} %copy-done.1) | copy-start | bytes 7077892
  125.2 10.4 %collective-permute-start.8 = (bf16[384,384]{0,1:T(8,128)(2,1)S(1)}, bf16[384,384]{0,1:T(8,128)(2,1)S(1)}, u32[]{:S(2)}, u32[]{:S(2)}) collective-permute-start(bf16[384,384]{0,1:T(8,128)(2,1)S(1)} %fusion.12), channel_id=1, source_target_pairs={{0,16},{16,0},{1,17},{17,1},{2,18},{18,2},{3,19},{19,3},{4,20},{20... | collective-permute-start | bytes 884744 | tf_op jit(solution)/shard_map/grad_weight/ppermute | solution.py:28
Sparse Core Ops, SparseCore 0:
  9.6 52.5 all-gather.2
  65.0 47.6 reduce-scatter.1

commit v12 on v11

--- a/solution.py
+++ b/solution.py
@@ -242,19 +242,22 @@
     with jax.named_scope("grad_weight"):
         if halving:
             rows = model_width // 8
-            cot_blocks = cot_all.reshape(-1, 2, 2, 2, rows)
+            cot_blocks = jnp.transpose(cot_all.reshape(-1, 2, 2, 2, rows), (0, 3, 2, 1, 4))
             weight_blocks = lax.dot_general(
                 cot_blocks, attended, (((0,), (0,)), ((), ())), preferred_element_type=jnp.float32
             )
-            weight_blocks = jnp.transpose(weight_blocks, (2, 1, 0, 3, 4))
             core = lax.axis_index("wa") % 2
             weight_own = lax.dynamic_index_in_dim(weight_blocks, core, 0, keepdims=False)
             weight_sent = lax.dynamic_index_in_dim(weight_blocks, 1 - core, 0, keepdims=False)
             weight_sent = weight_sent.astype(jnp.bfloat16)
-            weight_own, weight_sent, grad_attended = lax.optimization_barrier(
-                (weight_own, weight_sent, grad_attended)
-            )
             weight_x = weight_own + partner(weight_sent, "wa", 1).astype(jnp.float32)
+            column = lax.axis_index("wa") // 2
+            kept = lax.dynamic_index_in_dim(weight_x, column, 0, keepdims=False)
+            sent = lax.dynamic_index_in_dim(weight_x, 1 - column, 0, keepdims=False)
+            kept, sent, grad_attended = lax.optimization_barrier(
+                (kept, sent.astype(jnp.bfloat16), grad_attended)
+            )
+            weight_f = kept + partner(sent, "wa", 2).astype(jnp.float32)
         else:
             weight_part = lax.dot_general(
                 cot_all, attended, (((0,), (0,)), ((), ())), preferred_element_type=jnp.float32
@@ -272,10 +275,6 @@
 
     with jax.named_scope("grad_weight"):
         if halving:
-            column = lax.axis_index("wa") // 2
-            kept = lax.dynamic_index_in_dim(weight_x, column, 0, keepdims=False)
-            sent = lax.dynamic_index_in_dim(weight_x, 1 - column, 0, keepdims=False)
-            weight_f = kept + partner(sent.astype(jnp.bfloat16), "wa", 2).astype(jnp.float32)
             row = lax.axis_index("fh")
             kept = lax.dynamic_index_in_dim(weight_f, row, 0, keepdims=False)
             sent = lax.dynamic_index_in_dim(weight_f, 1 - row, 0, keepdims=False)

time: 145 us -> 174 us (1.20)
  waiting for transfers between devices: 52.7 us -> 75.8 us
  local copies, waits for them, and re-layouts: 15.4 us -> 19.3 us
  other arithmetic: 9.49 us -> 11.9 us
    ppermute x3, waiting for transfers between devices: 5.34 us -> 46.1 us  [partner(): return lax.ppermute(value, axis, [(i, i ^ bit) for i in range(count)])]
    ppermute x4, waiting for transfers between devices: 28.7 us -> 12.3 us  [shifted(): return lax.ppermute(value, axis, shift_pairs(lax.axis_size(axis), steps))]
    ppermute x2, waiting for transfers between devices: 18 us -> 13.4 us  [cyclic(): lax.ppermute(value, axis, [(i, (i + steps) % count) for i in range(count)])]
    reshape x0 -> x1, local copies, waits for them, and re-layouts: none -> 4.36 us  [body(): cot_all.reshape(-1, 2, 2, 2, rows)]
    all_gather x1, waiting for transfers between devices: 0.02 us -> 3.3 us  [body(): cot_all = lax.all_gather(out_cotangent[0, 0], 'ha', axis=0, tiled=True)]
    dot_general x1, matrix products: 2.12 us -> 3.93 us  [body(): lax.dot_general(cot_all, out_weight, (((1,), (1,)), ((), ())), preferred_...]
  transfers between devices with their start and end apart: 11 -> 11, of which waited for: 8 -> 6; matrix products, arithmetic and copies ran while one was open for 21% -> 14% of each run, Pallas kernels for 18% -> 15%
where the time goes in v12:
time: 174 us; the launch traced here: 173 us
  waiting for transfers between devices  75.8 us (44%)
  Pallas kernels  25.3 us (15%)
  local copies, waits for them, and re-layouts  19.3 us (11%)
  starting transfers between devices  16.4 us (9%)
  between operations  14.3 us (8%)
  other arithmetic  11.9 us (7%)
  matrix products  9.83 us (6%)
    ppermute x3, waiting for transfers between devices, partner(): return lax.ppermute(value, axis, [(i, i ^ bit) for i in range(count)])  46.1 us
    pallas_call x1, Pallas kernels, attention_backward(): pl.pallas_call(functools.partial(backward_kernel, scale, scale * LOG2E),...  15.2 us
    ppermute x2, waiting for transfers between devices, cyclic(): lax.ppermute(value, axis, [(i, (i + steps) % count) for i in range(count)])  13.4 us
    ppermute x4, waiting for transfers between devices, shifted(): return lax.ppermute(value, axis, shift_pairs(lax.axis_size(axis), steps))  12.3 us
    ppermute x4, starting transfers between devices, shifted(): return lax.ppermute(value, axis, shift_pairs(lax.axis_size(axis), steps))  11.8 us
    pallas_call x1, Pallas kernels, attention_forward(): pl.pallas_call(functools.partial(forward_kernel, scale * LOG2E), grid=(he...  10.1 us
    unnamed x21, local copies, waits for them, and re-layouts  6.1 us
    reshape x1, local copies, waits for them, and re-layouts, body(): cot_all.reshape(-1, 2, 2, 2, rows)  4.36 us
  transfers between devices with their start and end apart: 11, of which 6 were waited for; matrix products, arithmetic and copies ran while one was open for 14% of the time, Pallas kernels for 15%

profile of v12, /device:TPU:1, one launch (start us, length us, event | category | flops | bytes accessed | tf_op | source)
XLA Modules:
  0.0 172.7 jit_solution(17868912164203359627)
XLA Ops:
  7.2 0.0 copy-start
  7.2 0.0 all-gather.3.cloned.1.call-start
  7.2 0.7 all-gather.3.cloned.1.call-update
  7.9 0.0 reduce-scatter.2.cloned.1.call-start
  8.0 0.7 convert_bitcast_fusion
  8.6 1.2 fusion.11
  9.8 2.1 %collective-permute-start = (bf16[784,384]{1,0:T(8,128)(2,1)S(1)}, bf16[784,384]{1,0:T(8,128)(2,1)S(1)}, u32[]{:S(2)}, u32[]{:S(2)}) collective-permute-start(bf16[784,384]{1,0:T(8,128)(2,1)S(1)} %get-tuple-element.62), channel_id=1, source_target_pairs={{0,16},{16,0},{1,17},{17,1},{2,18},{18,2},{3,19},{19,3},{4,20},{20... | collective-permute-start | bytes 1806344 | tf_op jit(solution)/shard_map/halo_exchange/ppermute | solution.py:33
  11.9 13.4 %collective-permute-done = bf16[784,384]{1,0:T(8,128)(2,1)S(1)} collective-permute-done((bf16[784,384]{1,0:T(8,128)(2,1)S(1)}, bf16[784,384]{1,0:T(8,128)(2,1)S(1)}, u32[]{:S(2)}, u32[]{:S(2)}) %collective-permute-start) | collective-permute-done | bytes 602144 | tf_op jit(solution)/shard_map/halo_exchange/ppermute | solution.py:33
  25.4 0.0 copy-start.6
  25.4 0.8 copy-done.6
  26.2 1.2 pad_maximum_fusion.km.vm
  27.4 3.0 %collective-permute-start.2 = (bf16[2,784,384]{2,1,0:T(8,128)(2,1)}, bf16[2,784,384]{2,1,0:T(8,128)(2,1)}, u32[]{:S(2)}, u32[]{:S(2)}) collective-permute-start(bf16[2,784,384]{2,1,0:T(8,128)(2,1)} %pad_maximum_fusion.km.vm), channel_id=1, source_target_pairs={{4,0},{8,4},{12,8},{5,1},{9,5},{13,9},{6,2},{10,6},{14,10},{7,3},{... | collective-permute-start | bytes 3612680 | tf_op jit(solution)/shard_map/halo_exchange/ppermute | solution.py:23
  30.4 3.2 %collective-permute-start.1 = (bf16[2,784,384]{2,1,0:T(8,128)(2,1)}, bf16[2,784,384]{2,1,0:T(8,128)(2,1)}, u32[]{:S(2)}, u32[]{:S(2)}) collective-permute-start(bf16[2,784,384]{2,1,0:T(8,128)(2,1)} %pad_maximum_fusion.km.vm), channel_id=1, source_target_pairs={{0,4},{4,8},{8,12},{1,5},{5,9},{9,13},{2,6},{6,10},{10,14},{3,7},{... | collective-permute-start | bytes 3612680 | tf_op jit(solution)/shard_map/halo_exchange/ppermute | solution.py:23
  33.7 0.7 fusion.16
  34.4 12.1 %collective-permute-done.2.kr.vr = bf16[2,784,384]{2,1,0:T(8,128)(2,1)} collective-permute-done((bf16[2,784,384]{2,1,0:T(8,128)(2,1)}, bf16[2,784,384]{2,1,0:T(8,128)(2,1)}, u32[]{:S(2)}, u32[]{:S(2)}) %collective-permute-start.2) | collective-permute-done | bytes 1204256 | tf_op jit(solution)/shard_map/halo_exchange/ppermute | solution.py:23
  46.5 0.7 slice.47
  47.2 0.2 collective-permute-done.1.kl.vl
  47.4 0.7 slice.44
  48.1 0.6 copy.43
  48.7 10.1 %tile_attention_forward.1 = (bf16[384,384]{1,0:T(8,128)(2,1)}, f32[384,384]{1,0:T(8,128)}, f32[384,384]{1,0:T(8,128)}) custom-call(f32[1,2304]{1,0:T(1,128)} %bitcast.75, bf16[384,384]{1,0:T(8,128)(2,1)} %bitcast.71, bf16[2,784,384]{2,1,0:T(8,128)(2,1)} %collective-permute-done.1.kl.vl, bf16[2,784,384]{2,1,0:T(8,128)(2,1)} %pad_maximum_fusion.km.vm, ...), custom_call_target="tpu_custom_call" | custom-call | tf_op jit(solution)/shard_map/attention_forward/tile_attention_forward/pallas_call | solution.py:107
  58.8 3.3 %all-gather.3.cloned.1.call-done = bf16[1,1,384,3072]{3,2,1,0:T(8,128)(2,1)} async-done(((bf16[1,1,96,3072]{3,2,1,0:T(8,128)(2,1)}), bf16[1,1,384,3072]{3,2,1,0:T(8,128)(2,1)}) %all-gather.3.cloned.1.call-update) | async-done | bytes 2359312 | tf_op jit(solution)/shard_map/cotangent_gather/all_gather | solution.py:225
  62.1 4.3 %copy.36 = bf16[1,1,384,3072]{2,3,1,0:T(8,128)(2,1)} copy(bf16[1,1,384,3072]{3,2,1,0:T(8,128)(2,1)} %all-gather.3.cloned.1.call-done) | data formatting | bytes 4718592 | tf_op jit(solution)/shard_map/cotangent_gather/all_gather | solution.py:225
  66.4 0.0 copy-start.5
  66.4 4.4 %copy.37 = bf16[384,2,2,2,384]{4,0,1,2,3:T(8,128)(2,1)} copy(bf16[384,2,2,2,384]{0,4,3,2,1:T(8,128)(2,1)} %bitcast.68) | data formatting | bytes 4718592 | tf_op jit(solution)/shard_map/grad_weight/reshape | solution.py:245
  70.8 0.0 copy-done.5
  70.8 3.1 %fusion.2 = f32[384,2,2,2,384]{4,0,3,2,1:T(8,128)S(1)} fusion(bf16[384,2,2,2,384]{4,0,1,2,3:T(8,128)(2,1)} %copy.37, bf16[384,384]{1,0:T(8,128)(2,1)S(1)} %copy-done.5), kind=kOutput, calls=%fused_computation.4 | convolution fusion | flops 905969664 | bytes 7372800 | tf_op jit(solution)/shard_map/grad_weight/dot_general | solution.py:246
  73.9 0.0 copy-start.1
  73.9 2.1 %copy-done.1 = f32[384,2,2,2,384]{4,0,3,2,1:T(8,128)} copy-done((f32[384,2,2,2,384]{4,0,3,2,1:T(8,128)}, f32[384,2,2,2,384]{4,0,3,2,1:T(8,128)S(1)}, u32[]{:S(2)}) %copy-start.1) | copy-done | bytes 4718616
  76.0 1.2 fusion.8
  77.2 0.7 collective-permute-start.3
  77.9 0.0 copy-done
  77.9 2.8 %convolution_convert_fusion = bf16[384,3072]{1,0:T(8,128)(2,1)} fusion(bf16[384,384]{1,0:T(8,128)(2,1)S(1)} %copy-done.5, bf16[384,3072]{1,0:T(8,128)(2,1)S(1)} %copy-done), kind=kOutput, calls=%fused_computation | convolution fusion | flops 907149312 | bytes 5013504 | tf_op jit(solution)/shard_map/output_projection/dot_general | solution.py:231
  80.7 0.0 reduce-scatter.2.cloned.1.call-update
  80.8 0.0 copy-start.2
  80.8 3.9 %fusion.4.do_ref = bf16[384,384]{1,0:T(8,128)(2,1)} fusion(bf16[384,3072]{1,0:T(8,128)(2,1)S(1)} %copy-done, bf16[1,1,384,3072]{3,2,1,0:T(8,128)(2,1)} %all-gather.3.cloned.1.call-done), kind=kOutput, calls=%fused_computation.11 | convolution fusion | flops 906117120 | bytes 5013504 | tf_op jit(solution)/shard_map/grad_attended/dot_general | solution.py:237
  84.7 0.0 collective-permute-done.3
  84.7 0.0 copy-done.2
  84.7 1.8 %bitcast_add_fusion = f32[2,2,384,384]{2,3,1,0:T(8,128)S(1)} fusion(bf16[2,2,384,384]{2,3,1,0:T(8,128)(2,1)} %collective-permute-done.3, f32[384,2,2,2,384]{4,0,3,2,1:T(8,128)S(1)} %copy-done.2, s32[]{:T(128)S(6)} %select_n.41), kind=kLoop, calls=%fused_computation.1 | loop fusion | flops 1179648 | bytes 5898244 | tf_op jit(solution)/shard_map/grad_weight/add | solution.py:253
  86.5 0.9 fusion.12
  87.4 0.1 dynamic-slice_bitcast_fusion
  87.5 15.2 %tile_attention_backward.1 = (bf16[384,384]{1,0:T(8,128)(2,1)}, bf16[2,768,384]{2,1,0:T(8,128)(2,1)}, f32[2,768,384]{2,1,0:T(8,128)}, bf16[2,768,384]{2,1,0:T(8,128)(2,1)}) custom-call(f32[1,2304]{1,0:T(1,128)} %bitcast.76, bf16[384,384]{1,0:T(8,128)(2,1)} %bitcast.72, bf16[2,784,384]{2,1,0:T(8,128)(2,1)} %collective-permute-done.1.kl.vl, ...), custom_call_target="tpu_custom_call" | custom-call | tf_op jit(solution)/shard_map/attention_backward/tile_attention_backward/pallas_call | solution.py:133
  102.7 1.9 %collective-permute-start.4 = (bf16[2,768,384]{2,1,0:T(8,128)(2,1)}, bf16[2,768,384]{2,1,0:T(8,128)(2,1)}, u32[]{:S(2)}, u32[]{:S(2)}) collective-permute-start(bf16[2,768,384]{2,1,0:T(8,128)(2,1)} %get-tuple-element.33), channel_id=1, source_target_pairs={{4,0},{8,4},{12,8},{5,1},{9,5},{13,9},{6,2},{10,6},{14,10},{7,3},{... | collective-permute-start | bytes 3538952 | tf_op jit(solution)/shard_map/halo_reduction/ppermute | solution.py:23
  104.6 3.6 %collective-permute-start.5 = (bf16[2,768,384]{2,1,0:T(8,128)(2,1)}, bf16[2,768,384]{2,1,0:T(8,128)(2,1)}, u32[]{:S(2)}, u32[]{:S(2)}) collective-permute-start(bf16[2,768,384]{2,1,0:T(8,128)(2,1)} %get-tuple-element.34), channel_id=1, source_target_pairs={{0,4},{4,8},{8,12},{1,5},{5,9},{9,13},{2,6},{6,10},{10,14},{3,7},{... | collective-permute-start | bytes 3538952 | tf_op jit(solution)/shard_map/halo_reduction/ppermute | solution.py:23
  108.2 0.1 collective-permute-start.7
  108.3 0.0 copy-start.7
  108.3 26.0 %collective-permute-done.7 = bf16[2,384,384]{1,2,0:T(8,128)(2,1)} collective-permute-done((bf16[2,384,384]{1,2,0:T(8,128)(2,1)}, bf16[2,384,384]{1,2,0:T(8,128)(2,1)}, u32[]{:S(2)}, u32[]{:S(2)}) %collective-permute-start.7) | collective-permute-done | bytes 589856 | tf_op jit(solution)/shard_map/grad_weight/ppermute | solution.py:28
  134.3 1.2 convert_add_fusion.1
  135.5 0.0 copy-start.4
  135.5 0.0 collective-permute-done.4
  135.5 0.0 collective-permute-done.5
  135.5 0.0 copy-done.7
  135.5 2.4 %convert_add_fusion = f32[2,768,384]{2,1,0:T(8,128)S(1)} fusion(bf16[2,768,384]{2,1,0:T(8,128)(2,1)} %collective-permute-done.5, f32[2,768,384]{2,1,0:T(8,128)S(1)} %copy-done.7, bf16[2,768,384]{2,1,0:T(8,128)(2,1)} %collective-permute-done.4), kind=kLoop, calls=%fused_computation.6 | loop fusion | flops 2359296 | bytes 7077888 | tf_op jit(solution)/shard_map/halo_reduction/add | solution.py:287
  138.0 0.0 copy-start.3
  138.0 1.4 copy-done.3
  139.4 0.1 fusion.13
  139.5 1.1 collective-permute-start.6
  140.6 0.0 copy-done.4
  140.6 0.5 collective-permute-start.8
  141.1 20.1 %collective-permute-done.8 = bf16[384,384]{0,1:T(8,128)(2,1)} collective-permute-done((bf16[384,384]{0,1:T(8,128)(2,1)S(1)}, bf16[384,384]{0,1:T(8,128)(2,1)}, u32[]{:S(2)}, u32[]{:S(2)}) %collective-permute-start.8) | collective-permute-done | bytes 294944 | tf_op jit(solution)/shard_map/grad_weight/ppermute | solution.py:28
  161.2 1.2 bitcast_add_fusion.1
  162.4 1.1 copy.38
  163.5 0.0 collective-permute-done.6
  163.5 1.5 fusion.10
  165.0 0.9 slice_bitcast_fusion.1
  (6 shorter events, 0.1 us)
Async XLA Ops:
  7.2 70.7 %copy-start = (bf16[384,3072]{1,0:T(8,128)(2,1)S(1)}, bf16[384,3072]{1,0:T(8,128)(2,1)}, u32[]{:S(2)}) copy-start(bf16[384,3072]{1,0:T(8,128)(2,1)} %param.12) | copy-start | bytes 7077892
  7.2 55.0 %all-gather.3.cloned.1.call-start = ((), (), s32[]{:S(2)}) async-start(), calls=%async_computation.2 | async-start | bytes 2949120 | tf_op jit(solution)/shard_map/cotangent_gather/all_gather | solution.py:225
  7.9 158.0 %reduce-scatter.2.cloned.1.call-start = ((), (), s32[]{:S(2)}) async-start(), calls=%async_computation.1 | async-start | bytes 2949120 | tf_op jit(solution)/shard_map/output_projection/reduce_scatter | solution.py:232
  9.8 15.6 %collective-permute-start = (bf16[784,384]{1,0:T(8,128)(2,1)S(1)}, bf16[784,384]{1,0:T(8,128)(2,1)S(1)}, u32[]{:S(2)}, u32[]{:S(2)}) collective-permute-start(bf16[784,384]{1,0:T(8,128)(2,1)S(1)} %get-tuple-element.62), channel_id=1, source_target_pairs={{0,16},{16,0},{1,17},{17,1},{2,18},{18,2},{3,19},{19,3},{4,20},{20... | collective-permute-start | bytes 1806344 | tf_op jit(solution)/shard_map/halo_exchange/ppermute | solution.py:33
  25.4 0.8 copy-start.6
  27.4 19.1 %collective-permute-start.2 = (bf16[2,784,384]{2,1,0:T(8,128)(2,1)}, bf16[2,784,384]{2,1,0:T(8,128)(2,1)}, u32[]{:S(2)}, u32[]{:S(2)}) collective-permute-start(bf16[2,784,384]{2,1,0:T(8,128)(2,1)} %pad_maximum_fusion.km.vm), channel_id=1, source_target_pairs={{4,0},{8,4},{12,8},{5,1},{9,5},{13,9},{6,2},{10,6},{14,10},{7,3},{... | collective-permute-start | bytes 3612680 | tf_op jit(solution)/shard_map/halo_exchange/ppermute | solution.py:23
  30.4 17.0 %collective-permute-start.1 = (bf16[2,784,384]{2,1,0:T(8,128)(2,1)}, bf16[2,784,384]{2,1,0:T(8,128)(2,1)}, u32[]{:S(2)}, u32[]{:S(2)}) collective-permute-start(bf16[2,784,384]{2,1,0:T(8,128)(2,1)} %pad_maximum_fusion.km.vm), channel_id=1, source_target_pairs={{0,4},{4,8},{8,12},{1,5},{5,9},{9,13},{2,6},{6,10},{10,14},{3,7},{... | collective-permute-start | bytes 3612680 | tf_op jit(solution)/shard_map/halo_exchange/ppermute | solution.py:23
  66.4 4.4 %copy-start.5 = (bf16[384,384]{1,0:T(8,128)(2,1)S(1)}, bf16[384,384]{1,0:T(8,128)(2,1)}, u32[]{:S(2)}) copy-start(bf16[384,384]{1,0:T(8,128)(2,1)} %get-tuple-element.27.o_ref) | copy-start | bytes 884740
  73.9 2.1 %copy-start.1 = (f32[384,2,2,2,384]{4,0,3,2,1:T(8,128)}, f32[384,2,2,2,384]{4,0,3,2,1:T(8,128)S(1)}, u32[]{:S(2)}) copy-start(f32[384,2,2,2,384]{4,0,3,2,1:T(8,128)S(1)} %fusion.2) | copy-start | bytes 14155780
  77.2 7.5 %collective-permute-start.3 = (bf16[2,2,384,384]{2,3,1,0:T(8,128)(2,1)}, bf16[2,2,384,384]{2,3,1,0:T(8,128)(2,1)}, u32[]{:S(2)}, u32[]{:S(2)}) collective-permute-start(bf16[2,2,384,384]{2,3,1,0:T(8,128)(2,1)} %fusion.8), channel_id=1, source_target_pairs={{0,4},{4,0},{8,12},{12,8},{1,5},{5,1},{9,13},{13,9},{2,6},{6,2},{1... | collective-permute-start | bytes 3538952 | tf_op jit(solution)/shard_map/grad_weight/ppermute | solution.py:28
  80.8 3.9 %copy-start.2 = (f32[384,2,2,2,384]{4,0,3,2,1:T(8,128)S(1)}, f32[384,2,2,2,384]{4,0,3,2,1:T(8,128)}, u32[]{:S(2)}) copy-start(f32[384,2,2,2,384]{4,0,3,2,1:T(8,128)} %copy-done.1) | copy-start | bytes 14155780
  102.7 32.8 %collective-permute-start.4 = (bf16[2,768,384]{2,1,0:T(8,128)(2,1)}, bf16[2,768,384]{2,1,0:T(8,128)(2,1)}, u32[]{:S(2)}, u32[]{:S(2)}) collective-permute-start(bf16[2,768,384]{2,1,0:T(8,128)(2,1)} %get-tuple-element.33), channel_id=1, source_target_pairs={{4,0},{8,4},{12,8},{5,1},{9,5},{13,9},{6,2},{10,6},{14,10},{7,3},{... | collective-permute-start | bytes 3538952 | tf_op jit(solution)/shard_map/halo_reduction/ppermute | solution.py:23
  104.6 30.9 %collective-permute-start.5 = (bf16[2,768,384]{2,1,0:T(8,128)(2,1)}, bf16[2,768,384]{2,1,0:T(8,128)(2,1)}, u32[]{:S(2)}, u32[]{:S(2)}) collective-permute-start(bf16[2,768,384]{2,1,0:T(8,128)(2,1)} %get-tuple-element.34), channel_id=1, source_target_pairs={{0,4},{4,8},{8,12},{1,5},{5,9},{9,13},{2,6},{6,10},{10,14},{3,7},{... | collective-permute-start | bytes 3538952 | tf_op jit(solution)/shard_map/halo_reduction/ppermute | solution.py:23
  108.2 26.1 %collective-permute-start.7 = (bf16[2,384,384]{1,2,0:T(8,128)(2,1)}, bf16[2,384,384]{1,2,0:T(8,128)(2,1)}, u32[]{:S(2)}, u32[]{:S(2)}) collective-permute-start(bf16[2,384,384]{1,2,0:T(8,128)(2,1)} %fusion.12), channel_id=1, source_target_pairs={{0,8},{4,12},{8,0},{12,4},{1,9},{5,13},{9,1},{13,5},{2,10},{6,14},... | collective-permute-start | bytes 1769480 | tf_op jit(solution)/shard_map/grad_weight/ppermute | solution.py:28
  108.3 27.2 %copy-start.7 = (f32[2,768,384]{2,1,0:T(8,128)S(1)}, f32[2,768,384]{2,1,0:T(8,128)}, u32[]{:S(2)}) copy-start(f32[2,768,384]{2,1,0:T(8,128)} %get-tuple-element.32) | copy-start | bytes 7077892
  135.5 5.1 %copy-start.4 = (f32[2,384,384]{1,2,0:T(8,128)}, f32[2,384,384]{1,2,0:T(8,128)S(1)}, u32[]{:S(2)}) copy-start(f32[2,384,384]{1,2,0:T(8,128)S(1)} %convert_add_fusion.1) | copy-start | bytes 3538948
  138.0 1.4 copy-start.3
  139.5 24.0 %collective-permute-start.6 = (bf16[768,384]{1,0:T(8,128)(2,1)S(1)}, bf16[768,384]{1,0:T(8,128)(2,1)}, u32[]{:S(2)}, u32[]{:S(2)}) collective-permute-start(bf16[768,384]{1,0:T(8,128)(2,1)S(1)} %fusion.13), channel_id=1, source_target_pairs={{0,16},{16,0},{1,17},{17,1},{2,18},{18,2},{3,19},{19,3},{4,20},{20... | collective-permute-start | bytes 1769480 | tf_op jit(solution)/shard_map/halo_reduction/ppermute | solution.py:33
  140.6 20.6 %collective-permute-start.8 = (bf16[384,384]{0,1:T(8,128)(2,1)S(1)}, bf16[384,384]{0,1:T(8,128)(2,1)}, u32[]{:S(2)}, u32[]{:S(2)}) collective-permute-start(bf16[384,384]{0,1:T(8,128)(2,1)S(1)} %fusion.14), channel_id=1, source_target_pairs={{0,16},{16,0},{1,17},{17,1},{2,18},{18,2},{3,19},{19,3},{4,20},{20... | collective-permute-start | bytes 884744 | tf_op jit(solution)/shard_map/grad_weight/ppermute | solution.py:28
Sparse Core Ops, SparseCore 0:
  9.6 52.5 all-gather.2
  80.9 46.1 reduce-scatter.1

commit v13 on v11

--- a/solution.py
+++ b/solution.py
@@ -242,14 +242,13 @@
     with jax.named_scope("grad_weight"):
         if halving:
             rows = model_width // 8
-            cot_blocks = cot_all.reshape(-1, 2, 2, 2, rows)
-            weight_blocks = lax.dot_general(
-                cot_blocks, attended, (((0,), (0,)), ((), ())), preferred_element_type=jnp.float32
-            )
-            weight_blocks = jnp.transpose(weight_blocks, (2, 1, 0, 3, 4))
+            weight_part = lax.dot_general(
+                cot_all, attended, (((0,), (0,)), ((), ())), preferred_element_type=jnp.float32
+            )
+            weight_blocks = weight_part.reshape(2, 2, 2, rows, weight_part.shape[1])
             core = lax.axis_index("wa") % 2
-            weight_own = lax.dynamic_index_in_dim(weight_blocks, core, 0, keepdims=False)
-            weight_sent = lax.dynamic_index_in_dim(weight_blocks, 1 - core, 0, keepdims=False)
+            weight_own = lax.dynamic_index_in_dim(weight_blocks, core, 2, keepdims=False)
+            weight_sent = lax.dynamic_index_in_dim(weight_blocks, 1 - core, 2, keepdims=False)
             weight_sent = weight_sent.astype(jnp.bfloat16)
             weight_own, weight_sent, grad_attended = lax.optimization_barrier(
                 (weight_own, weight_sent, grad_attended)
@@ -273,8 +272,8 @@
     with jax.named_scope("grad_weight"):
         if halving:
             column = lax.axis_index("wa") // 2
-            kept = lax.dynamic_index_in_dim(weight_x, column, 0, keepdims=False)
-            sent = lax.dynamic_index_in_dim(weight_x, 1 - column, 0, keepdims=False)
+            kept = lax.dynamic_index_in_dim(weight_x, column, 1, keepdims=False)
+            sent = lax.dynamic_index_in_dim(weight_x, 1 - column, 1, keepdims=False)
             weight_f = kept + partner(sent.astype(jnp.bfloat16), "wa", 2).astype(jnp.float32)
             row = lax.axis_index("fh")
             kept = lax.dynamic_index_in_dim(weight_f, row, 0, keepdims=False)

time: 145 us -> 174 us (1.20)
  local copies, waits for them, and re-layouts: 15.4 us -> 37.6 us
  matrix products: 9 us -> 12.8 us
  other arithmetic: 9.49 us -> 11.7 us
    dynamic_slice x0 -> x3, local copies, waits for them, and re-layouts: none -> 18.5 us  [the longest x2 12.5 us: body(): lax.dynamic_index_in_dim(weight_blocks, core, 2, keepdims=False)]
    reshape x0 -> x1, local copies, waits for them, and re-layouts: none -> 7.2 us  [body(): weight_blocks = weight_part.reshape(2, 2, 2, rows, weight_part.shape[1])]
    unnamed x21 -> x19, local copies, waits for them, and re-layouts: 4.93 us -> 9.41 us
    all_gather x1 -> x0, local copies, waits for them, and re-layouts: 4.33 us -> none  [body(): cot_all = lax.all_gather(out_cotangent[0, 0], 'ha', axis=0, tiled=True)]
    dot_general x1, matrix products: 3.09 us -> 5.26 us  [body(): lax.dot_general(cot_all, attended, (((0,), (0,)), ((), ())), preferred_el...]
    ppermute x3, waiting for transfers between devices: 5.34 us -> 3.45 us  [partner(): return lax.ppermute(value, axis, [(i, i ^ bit) for i in range(count)])]
  transfers between devices with their start and end apart: 11 -> 11, of which waited for: 8 -> 8; matrix products, arithmetic and copies ran while one was open for 21% -> 34% of each run, Pallas kernels for 18% -> 15%
where the time goes in v13:
time: 174 us; the launch traced here: 172 us
  waiting for transfers between devices  51.9 us (30%)
  local copies, waits for them, and re-layouts  37.6 us (22%)
  Pallas kernels  25.5 us (15%)
  starting transfers between devices  18 us (10%)
  between operations  14.2 us (8%)
  matrix products  12.8 us (7%)
  other arithmetic  11.7 us (7%)
    ppermute x4, waiting for transfers between devices, shifted(): return lax.ppermute(value, axis, shift_pairs(lax.axis_size(axis), steps))  29 us
    ppermute x2, waiting for transfers between devices, cyclic(): lax.ppermute(value, axis, [(i, (i + steps) % count) for i in range(count)])  18.8 us
    pallas_call x1, Pallas kernels, attention_backward(): pl.pallas_call(functools.partial(backward_kernel, scale, scale * LOG2E),...  15.4 us
    ppermute x4, starting transfers between devices, shifted(): return lax.ppermute(value, axis, shift_pairs(lax.axis_size(axis), steps))  12.5 us
    dynamic_slice x2, local copies, waits for them, and re-layouts, body(): lax.dynamic_index_in_dim(weight_blocks, core, 2, keepdims=False)  12.5 us
    pallas_call x1, Pallas kernels, attention_forward(): pl.pallas_call(functools.partial(forward_kernel, scale * LOG2E), grid=(he...  10.1 us
    unnamed x19, local copies, waits for them, and re-layouts  9.41 us
    reshape x1, local copies, waits for them, and re-layouts, body(): weight_blocks = weight_part.reshape(2, 2, 2, rows, weight_part.shape[1])  7.2 us
  transfers between devices with their start and end apart: 11, of which 8 were waited for; matrix products, arithmetic and copies ran while one was open for 34% of the time, Pallas kernels for 15%

profile of v13, /device:TPU:1, one launch (start us, length us, event | category | flops | bytes accessed | tf_op | source)
XLA Modules:
  0.0 171.6 jit_solution(9923343092684342139)
XLA Ops:
  7.2 0.0 copy-start
  7.2 0.0 all-gather.3.cloned.1.call-start
  7.2 0.7 all-gather.3.cloned.1.call-update
  7.9 0.0 reduce-scatter.2.cloned.1.call-start
  8.0 0.7 convert_bitcast_fusion.1
  8.6 1.2 fusion.9
  9.8 2.1 %collective-permute-start = (bf16[784,384]{1,0:T(8,128)(2,1)S(1)}, bf16[784,384]{1,0:T(8,128)(2,1)S(1)}, u32[]{:S(2)}, u32[]{:S(2)}) collective-permute-start(bf16[784,384]{1,0:T(8,128)(2,1)S(1)} %get-tuple-element.37), channel_id=1, source_target_pairs={{0,16},{16,0},{1,17},{17,1},{2,18},{18,2},{3,19},{19,3},{4,20},{20... | collective-permute-start | bytes 1806344 | tf_op jit(solution)/shard_map/halo_exchange/ppermute | solution.py:33
  11.9 13.4 %collective-permute-done = bf16[784,384]{1,0:T(8,128)(2,1)S(1)} collective-permute-done((bf16[784,384]{1,0:T(8,128)(2,1)S(1)}, bf16[784,384]{1,0:T(8,128)(2,1)S(1)}, u32[]{:S(2)}, u32[]{:S(2)}) %collective-permute-start) | collective-permute-done | bytes 602144 | tf_op jit(solution)/shard_map/halo_exchange/ppermute | solution.py:33
  25.4 0.0 copy-start.5
  25.4 0.8 copy-done.5
  26.2 1.2 pad_maximum_fusion.km.vm
  27.4 3.0 %collective-permute-start.2 = (bf16[2,784,384]{2,1,0:T(8,128)(2,1)}, bf16[2,784,384]{2,1,0:T(8,128)(2,1)}, u32[]{:S(2)}, u32[]{:S(2)}) collective-permute-start(bf16[2,784,384]{2,1,0:T(8,128)(2,1)} %pad_maximum_fusion.km.vm), channel_id=1, source_target_pairs={{4,0},{8,4},{12,8},{5,1},{9,5},{13,9},{6,2},{10,6},{14,10},{7,3},{... | collective-permute-start | bytes 3612680 | tf_op jit(solution)/shard_map/halo_exchange/ppermute | solution.py:23
  30.4 3.2 %collective-permute-start.1 = (bf16[2,784,384]{2,1,0:T(8,128)(2,1)}, bf16[2,784,384]{2,1,0:T(8,128)(2,1)}, u32[]{:S(2)}, u32[]{:S(2)}) collective-permute-start(bf16[2,784,384]{2,1,0:T(8,128)(2,1)} %pad_maximum_fusion.km.vm), channel_id=1, source_target_pairs={{0,4},{4,8},{8,12},{1,5},{5,9},{9,13},{2,6},{6,10},{10,14},{3,7},{... | collective-permute-start | bytes 3612680 | tf_op jit(solution)/shard_map/halo_exchange/ppermute | solution.py:23
  33.7 0.7 fusion.13
  34.4 12.1 %collective-permute-done.2.kr.vr = bf16[2,784,384]{2,1,0:T(8,128)(2,1)} collective-permute-done((bf16[2,784,384]{2,1,0:T(8,128)(2,1)}, bf16[2,784,384]{2,1,0:T(8,128)(2,1)}, u32[]{:S(2)}, u32[]{:S(2)}) %collective-permute-start.2) | collective-permute-done | bytes 1204256 | tf_op jit(solution)/shard_map/halo_exchange/ppermute | solution.py:23
  46.5 0.7 slice.47
  47.2 0.2 collective-permute-done.1.kl.vl
  47.3 0.7 slice.44
  48.1 0.6 copy.38
  48.7 10.1 %tile_attention_forward.1 = (bf16[384,384]{1,0:T(8,128)(2,1)}, f32[384,384]{1,0:T(8,128)}, f32[384,384]{1,0:T(8,128)}) custom-call(f32[1,2304]{1,0:T(1,128)} %bitcast.70, bf16[384,384]{1,0:T(8,128)(2,1)} %bitcast.65, bf16[2,784,384]{2,1,0:T(8,128)(2,1)} %collective-permute-done.1.kl.vl, bf16[2,784,384]{2,1,0:T(8,128)(2,1)} %pad_maximum_fusion.km.vm, ...), custom_call_target="tpu_custom_call" | custom-call | tf_op jit(solution)/shard_map/attention_forward/tile_attention_forward/pallas_call | solution.py:107
  58.8 0.0 copy-done
  58.8 3.7 %convolution_convert_fusion = bf16[384,3072]{1,0:T(8,128)(2,1)} fusion(bf16[384,384]{1,0:T(8,128)(2,1)} %get-tuple-element.27.o_ref, bf16[384,3072]{1,0:T(8,128)(2,1)S(1)} %copy-done), kind=kOutput, calls=%fused_computation.1 | convolution fusion | flops 907149312 | bytes 5013504 | tf_op jit(solution)/shard_map/output_projection/dot_general | solution.py:231
  62.5 0.0 copy-start.4
  62.5 0.0 reduce-scatter.2.cloned.1.call-update
  62.6 0.0 all-gather.3.cloned.1.call-done
  62.6 0.9 copy-done.4
  63.5 5.3 %convolution_bitcast_fusion = f32[3072,384]{0,1:T(8,128)} fusion(bf16[384,384]{1,0:T(8,128)(2,1)S(1)} %copy-done.4, bf16[1,1,384,3072]{3,2,1,0:T(8,128)(2,1)} %all-gather.3.cloned.1.call-done), kind=kOutput, calls=%fused_computation | convolution fusion | flops 905969664 | bytes 7372800 | tf_op jit(solution)/shard_map/grad_weight/dot_general | solution.py:245
  68.8 7.2 %reshape.72 = f32[2,2,2,384,384]{3,2,1,0,4:T(2,128)} reshape(f32[3072,384]{0,1:T(8,128)} %convolution_bitcast_fusion) | data formatting | bytes 9437184 | tf_op jit(solution)/shard_map/grad_weight/reshape | solution.py:248
  76.0 6.0 %constant_dynamic-slice_fusion = bf16[2,2,1,384,384]{3,2,1,0,4:T(2,128)(2,1)} fusion(f32[2,2,2,384,384]{3,2,1,0,4:T(2,128)} %reshape.72, s32[]{:T(128)S(6)} %select_n.42), kind=kLoop, calls=%fused_computation.33 | loop fusion | bytes 2359300 | tf_op jit(solution)/shard_map/grad_weight/jit(dynamic_index_in_dim)/dynamic_slice | solution.py:251
  81.9 5.6 %copy.37 = bf16[2,2,1,384,384]{4,3,0,1,2:T(8,128)(2,1)S(1)} copy(bf16[2,2,1,384,384]{3,2,1,0,4:T(2,128)(2,1)} %constant_dynamic-slice_fusion) | data formatting | bytes 2359296
  87.5 5.8 %constant_dynamic-slice_fusion.1 = f32[2,2,1,384,384]{3,2,1,0,4:T(1,128)} fusion(f32[2,2,2,384,384]{3,2,1,0,4:T(2,128)} %reshape.72, s32[]{:T(128)S(6)} %select_n.41), kind=kLoop, calls=%fused_computation.34 | loop fusion | bytes 4718596 | tf_op jit(solution)/shard_map/grad_weight/jit(dynamic_index_in_dim)/dynamic_slice | solution.py:250
  93.3 6.7 %copy.32 = f32[2,2,1,384,384]{4,3,0,1,2:T(8,128)} copy(f32[2,2,1,384,384]{3,2,1,0,4:T(1,128)} %constant_dynamic-slice_fusion.1) | data formatting | bytes 4718592 | tf_op jit(solution)/shard_map/grad_weight/jit(dynamic_index_in_dim)/dynamic_slice | solution.py:250
  100.1 3.8 %fusion.3.do_ref = bf16[384,384]{1,0:T(8,128)(2,1)} fusion(bf16[384,3072]{1,0:T(8,128)(2,1)S(1)} %copy-done, bf16[1,1,384,3072]{3,2,1,0:T(8,128)(2,1)} %all-gather.3.cloned.1.call-done), kind=kOutput, calls=%fused_computation.10 | convolution fusion | flops 906117120 | bytes 5013504 | tf_op jit(solution)/shard_map/grad_attended/dot_general | solution.py:237
  103.8 0.0 collective-permute-start.6
  103.8 15.4 %tile_attention_backward.1 = (bf16[384,384]{1,0:T(8,128)(2,1)}, bf16[2,768,384]{2,1,0:T(8,128)(2,1)}, f32[2,768,384]{2,1,0:T(8,128)}, bf16[2,768,384]{2,1,0:T(8,128)(2,1)}) custom-call(f32[1,2304]{1,0:T(1,128)} %bitcast.71, bf16[384,384]{1,0:T(8,128)(2,1)} %bitcast.66, bf16[2,784,384]{2,1,0:T(8,128)(2,1)} %collective-permute-done.1.kl.vl, ...), custom_call_target="tpu_custom_call" | custom-call | tf_op jit(solution)/shard_map/attention_backward/tile_attention_backward/pallas_call | solution.py:133
  119.2 2.4 %collective-permute-start.3 = (bf16[2,768,384]{2,1,0:T(8,128)(2,1)}, bf16[2,768,384]{2,1,0:T(8,128)(2,1)}, u32[]{:S(2)}, u32[]{:S(2)}) collective-permute-start(bf16[2,768,384]{2,1,0:T(8,128)(2,1)} %get-tuple-element.33), channel_id=1, source_target_pairs={{4,0},{8,4},{12,8},{5,1},{9,5},{13,9},{6,2},{10,6},{14,10},{7,3},{... | collective-permute-start | bytes 3538952 | tf_op jit(solution)/shard_map/halo_reduction/ppermute | solution.py:23
  121.6 3.9 %collective-permute-start.4 = (bf16[2,768,384]{2,1,0:T(8,128)(2,1)}, bf16[2,768,384]{2,1,0:T(8,128)(2,1)}, u32[]{:S(2)}, u32[]{:S(2)}) collective-permute-start(bf16[2,768,384]{2,1,0:T(8,128)(2,1)} %get-tuple-element.34), channel_id=1, source_target_pairs={{0,4},{4,8},{8,12},{1,5},{5,9},{9,13},{2,6},{6,10},{10,14},{3,7},{... | collective-permute-start | bytes 3538952 | tf_op jit(solution)/shard_map/halo_reduction/ppermute | solution.py:23
  125.5 0.0 copy-start.6
  125.5 0.0 collective-permute-done.6
  125.6 2.3 %convert_add_fusion = f32[2,2,384,384]{3,2,0,1:T(8,128)S(1)} fusion(f32[2,2,384,384]{3,2,0,1:T(8,128)} %bitcast.62, bf16[2,2,384,384]{3,2,0,1:T(8,128)(2,1)} %collective-permute-done.6), kind=kLoop, calls=%fused_computation.5 | loop fusion | flops 1179648 | bytes 5898240 | tf_op jit(solution)/shard_map/grad_weight/add | solution.py:256
  127.9 0.0 copy-start.3
  127.9 0.1 fusion.10
  128.0 0.6 collective-permute-start.7
  128.6 15.5 %collective-permute-done.3 = bf16[2,768,384]{2,1,0:T(8,128)(2,1)} collective-permute-done((bf16[2,768,384]{2,1,0:T(8,128)(2,1)}, bf16[2,768,384]{2,1,0:T(8,128)(2,1)}, u32[]{:S(2)}, u32[]{:S(2)}) %collective-permute-start.3) | collective-permute-done | bytes 1179680 | tf_op jit(solution)/shard_map/halo_reduction/ppermute | solution.py:23
  144.1 1.2 collective-permute-done.4
  145.3 0.0 copy-done.3
  145.3 0.0 copy-done.6
  145.3 2.0 %convert_add_fusion.1 = f32[2,768,384]{2,1,0:T(8,128)S(1)} fusion(bf16[2,768,384]{2,1,0:T(8,128)(2,1)} %collective-permute-done.4, f32[2,768,384]{2,1,0:T(8,128)S(1)} %copy-done.6, bf16[2,768,384]{2,1,0:T(8,128)(2,1)} %collective-permute-done.3), kind=kLoop, calls=%fused_computation.6 | loop fusion | flops 2359296 | bytes 7077888 | tf_op jit(solution)/shard_map/halo_reduction/add | solution.py:287
  147.3 0.0 copy-start.1
  147.3 1.4 copy-done.1
  148.7 0.1 fusion.11
  148.8 1.3 collective-permute-start.5
  150.1 0.0 copy-start.2
  150.1 1.4 collective-permute-done.7
  151.5 1.6 bitcast_add_fusion
  153.1 1.3 collective-permute-start.8
  154.4 5.4 %collective-permute-done.5 = bf16[768,384]{1,0:T(8,128)(2,1)} collective-permute-done((bf16[768,384]{1,0:T(8,128)(2,1)S(1)}, bf16[768,384]{1,0:T(8,128)(2,1)}, u32[]{:S(2)}, u32[]{:S(2)}) %collective-permute-start.5) | collective-permute-done | bytes 589856 | tf_op jit(solution)/shard_map/halo_reduction/ppermute | solution.py:33
  159.8 0.0 copy-done.2
  159.8 1.2 fusion.8
  161.0 0.9 slice_bitcast_fusion.1
  161.9 2.1 %collective-permute-done.8 = bf16[384,384]{1,0:T(8,128)(2,1)S(1)} collective-permute-done((bf16[384,384]{1,0:T(8,128)(2,1)S(1)}, bf16[384,384]{1,0:T(8,128)(2,1)S(1)}, u32[]{:S(2)}, u32[]{:S(2)}) %collective-permute-start.8) | collective-permute-done | bytes 294944 | tf_op jit(solution)/shard_map/grad_weight/ppermute | solution.py:28
  163.9 0.9 bitcast_add_fusion.1
  164.8 0.0 reduce-scatter.2.cloned.1.call-done
  (5 shorter events, 0.1 us)
Async XLA Ops:
  7.2 51.6 %copy-start = (bf16[384,3072]{1,0:T(8,128)(2,1)S(1)}, bf16[384,3072]{1,0:T(8,128)(2,1)}, u32[]{:S(2)}) copy-start(bf16[384,3072]{1,0:T(8,128)(2,1)} %param.12) | copy-start | bytes 7077892
  7.2 55.4 %all-gather.3.cloned.1.call-start = ((), (), s32[]{:S(2)}) async-start(), calls=%async_computation.2 | async-start | bytes 2949120 | tf_op jit(solution)/shard_map/cotangent_gather/all_gather | solution.py:225
  7.9 156.9 %reduce-scatter.2.cloned.1.call-start = ((), (), s32[]{:S(2)}) async-start(), calls=%async_computation.1 | async-start | bytes 2949120 | tf_op jit(solution)/shard_map/output_projection/reduce_scatter | solution.py:232
  9.8 15.6 %collective-permute-start = (bf16[784,384]{1,0:T(8,128)(2,1)S(1)}, bf16[784,384]{1,0:T(8,128)(2,1)S(1)}, u32[]{:S(2)}, u32[]{:S(2)}) collective-permute-start(bf16[784,384]{1,0:T(8,128)(2,1)S(1)} %get-tuple-element.37), channel_id=1, source_target_pairs={{0,16},{16,0},{1,17},{17,1},{2,18},{18,2},{3,19},{19,3},{4,20},{20... | collective-permute-start | bytes 1806344 | tf_op jit(solution)/shard_map/halo_exchange/ppermute | solution.py:33
  25.4 0.8 copy-start.5
  27.4 19.1 %collective-permute-start.2 = (bf16[2,784,384]{2,1,0:T(8,128)(2,1)}, bf16[2,784,384]{2,1,0:T(8,128)(2,1)}, u32[]{:S(2)}, u32[]{:S(2)}) collective-permute-start(bf16[2,784,384]{2,1,0:T(8,128)(2,1)} %pad_maximum_fusion.km.vm), channel_id=1, source_target_pairs={{4,0},{8,4},{12,8},{5,1},{9,5},{13,9},{6,2},{10,6},{14,10},{7,3},{... | collective-permute-start | bytes 3612680 | tf_op jit(solution)/shard_map/halo_exchange/ppermute | solution.py:23
  30.4 17.0 %collective-permute-start.1 = (bf16[2,784,384]{2,1,0:T(8,128)(2,1)}, bf16[2,784,384]{2,1,0:T(8,128)(2,1)}, u32[]{:S(2)}, u32[]{:S(2)}) collective-permute-start(bf16[2,784,384]{2,1,0:T(8,128)(2,1)} %pad_maximum_fusion.km.vm), channel_id=1, source_target_pairs={{0,4},{4,8},{8,12},{1,5},{5,9},{9,13},{2,6},{6,10},{10,14},{3,7},{... | collective-permute-start | bytes 3612680 | tf_op jit(solution)/shard_map/halo_exchange/ppermute | solution.py:23
  62.5 1.0 copy-start.4
  103.8 21.7 %collective-permute-start.6 = (bf16[2,2,384,384]{3,2,0,1:T(8,128)(2,1)S(1)}, bf16[2,2,384,384]{3,2,0,1:T(8,128)(2,1)}, u32[]{:S(2)}, u32[]{:S(2)}) collective-permute-start(bf16[2,2,384,384]{3,2,0,1:T(8,128)(2,1)S(1)} %bitcast.67), channel_id=1, source_target_pairs={{0,4},{4,0},{8,12},{12,8},{1,5},{5,1},{9,13},{13,9},{2,6},{6,2},{1... | collective-permute-start | bytes 3538952 | tf_op jit(solution)/shard_map/grad_weight/ppermute | solution.py:28
  119.2 24.9 %collective-permute-start.3 = (bf16[2,768,384]{2,1,0:T(8,128)(2,1)}, bf16[2,768,384]{2,1,0:T(8,128)(2,1)}, u32[]{:S(2)}, u32[]{:S(2)}) collective-permute-start(bf16[2,768,384]{2,1,0:T(8,128)(2,1)} %get-tuple-element.33), channel_id=1, source_target_pairs={{4,0},{8,4},{12,8},{5,1},{9,5},{13,9},{6,2},{10,6},{14,10},{7,3},{... | collective-permute-start | bytes 3538952 | tf_op jit(solution)/shard_map/halo_reduction/ppermute | solution.py:23
  121.6 23.6 %collective-permute-start.4 = (bf16[2,768,384]{2,1,0:T(8,128)(2,1)}, bf16[2,768,384]{2,1,0:T(8,128)(2,1)}, u32[]{:S(2)}, u32[]{:S(2)}) collective-permute-start(bf16[2,768,384]{2,1,0:T(8,128)(2,1)} %get-tuple-element.34), channel_id=1, source_target_pairs={{0,4},{4,8},{8,12},{1,5},{5,9},{9,13},{2,6},{6,10},{10,14},{3,7},{... | collective-permute-start | bytes 3538952 | tf_op jit(solution)/shard_map/halo_reduction/ppermute | solution.py:23
  125.5 19.7 %copy-start.6 = (f32[2,768,384]{2,1,0:T(8,128)S(1)}, f32[2,768,384]{2,1,0:T(8,128)}, u32[]{:S(2)}) copy-start(f32[2,768,384]{2,1,0:T(8,128)} %get-tuple-element.32) | copy-start | bytes 7077892
  127.9 17.4 %copy-start.3 = (f32[2,2,384,384]{3,2,0,1:T(8,128)}, f32[2,2,384,384]{3,2,0,1:T(8,128)S(1)}, u32[]{:S(2)}) copy-start(f32[2,2,384,384]{3,2,0,1:T(8,128)S(1)} %convert_add_fusion) | copy-start | bytes 7077892
  128.0 23.5 %collective-permute-start.7 = (bf16[2,384,384]{2,1,0:T(8,128)(2,1)S(1)}, bf16[2,384,384]{2,1,0:T(8,128)(2,1)}, u32[]{:S(2)}, u32[]{:S(2)}) collective-permute-start(bf16[2,384,384]{2,1,0:T(8,128)(2,1)S(1)} %fusion.10), channel_id=1, source_target_pairs={{0,8},{4,12},{8,0},{12,4},{1,9},{5,13},{9,1},{13,5},{2,10},{6,14},... | collective-permute-start | bytes 1769480 | tf_op jit(solution)/shard_map/grad_weight/ppermute | solution.py:28
  147.3 1.4 copy-start.1
  148.8 11.0 %collective-permute-start.5 = (bf16[768,384]{1,0:T(8,128)(2,1)S(1)}, bf16[768,384]{1,0:T(8,128)(2,1)}, u32[]{:S(2)}, u32[]{:S(2)}) collective-permute-start(bf16[768,384]{1,0:T(8,128)(2,1)S(1)} %fusion.11), channel_id=1, source_target_pairs={{0,16},{16,0},{1,17},{17,1},{2,18},{18,2},{3,19},{19,3},{4,20},{20... | collective-permute-start | bytes 1769480 | tf_op jit(solution)/shard_map/halo_reduction/ppermute | solution.py:33
  150.1 9.7 %copy-start.2 = (f32[2,768,384]{2,1,0:T(8,128)S(1)}, f32[2,768,384]{2,1,0:T(8,128)}, u32[]{:S(2)}) copy-start(f32[2,768,384]{2,1,0:T(8,128)} %copy-done.1) | copy-start | bytes 7077892
  153.1 10.8 %collective-permute-start.8 = (bf16[384,384]{1,0:T(8,128)(2,1)S(1)}, bf16[384,384]{1,0:T(8,128)(2,1)S(1)}, u32[]{:S(2)}, u32[]{:S(2)}) collective-permute-start(bf16[384,384]{1,0:T(8,128)(2,1)S(1)} %fusion.12), channel_id=1, source_target_pairs={{0,16},{16,0},{1,17},{17,1},{2,18},{18,2},{3,19},{19,3},{4,20},{20... | collective-permute-start | bytes 884744 | tf_op jit(solution)/shard_map/grad_weight/ppermute | solution.py:28
Sparse Core Ops, SparseCore 0:
  9.6 52.5 all-gather.2
  65.0 47.4 reduce-scatter.1

commit v14 on v11

--- a/solution.py
+++ b/solution.py
@@ -10,7 +10,7 @@
 HD = 128
 MASKED = -1e30
 FORWARD_CHUNK = 384
-BACKWARD_CHUNK = 192
+BACKWARD_CHUNK = 384
 FLAG_ROWS = 16
 LOG2E = 1.4426950408889634
 

time: 145 us -> 141 us (0.972)
  Pallas kernels: 25.3 us -> 21.4 us
    pallas_call x1, Pallas kernels: 15.2 us -> 11.3 us  [attention_backward(): pl.pallas_call(functools.partial(backward_kernel, scale, scale * LOG2E),...]
  transfers between devices with their start and end apart: 11 -> 11, of which waited for: 8 -> 8; matrix products, arithmetic and copies ran while one was open for 21% -> 22% of each run, Pallas kernels for 18% -> 15%
where the time goes in v14:
time: 141 us; the launch traced here: 140 us
  waiting for transfers between devices  52.7 us (37%)
  Pallas kernels  21.4 us (15%)
  starting transfers between devices  17.4 us (12%)
  local copies, waits for them, and re-layouts  15.4 us (11%)
  between operations  14.2 us (10%)
  other arithmetic  9.52 us (7%)
  matrix products  9 us (6%)
    ppermute x4, waiting for transfers between devices, shifted(): return lax.ppermute(value, axis, shift_pairs(lax.axis_size(axis), steps))  28.6 us
    ppermute x2, waiting for transfers between devices, cyclic(): lax.ppermute(value, axis, [(i, (i + steps) % count) for i in range(count)])  18 us
    ppermute x4, starting transfers between devices, shifted(): return lax.ppermute(value, axis, shift_pairs(lax.axis_size(axis), steps))  12.5 us
    pallas_call x1, Pallas kernels, attention_backward(): pl.pallas_call(functools.partial(backward_kernel, scale, scale * LOG2E),...  11.3 us
    pallas_call x1, Pallas kernels, attention_forward(): pl.pallas_call(functools.partial(forward_kernel, scale * LOG2E), grid=(he...  10.1 us
    ppermute x3, waiting for transfers between devices, partner(): return lax.ppermute(value, axis, [(i, i ^ bit) for i in range(count)])  5.34 us
    unnamed x21, local copies, waits for them, and re-layouts  4.93 us
    all_gather x1, local copies, waits for them, and re-layouts, body(): cot_all = lax.all_gather(out_cotangent[0, 0], 'ha', axis=0, tiled=True)  4.33 us
  transfers between devices with their start and end apart: 11, of which 8 were waited for; matrix products, arithmetic and copies ran while one was open for 22% of the time, Pallas kernels for 15%

profile of v14, /device:TPU:1, one launch (start us, length us, event | category | flops | bytes accessed | tf_op | source)
XLA Modules:
  0.0 139.6 jit_solution(11971300951586025096)
XLA Ops:
  7.2 0.0 copy-start
  7.2 0.0 all-gather.3.cloned.1.call-start
  7.2 0.7 all-gather.3.cloned.1.call-update
  7.9 0.0 reduce-scatter.2.cloned.1.call-start
  8.0 0.7 convert_bitcast_fusion
  8.6 1.2 fusion.9
  9.8 2.1 %collective-permute-start = (bf16[784,384]{1,0:T(8,128)(2,1)S(1)}, bf16[784,384]{1,0:T(8,128)(2,1)S(1)}, u32[]{:S(2)}, u32[]{:S(2)}) collective-permute-start(bf16[784,384]{1,0:T(8,128)(2,1)S(1)} %get-tuple-element.62), channel_id=1, source_target_pairs={{0,16},{16,0},{1,17},{17,1},{2,18},{18,2},{3,19},{19,3},{4,20},{20... | collective-permute-start | bytes 1806344 | tf_op jit(solution)/shard_map/halo_exchange/ppermute | solution.py:33
  11.9 13.4 %collective-permute-done = bf16[784,384]{1,0:T(8,128)(2,1)S(1)} collective-permute-done((bf16[784,384]{1,0:T(8,128)(2,1)S(1)}, bf16[784,384]{1,0:T(8,128)(2,1)S(1)}, u32[]{:S(2)}, u32[]{:S(2)}) %collective-permute-start) | collective-permute-done | bytes 602144 | tf_op jit(solution)/shard_map/halo_exchange/ppermute | solution.py:33
  25.4 0.0 copy-start.5
  25.4 0.8 copy-done.5
  26.2 1.2 pad_maximum_fusion.km.vm
  27.4 3.0 %collective-permute-start.2 = (bf16[2,784,384]{2,1,0:T(8,128)(2,1)}, bf16[2,784,384]{2,1,0:T(8,128)(2,1)}, u32[]{:S(2)}, u32[]{:S(2)}) collective-permute-start(bf16[2,784,384]{2,1,0:T(8,128)(2,1)} %pad_maximum_fusion.km.vm), channel_id=1, source_target_pairs={{4,0},{8,4},{12,8},{5,1},{9,5},{13,9},{6,2},{10,6},{14,10},{7,3},{... | collective-permute-start | bytes 3612680 | tf_op jit(solution)/shard_map/halo_exchange/ppermute | solution.py:23
  30.5 3.2 %collective-permute-start.1 = (bf16[2,784,384]{2,1,0:T(8,128)(2,1)}, bf16[2,784,384]{2,1,0:T(8,128)(2,1)}, u32[]{:S(2)}, u32[]{:S(2)}) collective-permute-start(bf16[2,784,384]{2,1,0:T(8,128)(2,1)} %pad_maximum_fusion.km.vm), channel_id=1, source_target_pairs={{0,4},{4,8},{8,12},{1,5},{5,9},{9,13},{2,6},{6,10},{10,14},{3,7},{... | collective-permute-start | bytes 3612680 | tf_op jit(solution)/shard_map/halo_exchange/ppermute | solution.py:23
  33.7 0.7 fusion.15
  34.4 12.1 %collective-permute-done.2.kr.vr = bf16[2,784,384]{2,1,0:T(8,128)(2,1)} collective-permute-done((bf16[2,784,384]{2,1,0:T(8,128)(2,1)}, bf16[2,784,384]{2,1,0:T(8,128)(2,1)}, u32[]{:S(2)}, u32[]{:S(2)}) %collective-permute-start.2) | collective-permute-done | bytes 1204256 | tf_op jit(solution)/shard_map/halo_exchange/ppermute | solution.py:23
  46.5 0.7 slice.47
  47.2 0.2 collective-permute-done.1.kl.vl
  47.4 0.7 slice.44
  48.1 0.6 copy.50
  48.8 10.1 %tile_attention_forward.1 = (bf16[384,384]{1,0:T(8,128)(2,1)}, f32[384,384]{1,0:T(8,128)}, f32[384,384]{1,0:T(8,128)}) custom-call(f32[1,2304]{1,0:T(1,128)} %bitcast.75, bf16[384,384]{1,0:T(8,128)(2,1)} %bitcast.71, bf16[2,784,384]{2,1,0:T(8,128)(2,1)} %collective-permute-done.1.kl.vl, bf16[2,784,384]{2,1,0:T(8,128)(2,1)} %pad_maximum_fusion.km.vm, ...), custom_call_target="tpu_custom_call" | custom-call | tf_op jit(solution)/shard_map/attention_forward/tile_attention_forward/pallas_call | solution.py:107
  58.9 0.0 copy-done
  58.9 3.8 %convolution_convert_fusion = bf16[384,3072]{1,0:T(8,128)(2,1)} fusion(bf16[384,384]{1,0:T(8,128)(2,1)} %get-tuple-element.27.o_ref, bf16[384,3072]{1,0:T(8,128)(2,1)S(1)} %copy-done), kind=kOutput, calls=%fused_computation | convolution fusion | flops 907149312 | bytes 5013504 | tf_op jit(solution)/shard_map/output_projection/dot_general | solution.py:231
  62.7 0.0 reduce-scatter.2.cloned.1.call-update
  62.7 0.0 copy-start.4
  62.7 0.0 all-gather.3.cloned.1.call-done
  62.7 4.3 %copy.40 = bf16[1,1,384,3072]{2,3,1,0:T(8,128)(2,1)} copy(bf16[1,1,384,3072]{3,2,1,0:T(8,128)(2,1)} %all-gather.3.cloned.1.call-done) | data formatting | bytes 4718592 | tf_op jit(solution)/shard_map/cotangent_gather/all_gather | solution.py:225
  67.1 0.0 copy-done.4
  67.1 3.1 %fusion.13 = f32[384,2,2,2,384]{4,0,3,2,1:T(8,128)S(1)} fusion(bf16[384,2,2,2,384]{0,4,3,2,1:T(8,128)(2,1)} %bitcast.68, bf16[384,384]{1,0:T(8,128)(2,1)S(1)} %copy-done.4), kind=kOutput, calls=%fused_computation.28 | convolution fusion | flops 905969664 | bytes 7372800 | tf_op jit(solution)/shard_map/grad_weight/dot_general | solution.py:246
  70.2 1.1 fusion.6
  71.3 0.0 copy-start.7
  71.3 1.6 %dynamic-slice_bitcast_fusion = f32[2,2,384,384]{2,3,0,1:T(8,128)} fusion(f32[384,2,2,2,384]{4,0,3,2,1:T(8,128)S(1)} %fusion.13, s32[]{:T(128)S(6)} %select_n.41), kind=kLoop, calls=%fused_computation.6 | loop fusion | bytes 4718596 | tf_op jit(solution)/shard_map/grad_weight/jit(dynamic_index_in_dim)/squeeze | solution.py:251
  72.9 1.0 copy-done.7
  73.8 2.1 %fusion.2.do_ref = bf16[384,384]{1,0:T(8,128)(2,1)} fusion(bf16[384,3072]{1,0:T(8,128)(2,1)S(1)} %copy-done, bf16[1,1,384,3072]{3,2,1,0:T(8,128)(2,1)S(1)} %copy-done.7), kind=kOutput, calls=%fused_computation.10 | convolution fusion | flops 906117120 | bytes 5013504 | tf_op jit(solution)/shard_map/grad_attended/dot_general | solution.py:237
  76.0 0.1 collective-permute-start.6
  76.1 11.3 %tile_attention_backward.1 = (bf16[384,384]{1,0:T(8,128)(2,1)}, bf16[2,768,384]{2,1,0:T(8,128)(2,1)}, f32[2,768,384]{2,1,0:T(8,128)}, bf16[2,768,384]{2,1,0:T(8,128)(2,1)}) custom-call(f32[1,2304]{1,0:T(1,128)} %bitcast.76, bf16[384,384]{1,0:T(8,128)(2,1)} %bitcast.72, bf16[2,784,384]{2,1,0:T(8,128)(2,1)} %collective-permute-done.1.kl.vl, ...), custom_call_target="tpu_custom_call" | custom-call | tf_op jit(solution)/shard_map/attention_backward/tile_attention_backward/pallas_call | solution.py:133
  87.4 2.3 %collective-permute-start.3 = (bf16[2,768,384]{2,1,0:T(8,128)(2,1)}, bf16[2,768,384]{2,1,0:T(8,128)(2,1)S(1)}, u32[]{:S(2)}, u32[]{:S(2)}) collective-permute-start(bf16[2,768,384]{2,1,0:T(8,128)(2,1)} %get-tuple-element.33), channel_id=1, source_target_pairs={{4,0},{8,4},{12,8},{5,1},{9,5},{13,9},{6,2},{10,6},{14,10},{7,3},{... | collective-permute-start | bytes 3538952 | tf_op jit(solution)/shard_map/halo_reduction/ppermute | solution.py:23
  89.7 3.9 %collective-permute-start.4 = (bf16[2,768,384]{2,1,0:T(8,128)(2,1)}, bf16[2,768,384]{2,1,0:T(8,128)(2,1)}, u32[]{:S(2)}, u32[]{:S(2)}) collective-permute-start(bf16[2,768,384]{2,1,0:T(8,128)(2,1)} %get-tuple-element.34), channel_id=1, source_target_pairs={{0,4},{4,8},{8,12},{1,5},{5,9},{9,13},{2,6},{6,10},{10,14},{3,7},{... | collective-permute-start | bytes 3538952 | tf_op jit(solution)/shard_map/halo_reduction/ppermute | solution.py:23
  93.7 0.0 copy-start.6
  93.7 0.0 collective-permute-done.6
  93.7 2.3 %convert_add_fusion = f32[2,2,384,384]{2,3,0,1:T(8,128)S(1)} fusion(f32[2,2,384,384]{2,3,0,1:T(8,128)} %dynamic-slice_bitcast_fusion, bf16[2,2,384,384]{2,3,0,1:T(8,128)(2,1)} %collective-permute-done.6), kind=kLoop, calls=%fused_computation.3 | loop fusion | flops 1179648 | bytes 5898240 | tf_op jit(solution)/shard_map/grad_weight/add | solution.py:257
  96.0 0.0 copy-start.3
  96.0 1.0 fusion.10
  97.0 0.0 collective-permute-start.7
  97.0 15.1 %collective-permute-done.3 = bf16[2,768,384]{2,1,0:T(8,128)(2,1)S(1)} collective-permute-done((bf16[2,768,384]{2,1,0:T(8,128)(2,1)}, bf16[2,768,384]{2,1,0:T(8,128)(2,1)S(1)}, u32[]{:S(2)}, u32[]{:S(2)}) %collective-permute-start.3) | collective-permute-done | bytes 1179680 | tf_op jit(solution)/shard_map/halo_reduction/ppermute | solution.py:23
  112.1 1.3 collective-permute-done.4
  113.4 0.0 copy-done.3
  113.4 0.0 copy-done.6
  113.4 1.7 %convert_add_fusion.1 = f32[2,768,384]{2,1,0:T(8,128)S(1)} fusion(bf16[2,768,384]{2,1,0:T(8,128)(2,1)} %collective-permute-done.4, f32[2,768,384]{2,1,0:T(8,128)S(1)} %copy-done.6, bf16[2,768,384]{2,1,0:T(8,128)(2,1)S(1)} %collective-permute-done.3), kind=kLoop, calls=%fused_computation.4 | loop fusion | flops 2359296 | bytes 7077888 | tf_op jit(solution)/shard_map/halo_reduction/add | solution.py:288
  115.1 0.0 copy-start.1
  115.1 1.4 %copy-done.1 = f32[2,768,384]{2,1,0:T(8,128)} copy-done((f32[2,768,384]{2,1,0:T(8,128)}, f32[2,768,384]{2,1,0:T(8,128)S(1)}, u32[]{:S(2)}) %copy-start.1) | copy-done | bytes 2359320
  116.5 0.1 fusion.11
  116.6 1.3 collective-permute-start.5
  117.9 0.0 copy-start.2
  117.9 1.8 %collective-permute-done.7 = bf16[2,384,384]{1,2,0:T(8,128)(2,1)} collective-permute-done((bf16[2,384,384]{1,2,0:T(8,128)(2,1)}, bf16[2,384,384]{1,2,0:T(8,128)(2,1)}, u32[]{:S(2)}, u32[]{:S(2)}) %collective-permute-start.7) | collective-permute-done | bytes 589856 | tf_op jit(solution)/shard_map/grad_weight/ppermute | solution.py:28
  119.7 1.6 %bitcast_add_fusion = f32[2,384,384]{1,2,0:T(8,128)S(1)} fusion(bf16[2,384,384]{1,2,0:T(8,128)(2,1)} %collective-permute-done.7, f32[2,2,384,384]{2,3,0,1:T(8,128)} %copy-done.3, s32[]{:T(128)S(6)} %select_n.44), kind=kLoop, calls=%fused_computation.18 | loop fusion | flops 589824 | bytes 2949124 | tf_op jit(solution)/shard_map/grad_weight/add | solution.py:278
  121.3 1.3 collective-permute-start.8
  122.6 4.5 %collective-permute-done.5 = bf16[768,384]{1,0:T(8,128)(2,1)S(1)} collective-permute-done((bf16[768,384]{1,0:T(8,128)(2,1)S(1)}, bf16[768,384]{1,0:T(8,128)(2,1)S(1)}, u32[]{:S(2)}, u32[]{:S(2)}) %collective-permute-start.5) | collective-permute-done | bytes 589856 | tf_op jit(solution)/shard_map/halo_reduction/ppermute | solution.py:33
  127.2 0.0 copy-done.2
  127.2 0.1 fusion.8
  127.3 0.9 slice_bitcast_fusion.1
  128.2 3.5 %collective-permute-done.8 = bf16[384,384]{0,1:T(8,128)(2,1)S(1)} collective-permute-done((bf16[384,384]{0,1:T(8,128)(2,1)S(1)}, bf16[384,384]{0,1:T(8,128)(2,1)S(1)}, u32[]{:S(2)}, u32[]{:S(2)}) %collective-permute-start.8) | collective-permute-done | bytes 294944 | tf_op jit(solution)/shard_map/grad_weight/ppermute | solution.py:28
  131.7 0.1 bitcast_add_fusion.1
  131.7 1.1 copy.43
  132.8 0.0 reduce-scatter.2.cloned.1.call-done
  (5 shorter events, 0.1 us)
Async XLA Ops:
  7.2 51.7 %copy-start = (bf16[384,3072]{1,0:T(8,128)(2,1)S(1)}, bf16[384,3072]{1,0:T(8,128)(2,1)}, u32[]{:S(2)}) copy-start(bf16[384,3072]{1,0:T(8,128)(2,1)} %param.12) | copy-start | bytes 7077892
  7.2 55.5 %all-gather.3.cloned.1.call-start = ((), (), s32[]{:S(2)}) async-start(), calls=%async_computation.2 | async-start | bytes 2949120 | tf_op jit(solution)/shard_map/cotangent_gather/all_gather | solution.py:225
  7.9 124.9 %reduce-scatter.2.cloned.1.call-start = ((), (), s32[]{:S(2)}) async-start(), calls=%async_computation.1 | async-start | bytes 2949120 | tf_op jit(solution)/shard_map/output_projection/reduce_scatter | solution.py:232
  9.8 15.6 %collective-permute-start = (bf16[784,384]{1,0:T(8,128)(2,1)S(1)}, bf16[784,384]{1,0:T(8,128)(2,1)S(1)}, u32[]{:S(2)}, u32[]{:S(2)}) collective-permute-start(bf16[784,384]{1,0:T(8,128)(2,1)S(1)} %get-tuple-element.62), channel_id=1, source_target_pairs={{0,16},{16,0},{1,17},{17,1},{2,18},{18,2},{3,19},{19,3},{4,20},{20... | collective-permute-start | bytes 1806344 | tf_op jit(solution)/shard_map/halo_exchange/ppermute | solution.py:33
  25.4 0.8 copy-start.5
  27.4 19.1 %collective-permute-start.2 = (bf16[2,784,384]{2,1,0:T(8,128)(2,1)}, bf16[2,784,384]{2,1,0:T(8,128)(2,1)}, u32[]{:S(2)}, u32[]{:S(2)}) collective-permute-start(bf16[2,784,384]{2,1,0:T(8,128)(2,1)} %pad_maximum_fusion.km.vm), channel_id=1, source_target_pairs={{4,0},{8,4},{12,8},{5,1},{9,5},{13,9},{6,2},{10,6},{14,10},{7,3},{... | collective-permute-start | bytes 3612680 | tf_op jit(solution)/shard_map/halo_exchange/ppermute | solution.py:23
  30.5 17.0 %collective-permute-start.1 = (bf16[2,784,384]{2,1,0:T(8,128)(2,1)}, bf16[2,784,384]{2,1,0:T(8,128)(2,1)}, u32[]{:S(2)}, u32[]{:S(2)}) collective-permute-start(bf16[2,784,384]{2,1,0:T(8,128)(2,1)} %pad_maximum_fusion.km.vm), channel_id=1, source_target_pairs={{0,4},{4,8},{8,12},{1,5},{5,9},{9,13},{2,6},{6,10},{10,14},{3,7},{... | collective-permute-start | bytes 3612680 | tf_op jit(solution)/shard_map/halo_exchange/ppermute | solution.py:23
  62.7 4.4 %copy-start.4 = (bf16[384,384]{1,0:T(8,128)(2,1)S(1)}, bf16[384,384]{1,0:T(8,128)(2,1)}, u32[]{:S(2)}) copy-start(bf16[384,384]{1,0:T(8,128)(2,1)} %get-tuple-element.27.o_ref) | copy-start | bytes 884740
  71.3 2.5 %copy-start.7 = (bf16[1,1,384,3072]{3,2,1,0:T(8,128)(2,1)S(1)}, bf16[1,1,384,3072]{3,2,1,0:T(8,128)(2,1)}, u32[]{:S(2)}) copy-start(bf16[1,1,384,3072]{3,2,1,0:T(8,128)(2,1)} %all-gather.3.cloned.1.call-done) | copy-start | bytes 7077892
  76.0 17.7 %collective-permute-start.6 = (bf16[2,2,384,384]{2,3,0,1:T(8,128)(2,1)}, bf16[2,2,384,384]{2,3,0,1:T(8,128)(2,1)}, u32[]{:S(2)}, u32[]{:S(2)}) collective-permute-start(bf16[2,2,384,384]{2,3,0,1:T(8,128)(2,1)} %fusion.6), channel_id=1, source_target_pairs={{0,4},{4,0},{8,12},{12,8},{1,5},{5,1},{9,13},{13,9},{2,6},{6,2},{1... | collective-permute-start | bytes 3538952 | tf_op jit(solution)/shard_map/grad_weight/ppermute | solution.py:28
  87.4 24.7 %collective-permute-start.3 = (bf16[2,768,384]{2,1,0:T(8,128)(2,1)}, bf16[2,768,384]{2,1,0:T(8,128)(2,1)S(1)}, u32[]{:S(2)}, u32[]{:S(2)}) collective-permute-start(bf16[2,768,384]{2,1,0:T(8,128)(2,1)} %get-tuple-element.33), channel_id=1, source_target_pairs={{4,0},{8,4},{12,8},{5,1},{9,5},{13,9},{6,2},{10,6},{14,10},{7,3},{... | collective-permute-start | bytes 3538952 | tf_op jit(solution)/shard_map/halo_reduction/ppermute | solution.py:23
  89.7 23.7 %collective-permute-start.4 = (bf16[2,768,384]{2,1,0:T(8,128)(2,1)}, bf16[2,768,384]{2,1,0:T(8,128)(2,1)}, u32[]{:S(2)}, u32[]{:S(2)}) collective-permute-start(bf16[2,768,384]{2,1,0:T(8,128)(2,1)} %get-tuple-element.34), channel_id=1, source_target_pairs={{0,4},{4,8},{8,12},{1,5},{5,9},{9,13},{2,6},{6,10},{10,14},{3,7},{... | collective-permute-start | bytes 3538952 | tf_op jit(solution)/shard_map/halo_reduction/ppermute | solution.py:23
  93.7 19.7 %copy-start.6 = (f32[2,768,384]{2,1,0:T(8,128)S(1)}, f32[2,768,384]{2,1,0:T(8,128)}, u32[]{:S(2)}) copy-start(f32[2,768,384]{2,1,0:T(8,128)} %get-tuple-element.32) | copy-start | bytes 7077892
  96.0 17.4 %copy-start.3 = (f32[2,2,384,384]{2,3,0,1:T(8,128)}, f32[2,2,384,384]{2,3,0,1:T(8,128)S(1)}, u32[]{:S(2)}) copy-start(f32[2,2,384,384]{2,3,0,1:T(8,128)S(1)} %convert_add_fusion) | copy-start | bytes 7077892
  97.0 22.7 %collective-permute-start.7 = (bf16[2,384,384]{1,2,0:T(8,128)(2,1)}, bf16[2,384,384]{1,2,0:T(8,128)(2,1)}, u32[]{:S(2)}, u32[]{:S(2)}) collective-permute-start(bf16[2,384,384]{1,2,0:T(8,128)(2,1)} %fusion.10), channel_id=1, source_target_pairs={{0,8},{4,12},{8,0},{12,4},{1,9},{5,13},{9,1},{13,5},{2,10},{6,14},... | collective-permute-start | bytes 1769480 | tf_op jit(solution)/shard_map/grad_weight/ppermute | solution.py:28
  115.1 1.4 %copy-start.1 = (f32[2,768,384]{2,1,0:T(8,128)}, f32[2,768,384]{2,1,0:T(8,128)S(1)}, u32[]{:S(2)}) copy-start(f32[2,768,384]{2,1,0:T(8,128)S(1)} %convert_add_fusion.1) | copy-start | bytes 7077892
  116.6 10.6 %collective-permute-start.5 = (bf16[768,384]{1,0:T(8,128)(2,1)S(1)}, bf16[768,384]{1,0:T(8,128)(2,1)S(1)}, u32[]{:S(2)}, u32[]{:S(2)}) collective-permute-start(bf16[768,384]{1,0:T(8,128)(2,1)S(1)} %fusion.11), channel_id=1, source_target_pairs={{0,16},{16,0},{1,17},{17,1},{2,18},{18,2},{3,19},{19,3},{4,20},{20... | collective-permute-start | bytes 1769480 | tf_op jit(solution)/shard_map/halo_reduction/ppermute | solution.py:33
  117.9 9.3 %copy-start.2 = (f32[2,768,384]{2,1,0:T(8,128)S(1)}, f32[2,768,384]{2,1,0:T(8,128)}, u32[]{:S(2)}) copy-start(f32[2,768,384]{2,1,0:T(8,128)} %copy-done.1) | copy-start | bytes 7077892
  121.3 10.4 %collective-permute-start.8 = (bf16[384,384]{0,1:T(8,128)(2,1)S(1)}, bf16[384,384]{0,1:T(8,128)(2,1)S(1)}, u32[]{:S(2)}, u32[]{:S(2)}) collective-permute-start(bf16[384,384]{0,1:T(8,128)(2,1)S(1)} %fusion.12), channel_id=1, source_target_pairs={{0,16},{16,0},{1,17},{17,1},{2,18},{18,2},{3,19},{19,3},{4,20},{20... | collective-permute-start | bytes 884744 | tf_op jit(solution)/shard_map/grad_weight/ppermute | solution.py:28
Sparse Core Ops, SparseCore 0:
  9.6 52.5 all-gather.2
  65.0 47.6 reduce-scatter.1

commit v15 on v14

--- a/solution.py
+++ b/solution.py
@@ -21,6 +21,12 @@
 
 def shifted(value, axis, steps):
     return lax.ppermute(value, axis, shift_pairs(lax.axis_size(axis), steps))
+
+
+def halving_order(matrix):
+    rows = matrix.shape[1] // 8
+    blocks = matrix.reshape(matrix.shape[0], 2, 2, 2, rows)
+    return jnp.transpose(blocks, (0, 3, 2, 1, 4)).reshape(matrix.shape)
 
 
 def partner(value, axis, bit):
@@ -222,7 +228,12 @@
     mask = jnp.where(flags > 0, 0.0, MASKED / HD ** (-0.5)).astype(jnp.float32)
 
     with jax.named_scope("cotangent_gather"):
-        cot_all = lax.all_gather(out_cotangent[0, 0], "ha", axis=0, tiled=True)
+        cot_local = out_cotangent[0, 0]
+        weight_columns = out_weight
+        if lax.axis_size("fh") == 2 and lax.axis_size("wa") == 4:
+            cot_local = halving_order(cot_local)
+            weight_columns = halving_order(out_weight)
+        cot_all = lax.all_gather(cot_local, "ha", axis=0, tiled=True)
 
     with jax.named_scope("attention_forward"):
         attended, row_max, row_inverse = attention_forward(mask, q, columns)
@@ -235,18 +246,16 @@
 
     with jax.named_scope("grad_attended"):
         grad_attended = lax.dot_general(
-            cot_all, out_weight, (((1,), (1,)), ((), ())), preferred_element_type=jnp.float32
+            cot_all, weight_columns, (((1,), (1,)), ((), ())), preferred_element_type=jnp.float32
         ).astype(jnp.bfloat16)
 
     halving = lax.axis_size("fh") == 2 and lax.axis_size("wa") == 4
     with jax.named_scope("grad_weight"):
         if halving:
             rows = model_width // 8
-            cot_blocks = cot_all.reshape(-1, 2, 2, 2, rows)
             weight_blocks = lax.dot_general(
-                cot_blocks, attended, (((0,), (0,)), ((), ())), preferred_element_type=jnp.float32
-            )
-            weight_blocks = jnp.transpose(weight_blocks, (2, 1, 0, 3, 4))
+                cot_all, attended, (((0,), (0,)), ((), ())), preferred_element_type=jnp.float32
+            ).reshape(2, 2, 2, rows, attended.shape[1])
             core = lax.axis_index("wa") % 2
             weight_own = lax.dynamic_index_in_dim(weight_blocks, core, 0, keepdims=False)
             weight_sent = lax.dynamic_index_in_dim(weight_blocks, 1 - core, 0, keepdims=False)

time: 141 us -> 157 us (1.11)
  local copies, waits for them, and re-layouts: 15.4 us -> 35.3 us
  waiting for transfers between devices: 52.7 us -> 45.8 us
  matrix products: 9 us -> 13.6 us
  other arithmetic: 9.52 us -> 6.77 us
    dynamic_slice x0 -> x3, local copies, waits for them, and re-layouts: none -> 8.68 us  [the longest x2 6.02 us: body(): lax.dynamic_index_in_dim(weight_blocks, core, 0, keepdims=False)]
    reshape x0 -> x2, local copies, waits for them, and re-layouts: none -> 8.44 us  [the longest x1 7.2 us: body(): weight_blocks = lax.dot_general(cot_all, attended, (((0,), (0,)), ((), ()...]
    ppermute x4, waiting for transfers between devices: 28.6 us -> 21.9 us  [shifted(): return lax.ppermute(value, axis, shift_pairs(lax.axis_size(axis), steps))]
    unnamed x21 -> x28, local copies, waits for them, and re-layouts: 4.93 us -> 9.44 us
    all_gather x1 -> x0, local copies, waits for them, and re-layouts: 4.33 us -> none  [body(): cot_all = lax.all_gather(out_cotangent[0, 0], 'ha', axis=0, tiled=True)]
    dot_general x2, matrix products: 5.21 us -> 9.03 us  [the longest x1 5.28 us: body(): lax.dot_general(cot_all, attended, (((0,), (0,)), ((), ())), preferred_el...]
    transpose x0 -> x1, local copies, waits for them, and re-layouts: none -> 3.32 us  [halving_order(): return jnp.transpose(blocks, (0, 3, 2, 1, 4)).reshape(matrix.shape)]
    ppermute x3, waiting for transfers between devices: 5.34 us -> 8.42 us  [partner(): return lax.ppermute(value, axis, [(i, i ^ bit) for i in range(count)])]
  transfers between devices with their start and end apart: 11 -> 11, of which waited for: 8 -> 9; matrix products, arithmetic and copies ran while one was open for 22% -> 32% of each run, Pallas kernels for 15% -> 14%
where the time goes in v15:
time: 157 us; the launch traced here: 155 us
  waiting for transfers between devices  45.8 us (29%)
  local copies, waits for them, and re-layouts  35.3 us (22%)
  Pallas kernels  21.7 us (14%)
  starting transfers between devices  17.8 us (11%)
  between operations  14.3 us (9%)
  matrix products  13.6 us (9%)
  other arithmetic  6.77 us (4%)
    ppermute x4, waiting for transfers between devices, shifted(): return lax.ppermute(value, axis, shift_pairs(lax.axis_size(axis), steps))  21.9 us
    ppermute x2, waiting for transfers between devices, cyclic(): lax.ppermute(value, axis, [(i, (i + steps) % count) for i in range(count)])  15.1 us
    ppermute x4, starting transfers between devices, shifted(): return lax.ppermute(value, axis, shift_pairs(lax.axis_size(axis), steps))  12.8 us
    pallas_call x1, Pallas kernels, attention_backward(): pl.pallas_call(functools.partial(backward_kernel, scale, scale * LOG2E),...  11.6 us
    pallas_call x1, Pallas kernels, attention_forward(): pl.pallas_call(functools.partial(forward_kernel, scale * LOG2E), grid=(he...  10.1 us
    unnamed x28, local copies, waits for them, and re-layouts  9.44 us
    ppermute x3, waiting for transfers between devices, partner(): return lax.ppermute(value, axis, [(i, i ^ bit) for i in range(count)])  8.42 us
    reshape x1, local copies, waits for them, and re-layouts, body(): weight_blocks = lax.dot_general(cot_all, attended, (((0,), (0,)), ((), ()...  7.2 us
  transfers between devices with their start and end apart: 11, of which 9 were waited for; matrix products, arithmetic and copies ran while one was open for 32% of the time, Pallas kernels for 14%

profile of v15, /device:TPU:1, one launch (start us, length us, event | category | flops | bytes accessed | tf_op | source)
XLA Modules:
  0.0 155.3 jit_solution(18126439290454990838)
XLA Ops:
  7.2 0.0 copy-start.10
  7.2 0.0 copy-start.8
  7.2 0.0 copy-start.9
  7.2 0.0 all-gather.2.cloned.1.call-start
  7.2 2.3 %squeeze.49 = bf16[96,2,2,2,384]{4,3,2,1,0:T(2,128)(2,1)S(1)} reshape(bf16[1,1,96,3072]{3,2,1,0:T(8,128)(2,1)} %param.13) | data formatting | bytes 1179648 | tf_op jit(solution)/shard_map/cotangent_gather/reshape;cotangent_gather/squeeze | solution.py:28
  9.5 0.5 copy.50
  10.0 1.2 reshape.81
  11.2 0.0 all-gather.2.cloned.1.call-update
  11.3 0.0 reduce-scatter.2.cloned.1.call-start
  11.3 0.0 copy-done.10
  11.3 0.0 copy-done.8
  11.3 0.0 copy-done.9
  11.3 0.1 fusion.3
  11.5 2.1 %collective-permute-start = (bf16[784,384]{1,0:T(8,128)(2,1)S(1)}, bf16[784,384]{1,0:T(8,128)(2,1)S(1)}, u32[]{:S(2)}, u32[]{:S(2)}) collective-permute-start(bf16[784,384]{1,0:T(8,128)(2,1)S(1)} %get-tuple-element.37), channel_id=1, source_target_pairs={{0,16},{16,0},{1,17},{17,1},{2,18},{18,2},{3,19},{19,3},{4,20},{20... | collective-permute-start | bytes 1806344 | tf_op jit(solution)/shard_map/halo_exchange/ppermute | solution.py:39
  13.6 13.4 %collective-permute-done = bf16[784,384]{1,0:T(8,128)(2,1)S(1)} collective-permute-done((bf16[784,384]{1,0:T(8,128)(2,1)S(1)}, bf16[784,384]{1,0:T(8,128)(2,1)S(1)}, u32[]{:S(2)}, u32[]{:S(2)}) %collective-permute-start) | collective-permute-done | bytes 602144 | tf_op jit(solution)/shard_map/halo_exchange/ppermute | solution.py:39
  27.0 0.1 pad_maximum_fusion.km.vm
  27.2 0.7 copy-done.5
  27.9 3.0 %collective-permute-start.2 = (bf16[2,784,384]{2,1,0:T(8,128)(2,1)S(1)}, bf16[2,784,384]{2,1,0:T(8,128)(2,1)S(1)}, u32[]{:S(2)}, u32[]{:S(2)}) collective-permute-start(bf16[2,784,384]{2,1,0:T(8,128)(2,1)S(1)} %pad_maximum_fusion.km.vm), channel_id=1, source_target_pairs={{4,0},{8,4},{12,8},{5,1},{9,5},{13,9},{6,2},{10,6},{14,10},{7,3},{... | collective-permute-start | bytes 3612680 | tf_op jit(solution)/shard_map/halo_exchange/ppermute | solution.py:23
  30.9 3.4 %collective-permute-start.1 = (bf16[2,784,384]{2,1,0:T(8,128)(2,1)S(1)}, bf16[2,784,384]{2,1,0:T(8,128)(2,1)}, u32[]{:S(2)}, u32[]{:S(2)}) collective-permute-start(bf16[2,784,384]{2,1,0:T(8,128)(2,1)S(1)} %pad_maximum_fusion.km.vm), channel_id=1, source_target_pairs={{0,4},{4,8},{8,12},{1,5},{5,9},{9,13},{2,6},{6,10},{10,14},{3,7},{... | collective-permute-start | bytes 3612680 | tf_op jit(solution)/shard_map/halo_exchange/ppermute | solution.py:23
  34.3 4.3 %copy.39 = bf16[384,3072]{0,1:T(8,128)(2,1)} copy(bf16[384,3072]{1,0:T(8,128)(2,1)} %param.12) | data formatting | bytes 4718592 | tf_op args[4]
  38.6 0.0 copy-done
  38.6 3.3 %copy.40 = bf16[384,2,2,2,384]{0,4,3,2,1:T(8,128)(2,1)} copy(bf16[384,2,2,2,384]{0,4,1,2,3:T(8,128)(2,1)} %bitcast.66) | data formatting | bytes 4718592 | tf_op jit(solution)/shard_map/cotangent_gather/transpose | solution.py:29
  41.9 0.7 fusion.7
  42.6 4.1 %collective-permute-done.2.kr.vr = bf16[2,784,384]{2,1,0:T(8,128)(2,1)S(1)} collective-permute-done((bf16[2,784,384]{2,1,0:T(8,128)(2,1)S(1)}, bf16[2,784,384]{2,1,0:T(8,128)(2,1)S(1)}, u32[]{:S(2)}, u32[]{:S(2)}) %collective-permute-start.2) | collective-permute-done | bytes 1204256 | tf_op jit(solution)/shard_map/halo_exchange/ppermute | solution.py:23
  46.8 0.8 collective-permute-done.1.kl.vl
  47.5 0.7 slice.44
  48.2 0.6 copy.45
  48.9 0.0 copy-done.1
  48.9 10.1 %tile_attention_forward.1 = (bf16[384,384]{1,0:T(8,128)(2,1)}, f32[384,384]{1,0:T(8,128)}, f32[384,384]{1,0:T(8,128)}) custom-call(f32[1,2304]{1,0:T(1,128)} %bitcast.76, bf16[384,384]{1,0:T(8,128)(2,1)} %bitcast.72, bf16[2,784,384]{2,1,0:T(8,128)(2,1)} %collective-permute-done.1.kl.vl, bf16[2,784,384]{2,1,0:T(8,128)(2,1)} %copy-done, ...), custom_call_target="tpu_custom_call" | custom-call | tf_op jit(solution)/shard_map/attention_forward/tile_attention_forward/pallas_call | solution.py:113
  59.0 4.6 %convolution_convert_fusion = bf16[384,3072]{1,0:T(8,128)(2,1)} fusion(bf16[384,384]{1,0:T(8,128)(2,1)} %get-tuple-element.27.o_ref, bf16[384,3072]{1,0:T(8,128)(2,1)} %param.12), kind=kOutput, calls=%fused_computation.1 | convolution fusion | flops 907149312 | bytes 5013504 | tf_op jit(solution)/shard_map/output_projection/dot_general | solution.py:242
  63.6 0.0 reduce-scatter.2.cloned.1.call-update
  63.6 0.4 all-gather.2.cloned.1.call-done
  63.9 0.6 copy-done.4
  64.5 5.3 %convolution_bitcast_fusion = f32[3072,384]{0,1:T(8,128)} fusion(bf16[384,384]{1,0:T(8,128)(2,1)S(1)} %copy-done.4, bf16[384,3072]{1,0:T(8,128)(2,1)} %all-gather.2.cloned.1.call-done), kind=kOutput, calls=%fused_computation | convolution fusion | flops 905969664 | bytes 7372800 | tf_op jit(solution)/shard_map/grad_weight/dot_general | solution.py:256
  69.8 7.2 %reshape.82 = f32[2,2,2,384,384]{3,2,1,0,4:T(2,128)} reshape(f32[3072,384]{0,1:T(8,128)} %convolution_bitcast_fusion) | data formatting | bytes 9437184 | tf_op jit(solution)/shard_map/grad_weight/reshape | solution.py:258
  77.0 2.5 %constant_dynamic-slice_fusion.1 = f32[1,2,2,384,384]{3,2,1,0,4:T(2,128)S(1)} fusion(f32[2,2,2,384,384]{3,2,1,0,4:T(2,128)} %reshape.82, s32[]{:T(128)S(6)} %select_n.41), kind=kLoop, calls=%fused_computation.32 | loop fusion | bytes 4718596 | tf_op jit(solution)/shard_map/grad_weight/jit(dynamic_index_in_dim)/dynamic_slice | solution.py:260
  79.5 3.5 %copy.37 = f32[1,2,2,384,384]{4,3,2,1,0:T(8,128)} copy(f32[1,2,2,384,384]{3,2,1,0,4:T(2,128)S(1)} %constant_dynamic-slice_fusion.1) | data formatting | bytes 4718592 | tf_op jit(solution)/shard_map/grad_weight/jit(dynamic_index_in_dim)/dynamic_slice | solution.py:260
  83.0 2.7 %constant_dynamic-slice_fusion = bf16[1,2,2,384,384]{3,2,1,0,4:T(2,128)(2,1)S(1)} fusion(f32[2,2,2,384,384]{3,2,1,0,4:T(2,128)} %reshape.82, s32[]{:T(128)S(6)} %select_n.42), kind=kLoop, calls=%fused_computation.31 | loop fusion | bytes 2359300 | tf_op jit(solution)/shard_map/grad_weight/jit(dynamic_index_in_dim)/dynamic_slice | solution.py:261
  85.7 3.2 %copy.44 = bf16[1,2,2,384,384]{4,3,2,1,0:T(8,128)(2,1)} copy(bf16[1,2,2,384,384]{3,2,1,0,4:T(2,128)(2,1)S(1)} %constant_dynamic-slice_fusion) | data formatting | bytes 2359296
  88.9 0.0 copy-done.6
  88.9 3.8 %convolution_convert_fusion.1.do_ref = bf16[384,384]{1,0:T(8,128)(2,1)} fusion(bf16[384,3072]{1,0:T(8,128)(2,1)S(1)} %copy-done.6, bf16[384,3072]{0,1:T(8,128)(2,1)} %bitcast.70), kind=kOutput, calls=%fused_computation.7 | convolution fusion | flops 906117120 | bytes 5013504 | tf_op jit(solution)/shard_map/grad_attended/dot_general | solution.py:248
  92.6 0.1 collective-permute-start.6
  92.8 11.6 %tile_attention_backward.1 = (bf16[384,384]{1,0:T(8,128)(2,1)}, bf16[2,768,384]{2,1,0:T(8,128)(2,1)}, f32[2,768,384]{2,1,0:T(8,128)}, bf16[2,768,384]{2,1,0:T(8,128)(2,1)}) custom-call(f32[1,2304]{1,0:T(1,128)} %bitcast.77, bf16[384,384]{1,0:T(8,128)(2,1)} %bitcast.73, bf16[2,784,384]{2,1,0:T(8,128)(2,1)} %collective-permute-done.1.kl.vl, ...), custom_call_target="tpu_custom_call" | custom-call | tf_op jit(solution)/shard_map/attention_backward/tile_attention_backward/pallas_call | solution.py:139
  104.4 2.3 %collective-permute-start.3 = (bf16[2,768,384]{2,1,0:T(8,128)(2,1)}, bf16[2,768,384]{2,1,0:T(8,128)(2,1)S(1)}, u32[]{:S(2)}, u32[]{:S(2)}) collective-permute-start(bf16[2,768,384]{2,1,0:T(8,128)(2,1)} %get-tuple-element.33), channel_id=1, source_target_pairs={{4,0},{8,4},{12,8},{5,1},{9,5},{13,9},{6,2},{10,6},{14,10},{7,3},{... | collective-permute-start | bytes 3538952 | tf_op jit(solution)/shard_map/halo_reduction/ppermute | solution.py:23
  106.7 4.1 %collective-permute-start.4 = (bf16[2,768,384]{2,1,0:T(8,128)(2,1)}, bf16[2,768,384]{2,1,0:T(8,128)(2,1)}, u32[]{:S(2)}, u32[]{:S(2)}) collective-permute-start(bf16[2,768,384]{2,1,0:T(8,128)(2,1)} %get-tuple-element.34), channel_id=1, source_target_pairs={{0,4},{4,8},{8,12},{1,5},{5,9},{9,13},{2,6},{6,10},{10,14},{3,7},{... | collective-permute-start | bytes 3538952 | tf_op jit(solution)/shard_map/halo_reduction/ppermute | solution.py:23
  110.8 0.0 copy-start.7
  110.8 0.0 collective-permute-done.6
  110.8 1.6 %convert_add_fusion = f32[2,2,384,384]{3,2,1,0:T(8,128)S(1)} fusion(f32[2,2,384,384]{3,2,1,0:T(8,128)S(1)} %bitcast.67, bf16[2,2,384,384]{3,2,1,0:T(8,128)(2,1)} %collective-permute-done.6), kind=kLoop, calls=%fused_computation.2 | loop fusion | flops 1179648 | bytes 5898240 | tf_op jit(solution)/shard_map/grad_weight/add | solution.py:266
  112.4 1.0 fusion.4
  113.4 0.0 collective-permute-start.7
  113.4 15.8 %collective-permute-done.3 = bf16[2,768,384]{2,1,0:T(8,128)(2,1)S(1)} collective-permute-done((bf16[2,768,384]{2,1,0:T(8,128)(2,1)}, bf16[2,768,384]{2,1,0:T(8,128)(2,1)S(1)}, u32[]{:S(2)}, u32[]{:S(2)}) %collective-permute-start.3) | collective-permute-done | bytes 1179680 | tf_op jit(solution)/shard_map/halo_reduction/ppermute | solution.py:23
  129.2 1.3 collective-permute-done.4
  130.5 0.0 copy-done.3
  130.5 1.7 %convert_add_fusion.1 = f32[2,768,384]{2,1,0:T(8,128)S(1)} fusion(bf16[2,768,384]{2,1,0:T(8,128)(2,1)} %collective-permute-done.4, f32[2,768,384]{2,1,0:T(8,128)S(1)} %copy-done.7, bf16[2,768,384]{2,1,0:T(8,128)(2,1)S(1)} %collective-permute-done.3), kind=kLoop, calls=%fused_computation.3 | loop fusion | flops 2359296 | bytes 7077888 | tf_op jit(solution)/shard_map/halo_reduction/add | solution.py:297
  132.2 0.1 fusion.5
  132.3 1.3 collective-permute-start.5
  133.6 3.3 %collective-permute-done.7 = bf16[2,384,384]{2,1,0:T(8,128)(2,1)} collective-permute-done((bf16[2,384,384]{2,1,0:T(8,128)(2,1)}, bf16[2,384,384]{2,1,0:T(8,128)(2,1)}, u32[]{:S(2)}, u32[]{:S(2)}) %collective-permute-start.7) | collective-permute-done | bytes 589856 | tf_op jit(solution)/shard_map/grad_weight/ppermute | solution.py:34
  136.8 1.6 %bitcast_add_fusion = f32[2,384,384]{2,1,0:T(8,128)S(1)} fusion(bf16[2,384,384]{2,1,0:T(8,128)(2,1)} %collective-permute-done.7, f32[2,2,384,384]{3,2,1,0:T(8,128)} %copy-done.3, s32[]{:T(128)S(6)} %select_n.44), kind=kLoop, calls=%fused_computation.14 | loop fusion | flops 589824 | bytes 2949124 | tf_op jit(solution)/shard_map/grad_weight/add | solution.py:287
  138.5 1.3 collective-permute-start.8
  139.8 1.7 %collective-permute-done.5 = bf16[768,384]{1,0:T(8,128)(2,1)S(1)} collective-permute-done((bf16[768,384]{1,0:T(8,128)(2,1)S(1)}, bf16[768,384]{1,0:T(8,128)(2,1)S(1)}, u32[]{:S(2)}, u32[]{:S(2)}) %collective-permute-start.5) | collective-permute-done | bytes 589856 | tf_op jit(solution)/shard_map/halo_reduction/ppermute | solution.py:39
  141.4 0.1 fusion.2
  141.6 0.9 slice_bitcast_fusion.1
  142.4 5.1 %collective-permute-done.8 = bf16[384,384]{1,0:T(8,128)(2,1)S(1)} collective-permute-done((bf16[384,384]{1,0:T(8,128)(2,1)S(1)}, bf16[384,384]{1,0:T(8,128)(2,1)S(1)}, u32[]{:S(2)}, u32[]{:S(2)}) %collective-permute-start.8) | collective-permute-done | bytes 294944 | tf_op jit(solution)/shard_map/grad_weight/ppermute | solution.py:34
  147.6 0.9 bitcast_add_fusion.1
  (17 shorter events, 0.1 us)
Async XLA Ops:
  7.2 4.1 %copy-start.10 = (s32[1,1,384]{2,1,0:T(1,128)S(1)}, s32[1,1,384]{2,1,0:T(1,128)}, u32[]{:S(2)}) copy-start(s32[1,1,384]{2,1,0:T(1,128)} %param.11) | copy-start | bytes 4612
  7.2 4.1 %copy-start.8 = (bf16[1,1,384,384]{3,2,1,0:T(8,128)(2,1)S(1)}, bf16[1,1,384,384]{3,2,1,0:T(8,128)(2,1)}, u32[]{:S(2)}) copy-start(bf16[1,1,384,384]{3,2,1,0:T(8,128)(2,1)} %param.10) | copy-start | bytes 884740
  7.2 4.1 %copy-start.9 = (bf16[1,1,384,384]{3,2,1,0:T(8,128)(2,1)S(1)}, bf16[1,1,384,384]{3,2,1,0:T(8,128)(2,1)}, u32[]{:S(2)}) copy-start(bf16[1,1,384,384]{3,2,1,0:T(8,128)(2,1)} %param.9) | copy-start | bytes 884740
  7.2 56.7 %all-gather.2.cloned.1.call-start = ((), (), s32[]{:S(2)}) async-start(), calls=%async_computation.2 | async-start | bytes 2949120 | tf_op jit(solution)/shard_map/cotangent_gather/all_gather | solution.py:236
  11.3 137.2 %reduce-scatter.2.cloned.1.call-start = ((), (), s32[]{:S(2)}) async-start(), calls=%async_computation.1 | async-start | bytes 2949120 | tf_op jit(solution)/shard_map/output_projection/reduce_scatter | solution.py:243
  11.5 15.6 %collective-permute-start = (bf16[784,384]{1,0:T(8,128)(2,1)S(1)}, bf16[784,384]{1,0:T(8,128)(2,1)S(1)}, u32[]{:S(2)}, u32[]{:S(2)}) collective-permute-start(bf16[784,384]{1,0:T(8,128)(2,1)S(1)} %get-tuple-element.37), channel_id=1, source_target_pairs={{0,16},{16,0},{1,17},{17,1},{2,18},{18,2},{3,19},{19,3},{4,20},{20... | collective-permute-start | bytes 1806344 | tf_op jit(solution)/shard_map/halo_exchange/ppermute | solution.py:39
  27.0 0.8 copy-start.5
  27.8 10.8 %copy-start = (bf16[2,784,384]{2,1,0:T(8,128)(2,1)}, bf16[2,784,384]{2,1,0:T(8,128)(2,1)S(1)}, u32[]{:S(2)}) copy-start(bf16[2,784,384]{2,1,0:T(8,128)(2,1)S(1)} %pad_maximum_fusion.km.vm) | copy-start | bytes 3612676
  27.9 18.9 %collective-permute-start.2 = (bf16[2,784,384]{2,1,0:T(8,128)(2,1)S(1)}, bf16[2,784,384]{2,1,0:T(8,128)(2,1)S(1)}, u32[]{:S(2)}, u32[]{:S(2)}) collective-permute-start(bf16[2,784,384]{2,1,0:T(8,128)(2,1)S(1)} %pad_maximum_fusion.km.vm), channel_id=1, source_target_pairs={{4,0},{8,4},{12,8},{5,1},{9,5},{13,9},{6,2},{10,6},{14,10},{7,3},{... | collective-permute-start | bytes 3612680 | tf_op jit(solution)/shard_map/halo_exchange/ppermute | solution.py:23
  30.9 16.6 %collective-permute-start.1 = (bf16[2,784,384]{2,1,0:T(8,128)(2,1)S(1)}, bf16[2,784,384]{2,1,0:T(8,128)(2,1)}, u32[]{:S(2)}, u32[]{:S(2)}) collective-permute-start(bf16[2,784,384]{2,1,0:T(8,128)(2,1)S(1)} %pad_maximum_fusion.km.vm), channel_id=1, source_target_pairs={{0,4},{4,8},{8,12},{1,5},{5,9},{9,13},{2,6},{6,10},{10,14},{3,7},{... | collective-permute-start | bytes 3612680 | tf_op jit(solution)/shard_map/halo_exchange/ppermute | solution.py:23
  46.7 2.1 %copy-start.1 = (bf16[2,784,384]{2,1,0:T(8,128)(2,1)}, bf16[2,784,384]{2,1,0:T(8,128)(2,1)S(1)}, u32[]{:S(2)}) copy-start(bf16[2,784,384]{2,1,0:T(8,128)(2,1)S(1)} %collective-permute-done.2.kr.vr) | copy-start | bytes 3612676
  63.6 1.0 copy-start.4
  83.0 5.9 %copy-start.6 = (bf16[384,3072]{1,0:T(8,128)(2,1)S(1)}, bf16[384,3072]{1,0:T(8,128)(2,1)}, u32[]{:S(2)}) copy-start(bf16[384,3072]{1,0:T(8,128)(2,1)} %all-gather.2.cloned.1.call-done) | copy-start | bytes 7077892
  92.6 18.1 %collective-permute-start.6 = (bf16[2,2,384,384]{3,2,1,0:T(8,128)(2,1)}, bf16[2,2,384,384]{3,2,1,0:T(8,128)(2,1)}, u32[]{:S(2)}, u32[]{:S(2)}) collective-permute-start(bf16[2,2,384,384]{3,2,1,0:T(8,128)(2,1)} %bitcast.55), channel_id=1, source_target_pairs={{0,4},{4,0},{8,12},{12,8},{1,5},{5,1},{9,13},{13,9},{2,6},{6,2},{1... | collective-permute-start | bytes 3538952 | tf_op jit(solution)/shard_map/grad_weight/ppermute | solution.py:34
  92.8 18.0 %copy-start.2 = (f32[1,2,2,384,384]{4,3,2,1,0:T(8,128)S(1)}, f32[1,2,2,384,384]{4,3,2,1,0:T(8,128)}, u32[]{:S(2)}) copy-start(f32[1,2,2,384,384]{4,3,2,1,0:T(8,128)} %copy.37) | copy-start | bytes 7077892
  104.4 24.8 %collective-permute-start.3 = (bf16[2,768,384]{2,1,0:T(8,128)(2,1)}, bf16[2,768,384]{2,1,0:T(8,128)(2,1)S(1)}, u32[]{:S(2)}, u32[]{:S(2)}) collective-permute-start(bf16[2,768,384]{2,1,0:T(8,128)(2,1)} %get-tuple-element.33), channel_id=1, source_target_pairs={{4,0},{8,4},{12,8},{5,1},{9,5},{13,9},{6,2},{10,6},{14,10},{7,3},{... | collective-permute-start | bytes 3538952 | tf_op jit(solution)/shard_map/halo_reduction/ppermute | solution.py:23
  106.7 23.8 %collective-permute-start.4 = (bf16[2,768,384]{2,1,0:T(8,128)(2,1)}, bf16[2,768,384]{2,1,0:T(8,128)(2,1)}, u32[]{:S(2)}, u32[]{:S(2)}) collective-permute-start(bf16[2,768,384]{2,1,0:T(8,128)(2,1)} %get-tuple-element.34), channel_id=1, source_target_pairs={{0,4},{4,8},{8,12},{1,5},{5,9},{9,13},{2,6},{6,10},{10,14},{3,7},{... | collective-permute-start | bytes 3538952 | tf_op jit(solution)/shard_map/halo_reduction/ppermute | solution.py:23
  110.8 19.7 %copy-start.7 = (f32[2,768,384]{2,1,0:T(8,128)S(1)}, f32[2,768,384]{2,1,0:T(8,128)}, u32[]{:S(2)}) copy-start(f32[2,768,384]{2,1,0:T(8,128)} %get-tuple-element.32) | copy-start | bytes 7077892
  112.4 18.1 %copy-start.3 = (f32[2,2,384,384]{3,2,1,0:T(8,128)}, f32[2,2,384,384]{3,2,1,0:T(8,128)S(1)}, u32[]{:S(2)}) copy-start(f32[2,2,384,384]{3,2,1,0:T(8,128)S(1)} %convert_add_fusion) | copy-start | bytes 7077892
  113.4 23.4 %collective-permute-start.7 = (bf16[2,384,384]{2,1,0:T(8,128)(2,1)}, bf16[2,384,384]{2,1,0:T(8,128)(2,1)}, u32[]{:S(2)}, u32[]{:S(2)}) collective-permute-start(bf16[2,384,384]{2,1,0:T(8,128)(2,1)} %fusion.4), channel_id=1, source_target_pairs={{0,8},{4,12},{8,0},{12,4},{1,9},{5,13},{9,1},{13,5},{2,10},{6,14},... | collective-permute-start | bytes 1769480 | tf_op jit(solution)/shard_map/grad_weight/ppermute | solution.py:34
  132.3 9.2 %collective-permute-start.5 = (bf16[768,384]{1,0:T(8,128)(2,1)S(1)}, bf16[768,384]{1,0:T(8,128)(2,1)S(1)}, u32[]{:S(2)}, u32[]{:S(2)}) collective-permute-start(bf16[768,384]{1,0:T(8,128)(2,1)S(1)} %fusion.5), channel_id=1, source_target_pairs={{0,16},{16,0},{1,17},{17,1},{2,18},{18,2},{3,19},{19,3},{4,20},{20... | collective-permute-start | bytes 1769480 | tf_op jit(solution)/shard_map/halo_reduction/ppermute | solution.py:39
  138.5 9.1 %collective-permute-start.8 = (bf16[384,384]{1,0:T(8,128)(2,1)S(1)}, bf16[384,384]{1,0:T(8,128)(2,1)S(1)}, u32[]{:S(2)}, u32[]{:S(2)}) collective-permute-start(bf16[384,384]{1,0:T(8,128)(2,1)S(1)} %fusion.6), channel_id=1, source_target_pairs={{0,16},{16,0},{1,17},{17,1},{2,18},{18,2},{3,19},{19,3},{4,20},{20... | collective-permute-start | bytes 884744 | tf_op jit(solution)/shard_map/grad_weight/ppermute | solution.py:34
Sparse Core Ops, SparseCore 0:
  11.4 52.5 all-gather.1
  66.8 46.8 reduce-scatter.1

commit v16 on v14

--- a/solution.py
+++ b/solution.py
@@ -246,7 +246,7 @@
             weight_blocks = lax.dot_general(
                 cot_blocks, attended, (((0,), (0,)), ((), ())), preferred_element_type=jnp.float32
             )
-            weight_blocks = jnp.transpose(weight_blocks, (2, 1, 0, 3, 4))
+            weight_blocks = jnp.transpose(weight_blocks, (2, 0, 1, 3, 4))
             core = lax.axis_index("wa") % 2
             weight_own = lax.dynamic_index_in_dim(weight_blocks, core, 0, keepdims=False)
             weight_sent = lax.dynamic_index_in_dim(weight_blocks, 1 - core, 0, keepdims=False)
@@ -272,14 +272,14 @@
 
     with jax.named_scope("grad_weight"):
         if halving:
+            row = lax.axis_index("fh")
+            kept = lax.dynamic_index_in_dim(weight_x, row, 0, keepdims=False)
+            sent = lax.dynamic_index_in_dim(weight_x, 1 - row, 0, keepdims=False)
+            weight_f = kept + partner(sent.astype(jnp.bfloat16), "fh", 1).astype(jnp.float32)
             column = lax.axis_index("wa") // 2
-            kept = lax.dynamic_index_in_dim(weight_x, column, 0, keepdims=False)
-            sent = lax.dynamic_index_in_dim(weight_x, 1 - column, 0, keepdims=False)
-            weight_f = kept + partner(sent.astype(jnp.bfloat16), "wa", 2).astype(jnp.float32)
-            row = lax.axis_index("fh")
-            kept = lax.dynamic_index_in_dim(weight_f, row, 0, keepdims=False)
-            sent = lax.dynamic_index_in_dim(weight_f, 1 - row, 0, keepdims=False)
-            grad_weight = kept + partner(sent.astype(jnp.bfloat16), "fh", 1).astype(jnp.float32)
+            kept = lax.dynamic_index_in_dim(weight_f, column, 0, keepdims=False)
+            sent = lax.dynamic_index_in_dim(weight_f, 1 - column, 0, keepdims=False)
+            grad_weight = kept + partner(sent.astype(jnp.bfloat16), "wa", 2).astype(jnp.float32)
         else:
             grad_weight = scatter_sum(weight_rows, "wa", 0)
 

time: 141 us -> 135 us (0.957)
  waiting for transfers between devices: 52.7 us -> 46.9 us
    ppermute x4, waiting for transfers between devices: 28.6 us -> 21.1 us  [shifted(): return lax.ppermute(value, axis, shift_pairs(lax.axis_size(axis), steps))]
    ppermute x2, waiting for transfers between devices: 18 us -> 24 us  [cyclic(): lax.ppermute(value, axis, [(i, (i + steps) % count) for i in range(count)])]
    ppermute x3, waiting for transfers between devices: 5.34 us -> 1.05 us  [partner(): return lax.ppermute(value, axis, [(i, i ^ bit) for i in range(count)])]
    add x1, other arithmetic: 0.05 us -> 1.56 us  [body(): kept + partner(sent.astype(jnp.bfloat16), 'fh', 1).astype(jnp.float32)]
    add x1, other arithmetic: 1.56 us -> 0.05 us  [body(): kept + partner(sent.astype(jnp.bfloat16), 'wa', 2).astype(jnp.float32)]
  transfers between devices with their start and end apart: 11 -> 11, of which waited for: 8 -> 7; matrix products, arithmetic and copies ran while one was open for 22% -> 23% of each run, Pallas kernels for 15% -> 16%
where the time goes in v16:
time: 135 us; the launch traced here: 134 us
  waiting for transfers between devices  46.9 us (35%)
  Pallas kernels  21.4 us (16%)
  starting transfers between devices  17.4 us (13%)
  local copies, waits for them, and re-layouts  15.4 us (11%)
  between operations  14.2 us (11%)
  other arithmetic  9.52 us (7%)
  matrix products  9 us (7%)
    ppermute x2, waiting for transfers between devices, cyclic(): lax.ppermute(value, axis, [(i, (i + steps) % count) for i in range(count)])  24 us
    ppermute x4, waiting for transfers between devices, shifted(): return lax.ppermute(value, axis, shift_pairs(lax.axis_size(axis), steps))  21.1 us
    ppermute x4, starting transfers between devices, shifted(): return lax.ppermute(value, axis, shift_pairs(lax.axis_size(axis), steps))  12.5 us
    pallas_call x1, Pallas kernels, attention_backward(): pl.pallas_call(functools.partial(backward_kernel, scale, scale * LOG2E),...  11.3 us
    pallas_call x1, Pallas kernels, attention_forward(): pl.pallas_call(functools.partial(forward_kernel, scale * LOG2E), grid=(he...  10.1 us
    unnamed x21, local copies, waits for them, and re-layouts  4.93 us
    all_gather x1, local copies, waits for them, and re-layouts, body(): cot_all = lax.all_gather(out_cotangent[0, 0], 'ha', axis=0, tiled=True)  4.33 us
    dot_general x1, matrix products, body(): jnp.dot(attended, out_weight, preferred_element_type=jnp.float32)  3.79 us
  transfers between devices with their start and end apart: 11, of which 7 were waited for; matrix products, arithmetic and copies ran while one was open for 23% of the time, Pallas kernels for 16%

profile of v16, /device:TPU:1, one launch (start us, length us, event | category | flops | bytes accessed | tf_op | source)
XLA Modules:
  0.0 133.8 jit_solution(6644610993202452663)
XLA Ops:
  7.2 0.0 copy-start
  7.2 0.0 all-gather.3.cloned.1.call-start
  7.2 0.7 all-gather.3.cloned.1.call-update
  7.9 0.0 reduce-scatter.2.cloned.1.call-start
  8.0 0.7 convert_bitcast_fusion
  8.6 1.2 fusion.9
  9.8 2.1 %collective-permute-start = (bf16[784,384]{1,0:T(8,128)(2,1)S(1)}, bf16[784,384]{1,0:T(8,128)(2,1)S(1)}, u32[]{:S(2)}, u32[]{:S(2)}) collective-permute-start(bf16[784,384]{1,0:T(8,128)(2,1)S(1)} %get-tuple-element.62), channel_id=1, source_target_pairs={{0,16},{16,0},{1,17},{17,1},{2,18},{18,2},{3,19},{19,3},{4,20},{20... | collective-permute-start | bytes 1806344 | tf_op jit(solution)/shard_map/halo_exchange/ppermute | solution.py:33
  11.9 13.4 %collective-permute-done = bf16[784,384]{1,0:T(8,128)(2,1)S(1)} collective-permute-done((bf16[784,384]{1,0:T(8,128)(2,1)S(1)}, bf16[784,384]{1,0:T(8,128)(2,1)S(1)}, u32[]{:S(2)}, u32[]{:S(2)}) %collective-permute-start) | collective-permute-done | bytes 602144 | tf_op jit(solution)/shard_map/halo_exchange/ppermute | solution.py:33
  25.4 0.0 copy-start.5
  25.4 0.8 copy-done.5
  26.2 1.2 pad_maximum_fusion.km.vm
  27.4 3.0 %collective-permute-start.2 = (bf16[2,784,384]{2,1,0:T(8,128)(2,1)}, bf16[2,784,384]{2,1,0:T(8,128)(2,1)}, u32[]{:S(2)}, u32[]{:S(2)}) collective-permute-start(bf16[2,784,384]{2,1,0:T(8,128)(2,1)} %pad_maximum_fusion.km.vm), channel_id=1, source_target_pairs={{4,0},{8,4},{12,8},{5,1},{9,5},{13,9},{6,2},{10,6},{14,10},{7,3},{... | collective-permute-start | bytes 3612680 | tf_op jit(solution)/shard_map/halo_exchange/ppermute | solution.py:23
  30.5 3.2 %collective-permute-start.1 = (bf16[2,784,384]{2,1,0:T(8,128)(2,1)}, bf16[2,784,384]{2,1,0:T(8,128)(2,1)}, u32[]{:S(2)}, u32[]{:S(2)}) collective-permute-start(bf16[2,784,384]{2,1,0:T(8,128)(2,1)} %pad_maximum_fusion.km.vm), channel_id=1, source_target_pairs={{0,4},{4,8},{8,12},{1,5},{5,9},{9,13},{2,6},{6,10},{10,14},{3,7},{... | collective-permute-start | bytes 3612680 | tf_op jit(solution)/shard_map/halo_exchange/ppermute | solution.py:23
  33.7 0.7 fusion.15
  34.4 12.1 %collective-permute-done.2.kr.vr = bf16[2,784,384]{2,1,0:T(8,128)(2,1)} collective-permute-done((bf16[2,784,384]{2,1,0:T(8,128)(2,1)}, bf16[2,784,384]{2,1,0:T(8,128)(2,1)}, u32[]{:S(2)}, u32[]{:S(2)}) %collective-permute-start.2) | collective-permute-done | bytes 1204256 | tf_op jit(solution)/shard_map/halo_exchange/ppermute | solution.py:23
  46.5 0.7 slice.47
  47.2 0.2 collective-permute-done.1.kl.vl
  47.4 0.7 slice.44
  48.1 0.6 copy.50
  48.8 10.1 %tile_attention_forward.1 = (bf16[384,384]{1,0:T(8,128)(2,1)}, f32[384,384]{1,0:T(8,128)}, f32[384,384]{1,0:T(8,128)}) custom-call(f32[1,2304]{1,0:T(1,128)} %bitcast.75, bf16[384,384]{1,0:T(8,128)(2,1)} %bitcast.71, bf16[2,784,384]{2,1,0:T(8,128)(2,1)} %collective-permute-done.1.kl.vl, bf16[2,784,384]{2,1,0:T(8,128)(2,1)} %pad_maximum_fusion.km.vm, ...), custom_call_target="tpu_custom_call" | custom-call | tf_op jit(solution)/shard_map/attention_forward/tile_attention_forward/pallas_call | solution.py:107
  58.9 0.0 copy-done
  58.9 3.8 %convolution_convert_fusion = bf16[384,3072]{1,0:T(8,128)(2,1)} fusion(bf16[384,384]{1,0:T(8,128)(2,1)} %get-tuple-element.27.o_ref, bf16[384,3072]{1,0:T(8,128)(2,1)S(1)} %copy-done), kind=kOutput, calls=%fused_computation | convolution fusion | flops 907149312 | bytes 5013504 | tf_op jit(solution)/shard_map/output_projection/dot_general | solution.py:231
  62.7 0.0 reduce-scatter.2.cloned.1.call-update
  62.7 0.0 copy-start.4
  62.7 0.0 all-gather.3.cloned.1.call-done
  62.7 4.3 %copy.40 = bf16[1,1,384,3072]{2,3,1,0:T(8,128)(2,1)} copy(bf16[1,1,384,3072]{3,2,1,0:T(8,128)(2,1)} %all-gather.3.cloned.1.call-done) | data formatting | bytes 4718592 | tf_op jit(solution)/shard_map/cotangent_gather/all_gather | solution.py:225
  67.1 0.0 copy-done.4
  67.1 3.1 %fusion.13 = f32[384,2,2,2,384]{4,0,3,2,1:T(8,128)S(1)} fusion(bf16[384,2,2,2,384]{0,4,3,2,1:T(8,128)(2,1)} %bitcast.68, bf16[384,384]{1,0:T(8,128)(2,1)S(1)} %copy-done.4), kind=kOutput, calls=%fused_computation.28 | convolution fusion | flops 905969664 | bytes 7372800 | tf_op jit(solution)/shard_map/grad_weight/dot_general | solution.py:246
  70.2 1.1 fusion.6
  71.3 0.0 copy-start.7
  71.3 1.6 %dynamic-slice_bitcast_fusion = f32[2,2,384,384]{2,3,1,0:T(8,128)} fusion(f32[384,2,2,2,384]{4,0,3,2,1:T(8,128)S(1)} %fusion.13, s32[]{:T(128)S(6)} %select_n.41), kind=kLoop, calls=%fused_computation.6 | loop fusion | bytes 4718596 | tf_op jit(solution)/shard_map/grad_weight/jit(dynamic_index_in_dim)/squeeze | solution.py:251
  72.9 1.0 copy-done.7
  73.8 2.1 %fusion.2.do_ref = bf16[384,384]{1,0:T(8,128)(2,1)} fusion(bf16[384,3072]{1,0:T(8,128)(2,1)S(1)} %copy-done, bf16[1,1,384,3072]{3,2,1,0:T(8,128)(2,1)S(1)} %copy-done.7), kind=kOutput, calls=%fused_computation.10 | convolution fusion | flops 906117120 | bytes 5013504 | tf_op jit(solution)/shard_map/grad_attended/dot_general | solution.py:237
  76.0 0.1 collective-permute-start.6
  76.1 11.3 %tile_attention_backward.1 = (bf16[384,384]{1,0:T(8,128)(2,1)}, bf16[2,768,384]{2,1,0:T(8,128)(2,1)}, f32[2,768,384]{2,1,0:T(8,128)}, bf16[2,768,384]{2,1,0:T(8,128)(2,1)}) custom-call(f32[1,2304]{1,0:T(1,128)} %bitcast.76, bf16[384,384]{1,0:T(8,128)(2,1)} %bitcast.72, bf16[2,784,384]{2,1,0:T(8,128)(2,1)} %collective-permute-done.1.kl.vl, ...), custom_call_target="tpu_custom_call" | custom-call | tf_op jit(solution)/shard_map/attention_backward/tile_attention_backward/pallas_call | solution.py:133
  87.4 2.3 %collective-permute-start.3 = (bf16[2,768,384]{2,1,0:T(8,128)(2,1)}, bf16[2,768,384]{2,1,0:T(8,128)(2,1)S(1)}, u32[]{:S(2)}, u32[]{:S(2)}) collective-permute-start(bf16[2,768,384]{2,1,0:T(8,128)(2,1)} %get-tuple-element.33), channel_id=1, source_target_pairs={{4,0},{8,4},{12,8},{5,1},{9,5},{13,9},{6,2},{10,6},{14,10},{7,3},{... | collective-permute-start | bytes 3538952 | tf_op jit(solution)/shard_map/halo_reduction/ppermute | solution.py:23
  89.7 3.9 %collective-permute-start.4 = (bf16[2,768,384]{2,1,0:T(8,128)(2,1)}, bf16[2,768,384]{2,1,0:T(8,128)(2,1)}, u32[]{:S(2)}, u32[]{:S(2)}) collective-permute-start(bf16[2,768,384]{2,1,0:T(8,128)(2,1)} %get-tuple-element.34), channel_id=1, source_target_pairs={{0,4},{4,8},{8,12},{1,5},{5,9},{9,13},{2,6},{6,10},{10,14},{3,7},{... | collective-permute-start | bytes 3538952 | tf_op jit(solution)/shard_map/halo_reduction/ppermute | solution.py:23
  93.6 0.0 copy-start.6
  93.7 0.0 collective-permute-done.6
  93.7 2.4 %convert_add_fusion = f32[2,2,384,384]{2,3,1,0:T(8,128)S(1)} fusion(f32[2,2,384,384]{2,3,1,0:T(8,128)} %dynamic-slice_bitcast_fusion, bf16[2,2,384,384]{2,3,1,0:T(8,128)(2,1)} %collective-permute-done.6), kind=kLoop, calls=%fused_computation.3 | loop fusion | flops 1179648 | bytes 5898240 | tf_op jit(solution)/shard_map/grad_weight/add | solution.py:257
  96.0 0.0 copy-start.3
  96.0 1.0 fusion.10
  97.0 1.2 collective-permute-start.7
  98.2 7.9 %collective-permute-done.3 = bf16[2,768,384]{2,1,0:T(8,128)(2,1)S(1)} collective-permute-done((bf16[2,768,384]{2,1,0:T(8,128)(2,1)}, bf16[2,768,384]{2,1,0:T(8,128)(2,1)S(1)}, u32[]{:S(2)}, u32[]{:S(2)}) %collective-permute-start.3) | collective-permute-done | bytes 1179680 | tf_op jit(solution)/shard_map/halo_reduction/ppermute | solution.py:23
  106.2 0.9 collective-permute-done.4
  107.1 0.0 copy-done.3
  107.1 0.0 copy-done.6
  107.1 1.7 %convert_add_fusion.1 = f32[2,768,384]{2,1,0:T(8,128)S(1)} fusion(bf16[2,768,384]{2,1,0:T(8,128)(2,1)} %collective-permute-done.4, f32[2,768,384]{2,1,0:T(8,128)S(1)} %copy-done.6, bf16[2,768,384]{2,1,0:T(8,128)(2,1)S(1)} %collective-permute-done.3), kind=kLoop, calls=%fused_computation.4 | loop fusion | flops 2359296 | bytes 7077888 | tf_op jit(solution)/shard_map/halo_reduction/add | solution.py:288
  108.7 0.0 copy-start.1
  108.8 1.4 %copy-done.1 = f32[2,768,384]{2,1,0:T(8,128)} copy-done((f32[2,768,384]{2,1,0:T(8,128)}, f32[2,768,384]{2,1,0:T(8,128)S(1)}, u32[]{:S(2)}) %copy-start.1) | copy-done | bytes 2359320
  110.2 0.1 fusion.11
  110.2 1.3 collective-permute-start.5
  111.6 0.0 copy-start.2
  111.6 1.0 collective-permute-done.7
  112.6 1.6 %bitcast_add_fusion = f32[2,384,384]{1,2,0:T(8,128)S(1)} fusion(bf16[2,384,384]{1,2,0:T(8,128)(2,1)} %collective-permute-done.7, f32[2,2,384,384]{2,3,1,0:T(8,128)} %copy-done.3, s32[]{:T(128)S(6)} %select_n.43), kind=kLoop, calls=%fused_computation.18 | loop fusion | flops 589824 | bytes 2949124 | tf_op jit(solution)/shard_map/grad_weight/add | solution.py:278
  114.2 0.1 collective-permute-start.8
  114.3 10.6 %collective-permute-done.5 = bf16[768,384]{1,0:T(8,128)(2,1)S(1)} collective-permute-done((bf16[768,384]{1,0:T(8,128)(2,1)S(1)}, bf16[768,384]{1,0:T(8,128)(2,1)S(1)}, u32[]{:S(2)}, u32[]{:S(2)}) %collective-permute-start.5) | collective-permute-done | bytes 589856 | tf_op jit(solution)/shard_map/halo_reduction/ppermute | solution.py:33
  124.9 0.0 copy-done.2
  124.9 0.1 fusion.8
  125.0 0.9 slice_bitcast_fusion.1
  125.9 0.0 collective-permute-done.8
  125.9 0.1 bitcast_add_fusion.1
  126.0 1.1 copy.43
  127.0 0.0 reduce-scatter.2.cloned.1.call-done
  (5 shorter events, 0.1 us)
Async XLA Ops:
  7.2 51.7 %copy-start = (bf16[384,3072]{1,0:T(8,128)(2,1)S(1)}, bf16[384,3072]{1,0:T(8,128)(2,1)}, u32[]{:S(2)}) copy-start(bf16[384,3072]{1,0:T(8,128)(2,1)} %param.12) | copy-start | bytes 7077892
  7.2 55.5 %all-gather.3.cloned.1.call-start = ((), (), s32[]{:S(2)}) async-start(), calls=%async_computation.2 | async-start | bytes 2949120 | tf_op jit(solution)/shard_map/cotangent_gather/all_gather | solution.py:225
  7.9 119.1 %reduce-scatter.2.cloned.1.call-start = ((), (), s32[]{:S(2)}) async-start(), calls=%async_computation.1 | async-start | bytes 2949120 | tf_op jit(solution)/shard_map/output_projection/reduce_scatter | solution.py:232
  9.8 15.6 %collective-permute-start = (bf16[784,384]{1,0:T(8,128)(2,1)S(1)}, bf16[784,384]{1,0:T(8,128)(2,1)S(1)}, u32[]{:S(2)}, u32[]{:S(2)}) collective-permute-start(bf16[784,384]{1,0:T(8,128)(2,1)S(1)} %get-tuple-element.62), channel_id=1, source_target_pairs={{0,16},{16,0},{1,17},{17,1},{2,18},{18,2},{3,19},{19,3},{4,20},{20... | collective-permute-start | bytes 1806344 | tf_op jit(solution)/shard_map/halo_exchange/ppermute | solution.py:33
  25.4 0.8 copy-start.5
  27.4 19.1 %collective-permute-start.2 = (bf16[2,784,384]{2,1,0:T(8,128)(2,1)}, bf16[2,784,384]{2,1,0:T(8,128)(2,1)}, u32[]{:S(2)}, u32[]{:S(2)}) collective-permute-start(bf16[2,784,384]{2,1,0:T(8,128)(2,1)} %pad_maximum_fusion.km.vm), channel_id=1, source_target_pairs={{4,0},{8,4},{12,8},{5,1},{9,5},{13,9},{6,2},{10,6},{14,10},{7,3},{... | collective-permute-start | bytes 3612680 | tf_op jit(solution)/shard_map/halo_exchange/ppermute | solution.py:23
  30.5 17.0 %collective-permute-start.1 = (bf16[2,784,384]{2,1,0:T(8,128)(2,1)}, bf16[2,784,384]{2,1,0:T(8,128)(2,1)}, u32[]{:S(2)}, u32[]{:S(2)}) collective-permute-start(bf16[2,784,384]{2,1,0:T(8,128)(2,1)} %pad_maximum_fusion.km.vm), channel_id=1, source_target_pairs={{0,4},{4,8},{8,12},{1,5},{5,9},{9,13},{2,6},{6,10},{10,14},{3,7},{... | collective-permute-start | bytes 3612680 | tf_op jit(solution)/shard_map/halo_exchange/ppermute | solution.py:23
  62.7 4.4 %copy-start.4 = (bf16[384,384]{1,0:T(8,128)(2,1)S(1)}, bf16[384,384]{1,0:T(8,128)(2,1)}, u32[]{:S(2)}) copy-start(bf16[384,384]{1,0:T(8,128)(2,1)} %get-tuple-element.27.o_ref) | copy-start | bytes 884740
  71.3 2.5 %copy-start.7 = (bf16[1,1,384,3072]{3,2,1,0:T(8,128)(2,1)S(1)}, bf16[1,1,384,3072]{3,2,1,0:T(8,128)(2,1)}, u32[]{:S(2)}) copy-start(bf16[1,1,384,3072]{3,2,1,0:T(8,128)(2,1)} %all-gather.3.cloned.1.call-done) | copy-start | bytes 7077892
  76.0 17.7 %collective-permute-start.6 = (bf16[2,2,384,384]{2,3,1,0:T(8,128)(2,1)}, bf16[2,2,384,384]{2,3,1,0:T(8,128)(2,1)}, u32[]{:S(2)}, u32[]{:S(2)}) collective-permute-start(bf16[2,2,384,384]{2,3,1,0:T(8,128)(2,1)} %fusion.6), channel_id=1, source_target_pairs={{0,4},{4,0},{8,12},{12,8},{1,5},{5,1},{9,13},{13,9},{2,6},{6,2},{1... | collective-permute-start | bytes 3538952 | tf_op jit(solution)/shard_map/grad_weight/ppermute | solution.py:28
  87.4 18.8 %collective-permute-start.3 = (bf16[2,768,384]{2,1,0:T(8,128)(2,1)}, bf16[2,768,384]{2,1,0:T(8,128)(2,1)S(1)}, u32[]{:S(2)}, u32[]{:S(2)}) collective-permute-start(bf16[2,768,384]{2,1,0:T(8,128)(2,1)} %get-tuple-element.33), channel_id=1, source_target_pairs={{4,0},{8,4},{12,8},{5,1},{9,5},{13,9},{6,2},{10,6},{14,10},{7,3},{... | collective-permute-start | bytes 3538952 | tf_op jit(solution)/shard_map/halo_reduction/ppermute | solution.py:23
  89.7 17.4 %collective-permute-start.4 = (bf16[2,768,384]{2,1,0:T(8,128)(2,1)}, bf16[2,768,384]{2,1,0:T(8,128)(2,1)}, u32[]{:S(2)}, u32[]{:S(2)}) collective-permute-start(bf16[2,768,384]{2,1,0:T(8,128)(2,1)} %get-tuple-element.34), channel_id=1, source_target_pairs={{0,4},{4,8},{8,12},{1,5},{5,9},{9,13},{2,6},{6,10},{10,14},{3,7},{... | collective-permute-start | bytes 3538952 | tf_op jit(solution)/shard_map/halo_reduction/ppermute | solution.py:23
  93.6 13.4 %copy-start.6 = (f32[2,768,384]{2,1,0:T(8,128)S(1)}, f32[2,768,384]{2,1,0:T(8,128)}, u32[]{:S(2)}) copy-start(f32[2,768,384]{2,1,0:T(8,128)} %get-tuple-element.32) | copy-start | bytes 7077892
  96.0 11.1 %copy-start.3 = (f32[2,2,384,384]{2,3,1,0:T(8,128)}, f32[2,2,384,384]{2,3,1,0:T(8,128)S(1)}, u32[]{:S(2)}) copy-start(f32[2,2,384,384]{2,3,1,0:T(8,128)S(1)} %convert_add_fusion) | copy-start | bytes 7077892
  97.0 15.6 %collective-permute-start.7 = (bf16[2,384,384]{1,2,0:T(8,128)(2,1)}, bf16[2,384,384]{1,2,0:T(8,128)(2,1)}, u32[]{:S(2)}, u32[]{:S(2)}) collective-permute-start(bf16[2,384,384]{1,2,0:T(8,128)(2,1)} %fusion.10), channel_id=1, source_target_pairs={{0,16},{16,0},{1,17},{17,1},{2,18},{18,2},{3,19},{19,3},{4,20},{20... | collective-permute-start | bytes 1769480 | tf_op jit(solution)/shard_map/grad_weight/ppermute | solution.py:28
  108.7 1.4 %copy-start.1 = (f32[2,768,384]{2,1,0:T(8,128)}, f32[2,768,384]{2,1,0:T(8,128)S(1)}, u32[]{:S(2)}) copy-start(f32[2,768,384]{2,1,0:T(8,128)S(1)} %convert_add_fusion.1) | copy-start | bytes 7077892
  110.2 14.7 %collective-permute-start.5 = (bf16[768,384]{1,0:T(8,128)(2,1)S(1)}, bf16[768,384]{1,0:T(8,128)(2,1)S(1)}, u32[]{:S(2)}, u32[]{:S(2)}) collective-permute-start(bf16[768,384]{1,0:T(8,128)(2,1)S(1)} %fusion.11), channel_id=1, source_target_pairs={{0,16},{16,0},{1,17},{17,1},{2,18},{18,2},{3,19},{19,3},{4,20},{20... | collective-permute-start | bytes 1769480 | tf_op jit(solution)/shard_map/halo_reduction/ppermute | solution.py:33
  111.6 13.3 %copy-start.2 = (f32[2,768,384]{2,1,0:T(8,128)S(1)}, f32[2,768,384]{2,1,0:T(8,128)}, u32[]{:S(2)}) copy-start(f32[2,768,384]{2,1,0:T(8,128)} %copy-done.1) | copy-start | bytes 7077892
  114.2 11.7 %collective-permute-start.8 = (bf16[384,384]{0,1:T(8,128)(2,1)S(1)}, bf16[384,384]{0,1:T(8,128)(2,1)S(1)}, u32[]{:S(2)}, u32[]{:S(2)}) collective-permute-start(bf16[384,384]{0,1:T(8,128)(2,1)S(1)} %fusion.12), channel_id=1, source_target_pairs={{0,8},{4,12},{8,0},{12,4},{1,9},{5,13},{9,1},{13,5},{2,10},{6,14},... | collective-permute-start | bytes 884744 | tf_op jit(solution)/shard_map/grad_weight/ppermute | solution.py:28
Sparse Core Ops, SparseCore 0:
  9.6 52.5 all-gather.2
  65.0 47.6 reduce-scatter.1

commit v17 on v16

--- a/solution.py
+++ b/solution.py
@@ -251,9 +251,6 @@
             weight_own = lax.dynamic_index_in_dim(weight_blocks, core, 0, keepdims=False)
             weight_sent = lax.dynamic_index_in_dim(weight_blocks, 1 - core, 0, keepdims=False)
             weight_sent = weight_sent.astype(jnp.bfloat16)
-            weight_own, weight_sent, grad_attended = lax.optimization_barrier(
-                (weight_own, weight_sent, grad_attended)
-            )
             weight_x = weight_own + partner(weight_sent, "wa", 1).astype(jnp.float32)
         else:
             weight_part = lax.dot_general(

time: 135 us -> 135 us (level)
  other arithmetic: 9.52 us -> 7.82 us
  waiting for transfers between devices: 46.9 us -> 48.5 us
    unnamed x21 -> x27, local copies, waits for them, and re-layouts: 4.93 us -> 7.48 us
    another operation x2, other arithmetic: 1.92 us -> 0.14 us  [body(): column = jnp.stack([cyclic(packed, 'fh', 1), packed])]
    squeeze x1 -> x0, local copies, waits for them, and re-layouts: 1.58 us -> none  [body(): lax.dynamic_index_in_dim(weight_blocks, core, 0, keepdims=False)]
    slice x2, local copies, waits for them, and re-layouts: 1.42 us -> 0.01 us  [body(): side[:, 2 * tokens, :tokens]]
  transfers between devices with their start and end apart: 11 -> 11, of which waited for: 7 -> 8; matrix products, arithmetic and copies ran while one was open for 23% -> 19% of each run, Pallas kernels for 16% -> 16%
where the time goes in v17:
time: 135 us; the launch traced here: 133 us
  waiting for transfers between devices  48.5 us (36%)
  Pallas kernels  21.4 us (16%)
  starting transfers between devices  17.3 us (13%)
  local copies, waits for them, and re-layouts  14.8 us (11%)
  between operations  14.3 us (11%)
  matrix products  8.99 us (7%)
  other arithmetic  7.82 us (6%)
    ppermute x2, waiting for transfers between devices, cyclic(): lax.ppermute(value, axis, [(i, (i + steps) % count) for i in range(count)])  24.3 us
    ppermute x4, waiting for transfers between devices, shifted(): return lax.ppermute(value, axis, shift_pairs(lax.axis_size(axis), steps))  20.8 us
    ppermute x4, starting transfers between devices, shifted(): return lax.ppermute(value, axis, shift_pairs(lax.axis_size(axis), steps))  11.9 us
    pallas_call x1, Pallas kernels, attention_backward(): pl.pallas_call(functools.partial(backward_kernel, scale, scale * LOG2E),...  11.3 us
    pallas_call x1, Pallas kernels, attention_forward(): pl.pallas_call(functools.partial(forward_kernel, scale * LOG2E), grid=(he...  10.1 us
    unnamed x27, local copies, waits for them, and re-layouts  7.48 us
    all_gather x1, local copies, waits for them, and re-layouts, body(): cot_all = lax.all_gather(out_cotangent[0, 0], 'ha', axis=0, tiled=True)  4.28 us
    dot_general x1, matrix products, body(): jnp.dot(attended, out_weight, preferred_element_type=jnp.float32)  3.79 us
  transfers between devices with their start and end apart: 11, of which 8 were waited for; matrix products, arithmetic and copies ran while one was open for 19% of the time, Pallas kernels for 16%

profile of v17, /device:TPU:1, one launch (start us, length us, event | category | flops | bytes accessed | tf_op | source)
XLA Modules:
  0.0 133.2 jit_solution(17978411938427070722)
XLA Ops:
  7.2 0.0 copy-start
  7.2 0.0 all-gather.3.cloned.1.call-start
  7.2 0.7 all-gather.3.cloned.1.call-update
  7.9 0.0 reduce-scatter.2.cloned.1.call-start
  8.0 0.7 convert_bitcast_fusion
  8.6 1.2 fusion.9
  9.8 2.1 %collective-permute-start = (bf16[784,384]{1,0:T(8,128)(2,1)S(1)}, bf16[784,384]{1,0:T(8,128)(2,1)S(1)}, u32[]{:S(2)}, u32[]{:S(2)}) collective-permute-start(bf16[784,384]{1,0:T(8,128)(2,1)S(1)} %get-tuple-element.56), channel_id=1, source_target_pairs={{0,16},{16,0},{1,17},{17,1},{2,18},{18,2},{3,19},{19,3},{4,20},{20... | collective-permute-start | bytes 1806344 | tf_op jit(solution)/shard_map/halo_exchange/ppermute | solution.py:33
  11.9 13.4 %collective-permute-done = bf16[784,384]{1,0:T(8,128)(2,1)S(1)} collective-permute-done((bf16[784,384]{1,0:T(8,128)(2,1)S(1)}, bf16[784,384]{1,0:T(8,128)(2,1)S(1)}, u32[]{:S(2)}, u32[]{:S(2)}) %collective-permute-start) | collective-permute-done | bytes 602144 | tf_op jit(solution)/shard_map/halo_exchange/ppermute | solution.py:33
  25.4 0.1 pad_maximum_fusion.km.vm
  25.5 0.0 copy-start.1
  25.5 3.0 %collective-permute-start.2 = (bf16[2,784,384]{2,1,0:T(8,128)(2,1)S(1)}, bf16[2,784,384]{2,1,0:T(8,128)(2,1)S(1)}, u32[]{:S(2)}, u32[]{:S(2)}) collective-permute-start(bf16[2,784,384]{2,1,0:T(8,128)(2,1)S(1)} %pad_maximum_fusion.km.vm), channel_id=1, source_target_pairs={{4,0},{8,4},{12,8},{5,1},{9,5},{13,9},{6,2},{10,6},{14,10},{7,3},{... | collective-permute-start | bytes 3612680 | tf_op jit(solution)/shard_map/halo_exchange/ppermute | solution.py:23
  28.6 0.0 copy-done.1
  28.6 3.2 %collective-permute-start.1 = (bf16[2,784,384]{2,1,0:T(8,128)(2,1)S(1)}, bf16[2,784,384]{2,1,0:T(8,128)(2,1)S(1)}, u32[]{:S(2)}, u32[]{:S(2)}) collective-permute-start(bf16[2,784,384]{2,1,0:T(8,128)(2,1)S(1)} %pad_maximum_fusion.km.vm), channel_id=1, source_target_pairs={{0,4},{4,8},{8,12},{1,5},{5,9},{9,13},{2,6},{6,10},{10,14},{3,7},{... | collective-permute-start | bytes 3612680 | tf_op jit(solution)/shard_map/halo_exchange/ppermute | solution.py:23
  31.8 12.6 %collective-permute-done.2.kr.vr = bf16[2,784,384]{2,1,0:T(8,128)(2,1)S(1)} collective-permute-done((bf16[2,784,384]{2,1,0:T(8,128)(2,1)S(1)}, bf16[2,784,384]{2,1,0:T(8,128)(2,1)S(1)}, u32[]{:S(2)}, u32[]{:S(2)}) %collective-permute-start.2) | collective-permute-done | bytes 1204256 | tf_op jit(solution)/shard_map/halo_exchange/ppermute | solution.py:23
  44.4 0.0 copy-start.2
  44.4 0.8 collective-permute-done.1.kl.vl
  45.2 0.3 copy-done.2
  45.5 0.0 copy-start.3
  45.5 1.0 copy-done.3
  46.6 0.6 copy.50
  47.2 10.1 %tile_attention_forward.1 = (bf16[384,384]{1,0:T(8,128)(2,1)}, f32[384,384]{1,0:T(8,128)}, f32[384,384]{1,0:T(8,128)}) custom-call(f32[1,2304]{1,0:T(1,128)} %bitcast.75, bf16[384,384]{1,0:T(8,128)(2,1)} %bitcast.71, bf16[2,784,384]{2,1,0:T(8,128)(2,1)} %copy-done.3, bf16[2,784,384]{2,1,0:T(8,128)(2,1)} %copy-done.1, bf16[2,784,384]{2,1,0:T(8,128)(2,1)} %copy-done.2, ...), custom_call_target="tpu_custom_call" | custom-call | tf_op jit(solution)/shard_map/attention_forward/tile_attention_forward/pallas_call | solution.py:107
  57.3 0.0 copy-done
  57.3 3.8 %convolution_convert_fusion = bf16[384,3072]{1,0:T(8,128)(2,1)} fusion(bf16[384,384]{1,0:T(8,128)(2,1)} %get-tuple-element.24.o_ref, bf16[384,3072]{1,0:T(8,128)(2,1)S(1)} %copy-done), kind=kOutput, calls=%fused_computation | convolution fusion | flops 907149312 | bytes 5013504 | tf_op jit(solution)/shard_map/output_projection/dot_general | solution.py:231
  61.1 0.0 reduce-scatter.2.cloned.1.call-update
  61.1 0.0 copy-start.8
  61.1 1.0 all-gather.3.cloned.1.call-done
  62.1 4.3 %copy.40 = bf16[1,1,384,3072]{2,3,1,0:T(8,128)(2,1)} copy(bf16[1,1,384,3072]{3,2,1,0:T(8,128)(2,1)} %all-gather.3.cloned.1.call-done) | data formatting | bytes 4718592 | tf_op jit(solution)/shard_map/cotangent_gather/all_gather | solution.py:225
  66.4 0.0 copy-done.8
  66.4 3.1 %fusion.13 = f32[384,2,2,2,384]{4,0,3,2,1:T(8,128)S(1)} fusion(bf16[384,2,2,2,384]{0,4,3,2,1:T(8,128)(2,1)} %bitcast.68, bf16[384,384]{1,0:T(8,128)(2,1)S(1)} %copy-done.8), kind=kOutput, calls=%fused_computation.27 | convolution fusion | flops 905969664 | bytes 7372800 | tf_op jit(solution)/shard_map/grad_weight/dot_general | solution.py:246
  69.5 0.0 copy-start.4
  69.5 0.0 copy-start.10
  69.6 1.2 fusion.6
  70.7 0.7 collective-permute-start.6
  71.4 1.6 %copy-done.10 = bf16[1,1,384,3072]{3,2,1,0:T(8,128)(2,1)S(1)} copy-done((bf16[1,1,384,3072]{3,2,1,0:T(8,128)(2,1)S(1)}, bf16[1,1,384,3072]{3,2,1,0:T(8,128)(2,1)}, u32[]{:S(2)}) %copy-start.10) | copy-done | bytes 2359320
  73.0 2.1 %fusion.2.do_ref = bf16[384,384]{1,0:T(8,128)(2,1)} fusion(bf16[384,3072]{1,0:T(8,128)(2,1)S(1)} %copy-done, bf16[1,1,384,3072]{3,2,1,0:T(8,128)(2,1)S(1)} %copy-done.10), kind=kOutput, calls=%fused_computation.9 | convolution fusion | flops 906117120 | bytes 5013504 | tf_op jit(solution)/shard_map/grad_attended/dot_general | solution.py:237
  75.1 0.0 copy-done.4
  75.1 11.3 %tile_attention_backward.1 = (bf16[384,384]{1,0:T(8,128)(2,1)}, bf16[2,768,384]{2,1,0:T(8,128)(2,1)}, f32[2,768,384]{2,1,0:T(8,128)}, bf16[2,768,384]{2,1,0:T(8,128)(2,1)}) custom-call(f32[1,2304]{1,0:T(1,128)} %bitcast.76, bf16[384,384]{1,0:T(8,128)(2,1)} %bitcast.72, bf16[2,784,384]{2,1,0:T(8,128)(2,1)} %copy-done.3, bf16[2,784,384]{2,1,0:T(8,128)(2,1)} %copy-done.1, ...), custom_call_target="tpu_custom_call" | custom-call | tf_op jit(solution)/shard_map/attention_backward/tile_attention_backward/pallas_call | solution.py:133
  86.4 2.6 %collective-permute-start.3 = (bf16[2,768,384]{2,1,0:T(8,128)(2,1)}, bf16[2,768,384]{2,1,0:T(8,128)(2,1)S(1)}, u32[]{:S(2)}, u32[]{:S(2)}) collective-permute-start(bf16[2,768,384]{2,1,0:T(8,128)(2,1)} %get-tuple-element.29), channel_id=1, source_target_pairs={{4,0},{8,4},{12,8},{5,1},{9,5},{13,9},{6,2},{10,6},{14,10},{7,3},{... | collective-permute-start | bytes 3538952 | tf_op jit(solution)/shard_map/halo_reduction/ppermute | solution.py:23
  89.0 3.0 %collective-permute-start.4 = (bf16[2,768,384]{2,1,0:T(8,128)(2,1)}, bf16[2,768,384]{2,1,0:T(8,128)(2,1)}, u32[]{:S(2)}, u32[]{:S(2)}) collective-permute-start(bf16[2,768,384]{2,1,0:T(8,128)(2,1)} %get-tuple-element.30), channel_id=1, source_target_pairs={{0,4},{4,8},{8,12},{1,5},{5,9},{9,13},{2,6},{6,10},{10,14},{3,7},{... | collective-permute-start | bytes 3538952 | tf_op jit(solution)/shard_map/halo_reduction/ppermute | solution.py:23
  92.1 0.0 copy-start.9
  92.1 0.0 collective-permute-done.6
  92.1 2.4 %bitcast_add_fusion = f32[2,2,384,384]{2,3,1,0:T(8,128)S(1)} fusion(bf16[2,2,384,384]{2,3,1,0:T(8,128)(2,1)} %collective-permute-done.6, f32[384,2,2,2,384]{4,0,3,2,1:T(8,128)} %copy-done.4, s32[]{:T(128)S(6)} %select_n.41), kind=kLoop, calls=%fused_computation.1 | loop fusion | flops 1179648 | bytes 5898244 | tf_op jit(solution)/shard_map/grad_weight/add | solution.py:254
  94.5 0.0 copy-start.5
  94.5 1.4 %copy-done.5 = f32[2,2,384,384]{2,3,1,0:T(8,128)} copy-done((f32[2,2,384,384]{2,3,1,0:T(8,128)}, f32[2,2,384,384]{2,3,1,0:T(8,128)S(1)}, u32[]{:S(2)}) %copy-start.5) | copy-done | bytes 2359320
  96.0 0.9 fusion.10
  96.8 1.2 collective-permute-start.7
  98.0 6.6 %collective-permute-done.3 = bf16[2,768,384]{2,1,0:T(8,128)(2,1)S(1)} collective-permute-done((bf16[2,768,384]{2,1,0:T(8,128)(2,1)}, bf16[2,768,384]{2,1,0:T(8,128)(2,1)S(1)}, u32[]{:S(2)}, u32[]{:S(2)}) %collective-permute-start.3) | collective-permute-done | bytes 1179680 | tf_op jit(solution)/shard_map/halo_reduction/ppermute | solution.py:23
  104.6 0.9 collective-permute-done.4
  105.5 0.0 copy-done.9
  105.5 1.7 %convert_add_fusion = f32[2,768,384]{2,1,0:T(8,128)S(1)} fusion(bf16[2,768,384]{2,1,0:T(8,128)(2,1)} %collective-permute-done.4, f32[2,768,384]{2,1,0:T(8,128)S(1)} %copy-done.9, bf16[2,768,384]{2,1,0:T(8,128)(2,1)S(1)} %collective-permute-done.3), kind=kLoop, calls=%fused_computation.5 | loop fusion | flops 2359296 | bytes 7077888 | tf_op jit(solution)/shard_map/halo_reduction/add | solution.py:285
  107.2 0.0 copy-start.6
  107.2 1.4 %copy-done.6 = f32[2,768,384]{2,1,0:T(8,128)} copy-done((f32[2,768,384]{2,1,0:T(8,128)}, f32[2,768,384]{2,1,0:T(8,128)S(1)}, u32[]{:S(2)}) %copy-start.6) | copy-done | bytes 2359320
  108.6 0.1 fusion.11
  108.7 1.3 collective-permute-start.5
  109.9 1.7 %collective-permute-done.7 = bf16[2,384,384]{1,2,0:T(8,128)(2,1)} collective-permute-done((bf16[2,384,384]{1,2,0:T(8,128)(2,1)}, bf16[2,384,384]{1,2,0:T(8,128)(2,1)}, u32[]{:S(2)}, u32[]{:S(2)}) %collective-permute-start.7) | collective-permute-done | bytes 589856 | tf_op jit(solution)/shard_map/grad_weight/ppermute | solution.py:28
  111.7 1.6 %bitcast_add_fusion.1 = f32[2,384,384]{1,2,0:T(8,128)S(1)} fusion(bf16[2,384,384]{1,2,0:T(8,128)(2,1)} %collective-permute-done.7, f32[2,2,384,384]{2,3,1,0:T(8,128)} %copy-done.5, s32[]{:T(128)S(6)} %select_n.43), kind=kLoop, calls=%fused_computation.17 | loop fusion | flops 589824 | bytes 2949124 | tf_op jit(solution)/shard_map/grad_weight/add | solution.py:275
  113.3 0.1 collective-permute-start.8
  113.4 10.8 %collective-permute-done.5 = bf16[768,384]{1,0:T(8,128)(2,1)S(1)} collective-permute-done((bf16[768,384]{1,0:T(8,128)(2,1)S(1)}, bf16[768,384]{1,0:T(8,128)(2,1)S(1)}, u32[]{:S(2)}, u32[]{:S(2)}) %collective-permute-start.5) | collective-permute-done | bytes 589856 | tf_op jit(solution)/shard_map/halo_reduction/ppermute | solution.py:33
  124.2 0.0 copy-done.7
  124.2 0.1 fusion.8
  124.3 0.9 slice_bitcast_fusion.1
  125.2 0.0 collective-permute-done.8
  125.2 0.1 bitcast_add_fusion.2
  125.3 1.1 copy.43
  (10 shorter events, 0.1 us)
Async XLA Ops:
  7.2 50.1 %copy-start = (bf16[384,3072]{1,0:T(8,128)(2,1)S(1)}, bf16[384,3072]{1,0:T(8,128)(2,1)}, u32[]{:S(2)}) copy-start(bf16[384,3072]{1,0:T(8,128)(2,1)} %param.12) | copy-start | bytes 7077892
  7.2 55.0 %all-gather.3.cloned.1.call-start = ((), (), s32[]{:S(2)}) async-start(), calls=%async_computation.2 | async-start | bytes 2949120 | tf_op jit(solution)/shard_map/cotangent_gather/all_gather | solution.py:225
  7.9 118.4 %reduce-scatter.2.cloned.1.call-start = ((), (), s32[]{:S(2)}) async-start(), calls=%async_computation.1 | async-start | bytes 2949120 | tf_op jit(solution)/shard_map/output_projection/reduce_scatter | solution.py:232
  9.8 15.6 %collective-permute-start = (bf16[784,384]{1,0:T(8,128)(2,1)S(1)}, bf16[784,384]{1,0:T(8,128)(2,1)S(1)}, u32[]{:S(2)}, u32[]{:S(2)}) collective-permute-start(bf16[784,384]{1,0:T(8,128)(2,1)S(1)} %get-tuple-element.56), channel_id=1, source_target_pairs={{0,16},{16,0},{1,17},{17,1},{2,18},{18,2},{3,19},{19,3},{4,20},{20... | collective-permute-start | bytes 1806344 | tf_op jit(solution)/shard_map/halo_exchange/ppermute | solution.py:33
  25.5 3.1 %copy-start.1 = (bf16[2,784,384]{2,1,0:T(8,128)(2,1)}, bf16[2,784,384]{2,1,0:T(8,128)(2,1)S(1)}, u32[]{:S(2)}) copy-start(bf16[2,784,384]{2,1,0:T(8,128)(2,1)S(1)} %pad_maximum_fusion.km.vm) | copy-start | bytes 3612676
  25.5 18.9 %collective-permute-start.2 = (bf16[2,784,384]{2,1,0:T(8,128)(2,1)S(1)}, bf16[2,784,384]{2,1,0:T(8,128)(2,1)S(1)}, u32[]{:S(2)}, u32[]{:S(2)}) collective-permute-start(bf16[2,784,384]{2,1,0:T(8,128)(2,1)S(1)} %pad_maximum_fusion.km.vm), channel_id=1, source_target_pairs={{4,0},{8,4},{12,8},{5,1},{9,5},{13,9},{6,2},{10,6},{14,10},{7,3},{... | collective-permute-start | bytes 3612680 | tf_op jit(solution)/shard_map/halo_exchange/ppermute | solution.py:23
  28.6 16.6 %collective-permute-start.1 = (bf16[2,784,384]{2,1,0:T(8,128)(2,1)S(1)}, bf16[2,784,384]{2,1,0:T(8,128)(2,1)S(1)}, u32[]{:S(2)}, u32[]{:S(2)}) collective-permute-start(bf16[2,784,384]{2,1,0:T(8,128)(2,1)S(1)} %pad_maximum_fusion.km.vm), channel_id=1, source_target_pairs={{0,4},{4,8},{8,12},{1,5},{5,9},{9,13},{2,6},{6,10},{10,14},{3,7},{... | collective-permute-start | bytes 3612680 | tf_op jit(solution)/shard_map/halo_exchange/ppermute | solution.py:23
  44.4 1.1 copy-start.2
  45.5 1.1 copy-start.3
  61.1 5.3 %copy-start.8 = (bf16[384,384]{1,0:T(8,128)(2,1)S(1)}, bf16[384,384]{1,0:T(8,128)(2,1)}, u32[]{:S(2)}) copy-start(bf16[384,384]{1,0:T(8,128)(2,1)} %get-tuple-element.24.o_ref) | copy-start | bytes 884740
  69.5 5.6 %copy-start.4 = (f32[384,2,2,2,384]{4,0,3,2,1:T(8,128)}, f32[384,2,2,2,384]{4,0,3,2,1:T(8,128)S(1)}, u32[]{:S(2)}) copy-start(f32[384,2,2,2,384]{4,0,3,2,1:T(8,128)S(1)} %fusion.13) | copy-start | bytes 14155780
  69.5 3.5 %copy-start.10 = (bf16[1,1,384,3072]{3,2,1,0:T(8,128)(2,1)S(1)}, bf16[1,1,384,3072]{3,2,1,0:T(8,128)(2,1)}, u32[]{:S(2)}) copy-start(bf16[1,1,384,3072]{3,2,1,0:T(8,128)(2,1)} %all-gather.3.cloned.1.call-done) | copy-start | bytes 7077892
  70.7 21.4 %collective-permute-start.6 = (bf16[2,2,384,384]{2,3,1,0:T(8,128)(2,1)}, bf16[2,2,384,384]{2,3,1,0:T(8,128)(2,1)}, u32[]{:S(2)}, u32[]{:S(2)}) collective-permute-start(bf16[2,2,384,384]{2,3,1,0:T(8,128)(2,1)} %fusion.6), channel_id=1, source_target_pairs={{0,4},{4,0},{8,12},{12,8},{1,5},{5,1},{9,13},{13,9},{2,6},{6,2},{1... | collective-permute-start | bytes 3538952 | tf_op jit(solution)/shard_map/grad_weight/ppermute | solution.py:28
  86.4 18.2 %collective-permute-start.3 = (bf16[2,768,384]{2,1,0:T(8,128)(2,1)}, bf16[2,768,384]{2,1,0:T(8,128)(2,1)S(1)}, u32[]{:S(2)}, u32[]{:S(2)}) collective-permute-start(bf16[2,768,384]{2,1,0:T(8,128)(2,1)} %get-tuple-element.29), channel_id=1, source_target_pairs={{4,0},{8,4},{12,8},{5,1},{9,5},{13,9},{6,2},{10,6},{14,10},{7,3},{... | collective-permute-start | bytes 3538952 | tf_op jit(solution)/shard_map/halo_reduction/ppermute | solution.py:23
  89.0 16.5 %collective-permute-start.4 = (bf16[2,768,384]{2,1,0:T(8,128)(2,1)}, bf16[2,768,384]{2,1,0:T(8,128)(2,1)}, u32[]{:S(2)}, u32[]{:S(2)}) collective-permute-start(bf16[2,768,384]{2,1,0:T(8,128)(2,1)} %get-tuple-element.30), channel_id=1, source_target_pairs={{0,4},{4,8},{8,12},{1,5},{5,9},{9,13},{2,6},{6,10},{10,14},{3,7},{... | collective-permute-start | bytes 3538952 | tf_op jit(solution)/shard_map/halo_reduction/ppermute | solution.py:23
  92.1 13.4 %copy-start.9 = (f32[2,768,384]{2,1,0:T(8,128)S(1)}, f32[2,768,384]{2,1,0:T(8,128)}, u32[]{:S(2)}) copy-start(f32[2,768,384]{2,1,0:T(8,128)} %get-tuple-element.28) | copy-start | bytes 7077892
  94.5 1.4 %copy-start.5 = (f32[2,2,384,384]{2,3,1,0:T(8,128)}, f32[2,2,384,384]{2,3,1,0:T(8,128)S(1)}, u32[]{:S(2)}) copy-start(f32[2,2,384,384]{2,3,1,0:T(8,128)S(1)} %bitcast_add_fusion) | copy-start | bytes 7077892
  96.8 14.8 %collective-permute-start.7 = (bf16[2,384,384]{1,2,0:T(8,128)(2,1)}, bf16[2,384,384]{1,2,0:T(8,128)(2,1)}, u32[]{:S(2)}, u32[]{:S(2)}) collective-permute-start(bf16[2,384,384]{1,2,0:T(8,128)(2,1)} %fusion.10), channel_id=1, source_target_pairs={{0,16},{16,0},{1,17},{17,1},{2,18},{18,2},{3,19},{19,3},{4,20},{20... | collective-permute-start | bytes 1769480 | tf_op jit(solution)/shard_map/grad_weight/ppermute | solution.py:28
  107.2 1.4 %copy-start.6 = (f32[2,768,384]{2,1,0:T(8,128)}, f32[2,768,384]{2,1,0:T(8,128)S(1)}, u32[]{:S(2)}) copy-start(f32[2,768,384]{2,1,0:T(8,128)S(1)} %convert_add_fusion) | copy-start | bytes 7077892
  108.7 15.5 %collective-permute-start.5 = (bf16[768,384]{1,0:T(8,128)(2,1)S(1)}, bf16[768,384]{1,0:T(8,128)(2,1)S(1)}, u32[]{:S(2)}, u32[]{:S(2)}) collective-permute-start(bf16[768,384]{1,0:T(8,128)(2,1)S(1)} %fusion.11), channel_id=1, source_target_pairs={{0,16},{16,0},{1,17},{17,1},{2,18},{18,2},{3,19},{19,3},{4,20},{20... | collective-permute-start | bytes 1769480 | tf_op jit(solution)/shard_map/halo_reduction/ppermute | solution.py:33
  109.9 14.3 %copy-start.7 = (f32[2,768,384]{2,1,0:T(8,128)S(1)}, f32[2,768,384]{2,1,0:T(8,128)}, u32[]{:S(2)}) copy-start(f32[2,768,384]{2,1,0:T(8,128)} %copy-done.6) | copy-start | bytes 7077892
  113.3 11.9 %collective-permute-start.8 = (bf16[384,384]{0,1:T(8,128)(2,1)S(1)}, bf16[384,384]{0,1:T(8,128)(2,1)S(1)}, u32[]{:S(2)}, u32[]{:S(2)}) collective-permute-start(bf16[384,384]{0,1:T(8,128)(2,1)S(1)} %fusion.12), channel_id=1, source_target_pairs={{0,8},{4,12},{8,0},{12,4},{1,9},{5,13},{9,1},{13,5},{2,10},{6,14},... | collective-permute-start | bytes 884744 | tf_op jit(solution)/shard_map/grad_weight/ppermute | solution.py:28
Sparse Core Ops, SparseCore 0:
  9.6 52.5 all-gather.2
  65.0 46.7 reduce-scatter.1
